TPU v7x, 512 devices: a whole 4x8x8 slice. The times are simulated.
512 devices in a mesh: seq: 32 (over y, x), tp: 16 (over z, core).
Axes of the slice: x: 4, y: 8, z: 8, core: 2. Of those that a mesh axis runs over, the one named last changes fastest.
Arguments:
- segment_ids: int32 [8192], replicated, may hold values from 0 to 15, never falling along the last dimension, each value on 1 to 2048 neighbouring positions
- relayout: int32 [8192], replicated, may hold values from 0 to 8191, as said below
- queries: bfloat16 [8192, 4096], P('seq', 'tp'), may hold values from -8 to 8
- keys: bfloat16 [8192, 512], P(('seq', 'tp')), may hold values from -8 to 8
- values: bfloat16 [8192, 512], P(('seq', 'tp')), may hold values from -18 to 18
- out_weight: bfloat16 [4096, 8192], P('tp'), may hold values from -0.09375 to 0.09375
Outputs:
- block_out: bfloat16 [8192, 8192], P(('seq', 'tp'))
Inputs may be any that keep to these rules, and one draw needn't show every extreme that they name: relayout is a permutation; of the 256 tokens in each aligned block of 256 initial positions exactly 8 land in each aligned block of 256 new positions.
All inputs are finite; a program needn't handle non-finite values.
Results may differ from a plain program's by a relative error of at most 0.017.
Values may be sent and summed in bfloat16 or wider, within the bound.
No kernel may reach another device: no remote copies, remote signals or barrier semaphores. Data moves between devices by JAX's collectives and lax.ppermute only.
A program may use at most 64 MiB of HBM per device.

v0:
```python
import jax
import jax.numpy as jnp
from jax import lax
from jax.sharding import PartitionSpec as P

QH = 32
KVH = 4
HD = 128


def shards(segment_ids, relayout, queries, keys, values, out_weight):
    rows_here = queries.shape[0]
    seq_count = lax.axis_size("seq")
    seq_index = lax.axis_index("seq")
    tp_index = lax.axis_index("tp")
    total_rows = rows_here * seq_count
    heads_here = queries.shape[1] // HD
    group = QH // KVH
    shared_here = max(1, heads_here // group)
    per_shared = heads_here // shared_here
    scale = HD ** (-0.5)
    all_keys, all_values = (
        lax.all_gather(keys, "tp", axis=0, tiled=True),
        lax.all_gather(values, "tp", axis=0, tiled=True),
    )
    first_head = tp_index * heads_here // group
    own_keys = lax.dynamic_slice_in_dim(all_keys, first_head * HD, shared_here * HD, 1)
    own_values = lax.dynamic_slice_in_dim(all_values, first_head * HD, shared_here * HD, 1)
    own_pair = jnp.stack([own_keys, own_values])
    row_ids = jnp.arange(rows_here, dtype=jnp.int32)
    inverse = (
        jnp.zeros((total_rows,), jnp.int32)
        .at[relayout]
        .set(jnp.arange(total_rows, dtype=jnp.int32))
    )
    new_here = seq_index * rows_here + row_ids
    old_here = seq_index * rows_here + row_ids
    source_block = relayout[new_here] // rows_here
    arrival = jnp.argsort(source_block * total_rows + new_here)
    send_order = jnp.argsort(inverse[old_here])
    arrived = lax.all_to_all(queries[send_order], "seq", split_axis=0, concat_axis=0, tiled=True)
    query_pos = relayout[seq_index * rows_here + arrival]
    query_seg = segment_ids[query_pos]
    pieces = lax.all_gather(own_pair, "seq", axis=1, tiled=True)
    count = pieces.shape[1]
    key_pos = jnp.arange(count, dtype=jnp.int32)
    live = (
        (key_pos[None, :] <= query_pos[:, None])
        & (segment_ids[None, :] == query_seg[:, None])
        & (jnp.int32(0) >= 0)
    )
    query_split = arrived.reshape(rows_here, shared_here, per_shared, HD)
    key_split = pieces[0].reshape(count, shared_here, HD)
    value_split = pieces[1].reshape(count, shared_here, HD)
    scores = (
        jnp.einsum("qngd,knd->ngqk", query_split, key_split, preferred_element_type=jnp.float32)
        * scale
    )
    masked = jnp.where(live, scores, jnp.float32(-1e30))
    peak = jnp.full((shared_here, per_shared, rows_here), -1e30, jnp.float32)
    new_peak = jnp.maximum(peak, jnp.max(masked, axis=-1))
    expo = jnp.where(live, jnp.exp(masked - new_peak[..., None]), jnp.float32(0.0))
    denom = jnp.sum(expo, axis=-1)
    update = jnp.einsum(
        "ngqk,knd->ngqd", expo.astype(jnp.bfloat16), value_split, preferred_element_type=jnp.float32
    )
    attn = update / denom[..., None]
    attn_rows = (
        jnp.transpose(attn, (2, 0, 1, 3)).reshape(rows_here, heads_here * HD).astype(jnp.bfloat16)
    )
    attn_new = jnp.zeros_like(attn_rows).at[arrival].set(attn_rows)
    return lax.psum_scatter(
        jnp.dot(attn_new, out_weight, preferred_element_type=jnp.float32).astype(jnp.bfloat16),
        "tp",
        scatter_dimension=0,
        tiled=True,
    )


def solution(mesh):
    return jax.shard_map(
        shards,
        mesh=mesh,
        in_specs=(
            P(),
            P(),
            P("seq", "tp"),
            P(("seq", "tp"), None),
            P(("seq", "tp"), None),
            P("tp", None),
        ),
        out_specs=P(("seq", "tp"), None),
        check_vma=False,
    )
```

profile of v0, /device:TPU:6, one launch (start us, length us, event | category | flops | bytes accessed | tf_op | source)
XLA Modules:
  0.0 224.5 jit_solution(6411925314582195732)
XLA Ops:
  6.5 0.0 copy-start
  6.5 0.0 all-gather.2.cloned.1.call-start
  6.5 24.2 %all_gather.9 = bf16[256,512]{1,0:T(8,128)(2,1)S(1)} all-gather(bf16[16,512]{1,0:T(8,128)(2,1)} %param.9), channel_id=1, replica_groups=mesh['seq'=32,'tp'=16] {'tp'}, dimensions={0}, use_global_device_ids=true | all-gather | bytes 278528 | tf_op jit(solution)/shard_map/all_gather | solution.py:23
  30.8 15.4 %all_gather.10 = bf16[256,512]{1,0:T(8,128)(2,1)S(1)} all-gather(bf16[16,512]{1,0:T(8,128)(2,1)} %param.10), channel_id=1, replica_groups=mesh['seq'=32,'tp'=16] {'tp'}, dimensions={0}, use_global_device_ids=true | all-gather | bytes 278528 | tf_op jit(solution)/shard_map/all_gather | solution.py:24
  46.2 0.7 pad_maximum_fusion
  46.9 0.0 all-gather.2.cloned.1.call-update
  46.9 0.8 compare_select_fusion
  47.7 30.5 %scatter_custom_fusion = s32[8192]{0:T(1024)S(1)} fusion(s32[8192]{0:T(1024)S(1)} %compare_select_fusion, s32[8192]{0:T(1024)S(1)} %iota.23, s32[]{:T(128)} %constant.25.clone.1), kind=kCustom, calls=%fused_computation.30 | custom fusion | bytes 32772 | tf_op jit(solution)/shard_map/scatter | solution.py:34
  78.2 1.7 gather_fusion.3
  79.9 3.2 %sort.32 = (s32[256]{0:T(256)}, s32[256]{0:T(256)S(1)}) sort(s32[256]{0:T(256)S(1)} %gather_fusion.3, s32[256]{0:T(256)S(1)} %iota.24), dimensions={0}, to_apply=%region_2.3 | sort | flops 2048 | bytes 4096 | tf_op jit(solution)/shard_map/jit(argsort)/sort | solution.py:40
  83.1 0.0 copy-done
  83.1 1.8 gather_fusion.4
  84.9 10.2 %all-to-all-start = ((bf16[32,8,256]{2,1,0:T(8,128)(2,1)}), bf16[32,8,256]{2,1,0:T(8,128)(2,1)S(1)}, u32[]{:S(2)}, u32[]{:S(2)}) async-start(bf16[32,8,256]{2,1,0:T(8,128)(2,1)} %bitcast.7), calls=%async_computation | async-start | bytes 262144 | tf_op jit(solution)/shard_map/all_to_all | solution.py:41
  95.1 0.2 reduce-scatter.2.cloned.1.call-start
  95.4 2.0 gather_fusion
  97.4 3.1 %sort.31 = (s32[256]{0:T(256)}, s32[256]{0:T(256)S(1)}) sort(s32[256]{0:T(256)S(1)} %add_add_fusion, s32[256]{0:T(256)S(1)} %iota.22), dimensions={0}, to_apply=%region_0.1 | sort | flops 2048 | bytes 4096 | tf_op jit(solution)/shard_map/jit(argsort)/sort | solution.py:39
  100.5 2.0 gather_fusion.1
  102.6 2.0 gather_fusion.2
  104.6 4.3 %fusion.6 = pred[256,8192]{0,1:T(8,128)(4,1)S(1)} fusion(s32[256]{0:T(256)S(1)} %gather_fusion.2, s32[256]{0:T(256)S(1)} %gather_fusion.1, s32[8192]{0:T(1024)} %param.6), kind=kLoop, calls=%fused_computation.16 | loop fusion | flops 6291456 | bytes 2131968 | tf_op jit(solution)/shard_map/and | solution.py:48
  108.9 0.0 all-to-all-done
  108.9 22.0 %all-gather.2.cloned.1.call-done = bf16[2,8192,128]{2,1,0:T(8,128)(2,1)} async-done(((bf16[2,256,128]{2,1,0:T(8,128)(2,1)}), bf16[2,8192,128]{2,1,0:T(8,128)(2,1)}) %all-gather.2.cloned.1.call-update) | async-done | bytes 4194320 | tf_op jit(solution)/shard_map/all_gather | solution.py:44
  130.9 4.4 %fusion = (f32[2,256]{1,0:T(2,128)S(1)}, f32[8192,256,2]{1,0,2:T(8,128)S(1)}) fusion(pred[256,8192]{0,1:T(8,128)(4,1)S(1)} %fusion.6, bf16[256,2,128]{2,1,0:T(2,128)(2,1)S(1)} %reshape.74, bf16[2,8192,128]{2,1,0:T(8,128)(2,1)} %all-gather.2.cloned.1.call-done), kind=kOutput, calls=%fused_computation.9 | convolution fusion | flops 1086324224 | bytes 21104640 | tf_op jit(solution)/shard_map/qngd,knd->ngqk/dot_general | solution.py:56
  135.4 4.5 %fusion.1 = f32[2,256]{1,0:T(2,128)S(1)} fusion(f32[8192,256,2]{1,0,2:T(8,128)S(1)} %get-tuple-element.12, f32[2,256]{1,0:T(2,128)S(1)} %broadcast_maximum_fusion, pred[256,8192]{0,1:T(8,128)(4,1)S(1)} %fusion.6), kind=kLoop, calls=%fused_computation.10 | loop fusion | flops 20971008 | bytes 18878464 | tf_op jit(solution)/shard_map/reduce_sum | solution.py:63
  139.8 5.7 %fusion.12 = bf16[2,256,128]{1,2,0:T(8,128)(2,1)S(1)} fusion(bf16[2,8192,128]{2,1,0:T(8,128)(2,1)} %all-gather.2.cloned.1.call-done, f32[8192,256,2]{1,0,2:T(8,128)S(1)} %get-tuple-element.12, f32[2,256]{1,0:T(2,128)S(1)} %broadcast_maximum_fusion, pred[256,8192]{0,1:T(8,128)(4,1)S(1)} %fusion.6, f32[2,256]{1,0:T(2,128)S(1)} %fusion.1), kind=kOutput, calls=%fused_computation.22 | convolution fusion | flops 1094844416 | bytes 21106688 | tf_op jit(solution)/shard_map/ngqk,knd->ngqd/dot_general | solution.py:64
  145.6 0.1 copy.12
  145.7 1.5 scatter_custom_fusion.1
  147.2 5.4 %convolution_convert_fusion = bf16[256,8192]{1,0:T(8,128)(2,1)} fusion(bf16[256,256]{1,0:T(8,128)(2,1)S(1)} %scatter_custom_fusion.1, bf16[256,8192]{1,0:T(8,128)(2,1)} %param.11), kind=kOutput, calls=%fused_computation.12 | convolution fusion | flops 1075838976 | bytes 8519680 | tf_op jit(solution)/shard_map/dot_general | solution.py:73
  152.5 0.0 reduce-scatter.2.cloned.1.call-update
  152.6 65.1 %reduce-scatter.2.cloned.1.call-done = bf16[16,8192]{1,0:T(8,128)(2,1)} async-done(((bf16[256,8192]{1,0:T(8,128)(2,1)}), bf16[16,8192]{1,0:T(8,128)(2,1)}) %reduce-scatter.2.cloned.1.call-update) | async-done | bytes 262160 | tf_op jit(solution)/shard_map/reduce_scatter | solution.py:72
  (16 shorter events, 0.1 us)
Async XLA Ops:
  6.5 76.6 %copy-start = (bf16[256,256]{1,0:T(8,128)(2,1)S(1)}, bf16[256,256]{1,0:T(8,128)(2,1)}, u32[]{:S(2)}) copy-start(bf16[256,256]{1,0:T(8,128)(2,1)} %param.8) | copy-start | bytes 393220
  6.5 124.4 %all-gather.2.cloned.1.call-start = ((), (), s32[]{:S(2)}) async-start(), calls=%async_computation.2 | async-start | bytes 4325376 | tf_op jit(solution)/shard_map/all_gather | solution.py:44
  84.9 23.9 %all-to-all-start = ((bf16[32,8,256]{2,1,0:T(8,128)(2,1)}), bf16[32,8,256]{2,1,0:T(8,128)(2,1)S(1)}, u32[]{:S(2)}, u32[]{:S(2)}) async-start(bf16[32,8,256]{2,1,0:T(8,128)(2,1)} %bitcast.7), calls=%async_computation | async-start | bytes 262144 | tf_op jit(solution)/shard_map/all_to_all | solution.py:41
  95.1 122.6 %reduce-scatter.2.cloned.1.call-start = ((), (), s32[]{:S(2)}) async-start(), calls=%async_computation.3 | async-start | bytes 4456448 | tf_op jit(solution)/shard_map/reduce_scatter | solution.py:72
Sparse Core Ops, SparseCore 0:
  47.0 83.8 all-gather.1
  152.7 64.9 reduce-scatter.1
where the time goes:
time: 226 us; the launch traced here: 225 us
  waiting for transfers between devices  87.2 us (39%)
  local copies, waits for them, and re-layouts  41.7 us (18%)
  blocking collectives  39.6 us (18%)
  other arithmetic  16.6 us (7%)
  matrix products  15.5 us (7%)
  between operations  13.5 us (6%)
  starting transfers between devices  10.4 us (5%)
    reduce_scatter x1, waiting for transfers between devices, shards(): lax.psum_scatter(jnp.dot(attn_new, out_weight, preferred_element_type=jnp...  65.1 us
    scatter x1, local copies, waits for them, and re-layouts, shards(): inverse = jnp.zeros((total_rows,), jnp.int32).at[relayout].set(jnp.arange...  30.5 us
    all_gather x1, blocking collectives, shards(): lax.all_gather(keys, 'tp', axis=0, tiled=True)  24.2 us
    all_gather x1, waiting for transfers between devices, shards(): pieces = lax.all_gather(own_pair, 'seq', axis=1, tiled=True)  22 us
    all_gather x1, blocking collectives, shards(): lax.all_gather(values, 'tp', axis=0, tiled=True)  15.4 us
    all_to_all x1, starting transfers between devices, shards(): lax.all_to_all(queries[send_order], 'seq', split_axis=0, concat_axis=0, t...  10.2 us
    dot_general x1, matrix products, shards(): jnp.einsum('ngqk,knd->ngqd', expo.astype(jnp.bfloat16), value_split, pref...  5.7 us
    dot_general x1, matrix products, shards(): jnp.dot(attn_new, out_weight, preferred_element_type=jnp.float32)  5.38 us
  transfers between devices with their start and end apart: 3, of which 2 were waited for; matrix products, arithmetic and copies ran while one was open for 23% of the time, Pallas kernels for 0%

commit v1 on v0

v1 whole, which is shorter than its diff:
```python
import jax
import jax.numpy as jnp
import numpy as np
from jax import lax
from jax.sharding import Mesh
from jax.sharding import PartitionSpec as P

QH = 32
KVH = 4
HD = 128
MOST_LEN = 2048


def shards(segment_ids, relayout, queries, keys, values, out_weight):
    rows = queries.shape[0]
    n_seq = lax.axis_size("seq")
    n_z = lax.axis_size("z")
    n_core = lax.axis_size("core")
    s = lax.axis_index("seq")
    t = lax.axis_index("z") * n_core + lax.axis_index("core")
    heads_here = queries.shape[1] // HD
    group = QH // KVH
    kv_width = keys.shape[1]
    scale = HD ** (-0.5)
    back = -(-(MOST_LEN - 1) // rows)
    back = min(back, n_seq - 1)

    kv = jnp.concatenate([keys, values], axis=1)
    kv_block = lax.all_gather(kv, ("z", "core"), axis=0, tiled=True)
    g = t * heads_here // group
    own_k = lax.dynamic_slice_in_dim(kv_block, g * HD, HD, 1)
    own_v = lax.dynamic_slice_in_dim(kv_block, kv_width + g * HD, HD, 1)
    own = jnp.concatenate([own_k, own_v], axis=1)

    window = []
    for k in range(back, 0, -1):
        window.append(
            lax.ppermute(own, "seq", perm=[(i, i + k) for i in range(n_seq - k)])
        )
    window.append(own)
    kv_win = jnp.concatenate(window, axis=0)
    n_keys = kv_win.shape[0]
    k_win = kv_win[:, :HD]
    v_win = kv_win[:, HD:]

    q_pos = s * rows + jnp.arange(rows, dtype=jnp.int32)
    k_pos = (s - back) * rows + jnp.arange(n_keys, dtype=jnp.int32)
    q_seg = lax.dynamic_slice_in_dim(segment_ids, s * rows, rows, 0)
    k_seg = jnp.take(segment_ids, jnp.clip(k_pos, 0, segment_ids.shape[0] - 1))
    live = (
        (k_pos[None, :] <= q_pos[:, None])
        & (k_seg[None, :] == q_seg[:, None])
        & (k_pos[None, :] >= 0)
    )

    q = queries.reshape(rows, heads_here, HD)
    scores = jnp.einsum("qhd,kd->hqk", q, k_win, preferred_element_type=jnp.float32) * scale
    masked = jnp.where(live[None], scores, jnp.float32(-1e30))
    peak = jnp.max(masked, axis=-1)
    expo = jnp.where(live[None], jnp.exp(masked - peak[..., None]), jnp.float32(0.0))
    denom = jnp.sum(expo, axis=-1)
    summed = jnp.einsum(
        "hqk,kd->hqd", expo.astype(jnp.bfloat16), v_win, preferred_element_type=jnp.float32
    )
    attn = summed / denom[..., None]
    attn_rows = jnp.transpose(attn, (1, 0, 2)).reshape(rows, heads_here * HD).astype(jnp.bfloat16)

    chunk = rows // n_seq
    total = relayout.shape[0]
    here = s * rows + jnp.arange(rows, dtype=jnp.int32)
    new_of = jnp.sum(
        jnp.where(relayout[None, :] == here[:, None], jnp.arange(total, dtype=jnp.int32)[None, :], 0),
        axis=1,
    )
    rank = jnp.sum((new_of[None, :] < new_of[:, None]).astype(jnp.int32), axis=1)
    send_sel = (rank[None, :] == jnp.arange(rows, dtype=jnp.int32)[:, None]).astype(jnp.bfloat16)
    to_send = jnp.dot(send_sel, attn_rows, preferred_element_type=jnp.float32).astype(jnp.bfloat16)
    arrived = lax.all_to_all(to_send, "seq", split_axis=0, concat_axis=0, tiled=True)

    src = lax.dynamic_slice_in_dim(relayout, s * rows, rows, 0) // rows
    before = jnp.arange(rows)[None, :] < jnp.arange(rows)[:, None]
    nth = jnp.sum((before & (src[None, :] == src[:, None])).astype(jnp.int32), axis=1)
    slot = src * chunk + nth
    per_dev = rows // (n_z * n_core)
    r = jnp.arange(rows, dtype=jnp.int32)
    c_of = r // (n_z * per_dev)
    z_of = (r // per_dev) % n_z
    m_of = r % per_dev
    q_of = (z_of * n_core + c_of) * per_dev + m_of
    slot_of = jnp.take(slot, q_of)
    recv_sel = (slot_of[:, None] == jnp.arange(rows, dtype=jnp.int32)[None, :]).astype(jnp.bfloat16)
    relaid = jnp.dot(recv_sel, arrived, preferred_element_type=jnp.float32).astype(jnp.bfloat16)

    part = jnp.dot(relaid, out_weight, preferred_element_type=jnp.float32).astype(jnp.bfloat16)
    half = lax.psum_scatter(part, "core", scatter_dimension=0, tiled=True)
    return lax.psum_scatter(half, "z", scatter_dimension=0, tiled=True)


def solution(mesh):
    n_seq, n_tp = mesh.devices.shape
    mesh3 = Mesh(mesh.devices.reshape(n_seq, n_tp // 2, 2), ("seq", "z", "core"))
    tp = ("z", "core")
    return jax.shard_map(
        shards,
        mesh=mesh3,
        in_specs=(
            P(),
            P(),
            P("seq", tp),
            P(("seq",) + tp, None),
            P(("seq",) + tp, None),
            P(tp, None),
        ),
        out_specs=P(("seq",) + tp, None),
        check_vma=False,
    )
```

time: 226 us -> 190 us (0.84)
  starting transfers between devices: 10.4 us -> 45.5 us
  local copies, waits for them, and re-layouts: 41.7 us -> 15.1 us
  blocking collectives: 39.6 us -> 24.6 us
  waiting for transfers between devices: 87.2 us -> 72.7 us
  other arithmetic: 16.6 us -> 7 us
  matrix products: 15.5 us -> 11 us
    ppermute x0 -> x8, starting transfers between devices: none -> 35 us  [shards(): lax.ppermute(own, 'seq', perm=[(i, i + k) for i in range(n_seq - k)])]
    scatter x2 -> x0, local copies, waits for them, and re-layouts: 32 us -> none  [the longest x1 30.5 us: shards(): inverse = jnp.zeros((total_rows,), jnp.int32).at[relayout].set(jnp.arange...]
    all_gather x1 -> x0, waiting for transfers between devices: 22 us -> none  [shards(): pieces = lax.all_gather(own_pair, 'seq', axis=1, tiled=True)]
    all_gather x2 -> x1, blocking collectives: 39.6 us -> 24.6 us  [shards(): kv_block = lax.all_gather(kv, ('z', 'core'), axis=0, tiled=True)]
    all_to_all x1, waiting for transfers between devices: 0.01 us -> 6.84 us  [shards(): lax.all_to_all(to_send, 'seq', split_axis=0, concat_axis=0, tiled=True)]
    dot_general x3, matrix products: 15.5 us -> 8.78 us  [the longest x1 5.52 us: shards(): jnp.dot(relaid, out_weight, preferred_element_type=jnp.float32)]
    sort x2 -> x0, other arithmetic: 6.32 us -> none  [the longest x1 3.17 us: shards(): send_order = jnp.argsort(inverse[old_here])]
    gather x5 -> x2, local copies, waits for them, and re-layouts: 9.52 us -> 14.3 us  [the longest x1 12.3 us: shards(): k_seg = jnp.take(segment_ids, jnp.clip(k_pos, 0, segment_ids.shape[0] - 1))]
  transfers between devices with their start and end apart: 3 -> 11, of which waited for: 2 -> 5; matrix products, arithmetic and copies ran while one was open for 23% -> 11% of each run, Pallas kernels for 0% -> 0%
where the time goes in v1:
time: 190 us
  waiting for transfers between devices  72.7 us (38%)
  starting transfers between devices  45.5 us (24%)
  blocking collectives  24.6 us (13%)
  local copies, waits for them, and re-layouts  15.1 us (8%)
  between operations  13.7 us (7%)
  matrix products  11 us (6%)
  other arithmetic  7 us (4%)
    reduce_scatter x1, waiting for transfers between devices, shards(): return lax.psum_scatter(half, 'z', scatter_dimension=0, tiled=True)  50 us
    ppermute x8, starting transfers between devices, shards(): lax.ppermute(own, 'seq', perm=[(i, i + k) for i in range(n_seq - k)])  35 us
    all_gather x1, blocking collectives, shards(): kv_block = lax.all_gather(kv, ('z', 'core'), axis=0, tiled=True)  24.6 us
    reduce_scatter x1, waiting for transfers between devices, shards(): half = lax.psum_scatter(part, 'core', scatter_dimension=0, tiled=True)  12.3 us
    gather x1, local copies, waits for them, and re-layouts, shards(): k_seg = jnp.take(segment_ids, jnp.clip(k_pos, 0, segment_ids.shape[0] - 1))  12.3 us
    all_to_all x1, starting transfers between devices, shards(): lax.all_to_all(to_send, 'seq', split_axis=0, concat_axis=0, tiled=True)  10.4 us
    all_to_all x1, waiting for transfers between devices, shards(): lax.all_to_all(to_send, 'seq', split_axis=0, concat_axis=0, tiled=True)  6.84 us
    dot_general x1, matrix products, shards(): jnp.dot(relaid, out_weight, preferred_element_type=jnp.float32)  5.52 us
  transfers between devices with their start and end apart: 11, of which 5 were waited for; matrix products, arithmetic and copies ran while one was open for 11% of the time, Pallas kernels for 0%

profile of v1, /device:TPU:6, one launch (start us, length us, event | category | flops | bytes accessed | tf_op | source)
XLA Modules:
  0.0 189.7 jit_solution(11085602571010933191)
XLA Ops:
  6.5 0.8 pad_maximum_fusion.1
  7.3 24.6 %all_gather.3 = bf16[256,1024]{1,0:T(8,128)(2,1)S(1)} all-gather(bf16[16,1024]{1,0:T(8,128)(2,1)S(1)} %pad_maximum_fusion.1), channel_id=1, replica_groups=mesh['seq'=32,'z'=8,'core'=2] {'z','core'}, dimensions={0}, use_global_device_ids=true | all-gather | bytes 557056 | tf_op jit(solution)/shard_map/all_gather | solution.py:29
  32.0 3.4 %collective-permute-start.7 = (bf16[256,256]{1,0:T(8,128)(2,1)S(1)}, bf16[256,256]{1,0:T(8,128)(2,1)S(1)}, u32[]{:S(2)}, u32[]{:S(2)}) collective-permute-start(bf16[256,256]{1,0:T(8,128)(2,1)S(1)} %pad_maximum_fusion), channel_id=1, source_target_pairs={{0,16},{16,32},{32,48},{48,64},{64,80},{80,96},{96,112},{112,128},... | collective-permute-start | bytes 393224 | tf_op jit(solution)/shard_map/ppermute | solution.py:38
  35.4 4.3 %collective-permute-start.6 = (bf16[256,256]{1,0:T(8,128)(2,1)S(1)}, bf16[256,256]{1,0:T(8,128)(2,1)S(1)}, u32[]{:S(2)}, u32[]{:S(2)}) collective-permute-start(bf16[256,256]{1,0:T(8,128)(2,1)S(1)} %pad_maximum_fusion), channel_id=1, source_target_pairs={{0,32},{16,48},{32,64},{48,80},{64,96},{80,112},{96,128},{112,144}... | collective-permute-start | bytes 393224 | tf_op jit(solution)/shard_map/ppermute | solution.py:38
  39.7 2.9 %collective-permute-start.5 = (bf16[256,256]{1,0:T(8,128)(2,1)S(1)}, bf16[256,256]{1,0:T(8,128)(2,1)S(1)}, u32[]{:S(2)}, u32[]{:S(2)}) collective-permute-start(bf16[256,256]{1,0:T(8,128)(2,1)S(1)} %pad_maximum_fusion), channel_id=1, source_target_pairs={{0,48},{16,64},{32,80},{48,96},{64,112},{80,128},{96,144},{112,160... | collective-permute-start | bytes 393224 | tf_op jit(solution)/shard_map/ppermute | solution.py:38
  42.6 6.3 %collective-permute-start.1 = (bf16[256,256]{1,0:T(8,128)(2,1)S(1)}, bf16[256,256]{1,0:T(8,128)(2,1)S(1)}, u32[]{:S(2)}, u32[]{:S(2)}) collective-permute-start(bf16[256,256]{1,0:T(8,128)(2,1)S(1)} %pad_maximum_fusion), channel_id=1, source_target_pairs={{0,112},{16,128},{32,144},{48,160},{64,176},{80,192},{96,208},{112... | collective-permute-start | bytes 393224 | tf_op jit(solution)/shard_map/ppermute | solution.py:38
  48.9 2.7 %collective-permute-start = (bf16[256,256]{1,0:T(8,128)(2,1)S(1)}, bf16[256,256]{1,0:T(8,128)(2,1)S(1)}, u32[]{:S(2)}, u32[]{:S(2)}) collective-permute-start(bf16[256,256]{1,0:T(8,128)(2,1)S(1)} %pad_maximum_fusion), channel_id=1, source_target_pairs={{0,128},{16,144},{32,160},{48,176},{64,192},{80,208},{96,224},{112... | collective-permute-start | bytes 393224 | tf_op jit(solution)/shard_map/ppermute | solution.py:38
  51.6 2.0 %select_reduce_fusion = s32[256]{0:T(256)S(1)} fusion(s32[8192]{0:T(1024)} %param.7, s32[256]{0:T(256)S(1)} %iota_add_fusion.1), kind=kLoop, calls=%fused_computation.4 | loop fusion | flops 6291200 | bytes 34816 | tf_op jit(solution)/shard_map/reduce_sum | solution.py:71
  53.6 0.8 and_select_fusion.5
  54.4 0.8 dynamic_slice.13
  55.2 0.2 convert_reduce_fusion.1
  55.4 0.8 multiply_add_fusion
  56.2 12.3 %gather_fusion.1 = s32[2304]{0:T(1024)S(1)} fusion(s32[8192]{0:T(1024)S(1)} %copy-done.1, s32[3072]{0:T(1024)S(1)} %pad_clamp_fusion), kind=kCustom, calls=%fused_computation.1 | custom fusion | bytes 27648 | tf_op jit(solution)/shard_map/jit(_take)/gather | solution.py:49
  68.5 2.2 %and_and_fusion = pred[256,2304]{0,1:T(8,128)(4,1)S(1)} fusion(s32[256]{0:T(256)S(1)} %dynamic_slice.13, s32[256]{0:T(256)S(1)} %iota_add_fusion.1, s32[2304]{0:T(1024)S(1)} %get-tuple-element.8, s32[2304]{0:T(1024)S(1)} %get-tuple-element.7, pred[2304]{0:T(1024)(128)(4,1)S(1)} %fusion.32), kind=kLoop, calls=%fused_computation.13 | loop fusion | flops 2359296 | bytes 612608 | tf_op jit(solution)/shard_map/and | solution.py:51
  70.7 0.2 convert_reduce_fusion
  70.9 5.7 %collective-permute-start.2 = (bf16[256,256]{1,0:T(8,128)(2,1)S(1)}, bf16[256,256]{1,0:T(8,128)(2,1)S(1)}, u32[]{:S(2)}, u32[]{:S(2)}) collective-permute-start(bf16[256,256]{1,0:T(8,128)(2,1)S(1)} %pad_maximum_fusion), channel_id=1, source_target_pairs={{0,96},{16,112},{32,128},{48,144},{64,160},{80,176},{96,192},{112,... | collective-permute-start | bytes 393224 | tf_op jit(solution)/shard_map/ppermute | solution.py:38
  76.6 2.4 %collective-permute-start.3 = (bf16[256,256]{1,0:T(8,128)(2,1)S(1)}, bf16[256,256]{1,0:T(8,128)(2,1)S(1)}, u32[]{:S(2)}, u32[]{:S(2)}) collective-permute-start(bf16[256,256]{1,0:T(8,128)(2,1)S(1)} %pad_maximum_fusion), channel_id=1, source_target_pairs={{0,80},{16,96},{32,112},{48,128},{64,144},{80,160},{96,176},{112,1... | collective-permute-start | bytes 393224 | tf_op jit(solution)/shard_map/ppermute | solution.py:38
  79.0 1.0 collective-permute-done.2
  80.1 7.4 %collective-permute-start.4 = (bf16[256,256]{1,0:T(8,128)(2,1)S(1)}, bf16[256,256]{1,0:T(8,128)(2,1)S(1)}, u32[]{:S(2)}, u32[]{:S(2)}) collective-permute-start(bf16[256,256]{1,0:T(8,128)(2,1)S(1)} %pad_maximum_fusion), channel_id=1, source_target_pairs={{0,64},{16,80},{32,96},{48,112},{64,128},{80,144},{96,160},{112,17... | collective-permute-start | bytes 393224 | tf_op jit(solution)/shard_map/ppermute | solution.py:38
  87.5 2.4 %collective-permute-done.4 = bf16[256,256]{1,0:T(8,128)(2,1)S(1)} collective-permute-done((bf16[256,256]{1,0:T(8,128)(2,1)S(1)}, bf16[256,256]{1,0:T(8,128)(2,1)S(1)}, u32[]{:S(2)}, u32[]{:S(2)}) %collective-permute-start.4) | collective-permute-done | bytes 131104 | tf_op jit(solution)/shard_map/ppermute | solution.py:38
  90.1 2.3 %fusion.58 = f32[2,256]{1,0:T(2,128)S(1)} fusion(pred[256,2304]{0,1:T(8,128)(4,1)S(1)} %and_and_fusion, bf16[2304,256]{1,0:T(8,128)(2,1)S(1)} %constant_dynamic-update-slice_fusion, bf16[256,256]{1,0:T(8,128)(2,1)S(1)} %copy-done), kind=kOutput, calls=%fused_computation.105 | convolution fusion | flops 307890432 | bytes 1902592 | tf_op jit(solution)/shard_map/sub | solution.py:60
  92.4 2.4 %fusion.14 = bf16[256,2,128]{0,2,1:T(8,128)(2,1)S(1)} fusion(bf16[2304,256]{1,0:T(8,128)(2,1)S(1)} %constant_dynamic-update-slice_fusion, f32[256,2]{0,1:T(2,128)S(1)} %bitcast.72, pred[256,2304]{0,1:T(8,128)(4,1)S(1)} %and_and_fusion, bf16[256,256]{1,0:T(8,128)(2,1)S(1)} %copy-done), kind=kOutput, calls=%fused_computation.18 | convolution fusion | flops 610011904 | bytes 2623488 | tf_op jit(solution)/shard_map/hqk,kd->hqd/dot_general | solution.py:62
  94.7 0.9 fusion.17
  95.6 10.4 %all-to-all-start = ((bf16[32,8,256]{2,1,0:T(8,128)(2,1)}), bf16[32,8,256]{2,1,0:T(8,128)(2,1)S(1)}, u32[]{:S(2)}, u32[]{:S(2)}) async-start(bf16[32,8,256]{2,1,0:T(8,128)(2,1)} %fusion.17), calls=%async_computation | async-start | bytes 262144 | tf_op jit(solution)/shard_map/all_to_all | solution.py:78
  106.0 0.0 reduce-scatter.3.cloned.1.call-start
  106.1 1.9 %gather_fusion = s32[256]{0:T(256)S(1)} fusion(s32[256]{0:T(256)S(1)} %multiply_add_fusion, s32[1024]{0:T(1024)S(1)} %pad_clamp_fusion.1), kind=kCustom, calls=%fused_computation | custom fusion | bytes 3072 | tf_op jit(solution)/shard_map/jit(_take)/gather | solution.py:90
  108.0 6.8 %all-to-all-done = bf16[32,8,256]{2,1,0:T(8,128)(2,1)S(1)} async-done(((bf16[32,8,256]{2,1,0:T(8,128)(2,1)}), bf16[32,8,256]{2,1,0:T(8,128)(2,1)S(1)}, u32[]{:S(2)}, u32[]{:S(2)}) %all-to-all-start) | async-done | bytes 131104 | tf_op jit(solution)/shard_map/all_to_all | solution.py:78
  114.9 5.5 %convolution_convert_fusion = bf16[256,8192]{1,0:T(8,128)(2,1)} fusion(bf16[256,8192]{1,0:T(8,128)(2,1)} %param.11, bf16[32,8,256]{2,1,0:T(8,128)(2,1)S(1)} %all-to-all-done, s32[256]{0:T(256)S(1)} %and_select_fusion.6), kind=kOutput, calls=%fused_computation.3 | convolution fusion | flops 1109524480 | bytes 8520704 | tf_op jit(solution)/shard_map/dot_general | solution.py:94
  120.4 0.0 reduce-scatter.3.cloned.1.call-update
  120.4 0.0 reduce-scatter.5.cloned.1.call-start
  120.5 12.3 %reduce-scatter.3.cloned.1.call-done = bf16[128,8192]{1,0:T(8,128)(2,1)} async-done(((bf16[256,8192]{1,0:T(8,128)(2,1)}), bf16[128,8192]{1,0:T(8,128)(2,1)}) %reduce-scatter.3.cloned.1.call-update) | async-done | bytes 2097168 | tf_op jit(solution)/shard_map/reduce_scatter | solution.py:95
  132.8 50.0 %reduce-scatter.5.cloned.1.call-done = bf16[16,8192]{1,0:T(8,128)(2,1)} async-done(((bf16[128,8192]{1,0:T(8,128)(2,1)}), bf16[16,8192]{1,0:T(8,128)(2,1)}) %reduce-scatter.5.cloned.1.call-update) | async-done | bytes 262160 | tf_op jit(solution)/shard_map/reduce_scatter | solution.py:96
  (30 shorter events, 0.3 us)
Async XLA Ops:
  6.5 83.6 %copy-start = (bf16[256,256]{1,0:T(8,128)(2,1)S(1)}, bf16[256,256]{1,0:T(8,128)(2,1)}, u32[]{:S(2)}) copy-start(bf16[256,256]{1,0:T(8,128)(2,1)} %param.8) | copy-start | bytes 393220
  6.5 49.6 %copy-start.1 = (s32[8192]{0:T(1024)S(1)}, s32[8192]{0:T(1024)}, u32[]{:S(2)}) copy-start(s32[8192]{0:T(1024)} %param.6) | copy-start | bytes 98308
  32.0 58.1 %collective-permute-start.7 = (bf16[256,256]{1,0:T(8,128)(2,1)S(1)}, bf16[256,256]{1,0:T(8,128)(2,1)S(1)}, u32[]{:S(2)}, u32[]{:S(2)}) collective-permute-start(bf16[256,256]{1,0:T(8,128)(2,1)S(1)} %pad_maximum_fusion), channel_id=1, source_target_pairs={{0,16},{16,32},{32,48},{48,64},{64,80},{80,96},{96,112},{112,128},... | collective-permute-start | bytes 393224 | tf_op jit(solution)/shard_map/ppermute | solution.py:38
  35.4 54.6 %collective-permute-start.6 = (bf16[256,256]{1,0:T(8,128)(2,1)S(1)}, bf16[256,256]{1,0:T(8,128)(2,1)S(1)}, u32[]{:S(2)}, u32[]{:S(2)}) collective-permute-start(bf16[256,256]{1,0:T(8,128)(2,1)S(1)} %pad_maximum_fusion), channel_id=1, source_target_pairs={{0,32},{16,48},{32,64},{48,80},{64,96},{80,112},{96,128},{112,144}... | collective-permute-start | bytes 393224 | tf_op jit(solution)/shard_map/ppermute | solution.py:38
  39.7 50.3 %collective-permute-start.5 = (bf16[256,256]{1,0:T(8,128)(2,1)S(1)}, bf16[256,256]{1,0:T(8,128)(2,1)S(1)}, u32[]{:S(2)}, u32[]{:S(2)}) collective-permute-start(bf16[256,256]{1,0:T(8,128)(2,1)S(1)} %pad_maximum_fusion), channel_id=1, source_target_pairs={{0,48},{16,64},{32,80},{48,96},{64,112},{80,128},{96,144},{112,160... | collective-permute-start | bytes 393224 | tf_op jit(solution)/shard_map/ppermute | solution.py:38
  42.6 34.0 %collective-permute-start.1 = (bf16[256,256]{1,0:T(8,128)(2,1)S(1)}, bf16[256,256]{1,0:T(8,128)(2,1)S(1)}, u32[]{:S(2)}, u32[]{:S(2)}) collective-permute-start(bf16[256,256]{1,0:T(8,128)(2,1)S(1)} %pad_maximum_fusion), channel_id=1, source_target_pairs={{0,112},{16,128},{32,144},{48,160},{64,176},{80,192},{96,208},{112... | collective-permute-start | bytes 393224 | tf_op jit(solution)/shard_map/ppermute | solution.py:38
  48.9 22.0 %collective-permute-start = (bf16[256,256]{1,0:T(8,128)(2,1)S(1)}, bf16[256,256]{1,0:T(8,128)(2,1)S(1)}, u32[]{:S(2)}, u32[]{:S(2)}) collective-permute-start(bf16[256,256]{1,0:T(8,128)(2,1)S(1)} %pad_maximum_fusion), channel_id=1, source_target_pairs={{0,128},{16,144},{32,160},{48,176},{64,192},{80,208},{96,224},{112... | collective-permute-start | bytes 393224 | tf_op jit(solution)/shard_map/ppermute | solution.py:38
  70.9 9.2 %collective-permute-start.2 = (bf16[256,256]{1,0:T(8,128)(2,1)S(1)}, bf16[256,256]{1,0:T(8,128)(2,1)S(1)}, u32[]{:S(2)}, u32[]{:S(2)}) collective-permute-start(bf16[256,256]{1,0:T(8,128)(2,1)S(1)} %pad_maximum_fusion), channel_id=1, source_target_pairs={{0,96},{16,112},{32,128},{48,144},{64,160},{80,176},{96,192},{112,... | collective-permute-start | bytes 393224 | tf_op jit(solution)/shard_map/ppermute | solution.py:38
  76.6 10.9 %collective-permute-start.3 = (bf16[256,256]{1,0:T(8,128)(2,1)S(1)}, bf16[256,256]{1,0:T(8,128)(2,1)S(1)}, u32[]{:S(2)}, u32[]{:S(2)}) collective-permute-start(bf16[256,256]{1,0:T(8,128)(2,1)S(1)} %pad_maximum_fusion), channel_id=1, source_target_pairs={{0,80},{16,96},{32,112},{48,128},{64,144},{80,160},{96,176},{112,1... | collective-permute-start | bytes 393224 | tf_op jit(solution)/shard_map/ppermute | solution.py:38
  80.1 9.9 %collective-permute-start.4 = (bf16[256,256]{1,0:T(8,128)(2,1)S(1)}, bf16[256,256]{1,0:T(8,128)(2,1)S(1)}, u32[]{:S(2)}, u32[]{:S(2)}) collective-permute-start(bf16[256,256]{1,0:T(8,128)(2,1)S(1)} %pad_maximum_fusion), channel_id=1, source_target_pairs={{0,64},{16,80},{32,96},{48,112},{64,128},{80,144},{96,160},{112,17... | collective-permute-start | bytes 393224 | tf_op jit(solution)/shard_map/ppermute | solution.py:38
  95.6 19.3 %all-to-all-start = ((bf16[32,8,256]{2,1,0:T(8,128)(2,1)}), bf16[32,8,256]{2,1,0:T(8,128)(2,1)S(1)}, u32[]{:S(2)}, u32[]{:S(2)}) async-start(bf16[32,8,256]{2,1,0:T(8,128)(2,1)} %fusion.17), calls=%async_computation | async-start | bytes 262144 | tf_op jit(solution)/shard_map/all_to_all | solution.py:78
  106.0 26.8 %reduce-scatter.3.cloned.1.call-start = ((), (), s32[]{:S(2)}) async-start(), calls=%async_computation.3 | async-start | bytes 6291456 | tf_op jit(solution)/shard_map/reduce_scatter | solution.py:95
  120.4 62.4 %reduce-scatter.5.cloned.1.call-start = ((), (), s32[]{:S(2)}) async-start(), calls=%async_computation.4 | async-start | bytes 2359296 | tf_op jit(solution)/shard_map/reduce_scatter | solution.py:96
Sparse Core Ops, SparseCore 0:
  120.5 12.1 reduce-scatter.2
  135.9 46.8 reduce-scatter.4

commit v2 on v1

--- a/solution.py
+++ b/solution.py
@@ -13,10 +13,10 @@
 
 def shards(segment_ids, relayout, queries, keys, values, out_weight):
     rows = queries.shape[0]
-    n_seq = lax.axis_size("seq")
+    n_seq = lax.axis_size("y") * lax.axis_size("x")
     n_z = lax.axis_size("z")
     n_core = lax.axis_size("core")
-    s = lax.axis_index("seq")
+    s = lax.axis_index("y") * lax.axis_size("x") + lax.axis_index("x")
     t = lax.axis_index("z") * n_core + lax.axis_index("core")
     heads_here = queries.shape[1] // HD
     group = QH // KVH
@@ -26,27 +26,34 @@
     back = min(back, n_seq - 1)
 
     kv = jnp.concatenate([keys, values], axis=1)
-    kv_block = lax.all_gather(kv, ("z", "core"), axis=0, tiled=True)
+    kv_pair = lax.all_gather(kv, "core", axis=0, tiled=True)
+    kv_block = lax.all_gather(kv_pair, "z", axis=0, tiled=True)
     g = t * heads_here // group
     own_k = lax.dynamic_slice_in_dim(kv_block, g * HD, HD, 1)
     own_v = lax.dynamic_slice_in_dim(kv_block, kv_width + g * HD, HD, 1)
     own = jnp.concatenate([own_k, own_v], axis=1)
 
+    n_x = lax.axis_size("x")
+    n_y = lax.axis_size("y")
+    x = lax.axis_index("x")
+    row = lax.all_gather(own, "x", axis=0, tiled=True)
+    rows_back = -(-back // n_x)
     window = []
-    for k in range(back, 0, -1):
-        window.append(
-            lax.ppermute(own, "seq", perm=[(i, i + k) for i in range(n_seq - k)])
-        )
-    window.append(own)
-    kv_win = jnp.concatenate(window, axis=0)
-    n_keys = kv_win.shape[0]
+    for k in range(rows_back, 0, -1):
+        window.append(lax.ppermute(row, "y", perm=[(i, i + k) for i in range(n_y - k)]))
+    window.append(row)
+    kv_all = jnp.concatenate(window, axis=0)
+    n_keys = (back + 1) * rows
+    first = (rows_back * n_x - back + x) * rows
+    kv_win = lax.dynamic_slice_in_dim(kv_all, first, n_keys, 0)
     k_win = kv_win[:, :HD]
     v_win = kv_win[:, HD:]
 
     q_pos = s * rows + jnp.arange(rows, dtype=jnp.int32)
     k_pos = (s - back) * rows + jnp.arange(n_keys, dtype=jnp.int32)
     q_seg = lax.dynamic_slice_in_dim(segment_ids, s * rows, rows, 0)
-    k_seg = jnp.take(segment_ids, jnp.clip(k_pos, 0, segment_ids.shape[0] - 1))
+    seg_pad = jnp.concatenate([jnp.full((back * rows,), -1, jnp.int32), segment_ids])
+    k_seg = lax.dynamic_slice_in_dim(seg_pad, s * rows, n_keys, 0)
     live = (
         (k_pos[None, :] <= q_pos[:, None])
         & (k_seg[None, :] == q_seg[:, None])
@@ -75,19 +82,14 @@
     rank = jnp.sum((new_of[None, :] < new_of[:, None]).astype(jnp.int32), axis=1)
     send_sel = (rank[None, :] == jnp.arange(rows, dtype=jnp.int32)[:, None]).astype(jnp.bfloat16)
     to_send = jnp.dot(send_sel, attn_rows, preferred_element_type=jnp.float32).astype(jnp.bfloat16)
-    arrived = lax.all_to_all(to_send, "seq", split_axis=0, concat_axis=0, tiled=True)
+    arrived = lax.all_to_all(to_send, ("y", "x"), split_axis=0, concat_axis=0, tiled=True)
 
     src = lax.dynamic_slice_in_dim(relayout, s * rows, rows, 0) // rows
     before = jnp.arange(rows)[None, :] < jnp.arange(rows)[:, None]
     nth = jnp.sum((before & (src[None, :] == src[:, None])).astype(jnp.int32), axis=1)
     slot = src * chunk + nth
     per_dev = rows // (n_z * n_core)
-    r = jnp.arange(rows, dtype=jnp.int32)
-    c_of = r // (n_z * per_dev)
-    z_of = (r // per_dev) % n_z
-    m_of = r % per_dev
-    q_of = (z_of * n_core + c_of) * per_dev + m_of
-    slot_of = jnp.take(slot, q_of)
+    slot_of = jnp.transpose(slot.reshape(n_z, n_core, per_dev), (1, 0, 2)).reshape(rows)
     recv_sel = (slot_of[:, None] == jnp.arange(rows, dtype=jnp.int32)[None, :]).astype(jnp.bfloat16)
     relaid = jnp.dot(recv_sel, arrived, preferred_element_type=jnp.float32).astype(jnp.bfloat16)
 
@@ -98,19 +100,21 @@
 
 def solution(mesh):
     n_seq, n_tp = mesh.devices.shape
-    mesh3 = Mesh(mesh.devices.reshape(n_seq, n_tp // 2, 2), ("seq", "z", "core"))
+    n_x = 4
+    mesh4 = Mesh(mesh.devices.reshape(n_seq // n_x, n_x, n_tp // 2, 2), ("y", "x", "z", "core"))
+    seq = ("y", "x")
     tp = ("z", "core")
     return jax.shard_map(
         shards,
-        mesh=mesh3,
+        mesh=mesh4,
         in_specs=(
             P(),
             P(),
-            P("seq", tp),
-            P(("seq",) + tp, None),
-            P(("seq",) + tp, None),
+            P(seq, tp),
+            P(seq + tp, None),
+            P(seq + tp, None),
             P(tp, None),
         ),
-        out_specs=P(("seq",) + tp, None),
+        out_specs=P(seq + tp, None),
         check_vma=False,
     )

time: 190 us -> 190 us (level)
  blocking collectives: 24.6 us -> 46.6 us
  local copies, waits for them, and re-layouts: 15.1 us -> 0.97 us
  starting transfers between devices: 45.5 us -> 31.8 us
  other arithmetic: 7 us -> 10.6 us
    ppermute x8 -> x2, starting transfers between devices: 35 us -> 8 us  [shards(): lax.ppermute(row, 'y', perm=[(i, i + k) for i in range(n_y - k)])]
    all_gather x1 -> x3, blocking collectives: 24.6 us -> 46.6 us  [the longest x1 32 us: shards(): kv_block = lax.all_gather(kv_pair, 'z', axis=0, tiled=True)]
    gather x2 -> x0, local copies, waits for them, and re-layouts: 14.3 us -> none  [the longest x1 12.3 us: shards(): k_seg = jnp.take(segment_ids, jnp.clip(k_pos, 0, segment_ids.shape[0] - 1))]
    all_to_all x1, starting transfers between devices: 10.4 us -> 23.8 us  [shards(): lax.all_to_all(to_send, ('y', 'x'), split_axis=0, concat_axis=0, tiled=True)]
    concatenate x1, other arithmetic: 0.02 us -> 2.99 us  [shards(): kv_all = jnp.concatenate(window, axis=0)]
    reduce_scatter x1, waiting for transfers between devices: 12.3 us -> 14.3 us  [shards(): half = lax.psum_scatter(part, 'core', scatter_dimension=0, tiled=True)]
  transfers between devices with their start and end apart: 11 -> 5, of which waited for: 5 -> 4; matrix products, arithmetic and copies ran while one was open for 11% -> 4% of each run, Pallas kernels for 0% -> 0%
where the time goes in v2:
time: 190 us; the launch traced here: 189 us
  waiting for transfers between devices  74.5 us (39%)
  blocking collectives  46.6 us (25%)
  starting transfers between devices  31.8 us (17%)
  between operations  13.5 us (7%)
  matrix products  10.9 us (6%)
  other arithmetic  10.6 us (6%)
    reduce_scatter x1, waiting for transfers between devices, shards(): return lax.psum_scatter(half, 'z', scatter_dimension=0, tiled=True)  50.2 us
    all_gather x1, blocking collectives, shards(): kv_block = lax.all_gather(kv_pair, 'z', axis=0, tiled=True)  32 us
    all_to_all x1, starting transfers between devices, shards(): lax.all_to_all(to_send, ('y', 'x'), split_axis=0, concat_axis=0, tiled=True)  23.8 us
    reduce_scatter x1, waiting for transfers between devices, shards(): half = lax.psum_scatter(part, 'core', scatter_dimension=0, tiled=True)  14.3 us
    all_gather x1, blocking collectives, shards(): row = lax.all_gather(own, 'x', axis=0, tiled=True)  12.8 us
    ppermute x2, starting transfers between devices, shards(): lax.ppermute(row, 'y', perm=[(i, i + k) for i in range(n_y - k)])  8 us
    all_to_all x1, waiting for transfers between devices, shards(): lax.all_to_all(to_send, ('y', 'x'), split_axis=0, concat_axis=0, tiled=True)  7.68 us
    dot_general x1, matrix products, shards(): jnp.dot(relaid, out_weight, preferred_element_type=jnp.float32)  5.52 us
  transfers between devices with their start and end apart: 5, of which 4 were waited for; matrix products, arithmetic and copies ran while one was open for 4% of the time, Pallas kernels for 0%

profile of v2, /device:TPU:6, one launch (start us, length us, event | category | flops | bytes accessed | tf_op | source)
XLA Modules:
  0.0 189.0 jit_solution(4200735184962645888)
XLA Ops:
  6.5 0.0 copy-start
  6.5 0.8 pad_maximum_fusion.1
  7.3 1.8 all_gather.9
  9.2 32.0 %all_gather.10 = bf16[256,1024]{1,0:T(8,128)(2,1)S(1)} all-gather(bf16[32,1024]{1,0:T(8,128)(2,1)S(1)} %all_gather.9), channel_id=1, replica_groups=mesh['y'=8,'x'=4,'z'=8,'core'=2] {'z'}, dimensions={0}, use_global_device_ids=true | all-gather | bytes 589824 | tf_op jit(solution)/shard_map/all_gather | solution.py:30
  41.2 12.8 %all_gather.11 = bf16[1024,256]{1,0:T(8,128)(2,1)S(1)} all-gather(bf16[256,256]{1,0:T(8,128)(2,1)S(1)} %pad_maximum_fusion), channel_id=1, replica_groups=mesh['y'=8,'x'=4,'z'=8,'core'=2] {'x'}, dimensions={0}, use_global_device_ids=true | all-gather | bytes 655360 | tf_op jit(solution)/shard_map/all_gather | solution.py:39
  54.0 3.5 %collective-permute-start.1 = (bf16[1024,256]{1,0:T(8,128)(2,1)S(1)}, bf16[1024,256]{1,0:T(8,128)(2,1)S(1)}, u32[]{:S(2)}, u32[]{:S(2)}) collective-permute-start(bf16[1024,256]{1,0:T(8,128)(2,1)S(1)} %all_gather.11), channel_id=1, source_target_pairs={{0,64},{64,128},{128,192},{192,256},{256,320},{320,384},{384,448},... | collective-permute-start | bytes 1572872 | tf_op jit(solution)/shard_map/ppermute | solution.py:43
  57.5 4.5 %collective-permute-start = (bf16[1024,256]{1,0:T(8,128)(2,1)S(1)}, bf16[1024,256]{1,0:T(8,128)(2,1)S(1)}, u32[]{:S(2)}, u32[]{:S(2)}) collective-permute-start(bf16[1024,256]{1,0:T(8,128)(2,1)S(1)} %all_gather.11), channel_id=1, source_target_pairs={{0,128},{64,192},{128,256},{192,320},{256,384},{320,448},{1,129},{... | collective-permute-start | bytes 1572872 | tf_op jit(solution)/shard_map/ppermute | solution.py:43
  62.0 2.0 %select_reduce_fusion = s32[256]{0:T(256)S(1)} fusion(s32[8192]{0:T(1024)} %param.7, s32[256]{0:T(256)S(1)} %iota_add_fusion.1), kind=kLoop, calls=%fused_computation.2 | loop fusion | flops 6291200 | bytes 34816 | tf_op jit(solution)/shard_map/reduce_sum | solution.py:78
  64.0 0.2 convert_reduce_fusion
  64.2 0.8 and_select_fusion
  65.0 0.8 dynamic_slice.20
  65.8 0.8 pad_dynamic-slice_fusion.3
  66.5 2.1 %and_and_fusion = pred[256,2304]{0,1:T(8,128)(4,1)S(1)} fusion(s32[256]{0:T(256)S(1)} %dynamic_slice.20, s32[256]{0:T(256)S(1)} %iota_add_fusion.1, s32[2304]{0:T(1024)S(1)} %get-tuple-element.7, s32[2304]{0:T(1024)S(1)} %get-tuple-element.8, pred[2304]{0:T(1024)(128)(4,1)S(1)} %broadcast_compare_fusion), kind=kLoop, calls=%fused_computation.11 | loop fusion | flops 2359296 | bytes 612608 | tf_op jit(solution)/shard_map/and | solution.py:58
  68.7 0.0 collective-permute-done.1
  68.7 2.3 %collective-permute-done = bf16[1024,256]{1,0:T(8,128)(2,1)S(1)} collective-permute-done((bf16[1024,256]{1,0:T(8,128)(2,1)S(1)}, bf16[1024,256]{1,0:T(8,128)(2,1)S(1)}, u32[]{:S(2)}, u32[]{:S(2)}) %collective-permute-start) | collective-permute-done | bytes 524320 | tf_op jit(solution)/shard_map/ppermute | solution.py:43
  71.0 3.0 %fusion.9 = bf16[2304,256]{1,0:T(8,128)(2,1)S(1)} fusion(s32[]{:T(128)S(6)} %select_n.44, bf16[1024,256]{1,0:T(8,128)(2,1)S(1)} %collective-permute-done, bf16[1024,256]{1,0:T(8,128)(2,1)S(1)} %collective-permute-done.1, bf16[1024,256]{1,0:T(8,128)(2,1)S(1)} %all_gather.11), kind=kLoop, calls=%fused_computation.16 | loop fusion | flops 3538944 | bytes 2752516 | tf_op jit(solution)/shard_map/concatenate | solution.py:45
  74.0 2.2 %fusion.45 = f32[2,256]{1,0:T(2,128)S(1)} fusion(pred[256,2304]{0,1:T(8,128)(4,1)S(1)} %and_and_fusion, bf16[2304,256]{1,0:T(8,128)(2,1)S(1)} %fusion.9, bf16[256,256]{1,0:T(8,128)(2,1)S(1)} %copy-done), kind=kOutput, calls=%fused_computation.56 | convolution fusion | flops 307890432 | bytes 1902592 | tf_op jit(solution)/shard_map/sub | solution.py:67
  76.3 2.3 %fusion.16 = bf16[256,2,128]{0,2,1:T(8,128)(2,1)S(1)} fusion(bf16[2304,256]{1,0:T(8,128)(2,1)S(1)} %fusion.9, f32[256,2]{0,1:T(2,128)S(1)} %bitcast.72, pred[256,2304]{0,1:T(8,128)(4,1)S(1)} %and_and_fusion, bf16[256,256]{1,0:T(8,128)(2,1)S(1)} %copy-done), kind=kOutput, calls=%fused_computation.21 | convolution fusion | flops 610011904 | bytes 2623488 | tf_op jit(solution)/shard_map/hqk,kd->hqd/dot_general | solution.py:69
  78.6 0.9 fusion.19
  79.5 23.8 %all-to-all-start = ((bf16[32,8,256]{2,1,0:T(8,128)(2,1)}), bf16[32,8,256]{2,1,0:T(8,128)(2,1)S(1)}, u32[]{:S(2)}, u32[]{:S(2)}) async-start(bf16[32,8,256]{2,1,0:T(8,128)(2,1)} %fusion.19), calls=%async_computation | async-start | bytes 262144 | tf_op jit(solution)/shard_map/all_to_all | solution.py:85
  103.2 0.0 reduce-scatter.3.cloned.1.call-start
  103.3 0.2 convert_reduce_fusion.1
  103.5 0.8 multiply_add_fusion
  104.2 0.1 reshape.101
  104.3 0.1 eq.70
  104.4 7.7 %all-to-all-done = bf16[32,8,256]{2,1,0:T(8,128)(2,1)S(1)} async-done(((bf16[32,8,256]{2,1,0:T(8,128)(2,1)}), bf16[32,8,256]{2,1,0:T(8,128)(2,1)S(1)}, u32[]{:S(2)}, u32[]{:S(2)}) %all-to-all-start) | async-done | bytes 131104 | tf_op jit(solution)/shard_map/all_to_all | solution.py:85
  112.1 5.5 %convolution_convert_fusion = bf16[256,8192]{1,0:T(8,128)(2,1)} fusion(bf16[256,8192]{1,0:T(8,128)(2,1)} %param.11, bf16[32,8,256]{2,1,0:T(8,128)(2,1)S(1)} %all-to-all-done, s32[256]{0:T(256)S(1)} %eq.70), kind=kOutput, calls=%fused_computation.1 | convolution fusion | flops 1109524480 | bytes 8520704 | tf_op jit(solution)/shard_map/dot_general | solution.py:96
  117.6 0.0 reduce-scatter.3.cloned.1.call-update
  117.6 0.0 reduce-scatter.5.cloned.1.call-start
  117.7 14.3 %reduce-scatter.3.cloned.1.call-done = bf16[128,8192]{1,0:T(8,128)(2,1)} async-done(((bf16[256,8192]{1,0:T(8,128)(2,1)}), bf16[128,8192]{1,0:T(8,128)(2,1)}) %reduce-scatter.3.cloned.1.call-update) | async-done | bytes 2097168 | tf_op jit(solution)/shard_map/reduce_scatter | solution.py:97
  132.0 0.0 reduce-scatter.5.cloned.1.call-update
  132.0 50.2 %reduce-scatter.5.cloned.1.call-done = bf16[16,8192]{1,0:T(8,128)(2,1)} async-done(((bf16[128,8192]{1,0:T(8,128)(2,1)}), bf16[16,8192]{1,0:T(8,128)(2,1)}) %reduce-scatter.5.cloned.1.call-update) | async-done | bytes 262160 | tf_op jit(solution)/shard_map/reduce_scatter | solution.py:98
  (6 shorter events, 0.1 us)
Async XLA Ops:
  6.5 67.5 %copy-start = (bf16[256,256]{1,0:T(8,128)(2,1)S(1)}, bf16[256,256]{1,0:T(8,128)(2,1)}, u32[]{:S(2)}) copy-start(bf16[256,256]{1,0:T(8,128)(2,1)} %param.8) | copy-start | bytes 393220
  54.0 14.7 %collective-permute-start.1 = (bf16[1024,256]{1,0:T(8,128)(2,1)S(1)}, bf16[1024,256]{1,0:T(8,128)(2,1)S(1)}, u32[]{:S(2)}, u32[]{:S(2)}) collective-permute-start(bf16[1024,256]{1,0:T(8,128)(2,1)S(1)} %all_gather.11), channel_id=1, source_target_pairs={{0,64},{64,128},{128,192},{192,256},{256,320},{320,384},{384,448},... | collective-permute-start | bytes 1572872 | tf_op jit(solution)/shard_map/ppermute | solution.py:43
  57.5 13.5 %collective-permute-start = (bf16[1024,256]{1,0:T(8,128)(2,1)S(1)}, bf16[1024,256]{1,0:T(8,128)(2,1)S(1)}, u32[]{:S(2)}, u32[]{:S(2)}) collective-permute-start(bf16[1024,256]{1,0:T(8,128)(2,1)S(1)} %all_gather.11), channel_id=1, source_target_pairs={{0,128},{64,192},{128,256},{192,320},{256,384},{320,448},{1,129},{... | collective-permute-start | bytes 1572872 | tf_op jit(solution)/shard_map/ppermute | solution.py:43
  79.5 32.6 %all-to-all-start = ((bf16[32,8,256]{2,1,0:T(8,128)(2,1)}), bf16[32,8,256]{2,1,0:T(8,128)(2,1)S(1)}, u32[]{:S(2)}, u32[]{:S(2)}) async-start(bf16[32,8,256]{2,1,0:T(8,128)(2,1)} %fusion.19), calls=%async_computation | async-start | bytes 262144 | tf_op jit(solution)/shard_map/all_to_all | solution.py:85
  103.2 28.8 %reduce-scatter.3.cloned.1.call-start = ((), (), s32[]{:S(2)}) async-start(), calls=%async_computation.3 | async-start | bytes 6291456 | tf_op jit(solution)/shard_map/reduce_scatter | solution.py:97
  117.6 64.5 %reduce-scatter.5.cloned.1.call-start = ((), (), s32[]{:S(2)}) async-start(), calls=%async_computation.4 | async-start | bytes 2359296 | tf_op jit(solution)/shard_map/reduce_scatter | solution.py:98
Sparse Core Ops, SparseCore 0:
  117.8 14.1 reduce-scatter.2
  135.1 47.0 reduce-scatter.4

commit v3 on v2

--- a/solution.py
+++ b/solution.py
@@ -26,8 +26,7 @@
     back = min(back, n_seq - 1)
 
     kv = jnp.concatenate([keys, values], axis=1)
-    kv_pair = lax.all_gather(kv, "core", axis=0, tiled=True)
-    kv_block = lax.all_gather(kv_pair, "z", axis=0, tiled=True)
+    kv_block = lax.all_gather(kv, ("z", "core"), axis=0, tiled=True)
     g = t * heads_here // group
     own_k = lax.dynamic_slice_in_dim(kv_block, g * HD, HD, 1)
     own_v = lax.dynamic_slice_in_dim(kv_block, kv_width + g * HD, HD, 1)
@@ -89,14 +88,21 @@
     nth = jnp.sum((before & (src[None, :] == src[:, None])).astype(jnp.int32), axis=1)
     slot = src * chunk + nth
     per_dev = rows // (n_z * n_core)
-    slot_of = jnp.transpose(slot.reshape(n_z, n_core, per_dev), (1, 0, 2)).reshape(rows)
-    recv_sel = (slot_of[:, None] == jnp.arange(rows, dtype=jnp.int32)[None, :]).astype(jnp.bfloat16)
-    relaid = jnp.dot(recv_sel, arrived, preferred_element_type=jnp.float32).astype(jnp.bfloat16)
+    c = lax.axis_index("core")
+    slot3 = slot.reshape(n_z, n_core, per_dev)
+    cols = jnp.arange(rows, dtype=jnp.int32)[None, :]
 
-    part = jnp.dot(relaid, out_weight, preferred_element_type=jnp.float32).astype(jnp.bfloat16)
-    half = lax.psum_scatter(part, "core", scatter_dimension=0, tiled=True)
+    def project(which):
+        chosen = jnp.take(slot3, which, axis=1).reshape(-1)
+        sel = (chosen[:, None] == cols).astype(jnp.bfloat16)
+        relaid = jnp.dot(sel, arrived, preferred_element_type=jnp.float32).astype(jnp.bfloat16)
+        return jnp.dot(relaid, out_weight, preferred_element_type=jnp.float32).astype(jnp.bfloat16)
+
+    part_other = project(n_core - 1 - c)
+    got = lax.ppermute(part_other, "core", perm=[(0, 1), (1, 0)])
+    part_own = project(c)
+    half = (part_own.astype(jnp.float32) + got.astype(jnp.float32)).astype(jnp.bfloat16)
     return lax.psum_scatter(half, "z", scatter_dimension=0, tiled=True)
-
 
 def solution(mesh):
     n_seq, n_tp = mesh.devices.shape

time: 190 us -> 169 us (0.89)
  waiting for transfers between devices: 74.5 us -> 58.2 us
  blocking collectives: 46.6 us -> 38 us
  starting transfers between devices: 31.8 us -> 35.1 us
  matrix products: 10.9 us -> 13.5 us
    reduce_scatter x1 -> x0, waiting for transfers between devices: 14.3 us -> none  [shards(): half = lax.psum_scatter(part, 'core', scatter_dimension=0, tiled=True)]
    reduce_scatter x1, waiting for transfers between devices: 50.2 us -> 37.8 us  [shards(): return lax.psum_scatter(half, 'z', scatter_dimension=0, tiled=True)]
    all_gather x2 -> x1, blocking collectives: 33.8 us -> 24.6 us  [shards(): kv_block = lax.all_gather(kv, ('z', 'core'), axis=0, tiled=True)]
    ppermute x2, waiting for transfers between devices: 2.35 us -> 8.4 us  [shards(): lax.ppermute(row, 'y', perm=[(i, i + k) for i in range(n_y - k)])]
    ppermute x0 -> x1, waiting for transfers between devices: none -> 4.18 us  [shards(): got = lax.ppermute(part_other, 'core', perm=[(0, 1), (1, 0)])]
    dot_general x1 -> x2, matrix products: 5.52 us -> 8.13 us  [project(): jnp.dot(relaid, out_weight, preferred_element_type=jnp.float32)]
    ppermute x0 -> x1, starting transfers between devices: none -> 1.92 us  [shards(): got = lax.ppermute(part_other, 'core', perm=[(0, 1), (1, 0)])]
  transfers between devices with their start and end apart: 5 -> 5, of which waited for: 4 -> 5; matrix products, arithmetic and copies ran while one was open for 4% -> 5% of each run, Pallas kernels for 0% -> 0%
where the time goes in v3:
time: 169 us
  waiting for transfers between devices  58.2 us (34%)
  blocking collectives  38 us (22%)
  starting transfers between devices  35.1 us (21%)
  matrix products  13.5 us (8%)
  between operations  13.5 us (8%)
  other arithmetic  9.36 us (6%)
    reduce_scatter x1, waiting for transfers between devices, shards(): return lax.psum_scatter(half, 'z', scatter_dimension=0, tiled=True)  37.8 us
    all_to_all x1, starting transfers between devices, shards(): lax.all_to_all(to_send, ('y', 'x'), split_axis=0, concat_axis=0, tiled=True)  25.1 us
    all_gather x1, blocking collectives, shards(): kv_block = lax.all_gather(kv, ('z', 'core'), axis=0, tiled=True)  24.6 us
    all_gather x1, blocking collectives, shards(): row = lax.all_gather(own, 'x', axis=0, tiled=True)  13.5 us
    ppermute x2, waiting for transfers between devices, shards(): lax.ppermute(row, 'y', perm=[(i, i + k) for i in range(n_y - k)])  8.4 us
    dot_general x2, matrix products, project(): jnp.dot(relaid, out_weight, preferred_element_type=jnp.float32)  8.13 us
    ppermute x2, starting transfers between devices, shards(): lax.ppermute(row, 'y', perm=[(i, i + k) for i in range(n_y - k)])  8 us
    all_to_all x1, waiting for transfers between devices, shards(): lax.all_to_all(to_send, ('y', 'x'), split_axis=0, concat_axis=0, tiled=True)  7.84 us
  transfers between devices with their start and end apart: 5, of which 5 were waited for; matrix products, arithmetic and copies ran while one was open for 5% of the time, Pallas kernels for 0%

profile of v3, /device:TPU:6, one launch (start us, length us, event | category | flops | bytes accessed | tf_op | source)
XLA Modules:
  0.0 168.8 jit_solution(560177832577715488)
XLA Ops:
  6.5 0.8 pad_maximum_fusion.1
  7.3 24.6 %all_gather.6 = bf16[256,1024]{1,0:T(8,128)(2,1)S(1)} all-gather(bf16[16,1024]{1,0:T(8,128)(2,1)S(1)} %pad_maximum_fusion.1), channel_id=1, replica_groups=mesh['y'=8,'x'=4,'z'=8,'core'=2] {'z','core'}, dimensions={0}, use_global_device_ids=true | all-gather | bytes 557056 | tf_op jit(solution)/shard_map/all_gather | solution.py:29
  31.9 13.5 %all_gather.7 = bf16[1024,256]{1,0:T(8,128)(2,1)S(1)} all-gather(bf16[256,256]{1,0:T(8,128)(2,1)S(1)} %pad_maximum_fusion), channel_id=1, replica_groups=mesh['y'=8,'x'=4,'z'=8,'core'=2] {'x'}, dimensions={0}, use_global_device_ids=true | all-gather | bytes 655360 | tf_op jit(solution)/shard_map/all_gather | solution.py:38
  45.4 3.5 %collective-permute-start.1 = (bf16[1024,256]{1,0:T(8,128)(2,1)S(1)}, bf16[1024,256]{1,0:T(8,128)(2,1)S(1)}, u32[]{:S(2)}, u32[]{:S(2)}) collective-permute-start(bf16[1024,256]{1,0:T(8,128)(2,1)S(1)} %all_gather.7), channel_id=1, source_target_pairs={{0,64},{64,128},{128,192},{192,256},{256,320},{320,384},{384,448},... | collective-permute-start | bytes 1572872 | tf_op jit(solution)/shard_map/ppermute | solution.py:42
  48.9 4.5 %collective-permute-start = (bf16[1024,256]{1,0:T(8,128)(2,1)S(1)}, bf16[1024,256]{1,0:T(8,128)(2,1)S(1)}, u32[]{:S(2)}, u32[]{:S(2)}) collective-permute-start(bf16[1024,256]{1,0:T(8,128)(2,1)S(1)} %all_gather.7), channel_id=1, source_target_pairs={{0,128},{64,192},{128,256},{192,320},{256,384},{320,448},{1,129},{... | collective-permute-start | bytes 1572872 | tf_op jit(solution)/shard_map/ppermute | solution.py:42
  53.5 2.0 %select_reduce_fusion = s32[256]{0:T(256)S(1)} fusion(s32[8192]{0:T(1024)} %param.9, s32[256]{0:T(256)S(1)} %iota_add_fusion.1), kind=kLoop, calls=%fused_computation.4 | loop fusion | flops 6291200 | bytes 34816 | tf_op jit(solution)/shard_map/reduce_sum | solution.py:77
  55.5 0.2 convert_reduce_fusion
  55.6 0.8 and_select_fusion
  56.4 0.8 dynamic_slice.20
  57.2 0.2 convert_reduce_fusion.1
  57.4 0.8 pad_dynamic-slice_fusion.3
  58.2 2.1 %and_and_fusion = pred[256,2304]{0,1:T(8,128)(4,1)S(1)} fusion(s32[256]{0:T(256)S(1)} %dynamic_slice.20, s32[256]{0:T(256)S(1)} %iota_add_fusion.1, s32[2304]{0:T(1024)S(1)} %get-tuple-element.21, s32[2304]{0:T(1024)S(1)} %get-tuple-element.22, pred[2304]{0:T(1024)(128)(4,1)S(1)} %broadcast_compare_fusion), kind=kLoop, calls=%fused_computation.14 | loop fusion | flops 2359296 | bytes 612608 | tf_op jit(solution)/shard_map/and | solution.py:57
  60.3 0.9 collective-permute-done.1
  61.2 7.5 %collective-permute-done = bf16[1024,256]{1,0:T(8,128)(2,1)S(1)} collective-permute-done((bf16[1024,256]{1,0:T(8,128)(2,1)S(1)}, bf16[1024,256]{1,0:T(8,128)(2,1)S(1)}, u32[]{:S(2)}, u32[]{:S(2)}) %collective-permute-start) | collective-permute-done | bytes 524320 | tf_op jit(solution)/shard_map/ppermute | solution.py:42
  68.7 1.7 %fusion.10 = bf16[2304,256]{1,0:T(8,128)(2,1)S(1)} fusion(s32[]{:T(128)S(6)} %select_n.50, bf16[1024,256]{1,0:T(8,128)(2,1)S(1)} %collective-permute-done, bf16[1024,256]{1,0:T(8,128)(2,1)S(1)} %collective-permute-done.1, bf16[1024,256]{1,0:T(8,128)(2,1)S(1)} %all_gather.7), kind=kLoop, calls=%fused_computation.19 | loop fusion | flops 3538944 | bytes 2752516 | tf_op jit(solution)/shard_map/concatenate | solution.py:44
  70.4 0.0 copy-done
  70.4 2.2 %fusion.50 = f32[2,256]{1,0:T(2,128)S(1)} fusion(pred[256,2304]{0,1:T(8,128)(4,1)S(1)} %and_and_fusion, bf16[2304,256]{1,0:T(8,128)(2,1)S(1)} %fusion.10, bf16[256,256]{1,0:T(8,128)(2,1)S(1)} %copy-done), kind=kOutput, calls=%fused_computation.65 | convolution fusion | flops 307890432 | bytes 1902592 | tf_op jit(solution)/shard_map/sub | solution.py:66
  72.6 2.3 %fusion.17 = bf16[256,2,128]{0,2,1:T(8,128)(2,1)S(1)} fusion(bf16[2304,256]{1,0:T(8,128)(2,1)S(1)} %fusion.10, f32[256,2]{0,1:T(2,128)S(1)} %bitcast.78, pred[256,2304]{0,1:T(8,128)(4,1)S(1)} %and_and_fusion, bf16[256,256]{1,0:T(8,128)(2,1)S(1)} %copy-done), kind=kOutput, calls=%fused_computation.23 | convolution fusion | flops 610011904 | bytes 2623488 | tf_op jit(solution)/shard_map/hqk,kd->hqd/dot_general | solution.py:68
  75.0 0.9 fusion.20
  75.8 25.1 %all-to-all-start = ((bf16[32,8,256]{2,1,0:T(8,128)(2,1)}), bf16[32,8,256]{2,1,0:T(8,128)(2,1)S(1)}, u32[]{:S(2)}, u32[]{:S(2)}) async-start(bf16[32,8,256]{2,1,0:T(8,128)(2,1)} %fusion.20), calls=%async_computation | async-start | bytes 262144 | tf_op jit(solution)/shard_map/all_to_all | solution.py:84
  100.9 0.0 reduce-scatter.2.cloned.1.call-start
  101.0 0.8 multiply_add_fusion
  101.8 0.1 reshape.103
  101.9 0.1 eq.99
  102.0 7.8 %all-to-all-done = bf16[32,8,256]{2,1,0:T(8,128)(2,1)S(1)} async-done(((bf16[32,8,256]{2,1,0:T(8,128)(2,1)}), bf16[32,8,256]{2,1,0:T(8,128)(2,1)S(1)}, u32[]{:S(2)}, u32[]{:S(2)}) %all-to-all-start) | async-done | bytes 131104 | tf_op jit(solution)/shard_map/all_to_all | solution.py:84
  109.8 3.1 %convolution_convert_fusion = bf16[128,8192]{1,0:T(8,128)(2,1)S(1)} fusion(bf16[256,8192]{1,0:T(8,128)(2,1)} %param.13, bf16[32,8,256]{2,1,0:T(8,128)(2,1)S(1)} %all-to-all-done, s32[128]{0:T(128)S(1)} %eq.99), kind=kOutput, calls=%fused_computation.1 | convolution fusion | flops 554762240 | bytes 6423040 | tf_op jit(solution)/shard_map/dot_general | solution.py:99
  112.9 1.9 %collective-permute-start.2 = (bf16[128,8192]{1,0:T(8,128)(2,1)S(1)}, bf16[128,8192]{1,0:T(8,128)(2,1)}, u32[]{:S(2)}, u32[]{:S(2)}) collective-permute-start(bf16[128,8192]{1,0:T(8,128)(2,1)S(1)} %convolution_convert_fusion), channel_id=1, source_target_pairs={{0,1},{1,0},{2,3},{3,2},{4,5},{5,4},{6,7},{7,6},{8,9},{9,8},{10,11... | collective-permute-start | bytes 6291464 | tf_op jit(solution)/shard_map/ppermute | solution.py:102
  114.8 0.1 eq.87
  114.9 4.2 %collective-permute-done.2 = bf16[128,8192]{1,0:T(8,128)(2,1)} collective-permute-done((bf16[128,8192]{1,0:T(8,128)(2,1)S(1)}, bf16[128,8192]{1,0:T(8,128)(2,1)}, u32[]{:S(2)}, u32[]{:S(2)}) %collective-permute-start.2) | collective-permute-done | bytes 2097184 | tf_op jit(solution)/shard_map/ppermute | solution.py:102
  119.1 5.1 %add_convert_fusion = bf16[128,8192]{1,0:T(8,128)(2,1)} fusion(bf16[128,8192]{1,0:T(8,128)(2,1)} %collective-permute-done.2, bf16[256,8192]{1,0:T(8,128)(2,1)} %param.13, bf16[32,8,256]{2,1,0:T(8,128)(2,1)S(1)} %all-to-all-done, s32[128]{0:T(128)S(1)} %eq.87), kind=kOutput, calls=%fused_computation.11 | convolution fusion | flops 558956544 | bytes 8520192 | tf_op jit(solution)/shard_map/dot_general | solution.py:99
  124.1 0.0 reduce-scatter.2.cloned.1.call-update
  124.2 37.8 %reduce-scatter.2.cloned.1.call-done = bf16[16,8192]{1,0:T(8,128)(2,1)} async-done(((bf16[128,8192]{1,0:T(8,128)(2,1)}), bf16[16,8192]{1,0:T(8,128)(2,1)}) %reduce-scatter.2.cloned.1.call-update) | async-done | bytes 262160 | tf_op jit(solution)/shard_map/reduce_scatter | solution.py:105
  (6 shorter events, 0.1 us)
Async XLA Ops:
  6.5 63.9 %copy-start = (bf16[256,256]{1,0:T(8,128)(2,1)S(1)}, bf16[256,256]{1,0:T(8,128)(2,1)}, u32[]{:S(2)}) copy-start(bf16[256,256]{1,0:T(8,128)(2,1)} %param.10) | copy-start | bytes 393220
  45.4 15.8 %collective-permute-start.1 = (bf16[1024,256]{1,0:T(8,128)(2,1)S(1)}, bf16[1024,256]{1,0:T(8,128)(2,1)S(1)}, u32[]{:S(2)}, u32[]{:S(2)}) collective-permute-start(bf16[1024,256]{1,0:T(8,128)(2,1)S(1)} %all_gather.7), channel_id=1, source_target_pairs={{0,64},{64,128},{128,192},{192,256},{256,320},{320,384},{384,448},... | collective-permute-start | bytes 1572872 | tf_op jit(solution)/shard_map/ppermute | solution.py:42
  48.9 19.8 %collective-permute-start = (bf16[1024,256]{1,0:T(8,128)(2,1)S(1)}, bf16[1024,256]{1,0:T(8,128)(2,1)S(1)}, u32[]{:S(2)}, u32[]{:S(2)}) collective-permute-start(bf16[1024,256]{1,0:T(8,128)(2,1)S(1)} %all_gather.7), channel_id=1, source_target_pairs={{0,128},{64,192},{128,256},{192,320},{256,384},{320,448},{1,129},{... | collective-permute-start | bytes 1572872 | tf_op jit(solution)/shard_map/ppermute | solution.py:42
  75.8 34.0 %all-to-all-start = ((bf16[32,8,256]{2,1,0:T(8,128)(2,1)}), bf16[32,8,256]{2,1,0:T(8,128)(2,1)S(1)}, u32[]{:S(2)}, u32[]{:S(2)}) async-start(bf16[32,8,256]{2,1,0:T(8,128)(2,1)} %fusion.20), calls=%async_computation | async-start | bytes 262144 | tf_op jit(solution)/shard_map/all_to_all | solution.py:84
  100.9 61.0 %reduce-scatter.2.cloned.1.call-start = ((), (), s32[]{:S(2)}) async-start(), calls=%async_computation.2 | async-start | bytes 2359296 | tf_op jit(solution)/shard_map/reduce_scatter | solution.py:105
  112.9 6.2 %collective-permute-start.2 = (bf16[128,8192]{1,0:T(8,128)(2,1)S(1)}, bf16[128,8192]{1,0:T(8,128)(2,1)}, u32[]{:S(2)}, u32[]{:S(2)}) collective-permute-start(bf16[128,8192]{1,0:T(8,128)(2,1)S(1)} %convolution_convert_fusion), channel_id=1, source_target_pairs={{0,1},{1,0},{2,3},{3,2},{4,5},{5,4},{6,7},{7,6},{8,9},{9,8},{10,11... | collective-permute-start | bytes 6291464 | tf_op jit(solution)/shard_map/ppermute | solution.py:102
Sparse Core Ops, SparseCore 0:
  124.3 37.6 reduce-scatter.1

commit v4 on v3

--- a/solution.py
+++ b/solution.py
@@ -25,23 +25,30 @@
     back = -(-(MOST_LEN - 1) // rows)
     back = min(back, n_seq - 1)
 
-    kv = jnp.concatenate([keys, values], axis=1)
-    kv_block = lax.all_gather(kv, ("z", "core"), axis=0, tiled=True)
-    g = t * heads_here // group
-    own_k = lax.dynamic_slice_in_dim(kv_block, g * HD, HD, 1)
-    own_v = lax.dynamic_slice_in_dim(kv_block, kv_width + g * HD, HD, 1)
-    own = jnp.concatenate([own_k, own_v], axis=1)
+    n_tp = n_z * n_core
+    pieces = []
+    for dest in range(n_tp):
+        h = dest * heads_here // group
+        pieces.append(jnp.concatenate([keys[:, h * HD:(h + 1) * HD], values[:, h * HD:(h + 1) * HD]], axis=1))
+    own = lax.all_to_all(jnp.stack(pieces), ("z", "core"), split_axis=0, concat_axis=0, tiled=True)
+    own = own.reshape(rows, 2 * HD)
 
     n_x = lax.axis_size("x")
     n_y = lax.axis_size("y")
     x = lax.axis_index("x")
+    c = lax.axis_index("core")
     row = lax.all_gather(own, "x", axis=0, tiled=True)
     rows_back = -(-back // n_x)
-    window = []
-    for k in range(rows_back, 0, -1):
-        window.append(lax.ppermute(row, "y", perm=[(i, i + k) for i in range(n_y - k)]))
-    window.append(row)
-    kv_all = jnp.concatenate(window, axis=0)
+    assert rows_back <= n_core
+    perm = []
+    for cc in range(n_core):
+        k = cc + 1
+        if k <= rows_back:
+            perm += [(yy * n_core + cc, (yy + k) * n_core + cc) for yy in range(n_y - k)]
+    fetched = lax.ppermute(row, ("y", "core"), perm=perm)
+    swapped = lax.ppermute(fetched, "core", perm=[(i, (i + 1) % n_core) for i in range(n_core)])
+    earlier = [jnp.where(c == k - 1, fetched, swapped) for k in range(rows_back, 0, -1)]
+    kv_all = jnp.concatenate(earlier + [row], axis=0)
     n_keys = (back + 1) * rows
     first = (rows_back * n_x - back + x) * rows
     kv_win = lax.dynamic_slice_in_dim(kv_all, first, n_keys, 0)
@@ -88,7 +95,6 @@
     nth = jnp.sum((before & (src[None, :] == src[:, None])).astype(jnp.int32), axis=1)
     slot = src * chunk + nth
     per_dev = rows // (n_z * n_core)
-    c = lax.axis_index("core")
     slot3 = slot.reshape(n_z, n_core, per_dev)
     cols = jnp.arange(rows, dtype=jnp.int32)[None, :]
 

time: 169 us -> 162 us (0.959)
  blocking collectives: 38 us -> 13.5 us
  other arithmetic: 9.36 us -> 20.2 us
  waiting for transfers between devices: 58.2 us -> 63.9 us
    all_gather x1 -> x0, blocking collectives: 24.6 us -> none  [shards(): kv_block = lax.all_gather(kv, ('z', 'core'), axis=0, tiled=True)]
    all_to_all x0 -> x1, starting transfers between devices: none -> 10.4 us  [shards(): lax.all_to_all(jnp.stack(pieces), ('z', 'core'), split_axis=0, concat_axi...]
    unnamed x0 -> x15, other arithmetic: none -> 9.01 us
    all_to_all x1, starting transfers between devices: 25.1 us -> 17 us  [shards(): lax.all_to_all(to_send, ('y', 'x'), split_axis=0, concat_axis=0, tiled=True)]
    all_to_all x0 -> x1, waiting for transfers between devices: none -> 6.41 us  [shards(): lax.all_to_all(jnp.stack(pieces), ('z', 'core'), split_axis=0, concat_axi...]
    ppermute x2, starting transfers between devices: 8 us -> 5.41 us  [the longest x1 3.5 us: shards(): fetched = lax.ppermute(row, ('y', 'core'), perm=perm)]
    concatenate x3 -> x1, other arithmetic: 2.49 us -> 3.65 us  [shards(): kv_all = jnp.concatenate(earlier + [row], axis=0)]
  transfers between devices with their start and end apart: 5 -> 6, of which waited for: 5 -> 5; matrix products, arithmetic and copies ran while one was open for 5% -> 5% of each run, Pallas kernels for 0% -> 0%
where the time goes in v4:
time: 162 us; the launch traced here: 161 us
  waiting for transfers between devices  63.9 us (39%)
  starting transfers between devices  34.8 us (21%)
  other arithmetic  20.2 us (12%)
  blocking collectives  13.5 us (8%)
  matrix products  13.5 us (8%)
  between operations  13.5 us (8%)
  local copies, waits for them, and re-layouts  1.85 us (1%)
    reduce_scatter x1, waiting for transfers between devices, shards(): return lax.psum_scatter(half, 'z', scatter_dimension=0, tiled=True)  37 us
    all_to_all x1, starting transfers between devices, shards(): lax.all_to_all(to_send, ('y', 'x'), split_axis=0, concat_axis=0, tiled=True)  17 us
    all_gather x1, blocking collectives, shards(): row = lax.all_gather(own, 'x', axis=0, tiled=True)  13.5 us
    all_to_all x1, starting transfers between devices, shards(): lax.all_to_all(jnp.stack(pieces), ('z', 'core'), split_axis=0, concat_axi...  10.4 us
    unnamed x15, other arithmetic  9.01 us
    ppermute x1, waiting for transfers between devices, shards(): fetched = lax.ppermute(row, ('y', 'core'), perm=perm)  8.33 us
    dot_general x2, matrix products, project(): jnp.dot(relaid, out_weight, preferred_element_type=jnp.float32)  8.13 us
    all_to_all x1, waiting for transfers between devices, shards(): lax.all_to_all(to_send, ('y', 'x'), split_axis=0, concat_axis=0, tiled=True)  7.91 us
  transfers between devices with their start and end apart: 6, of which 5 were waited for; matrix products, arithmetic and copies ran while one was open for 5% of the time, Pallas kernels for 0%

profile of v4, /device:TPU:6, one launch (start us, length us, event | category | flops | bytes accessed | tf_op | source)
XLA Modules:
  0.0 161.3 jit_solution(9047418156062273464)
XLA Ops:
  6.5 0.8 fusion.50
  7.4 0.6 constant_dynamic-update-slice_fusion.15
  8.0 0.6 constant_dynamic-update-slice_fusion.14
  8.6 0.6 constant_dynamic-update-slice_fusion.13
  9.2 0.6 constant_dynamic-update-slice_fusion.12
  11.0 0.6 constant_dynamic-update-slice_fusion.9
  12.8 0.6 constant_dynamic-update-slice_fusion.6
  14.0 0.6 constant_dynamic-update-slice_fusion.4
  15.8 0.6 constant_dynamic-update-slice_fusion.1
  17.0 10.4 %all-to-all-start = ((bf16[16,16,256]{2,1,0:T(8,128)(2,1)}), bf16[16,16,256]{2,1,0:T(8,128)(2,1)S(1)}, u32[]{:S(2)}, u32[]{:S(2)}) async-start(bf16[16,16,256]{2,1,0:T(8,128)(2,1)} %constant_dynamic-update-slice_fusion), calls=%async_computation | async-start | bytes 262144 | tf_op jit(solution)/shard_map/all_to_all | solution.py:33
  27.4 0.8 and_select_fusion
  28.2 0.8 dynamic_slice.14
  29.0 0.8 pad_dynamic-slice_fusion.3
  29.8 6.4 %all-to-all-done = bf16[16,16,256]{2,1,0:T(8,128)(2,1)S(1)} async-done(((bf16[16,16,256]{2,1,0:T(8,128)(2,1)}), bf16[16,16,256]{2,1,0:T(8,128)(2,1)S(1)}, u32[]{:S(2)}, u32[]{:S(2)}) %all-to-all-start) | async-done | bytes 131104 | tf_op jit(solution)/shard_map/all_to_all | solution.py:33
  36.2 13.5 %all_gather.3 = bf16[1024,256]{1,0:T(8,128)(2,1)S(1)} all-gather(bf16[256,256]{1,0:T(8,128)(2,1)S(1)} %bitcast.116), channel_id=1, replica_groups=mesh['y'=8,'x'=4,'z'=8,'core'=2] {'x'}, dimensions={0}, use_global_device_ids=true | all-gather | bytes 655360 | tf_op jit(solution)/shard_map/all_gather | solution.py:40
  49.7 3.5 %collective-permute-start = (bf16[1024,256]{1,0:T(8,128)(2,1)S(1)}, bf16[1024,256]{1,0:T(8,128)(2,1)S(1)}, u32[]{:S(2)}, u32[]{:S(2)}) collective-permute-start(bf16[1024,256]{1,0:T(8,128)(2,1)S(1)} %all_gather.3), channel_id=1, source_target_pairs={{0,64},{64,128},{128,192},{192,256},{256,320},{320,384},{384,448},... | collective-permute-start | bytes 1572872 | tf_op jit(solution)/shard_map/ppermute | solution.py:48
  53.2 2.0 %select_reduce_fusion = s32[256]{0:T(256)S(1)} fusion(s32[8192]{0:T(1024)} %param.9, s32[256]{0:T(256)S(1)} %iota_add_fusion.1), kind=kLoop, calls=%fused_computation.4 | loop fusion | flops 6291200 | bytes 34816 | tf_op jit(solution)/shard_map/reduce_sum | solution.py:84
  55.6 8.3 %collective-permute-done = bf16[1024,256]{1,0:T(8,128)(2,1)S(1)} collective-permute-done((bf16[1024,256]{1,0:T(8,128)(2,1)S(1)}, bf16[1024,256]{1,0:T(8,128)(2,1)S(1)}, u32[]{:S(2)}, u32[]{:S(2)}) %collective-permute-start) | collective-permute-done | bytes 524320 | tf_op jit(solution)/shard_map/ppermute | solution.py:48
  63.9 1.9 %collective-permute-start.1 = (bf16[1024,256]{1,0:T(8,128)(2,1)S(1)}, bf16[1024,256]{1,0:T(8,128)(2,1)S(1)}, u32[]{:S(2)}, u32[]{:S(2)}) collective-permute-start(bf16[1024,256]{1,0:T(8,128)(2,1)S(1)} %collective-permute-done), channel_id=1, source_target_pairs={{0,1},{1,0},{2,3},{3,2},{4,5},{5,4},{6,7},{7,6},{8,9},{9,8},{10,11... | collective-permute-start | bytes 1572872 | tf_op jit(solution)/shard_map/ppermute | solution.py:49
  65.8 2.2 %and_and_fusion = pred[256,2304]{0,1:T(8,128)(4,1)S(1)} fusion(s32[256]{0:T(256)S(1)} %dynamic_slice.14, s32[256]{0:T(256)S(1)} %iota_add_fusion.1, s32[2304]{0:T(1024)S(1)} %get-tuple-element.33, s32[2304]{0:T(1024)S(1)} %get-tuple-element.34, pred[2304]{0:T(1024)(128)(4,1)S(1)} %broadcast_compare_fusion), kind=kLoop, calls=%fused_computation.14 | loop fusion | flops 2359296 | bytes 612608 | tf_op jit(solution)/shard_map/and | solution.py:64
  68.1 3.7 %fusion.10 = bf16[2304,256]{1,0:T(8,128)(2,1)S(1)} fusion(s32[]{:T(128)S(6)} %select_n.55, bf16[1024,256]{1,0:T(8,128)(2,1)S(1)} %get-tuple-element.18, bf16[1024,256]{1,0:T(8,128)(2,1)S(1)} %get-tuple-element.17, bf16[1024,256]{1,0:T(8,128)(2,1)S(1)} %all_gather.3), kind=kLoop, calls=%fused_computation.19 | loop fusion | flops 3538944 | bytes 2752516 | tf_op jit(solution)/shard_map/concatenate | solution.py:51
  71.7 2.2 %fusion.52 = f32[2,256]{1,0:T(2,128)S(1)} fusion(pred[256,2304]{0,1:T(8,128)(4,1)S(1)} %and_and_fusion, bf16[2304,256]{1,0:T(8,128)(2,1)S(1)} %fusion.10, bf16[256,256]{1,0:T(8,128)(2,1)S(1)} %copy-done), kind=kOutput, calls=%fused_computation.85 | convolution fusion | flops 307890432 | bytes 1902592 | tf_op jit(solution)/shard_map/sub | solution.py:73
  74.0 2.3 %fusion.17 = bf16[256,2,128]{0,2,1:T(8,128)(2,1)S(1)} fusion(bf16[2304,256]{1,0:T(8,128)(2,1)S(1)} %fusion.10, f32[256,2]{0,1:T(2,128)S(1)} %bitcast.120, pred[256,2304]{0,1:T(8,128)(4,1)S(1)} %and_and_fusion, bf16[256,256]{1,0:T(8,128)(2,1)S(1)} %copy-done), kind=kOutput, calls=%fused_computation.23 | convolution fusion | flops 610011904 | bytes 2623488 | tf_op jit(solution)/shard_map/hqk,kd->hqd/dot_general | solution.py:75
  76.3 0.9 fusion.20
  77.2 17.0 %all-to-all-start.1 = ((bf16[32,8,256]{2,1,0:T(8,128)(2,1)}), bf16[32,8,256]{2,1,0:T(8,128)(2,1)S(1)}, u32[]{:S(2)}, u32[]{:S(2)}) async-start(bf16[32,8,256]{2,1,0:T(8,128)(2,1)} %fusion.20), calls=%async_computation.1 | async-start | bytes 262144 | tf_op jit(solution)/shard_map/all_to_all | solution.py:91
  94.2 0.8 multiply_add_fusion
  95.2 7.9 %all-to-all-done.1 = bf16[32,8,256]{2,1,0:T(8,128)(2,1)S(1)} async-done(((bf16[32,8,256]{2,1,0:T(8,128)(2,1)}), bf16[32,8,256]{2,1,0:T(8,128)(2,1)S(1)}, u32[]{:S(2)}, u32[]{:S(2)}) %all-to-all-start.1) | async-done | bytes 131104 | tf_op jit(solution)/shard_map/all_to_all | solution.py:91
  103.1 3.1 %convolution_convert_fusion = bf16[128,8192]{1,0:T(8,128)(2,1)S(1)} fusion(bf16[256,8192]{1,0:T(8,128)(2,1)} %param.13, bf16[32,8,256]{2,1,0:T(8,128)(2,1)S(1)} %all-to-all-done.1, s32[128]{0:T(128)S(1)} %eq.107), kind=kOutput, calls=%fused_computation.1 | convolution fusion | flops 554762240 | bytes 6423040 | tf_op jit(solution)/shard_map/dot_general | solution.py:105
  106.2 1.9 %collective-permute-start.2 = (bf16[128,8192]{1,0:T(8,128)(2,1)S(1)}, bf16[128,8192]{1,0:T(8,128)(2,1)}, u32[]{:S(2)}, u32[]{:S(2)}) collective-permute-start(bf16[128,8192]{1,0:T(8,128)(2,1)S(1)} %convolution_convert_fusion), channel_id=1, source_target_pairs={{0,1},{1,0},{2,3},{3,2},{4,5},{5,4},{6,7},{7,6},{8,9},{9,8},{10,11... | collective-permute-start | bytes 6291464 | tf_op jit(solution)/shard_map/ppermute | solution.py:108
  108.2 4.2 %collective-permute-done.2 = bf16[128,8192]{1,0:T(8,128)(2,1)} collective-permute-done((bf16[128,8192]{1,0:T(8,128)(2,1)S(1)}, bf16[128,8192]{1,0:T(8,128)(2,1)}, u32[]{:S(2)}, u32[]{:S(2)}) %collective-permute-start.2) | collective-permute-done | bytes 2097184 | tf_op jit(solution)/shard_map/ppermute | solution.py:108
  112.4 5.1 %add_convert_fusion = bf16[128,8192]{1,0:T(8,128)(2,1)} fusion(bf16[128,8192]{1,0:T(8,128)(2,1)} %collective-permute-done.2, bf16[256,8192]{1,0:T(8,128)(2,1)} %param.13, bf16[32,8,256]{2,1,0:T(8,128)(2,1)S(1)} %all-to-all-done.1, s32[128]{0:T(128)S(1)} %eq.93), kind=kOutput, calls=%fused_computation.11 | convolution fusion | flops 558956544 | bytes 8520192 | tf_op jit(solution)/shard_map/dot_general | solution.py:105
  117.4 37.0 %reduce-scatter.2.cloned.1.call-done = bf16[16,8192]{1,0:T(8,128)(2,1)} async-done(((bf16[128,8192]{1,0:T(8,128)(2,1)}), bf16[16,8192]{1,0:T(8,128)(2,1)}) %reduce-scatter.2.cloned.1.call-update) | async-done | bytes 262160 | tf_op jit(solution)/shard_map/reduce_scatter | solution.py:111
  (22 shorter events, 5.6 us)
Async XLA Ops:
  6.5 65.2 %copy-start = (bf16[256,256]{1,0:T(8,128)(2,1)S(1)}, bf16[256,256]{1,0:T(8,128)(2,1)}, u32[]{:S(2)}) copy-start(bf16[256,256]{1,0:T(8,128)(2,1)} %param.10) | copy-start | bytes 393220
  17.0 19.2 %all-to-all-start = ((bf16[16,16,256]{2,1,0:T(8,128)(2,1)}), bf16[16,16,256]{2,1,0:T(8,128)(2,1)S(1)}, u32[]{:S(2)}, u32[]{:S(2)}) async-start(bf16[16,16,256]{2,1,0:T(8,128)(2,1)} %constant_dynamic-update-slice_fusion), calls=%async_computation | async-start | bytes 262144 | tf_op jit(solution)/shard_map/all_to_all | solution.py:33
  49.7 14.2 %collective-permute-start = (bf16[1024,256]{1,0:T(8,128)(2,1)S(1)}, bf16[1024,256]{1,0:T(8,128)(2,1)S(1)}, u32[]{:S(2)}, u32[]{:S(2)}) collective-permute-start(bf16[1024,256]{1,0:T(8,128)(2,1)S(1)} %all_gather.3), channel_id=1, source_target_pairs={{0,64},{64,128},{128,192},{192,256},{256,320},{320,384},{384,448},... | collective-permute-start | bytes 1572872 | tf_op jit(solution)/shard_map/ppermute | solution.py:48
  63.9 4.1 %collective-permute-start.1 = (bf16[1024,256]{1,0:T(8,128)(2,1)S(1)}, bf16[1024,256]{1,0:T(8,128)(2,1)S(1)}, u32[]{:S(2)}, u32[]{:S(2)}) collective-permute-start(bf16[1024,256]{1,0:T(8,128)(2,1)S(1)} %collective-permute-done), channel_id=1, source_target_pairs={{0,1},{1,0},{2,3},{3,2},{4,5},{5,4},{6,7},{7,6},{8,9},{9,8},{10,11... | collective-permute-start | bytes 1572872 | tf_op jit(solution)/shard_map/ppermute | solution.py:49
  77.2 25.9 %all-to-all-start.1 = ((bf16[32,8,256]{2,1,0:T(8,128)(2,1)}), bf16[32,8,256]{2,1,0:T(8,128)(2,1)S(1)}, u32[]{:S(2)}, u32[]{:S(2)}) async-start(bf16[32,8,256]{2,1,0:T(8,128)(2,1)} %fusion.20), calls=%async_computation.1 | async-start | bytes 262144 | tf_op jit(solution)/shard_map/all_to_all | solution.py:91
  94.2 60.3 %reduce-scatter.2.cloned.1.call-start = ((), (), s32[]{:S(2)}) async-start(), calls=%async_computation.3 | async-start | bytes 2359296 | tf_op jit(solution)/shard_map/reduce_scatter | solution.py:111
  106.2 6.2 %collective-permute-start.2 = (bf16[128,8192]{1,0:T(8,128)(2,1)S(1)}, bf16[128,8192]{1,0:T(8,128)(2,1)}, u32[]{:S(2)}, u32[]{:S(2)}) collective-permute-start(bf16[128,8192]{1,0:T(8,128)(2,1)S(1)} %convolution_convert_fusion), channel_id=1, source_target_pairs={{0,1},{1,0},{2,3},{3,2},{4,5},{5,4},{6,7},{7,6},{8,9},{9,8},{10,11... | collective-permute-start | bytes 6291464 | tf_op jit(solution)/shard_map/ppermute | solution.py:108
Sparse Core Ops, SparseCore 0:
  117.6 36.8 reduce-scatter.1

commit v5 on v4

--- a/solution.py
+++ b/solution.py
@@ -26,18 +26,20 @@
     back = min(back, n_seq - 1)
 
     n_tp = n_z * n_core
-    pieces = []
-    for dest in range(n_tp):
-        h = dest * heads_here // group
-        pieces.append(jnp.concatenate([keys[:, h * HD:(h + 1) * HD], values[:, h * HD:(h + 1) * HD]], axis=1))
-    own = lax.all_to_all(jnp.stack(pieces), ("z", "core"), split_axis=0, concat_axis=0, tiled=True)
+    kv_heads = kv_width // HD
+    heads_of = np.arange(n_tp) * heads_here // group
+    k_h = jnp.transpose(keys.reshape(keys.shape[0], kv_heads, HD), (1, 0, 2))
+    v_h = jnp.transpose(values.reshape(values.shape[0], kv_heads, HD), (1, 0, 2))
+    pieces = jnp.concatenate([k_h, v_h], axis=2)[heads_of]
+    own = lax.all_to_all(pieces, ("z", "core"), split_axis=0, concat_axis=0, tiled=True)
     own = own.reshape(rows, 2 * HD)
 
     n_x = lax.axis_size("x")
     n_y = lax.axis_size("y")
     x = lax.axis_index("x")
     c = lax.axis_index("core")
-    row = lax.all_gather(own, "x", axis=0, tiled=True)
+    row = lax.all_to_all(jnp.broadcast_to(own[None], (n_x,) + own.shape), "x", split_axis=0, concat_axis=0, tiled=True)
+    row = row.reshape(n_x * rows, own.shape[1])
     rows_back = -(-back // n_x)
     assert rows_back <= n_core
     perm = []
@@ -108,7 +110,25 @@
     got = lax.ppermute(part_other, "core", perm=[(0, 1), (1, 0)])
     part_own = project(c)
     half = (part_own.astype(jnp.float32) + got.astype(jnp.float32)).astype(jnp.bfloat16)
-    return lax.psum_scatter(half, "z", scatter_dimension=0, tiled=True)
+    ring_cols = 3072
+    sc_cols = half.shape[1] - ring_cols
+    from_sc = lax.psum_scatter(half[:, :sc_cols], "z", scatter_dimension=0, tiled=True)
+    z = lax.axis_index("z")
+    step = 1 - 2 * c
+    chunks = half[:, sc_cols:].reshape(n_z, per_dev, ring_cols)
+    ring_perm = []
+    for zz in range(n_z):
+        ring_perm.append((zz * n_core, ((zz + 1) % n_z) * n_core))
+        ring_perm.append((zz * n_core + 1, ((zz - 1) % n_z) * n_core + 1))
+
+    def own_chunk(k):
+        return lax.dynamic_index_in_dim(chunks, (z - step * k) % n_z, 0, keepdims=False)
+
+    acc = own_chunk(1)
+    for k in range(1, n_z):
+        got_k = lax.ppermute(acc, ("z", "core"), perm=ring_perm)
+        acc = (got_k.astype(jnp.float32) + own_chunk(k + 1).astype(jnp.float32)).astype(jnp.bfloat16)
+    return jnp.concatenate([from_sc, acc], axis=1)
 
 def solution(mesh):
     n_seq, n_tp = mesh.devices.shape

time: 162 us -> 184 us (1.14)
  waiting for transfers between devices: 63.9 us -> 88.2 us
  starting transfers between devices: 34.8 us -> 53.4 us
  blocking collectives: 13.5 us -> 0 us
  other arithmetic: 20.2 us -> 10.3 us
  local copies, waits for them, and re-layouts: 1.85 us -> 5.04 us
    ppermute x0 -> x7, waiting for transfers between devices: none -> 41.4 us  [shards(): got_k = lax.ppermute(acc, ('z', 'core'), perm=ring_perm)]
    reduce_scatter x1, waiting for transfers between devices: 37 us -> 7.02 us  [shards(): lax.psum_scatter(half[:, :sc_cols], 'z', scatter_dimension=0, tiled=True)]
    ppermute x0 -> x7, starting transfers between devices: none -> 13.9 us  [shards(): got_k = lax.ppermute(acc, ('z', 'core'), perm=ring_perm)]
    all_gather x1 -> x0, blocking collectives: 13.5 us -> none  [shards(): row = lax.all_gather(own, 'x', axis=0, tiled=True)]
    all_to_all x1 -> x2, waiting for transfers between devices: 6.41 us -> 16.2 us  [the longest x1 8.22 us: shards(): lax.all_to_all(jnp.broadcast_to(own[None], (n_x,) + own.shape), 'x', spli...]
    unnamed x15 -> x0, other arithmetic: 9.01 us -> none
    all_to_all x1 -> x2, starting transfers between devices: 10.4 us -> 15.2 us  [the longest x1 10.4 us: shards(): lax.all_to_all(pieces, ('z', 'core'), split_axis=0, concat_axis=0, tiled=...]
    ppermute x1, waiting for transfers between devices: 8.33 us -> 10.5 us  [shards(): fetched = lax.ppermute(row, ('y', 'core'), perm=perm)]
  transfers between devices with their start and end apart: 6 -> 14, of which waited for: 5 -> 13; matrix products, arithmetic and copies ran while one was open for 5% -> 3% of each run, Pallas kernels for 0% -> 0%
where the time goes in v5:
time: 184 us; the launch traced here: 183 us
  waiting for transfers between devices  88.2 us (48%)
  starting transfers between devices  53.4 us (29%)
  between operations  13.9 us (8%)
  matrix products  12.2 us (7%)
  other arithmetic  10.3 us (6%)
  local copies, waits for them, and re-layouts  5.04 us (3%)
    ppermute x7, waiting for transfers between devices, shards(): got_k = lax.ppermute(acc, ('z', 'core'), perm=ring_perm)  41.4 us
    all_to_all x1, starting transfers between devices, shards(): lax.all_to_all(to_send, ('y', 'x'), split_axis=0, concat_axis=0, tiled=True)  16.7 us
    ppermute x7, starting transfers between devices, shards(): got_k = lax.ppermute(acc, ('z', 'core'), perm=ring_perm)  13.9 us
    ppermute x1, waiting for transfers between devices, shards(): fetched = lax.ppermute(row, ('y', 'core'), perm=perm)  10.5 us
    all_to_all x1, starting transfers between devices, shards(): lax.all_to_all(pieces, ('z', 'core'), split_axis=0, concat_axis=0, tiled=...  10.4 us
    all_to_all x1, waiting for transfers between devices, shards(): lax.all_to_all(to_send, ('y', 'x'), split_axis=0, concat_axis=0, tiled=True)  8.95 us
    all_to_all x1, waiting for transfers between devices, shards(): lax.all_to_all(jnp.broadcast_to(own[None], (n_x,) + own.shape), 'x', spli...  8.22 us
    all_to_all x1, waiting for transfers between devices, shards(): lax.all_to_all(pieces, ('z', 'core'), split_axis=0, concat_axis=0, tiled=...  7.96 us
  transfers between devices with their start and end apart: 14, of which 13 were waited for; matrix products, arithmetic and copies ran while one was open for 3% of the time, Pallas kernels for 0%

profile of v5, /device:TPU:6, one launch (start us, length us, event | category | flops | bytes accessed | tf_op | source)
XLA Modules:
  0.0 183.0 jit_solution(9810945672868258911)
XLA Ops:
  9.2 10.4 %all-to-all-start = ((bf16[16,16,256]{2,1,0:T(8,128)(2,1)}), bf16[16,16,256]{2,1,0:T(8,128)(2,1)S(1)}, u32[]{:S(2)}, u32[]{:S(2)}) async-start(bf16[16,16,256]{2,1,0:T(8,128)(2,1)} %gather_fusion), calls=%async_computation | async-start | bytes 262144 | tf_op jit(solution)/shard_map/all_to_all | solution.py:34
  20.4 8.0 %all-to-all-done = bf16[16,16,256]{2,1,0:T(8,128)(2,1)S(1)} async-done(((bf16[16,16,256]{2,1,0:T(8,128)(2,1)}), bf16[16,16,256]{2,1,0:T(8,128)(2,1)S(1)}, u32[]{:S(2)}, u32[]{:S(2)}) %all-to-all-start) | async-done | bytes 131104 | tf_op jit(solution)/shard_map/all_to_all | solution.py:34
  29.2 4.8 %all-to-all-start.1 = ((bf16[4,256,256]{2,1,0:T(8,128)(2,1)}), bf16[4,256,256]{2,1,0:T(8,128)(2,1)S(1)}, u32[]{:S(2)}, u32[]{:S(2)}) async-start(bf16[4,256,256]{2,1,0:T(8,128)(2,1)} %broadcast_in_dim.76), calls=%async_computation.1 | async-start | bytes 1048576 | tf_op jit(solution)/shard_map/all_to_all | solution.py:41
  34.2 8.2 %all-to-all-done.1 = bf16[4,256,256]{2,1,0:T(8,128)(2,1)S(1)} async-done(((bf16[4,256,256]{2,1,0:T(8,128)(2,1)}), bf16[4,256,256]{2,1,0:T(8,128)(2,1)S(1)}, u32[]{:S(2)}, u32[]{:S(2)}) %all-to-all-start.1) | async-done | bytes 524320 | tf_op jit(solution)/shard_map/all_to_all | solution.py:41
  42.4 3.5 %collective-permute-start = (bf16[1024,256]{1,0:T(8,128)(2,1)S(1)}, bf16[1024,256]{1,0:T(8,128)(2,1)S(1)}, u32[]{:S(2)}, u32[]{:S(2)}) collective-permute-start(bf16[1024,256]{1,0:T(8,128)(2,1)S(1)} %bitcast.123), channel_id=1, source_target_pairs={{0,64},{64,128},{128,192},{192,256},{256,320},{320,384},{384,448},... | collective-permute-start | bytes 1572872 | tf_op jit(solution)/shard_map/ppermute | solution.py:50
  47.5 10.5 %collective-permute-done = bf16[1024,256]{1,0:T(8,128)(2,1)S(1)} collective-permute-done((bf16[1024,256]{1,0:T(8,128)(2,1)S(1)}, bf16[1024,256]{1,0:T(8,128)(2,1)S(1)}, u32[]{:S(2)}, u32[]{:S(2)}) %collective-permute-start) | collective-permute-done | bytes 524320 | tf_op jit(solution)/shard_map/ppermute | solution.py:50
  58.0 1.9 %collective-permute-start.1 = (bf16[1024,256]{1,0:T(8,128)(2,1)S(1)}, bf16[1024,256]{1,0:T(8,128)(2,1)S(1)}, u32[]{:S(2)}, u32[]{:S(2)}) collective-permute-start(bf16[1024,256]{1,0:T(8,128)(2,1)S(1)} %collective-permute-done), channel_id=1, source_target_pairs={{0,1},{1,0},{2,3},{3,2},{4,5},{5,4},{6,7},{7,6},{8,9},{9,8},{10,11... | collective-permute-start | bytes 1572872 | tf_op jit(solution)/shard_map/ppermute | solution.py:51
  59.9 2.2 %and_and_fusion = pred[256,2304]{0,1:T(8,128)(4,1)S(1)} fusion(s32[256]{0:T(256)S(1)} %dynamic_slice.39, s32[256]{0:T(256)S(1)} %iota_add_fusion.1, s32[2304]{0:T(1024)S(1)} %get-tuple-element.23, s32[2304]{0:T(1024)S(1)} %get-tuple-element.24, pred[2304]{0:T(1024)(128)(4,1)S(1)} %broadcast_compare_fusion), kind=kLoop, calls=%fused_computation.15 | loop fusion | flops 2359296 | bytes 612608 | tf_op jit(solution)/shard_map/and | solution.py:66
  62.2 3.6 %fusion.10 = bf16[2304,256]{1,0:T(8,128)(2,1)S(1)} fusion(s32[]{:T(128)S(6)} %select_n.118, bf16[1024,256]{1,0:T(8,128)(2,1)S(1)} %get-tuple-element.18, bf16[1024,256]{1,0:T(8,128)(2,1)S(1)} %get-tuple-element.17, bf16[1024,256]{1,0:T(8,128)(2,1)S(1)} %bitcast.124), kind=kLoop, calls=%fused_computation.20 | loop fusion | flops 3538944 | bytes 2752516 | tf_op jit(solution)/shard_map/concatenate | solution.py:53
  65.8 2.2 %fusion.57 = f32[2,256]{1,0:T(2,128)S(1)} fusion(pred[256,2304]{0,1:T(8,128)(4,1)S(1)} %and_and_fusion, bf16[2304,256]{1,0:T(8,128)(2,1)S(1)} %fusion.10, bf16[256,256]{1,0:T(8,128)(2,1)S(1)} %copy-done), kind=kOutput, calls=%fused_computation.84 | convolution fusion | flops 307890432 | bytes 1902592 | tf_op jit(solution)/shard_map/sub | solution.py:75
  68.0 2.3 %fusion.17 = bf16[256,2,128]{0,2,1:T(8,128)(2,1)S(1)} fusion(bf16[2304,256]{1,0:T(8,128)(2,1)S(1)} %fusion.10, f32[256,2]{0,1:T(2,128)S(1)} %bitcast.129, pred[256,2304]{0,1:T(8,128)(4,1)S(1)} %and_and_fusion, bf16[256,256]{1,0:T(8,128)(2,1)S(1)} %copy-done), kind=kOutput, calls=%fused_computation.24 | convolution fusion | flops 610011904 | bytes 2623488 | tf_op jit(solution)/shard_map/hqk,kd->hqd/dot_general | solution.py:77
  71.2 16.7 %all-to-all-start.2 = ((bf16[32,8,256]{2,1,0:T(8,128)(2,1)}), bf16[32,8,256]{2,1,0:T(8,128)(2,1)S(1)}, u32[]{:S(2)}, u32[]{:S(2)}) async-start(bf16[32,8,256]{2,1,0:T(8,128)(2,1)} %fusion.20), calls=%async_computation.2 | async-start | bytes 262144 | tf_op jit(solution)/shard_map/all_to_all | solution.py:93
  88.5 9.0 %all-to-all-done.2 = bf16[32,8,256]{2,1,0:T(8,128)(2,1)S(1)} async-done(((bf16[32,8,256]{2,1,0:T(8,128)(2,1)}), bf16[32,8,256]{2,1,0:T(8,128)(2,1)S(1)}, u32[]{:S(2)}, u32[]{:S(2)}) %all-to-all-start.2) | async-done | bytes 131104 | tf_op jit(solution)/shard_map/all_to_all | solution.py:93
  97.5 3.1 %convolution_convert_fusion = bf16[128,8192]{1,0:T(8,128)(2,1)S(1)} fusion(bf16[256,8192]{1,0:T(8,128)(2,1)} %param.15, bf16[32,8,256]{2,1,0:T(8,128)(2,1)S(1)} %all-to-all-done.2, s32[128]{0:T(128)S(1)} %eq.116), kind=kOutput, calls=%fused_computation.2 | convolution fusion | flops 554762240 | bytes 6423040 | tf_op jit(solution)/shard_map/dot_general | solution.py:107
  100.6 1.9 %collective-permute-start.2 = (bf16[128,8192]{1,0:T(8,128)(2,1)S(1)}, bf16[128,8192]{1,0:T(8,128)(2,1)}, u32[]{:S(2)}, u32[]{:S(2)}) collective-permute-start(bf16[128,8192]{1,0:T(8,128)(2,1)S(1)} %convolution_convert_fusion), channel_id=1, source_target_pairs={{0,1},{1,0},{2,3},{3,2},{4,5},{5,4},{6,7},{7,6},{8,9},{9,8},{10,11... | collective-permute-start | bytes 6291464 | tf_op jit(solution)/shard_map/ppermute | solution.py:110
  102.6 4.1 %collective-permute-done.2 = bf16[128,8192]{1,0:T(8,128)(2,1)} collective-permute-done((bf16[128,8192]{1,0:T(8,128)(2,1)S(1)}, bf16[128,8192]{1,0:T(8,128)(2,1)}, u32[]{:S(2)}, u32[]{:S(2)}) %collective-permute-start.2) | collective-permute-done | bytes 2097184 | tf_op jit(solution)/shard_map/ppermute | solution.py:110
  106.7 3.8 %add_convert_fusion = bf16[128,8192]{1,0:T(8,128)(2,1)S(1)} fusion(bf16[128,8192]{1,0:T(8,128)(2,1)} %collective-permute-done.2, bf16[256,8192]{1,0:T(8,128)(2,1)} %param.15, bf16[32,8,256]{2,1,0:T(8,128)(2,1)S(1)} %all-to-all-done.2, s32[128]{0:T(128)S(1)} %eq.102), kind=kOutput, calls=%fused_computation.12 | convolution fusion | flops 558956544 | bytes 8520192 | tf_op jit(solution)/shard_map/dot_general | solution.py:107
  110.6 2.0 %collective-permute-start.3 = (bf16[16,3072]{1,0:T(8,128)(2,1)S(1)}, bf16[16,3072]{1,0:T(8,128)(2,1)S(1)}, u32[]{:S(2)}, u32[]{:S(2)}) collective-permute-start(bf16[16,3072]{1,0:T(8,128)(2,1)S(1)} %dynamic-slice_bitcast_fusion), channel_id=1, source_target_pairs={{0,2},{1,15},{2,4},{3,1},{4,6},{5,3},{6,8},{7,5},{8,10},{9,7},{10,... | collective-permute-start | bytes 294920 | tf_op jit(solution)/shard_map/ppermute | solution.py:129
  112.7 5.6 %collective-permute-done.3 = bf16[16,3072]{1,0:T(8,128)(2,1)S(1)} collective-permute-done((bf16[16,3072]{1,0:T(8,128)(2,1)S(1)}, bf16[16,3072]{1,0:T(8,128)(2,1)S(1)}, u32[]{:S(2)}, u32[]{:S(2)}) %collective-permute-start.3) | collective-permute-done | bytes 98336 | tf_op jit(solution)/shard_map/ppermute | solution.py:129
  118.3 1.9 %collective-permute-start.4 = (bf16[16,3072]{1,0:T(8,128)(2,1)S(1)}, bf16[16,3072]{1,0:T(8,128)(2,1)S(1)}, u32[]{:S(2)}, u32[]{:S(2)}) collective-permute-start(bf16[16,3072]{1,0:T(8,128)(2,1)S(1)} %fusion.28), channel_id=1, source_target_pairs={{0,2},{1,15},{2,4},{3,1},{4,6},{5,3},{6,8},{7,5},{8,10},{9,7},{10,... | collective-permute-start | bytes 294920 | tf_op jit(solution)/shard_map/ppermute | solution.py:129
  120.3 5.8 %collective-permute-done.4 = bf16[16,3072]{1,0:T(8,128)(2,1)S(1)} collective-permute-done((bf16[16,3072]{1,0:T(8,128)(2,1)S(1)}, bf16[16,3072]{1,0:T(8,128)(2,1)S(1)}, u32[]{:S(2)}, u32[]{:S(2)}) %collective-permute-start.4) | collective-permute-done | bytes 98336 | tf_op jit(solution)/shard_map/ppermute | solution.py:129
  126.1 1.9 %collective-permute-start.5 = (bf16[16,3072]{1,0:T(8,128)(2,1)S(1)}, bf16[16,3072]{1,0:T(8,128)(2,1)S(1)}, u32[]{:S(2)}, u32[]{:S(2)}) collective-permute-start(bf16[16,3072]{1,0:T(8,128)(2,1)S(1)} %fusion.27), channel_id=1, source_target_pairs={{0,2},{1,15},{2,4},{3,1},{4,6},{5,3},{6,8},{7,5},{8,10},{9,7},{10,... | collective-permute-start | bytes 294920 | tf_op jit(solution)/shard_map/ppermute | solution.py:129
  128.1 5.8 %collective-permute-done.5 = bf16[16,3072]{1,0:T(8,128)(2,1)S(1)} collective-permute-done((bf16[16,3072]{1,0:T(8,128)(2,1)S(1)}, bf16[16,3072]{1,0:T(8,128)(2,1)S(1)}, u32[]{:S(2)}, u32[]{:S(2)}) %collective-permute-start.5) | collective-permute-done | bytes 98336 | tf_op jit(solution)/shard_map/ppermute | solution.py:129
  133.8 1.9 %collective-permute-start.6 = (bf16[16,3072]{1,0:T(8,128)(2,1)S(1)}, bf16[16,3072]{1,0:T(8,128)(2,1)S(1)}, u32[]{:S(2)}, u32[]{:S(2)}) collective-permute-start(bf16[16,3072]{1,0:T(8,128)(2,1)S(1)} %fusion.26), channel_id=1, source_target_pairs={{0,2},{1,15},{2,4},{3,1},{4,6},{5,3},{6,8},{7,5},{8,10},{9,7},{10,... | collective-permute-start | bytes 294920 | tf_op jit(solution)/shard_map/ppermute | solution.py:129
  137.0 4.6 %collective-permute-done.6 = bf16[16,3072]{1,0:T(8,128)(2,1)S(1)} collective-permute-done((bf16[16,3072]{1,0:T(8,128)(2,1)S(1)}, bf16[16,3072]{1,0:T(8,128)(2,1)S(1)}, u32[]{:S(2)}, u32[]{:S(2)}) %collective-permute-start.6) | collective-permute-done | bytes 98336 | tf_op jit(solution)/shard_map/ppermute | solution.py:129
  141.6 1.9 %collective-permute-start.7 = (bf16[16,3072]{1,0:T(8,128)(2,1)S(1)}, bf16[16,3072]{1,0:T(8,128)(2,1)S(1)}, u32[]{:S(2)}, u32[]{:S(2)}) collective-permute-start(bf16[16,3072]{1,0:T(8,128)(2,1)S(1)} %fusion.25), channel_id=1, source_target_pairs={{0,2},{1,15},{2,4},{3,1},{4,6},{5,3},{6,8},{7,5},{8,10},{9,7},{10,... | collective-permute-start | bytes 294920 | tf_op jit(solution)/shard_map/ppermute | solution.py:129
  143.6 5.9 %collective-permute-done.7 = bf16[16,3072]{1,0:T(8,128)(2,1)S(1)} collective-permute-done((bf16[16,3072]{1,0:T(8,128)(2,1)S(1)}, bf16[16,3072]{1,0:T(8,128)(2,1)S(1)}, u32[]{:S(2)}, u32[]{:S(2)}) %collective-permute-start.7) | collective-permute-done | bytes 98336 | tf_op jit(solution)/shard_map/ppermute | solution.py:129
  149.5 2.2 %collective-permute-start.8 = (bf16[16,3072]{1,0:T(8,128)(2,1)S(1)}, bf16[16,3072]{1,0:T(8,128)(2,1)S(1)}, u32[]{:S(2)}, u32[]{:S(2)}) collective-permute-start(bf16[16,3072]{1,0:T(8,128)(2,1)S(1)} %fusion.24), channel_id=1, source_target_pairs={{0,2},{1,15},{2,4},{3,1},{4,6},{5,3},{6,8},{7,5},{8,10},{9,7},{10,... | collective-permute-start | bytes 294920 | tf_op jit(solution)/shard_map/ppermute | solution.py:129
  151.8 6.9 %collective-permute-done.8 = bf16[16,3072]{1,0:T(8,128)(2,1)S(1)} collective-permute-done((bf16[16,3072]{1,0:T(8,128)(2,1)S(1)}, bf16[16,3072]{1,0:T(8,128)(2,1)S(1)}, u32[]{:S(2)}, u32[]{:S(2)}) %collective-permute-start.8) | collective-permute-done | bytes 98336 | tf_op jit(solution)/shard_map/ppermute | solution.py:129
  158.7 1.9 %collective-permute-start.9 = (bf16[16,3072]{1,0:T(8,128)(2,1)S(1)}, bf16[16,3072]{1,0:T(8,128)(2,1)S(1)}, u32[]{:S(2)}, u32[]{:S(2)}) collective-permute-start(bf16[16,3072]{1,0:T(8,128)(2,1)S(1)} %fusion.23), channel_id=1, source_target_pairs={{0,2},{1,15},{2,4},{3,1},{4,6},{5,3},{6,8},{7,5},{8,10},{9,7},{10,... | collective-permute-start | bytes 294920 | tf_op jit(solution)/shard_map/ppermute | solution.py:129
  160.6 6.9 %collective-permute-done.9 = bf16[16,3072]{1,0:T(8,128)(2,1)S(1)} collective-permute-done((bf16[16,3072]{1,0:T(8,128)(2,1)S(1)}, bf16[16,3072]{1,0:T(8,128)(2,1)S(1)}, u32[]{:S(2)}, u32[]{:S(2)}) %collective-permute-start.9) | collective-permute-done | bytes 98336 | tf_op jit(solution)/shard_map/ppermute | solution.py:129
  167.5 7.0 %reduce-scatter.2.cloned.1.call-done = bf16[16,5120]{1,0:T(8,128)(2,1)} async-done(((bf16[128,5120]{1,0:T(8,128)(2,1)}), bf16[16,5120]{1,0:T(8,128)(2,1)}) %reduce-scatter.2.cloned.1.call-update) | async-done | bytes 163856 | tf_op jit(solution)/shard_map/reduce_scatter | solution.py:115
  (40 shorter events, 10.7 us)
Async XLA Ops:
  6.5 59.3 %copy-start = (bf16[256,256]{1,0:T(8,128)(2,1)S(1)}, bf16[256,256]{1,0:T(8,128)(2,1)}, u32[]{:S(2)}) copy-start(bf16[256,256]{1,0:T(8,128)(2,1)} %param.12) | copy-start | bytes 393220
  6.5 27.5 %copy-start.2 = (s32[8192]{0:T(1024)S(1)}, s32[8192]{0:T(1024)}, u32[]{:S(2)}) copy-start(s32[8192]{0:T(1024)} %param.10) | copy-start | bytes 98308
  6.5 27.4 %copy-start.1 = (s32[8192]{0:T(1024)S(1)}, s32[8192]{0:T(1024)}, u32[]{:S(2)}) copy-start(s32[8192]{0:T(1024)} %param.11) | copy-start | bytes 98308
  9.2 19.2 %all-to-all-start = ((bf16[16,16,256]{2,1,0:T(8,128)(2,1)}), bf16[16,16,256]{2,1,0:T(8,128)(2,1)S(1)}, u32[]{:S(2)}, u32[]{:S(2)}) async-start(bf16[16,16,256]{2,1,0:T(8,128)(2,1)} %gather_fusion), calls=%async_computation | async-start | bytes 262144 | tf_op jit(solution)/shard_map/all_to_all | solution.py:34
  29.2 13.2 %all-to-all-start.1 = ((bf16[4,256,256]{2,1,0:T(8,128)(2,1)}), bf16[4,256,256]{2,1,0:T(8,128)(2,1)S(1)}, u32[]{:S(2)}, u32[]{:S(2)}) async-start(bf16[4,256,256]{2,1,0:T(8,128)(2,1)} %broadcast_in_dim.76), calls=%async_computation.1 | async-start | bytes 1048576 | tf_op jit(solution)/shard_map/all_to_all | solution.py:41
  42.4 15.6 %collective-permute-start = (bf16[1024,256]{1,0:T(8,128)(2,1)S(1)}, bf16[1024,256]{1,0:T(8,128)(2,1)S(1)}, u32[]{:S(2)}, u32[]{:S(2)}) collective-permute-start(bf16[1024,256]{1,0:T(8,128)(2,1)S(1)} %bitcast.123), channel_id=1, source_target_pairs={{0,64},{64,128},{128,192},{192,256},{256,320},{320,384},{384,448},... | collective-permute-start | bytes 1572872 | tf_op jit(solution)/shard_map/ppermute | solution.py:50
  58.0 4.1 %collective-permute-start.1 = (bf16[1024,256]{1,0:T(8,128)(2,1)S(1)}, bf16[1024,256]{1,0:T(8,128)(2,1)S(1)}, u32[]{:S(2)}, u32[]{:S(2)}) collective-permute-start(bf16[1024,256]{1,0:T(8,128)(2,1)S(1)} %collective-permute-done), channel_id=1, source_target_pairs={{0,1},{1,0},{2,3},{3,2},{4,5},{5,4},{6,7},{7,6},{8,9},{9,8},{10,11... | collective-permute-start | bytes 1572872 | tf_op jit(solution)/shard_map/ppermute | solution.py:51
  71.2 26.2 %all-to-all-start.2 = ((bf16[32,8,256]{2,1,0:T(8,128)(2,1)}), bf16[32,8,256]{2,1,0:T(8,128)(2,1)S(1)}, u32[]{:S(2)}, u32[]{:S(2)}) async-start(bf16[32,8,256]{2,1,0:T(8,128)(2,1)} %fusion.20), calls=%async_computation.2 | async-start | bytes 262144 | tf_op jit(solution)/shard_map/all_to_all | solution.py:93
  88.0 86.6 %reduce-scatter.2.cloned.1.call-start = ((), (), s32[]{:S(2)}) async-start(), calls=%async_computation.4 | async-start | bytes 1474560 | tf_op jit(solution)/shard_map/reduce_scatter | solution.py:115
  100.6 6.2 %collective-permute-start.2 = (bf16[128,8192]{1,0:T(8,128)(2,1)S(1)}, bf16[128,8192]{1,0:T(8,128)(2,1)}, u32[]{:S(2)}, u32[]{:S(2)}) collective-permute-start(bf16[128,8192]{1,0:T(8,128)(2,1)S(1)} %convolution_convert_fusion), channel_id=1, source_target_pairs={{0,1},{1,0},{2,3},{3,2},{4,5},{5,4},{6,7},{7,6},{8,9},{9,8},{10,11... | collective-permute-start | bytes 6291464 | tf_op jit(solution)/shard_map/ppermute | solution.py:110
  110.6 7.7 %collective-permute-start.3 = (bf16[16,3072]{1,0:T(8,128)(2,1)S(1)}, bf16[16,3072]{1,0:T(8,128)(2,1)S(1)}, u32[]{:S(2)}, u32[]{:S(2)}) collective-permute-start(bf16[16,3072]{1,0:T(8,128)(2,1)S(1)} %dynamic-slice_bitcast_fusion), channel_id=1, source_target_pairs={{0,2},{1,15},{2,4},{3,1},{4,6},{5,3},{6,8},{7,5},{8,10},{9,7},{10,... | collective-permute-start | bytes 294920 | tf_op jit(solution)/shard_map/ppermute | solution.py:129
  118.3 7.7 %collective-permute-start.4 = (bf16[16,3072]{1,0:T(8,128)(2,1)S(1)}, bf16[16,3072]{1,0:T(8,128)(2,1)S(1)}, u32[]{:S(2)}, u32[]{:S(2)}) collective-permute-start(bf16[16,3072]{1,0:T(8,128)(2,1)S(1)} %fusion.28), channel_id=1, source_target_pairs={{0,2},{1,15},{2,4},{3,1},{4,6},{5,3},{6,8},{7,5},{8,10},{9,7},{10,... | collective-permute-start | bytes 294920 | tf_op jit(solution)/shard_map/ppermute | solution.py:129
  126.1 7.7 %collective-permute-start.5 = (bf16[16,3072]{1,0:T(8,128)(2,1)S(1)}, bf16[16,3072]{1,0:T(8,128)(2,1)S(1)}, u32[]{:S(2)}, u32[]{:S(2)}) collective-permute-start(bf16[16,3072]{1,0:T(8,128)(2,1)S(1)} %fusion.27), channel_id=1, source_target_pairs={{0,2},{1,15},{2,4},{3,1},{4,6},{5,3},{6,8},{7,5},{8,10},{9,7},{10,... | collective-permute-start | bytes 294920 | tf_op jit(solution)/shard_map/ppermute | solution.py:129
  133.8 7.7 %collective-permute-start.6 = (bf16[16,3072]{1,0:T(8,128)(2,1)S(1)}, bf16[16,3072]{1,0:T(8,128)(2,1)S(1)}, u32[]{:S(2)}, u32[]{:S(2)}) collective-permute-start(bf16[16,3072]{1,0:T(8,128)(2,1)S(1)} %fusion.26), channel_id=1, source_target_pairs={{0,2},{1,15},{2,4},{3,1},{4,6},{5,3},{6,8},{7,5},{8,10},{9,7},{10,... | collective-permute-start | bytes 294920 | tf_op jit(solution)/shard_map/ppermute | solution.py:129
  141.6 7.9 %collective-permute-start.7 = (bf16[16,3072]{1,0:T(8,128)(2,1)S(1)}, bf16[16,3072]{1,0:T(8,128)(2,1)S(1)}, u32[]{:S(2)}, u32[]{:S(2)}) collective-permute-start(bf16[16,3072]{1,0:T(8,128)(2,1)S(1)} %fusion.25), channel_id=1, source_target_pairs={{0,2},{1,15},{2,4},{3,1},{4,6},{5,3},{6,8},{7,5},{8,10},{9,7},{10,... | collective-permute-start | bytes 294920 | tf_op jit(solution)/shard_map/ppermute | solution.py:129
  149.5 9.2 %collective-permute-start.8 = (bf16[16,3072]{1,0:T(8,128)(2,1)S(1)}, bf16[16,3072]{1,0:T(8,128)(2,1)S(1)}, u32[]{:S(2)}, u32[]{:S(2)}) collective-permute-start(bf16[16,3072]{1,0:T(8,128)(2,1)S(1)} %fusion.24), channel_id=1, source_target_pairs={{0,2},{1,15},{2,4},{3,1},{4,6},{5,3},{6,8},{7,5},{8,10},{9,7},{10,... | collective-permute-start | bytes 294920 | tf_op jit(solution)/shard_map/ppermute | solution.py:129
  158.7 8.8 %collective-permute-start.9 = (bf16[16,3072]{1,0:T(8,128)(2,1)S(1)}, bf16[16,3072]{1,0:T(8,128)(2,1)S(1)}, u32[]{:S(2)}, u32[]{:S(2)}) collective-permute-start(bf16[16,3072]{1,0:T(8,128)(2,1)S(1)} %fusion.23), channel_id=1, source_target_pairs={{0,2},{1,15},{2,4},{3,1},{4,6},{5,3},{6,8},{7,5},{8,10},{9,7},{10,... | collective-permute-start | bytes 294920 | tf_op jit(solution)/shard_map/ppermute | solution.py:129
Sparse Core Ops, SparseCore 0:
  137.1 37.3 reduce-scatter.1

commit v6 on v4

--- a/solution.py
+++ b/solution.py
@@ -26,18 +26,18 @@
     back = min(back, n_seq - 1)
 
     n_tp = n_z * n_core
-    pieces = []
-    for dest in range(n_tp):
-        h = dest * heads_here // group
-        pieces.append(jnp.concatenate([keys[:, h * HD:(h + 1) * HD], values[:, h * HD:(h + 1) * HD]], axis=1))
-    own = lax.all_to_all(jnp.stack(pieces), ("z", "core"), split_axis=0, concat_axis=0, tiled=True)
-    own = own.reshape(rows, 2 * HD)
+    kv_heads = kv_width // HD
+    n_x = lax.axis_size("x")
+    heads_of = np.tile(np.arange(n_tp) * heads_here // group, n_x)
+    k_h = jnp.transpose(keys.reshape(keys.shape[0], kv_heads, HD), (1, 0, 2))
+    v_h = jnp.transpose(values.reshape(values.shape[0], kv_heads, HD), (1, 0, 2))
+    pieces = jnp.concatenate([k_h, v_h], axis=2)[heads_of]
+    row = lax.all_to_all(pieces, ("x", "z", "core"), split_axis=0, concat_axis=0, tiled=True)
+    row = row.reshape(n_x * rows, 2 * HD)
 
-    n_x = lax.axis_size("x")
     n_y = lax.axis_size("y")
     x = lax.axis_index("x")
     c = lax.axis_index("core")
-    row = lax.all_gather(own, "x", axis=0, tiled=True)
     rows_back = -(-back // n_x)
     assert rows_back <= n_core
     perm = []

time: 162 us -> 156 us (0.963)
  blocking collectives: 13.5 us -> 0 us
  waiting for transfers between devices: 63.9 us -> 74 us
  other arithmetic: 20.2 us -> 11.3 us
  starting transfers between devices: 34.8 us -> 39.6 us
    all_gather x1 -> x0, blocking collectives: 13.5 us -> none  [shards(): row = lax.all_gather(own, 'x', axis=0, tiled=True)]
    unnamed x15 -> x0, other arithmetic: 9.01 us -> none
    all_to_all x1, waiting for transfers between devices: 6.41 us -> 14.4 us  [shards(): lax.all_to_all(pieces, ('x', 'z', 'core'), split_axis=0, concat_axis=0, t...]
    all_to_all x1, starting transfers between devices: 10.4 us -> 14 us  [shards(): lax.all_to_all(pieces, ('x', 'z', 'core'), split_axis=0, concat_axis=0, t...]
where the time goes in v6:
time: 156 us; the launch traced here: 155 us
  waiting for transfers between devices  74 us (47%)
  starting transfers between devices  39.6 us (25%)
  matrix products  13.5 us (9%)
  between operations  13.5 us (9%)
  other arithmetic  11.3 us (7%)
  local copies, waits for them, and re-layouts  3.14 us (2%)
    reduce_scatter x1, waiting for transfers between devices, shards(): return lax.psum_scatter(half, 'z', scatter_dimension=0, tiled=True)  37.7 us
    all_to_all x1, starting transfers between devices, shards(): lax.all_to_all(to_send, ('y', 'x'), split_axis=0, concat_axis=0, tiled=True)  17.5 us
    all_to_all x1, waiting for transfers between devices, shards(): lax.all_to_all(pieces, ('x', 'z', 'core'), split_axis=0, concat_axis=0, t...  14.4 us
    all_to_all x1, starting transfers between devices, shards(): lax.all_to_all(pieces, ('x', 'z', 'core'), split_axis=0, concat_axis=0, t...  14 us
    ppermute x1, waiting for transfers between devices, shards(): fetched = lax.ppermute(row, ('y', 'core'), perm=perm)  9.28 us
    all_to_all x1, waiting for transfers between devices, shards(): lax.all_to_all(to_send, ('y', 'x'), split_axis=0, concat_axis=0, tiled=True)  8.45 us
    dot_general x2, matrix products, project(): jnp.dot(relaid, out_weight, preferred_element_type=jnp.float32)  8.13 us
    ppermute x1, waiting for transfers between devices, shards(): got = lax.ppermute(part_other, 'core', perm=[(0, 1), (1, 0)])  4.18 us
  transfers between devices with their start and end apart: 6, of which 5 were waited for; matrix products, arithmetic and copies ran while one was open for 5% of the time, Pallas kernels for 0%

profile of v6, /device:TPU:6, one launch (start us, length us, event | category | flops | bytes accessed | tf_op | source)
XLA Modules:
  0.0 155.1 jit_solution(8466717036042479760)
XLA Ops:
  6.5 0.7 pad_clamp_fusion
  7.2 0.7 bitcast_bitcast_fusion
  8.0 1.4 gather_fusion
  9.4 14.0 %all-to-all-start = ((bf16[64,16,256]{2,1,0:T(8,128)(2,1)}), bf16[64,16,256]{2,1,0:T(8,128)(2,1)S(1)}, u32[]{:S(2)}, u32[]{:S(2)}) async-start(bf16[64,16,256]{2,1,0:T(8,128)(2,1)} %gather_fusion), calls=%async_computation | async-start | bytes 1048576 | tf_op jit(solution)/shard_map/all_to_all | solution.py:35
  23.4 0.8 dynamic_slice.14
  24.2 0.8 and_select_fusion
  25.0 0.8 pad_dynamic-slice_fusion.3
  25.7 14.4 %all-to-all-done = bf16[64,16,256]{2,1,0:T(8,128)(2,1)S(1)} async-done(((bf16[64,16,256]{2,1,0:T(8,128)(2,1)}), bf16[64,16,256]{2,1,0:T(8,128)(2,1)S(1)}, u32[]{:S(2)}, u32[]{:S(2)}) %all-to-all-start) | async-done | bytes 524320 | tf_op jit(solution)/shard_map/all_to_all | solution.py:35
  40.1 3.5 %collective-permute-start = (bf16[1024,256]{1,0:T(8,128)(2,1)S(1)}, bf16[1024,256]{1,0:T(8,128)(2,1)S(1)}, u32[]{:S(2)}, u32[]{:S(2)}) collective-permute-start(bf16[1024,256]{1,0:T(8,128)(2,1)S(1)} %bitcast.90), channel_id=1, source_target_pairs={{0,64},{64,128},{128,192},{192,256},{256,320},{320,384},{384,448},... | collective-permute-start | bytes 1572872 | tf_op jit(solution)/shard_map/ppermute | solution.py:48
  43.6 2.0 %select_reduce_fusion = s32[256]{0:T(256)S(1)} fusion(s32[8192]{0:T(1024)} %param.11, s32[256]{0:T(256)S(1)} %iota_add_fusion.1), kind=kLoop, calls=%fused_computation.5 | loop fusion | flops 6291200 | bytes 34816 | tf_op jit(solution)/shard_map/reduce_sum | solution.py:84
  45.6 0.2 convert_reduce_fusion
  45.8 0.2 convert_reduce_fusion.1
  46.0 9.3 %collective-permute-done = bf16[1024,256]{1,0:T(8,128)(2,1)S(1)} collective-permute-done((bf16[1024,256]{1,0:T(8,128)(2,1)S(1)}, bf16[1024,256]{1,0:T(8,128)(2,1)S(1)}, u32[]{:S(2)}, u32[]{:S(2)}) %collective-permute-start) | collective-permute-done | bytes 524320 | tf_op jit(solution)/shard_map/ppermute | solution.py:48
  55.3 2.6 %collective-permute-start.1 = (bf16[1024,256]{1,0:T(8,128)(2,1)S(1)}, bf16[1024,256]{1,0:T(8,128)(2,1)S(1)}, u32[]{:S(2)}, u32[]{:S(2)}) collective-permute-start(bf16[1024,256]{1,0:T(8,128)(2,1)S(1)} %collective-permute-done), channel_id=1, source_target_pairs={{0,1},{1,0},{2,3},{3,2},{4,5},{5,4},{6,7},{7,6},{8,9},{9,8},{10,11... | collective-permute-start | bytes 1572872 | tf_op jit(solution)/shard_map/ppermute | solution.py:49
  57.9 2.2 %and_and_fusion = pred[256,2304]{0,1:T(8,128)(4,1)S(1)} fusion(s32[256]{0:T(256)S(1)} %dynamic_slice.14, s32[256]{0:T(256)S(1)} %iota_add_fusion.1, s32[2304]{0:T(1024)S(1)} %get-tuple-element.23, s32[2304]{0:T(1024)S(1)} %get-tuple-element.24, pred[2304]{0:T(1024)(128)(4,1)S(1)} %broadcast_compare_fusion), kind=kLoop, calls=%fused_computation.15 | loop fusion | flops 2359296 | bytes 612608 | tf_op jit(solution)/shard_map/and | solution.py:64
  60.1 0.1 broadcast_select_fusion
  60.2 3.6 %fusion.10 = bf16[2304,256]{1,0:T(8,128)(2,1)S(1)} fusion(s32[]{:T(128)S(6)} %select_n.59, bf16[1024,256]{1,0:T(8,128)(2,1)S(1)} %get-tuple-element.18, bf16[1024,256]{1,0:T(8,128)(2,1)S(1)} %get-tuple-element.17, bf16[1024,256]{1,0:T(8,128)(2,1)S(1)} %bitcast.91), kind=kLoop, calls=%fused_computation.20 | loop fusion | flops 3538944 | bytes 2752516 | tf_op jit(solution)/shard_map/concatenate | solution.py:51
  63.8 2.2 %fusion.50 = f32[2,256]{1,0:T(2,128)S(1)} fusion(pred[256,2304]{0,1:T(8,128)(4,1)S(1)} %and_and_fusion, bf16[2304,256]{1,0:T(8,128)(2,1)S(1)} %fusion.10, bf16[256,256]{1,0:T(8,128)(2,1)S(1)} %copy-done), kind=kOutput, calls=%fused_computation.68 | convolution fusion | flops 307890432 | bytes 1902592 | tf_op jit(solution)/shard_map/sub | solution.py:73
  66.0 2.3 %fusion.17 = bf16[256,2,128]{0,2,1:T(8,128)(2,1)S(1)} fusion(bf16[2304,256]{1,0:T(8,128)(2,1)S(1)} %fusion.10, f32[256,2]{0,1:T(2,128)S(1)} %bitcast.95, pred[256,2304]{0,1:T(8,128)(4,1)S(1)} %and_and_fusion, bf16[256,256]{1,0:T(8,128)(2,1)S(1)} %copy-done), kind=kOutput, calls=%fused_computation.24 | convolution fusion | flops 610011904 | bytes 2623488 | tf_op jit(solution)/shard_map/hqk,kd->hqd/dot_general | solution.py:75
  68.3 0.9 fusion.20
  69.2 17.5 %all-to-all-start.1 = ((bf16[32,8,256]{2,1,0:T(8,128)(2,1)}), bf16[32,8,256]{2,1,0:T(8,128)(2,1)S(1)}, u32[]{:S(2)}, u32[]{:S(2)}) async-start(bf16[32,8,256]{2,1,0:T(8,128)(2,1)} %fusion.20), calls=%async_computation.1 | async-start | bytes 262144 | tf_op jit(solution)/shard_map/all_to_all | solution.py:91
  86.7 0.0 reduce-scatter.2.cloned.1.call-start
  86.8 0.8 multiply_add_fusion
  87.5 0.1 reshape.112
  87.7 0.1 eq.107
  87.8 8.4 %all-to-all-done.1 = bf16[32,8,256]{2,1,0:T(8,128)(2,1)S(1)} async-done(((bf16[32,8,256]{2,1,0:T(8,128)(2,1)}), bf16[32,8,256]{2,1,0:T(8,128)(2,1)S(1)}, u32[]{:S(2)}, u32[]{:S(2)}) %all-to-all-start.1) | async-done | bytes 131104 | tf_op jit(solution)/shard_map/all_to_all | solution.py:91
  96.2 3.1 %convolution_convert_fusion = bf16[128,8192]{1,0:T(8,128)(2,1)S(1)} fusion(bf16[256,8192]{1,0:T(8,128)(2,1)} %param.15, bf16[32,8,256]{2,1,0:T(8,128)(2,1)S(1)} %all-to-all-done.1, s32[128]{0:T(128)S(1)} %eq.107), kind=kOutput, calls=%fused_computation.2 | convolution fusion | flops 554762240 | bytes 6423040 | tf_op jit(solution)/shard_map/dot_general | solution.py:105
  99.3 1.9 %collective-permute-start.2 = (bf16[128,8192]{1,0:T(8,128)(2,1)S(1)}, bf16[128,8192]{1,0:T(8,128)(2,1)}, u32[]{:S(2)}, u32[]{:S(2)}) collective-permute-start(bf16[128,8192]{1,0:T(8,128)(2,1)S(1)} %convolution_convert_fusion), channel_id=1, source_target_pairs={{0,1},{1,0},{2,3},{3,2},{4,5},{5,4},{6,7},{7,6},{8,9},{9,8},{10,11... | collective-permute-start | bytes 6291464 | tf_op jit(solution)/shard_map/ppermute | solution.py:108
  101.2 0.1 eq.93
  101.3 4.2 %collective-permute-done.2 = bf16[128,8192]{1,0:T(8,128)(2,1)} collective-permute-done((bf16[128,8192]{1,0:T(8,128)(2,1)S(1)}, bf16[128,8192]{1,0:T(8,128)(2,1)}, u32[]{:S(2)}, u32[]{:S(2)}) %collective-permute-start.2) | collective-permute-done | bytes 2097184 | tf_op jit(solution)/shard_map/ppermute | solution.py:108
  105.5 5.1 %add_convert_fusion = bf16[128,8192]{1,0:T(8,128)(2,1)} fusion(bf16[128,8192]{1,0:T(8,128)(2,1)} %collective-permute-done.2, bf16[256,8192]{1,0:T(8,128)(2,1)} %param.15, bf16[32,8,256]{2,1,0:T(8,128)(2,1)S(1)} %all-to-all-done.1, s32[128]{0:T(128)S(1)} %eq.93), kind=kOutput, calls=%fused_computation.12 | convolution fusion | flops 558956544 | bytes 8520192 | tf_op jit(solution)/shard_map/dot_general | solution.py:105
  110.6 37.7 %reduce-scatter.2.cloned.1.call-done = bf16[16,8192]{1,0:T(8,128)(2,1)} async-done(((bf16[128,8192]{1,0:T(8,128)(2,1)}), bf16[16,8192]{1,0:T(8,128)(2,1)}) %reduce-scatter.2.cloned.1.call-update) | async-done | bytes 262160 | tf_op jit(solution)/shard_map/reduce_scatter | solution.py:111
  (8 shorter events, 0.1 us)
Async XLA Ops:
  6.5 57.3 %copy-start = (bf16[256,256]{1,0:T(8,128)(2,1)S(1)}, bf16[256,256]{1,0:T(8,128)(2,1)}, u32[]{:S(2)}) copy-start(bf16[256,256]{1,0:T(8,128)(2,1)} %param.12) | copy-start | bytes 393220
  9.4 30.7 %all-to-all-start = ((bf16[64,16,256]{2,1,0:T(8,128)(2,1)}), bf16[64,16,256]{2,1,0:T(8,128)(2,1)S(1)}, u32[]{:S(2)}, u32[]{:S(2)}) async-start(bf16[64,16,256]{2,1,0:T(8,128)(2,1)} %gather_fusion), calls=%async_computation | async-start | bytes 1048576 | tf_op jit(solution)/shard_map/all_to_all | solution.py:35
  40.1 15.2 %collective-permute-start = (bf16[1024,256]{1,0:T(8,128)(2,1)S(1)}, bf16[1024,256]{1,0:T(8,128)(2,1)S(1)}, u32[]{:S(2)}, u32[]{:S(2)}) collective-permute-start(bf16[1024,256]{1,0:T(8,128)(2,1)S(1)} %bitcast.90), channel_id=1, source_target_pairs={{0,64},{64,128},{128,192},{192,256},{256,320},{320,384},{384,448},... | collective-permute-start | bytes 1572872 | tf_op jit(solution)/shard_map/ppermute | solution.py:48
  55.3 4.8 %collective-permute-start.1 = (bf16[1024,256]{1,0:T(8,128)(2,1)S(1)}, bf16[1024,256]{1,0:T(8,128)(2,1)S(1)}, u32[]{:S(2)}, u32[]{:S(2)}) collective-permute-start(bf16[1024,256]{1,0:T(8,128)(2,1)S(1)} %collective-permute-done), channel_id=1, source_target_pairs={{0,1},{1,0},{2,3},{3,2},{4,5},{5,4},{6,7},{7,6},{8,9},{9,8},{10,11... | collective-permute-start | bytes 1572872 | tf_op jit(solution)/shard_map/ppermute | solution.py:49
  69.2 27.0 %all-to-all-start.1 = ((bf16[32,8,256]{2,1,0:T(8,128)(2,1)}), bf16[32,8,256]{2,1,0:T(8,128)(2,1)S(1)}, u32[]{:S(2)}, u32[]{:S(2)}) async-start(bf16[32,8,256]{2,1,0:T(8,128)(2,1)} %fusion.20), calls=%async_computation.1 | async-start | bytes 262144 | tf_op jit(solution)/shard_map/all_to_all | solution.py:91
  86.7 61.5 %reduce-scatter.2.cloned.1.call-start = ((), (), s32[]{:S(2)}) async-start(), calls=%async_computation.3 | async-start | bytes 2359296 | tf_op jit(solution)/shard_map/reduce_scatter | solution.py:111
  99.3 6.2 %collective-permute-start.2 = (bf16[128,8192]{1,0:T(8,128)(2,1)S(1)}, bf16[128,8192]{1,0:T(8,128)(2,1)}, u32[]{:S(2)}, u32[]{:S(2)}) collective-permute-start(bf16[128,8192]{1,0:T(8,128)(2,1)S(1)} %convolution_convert_fusion), channel_id=1, source_target_pairs={{0,1},{1,0},{2,3},{3,2},{4,5},{5,4},{6,7},{7,6},{8,9},{9,8},{10,11... | collective-permute-start | bytes 6291464 | tf_op jit(solution)/shard_map/ppermute | solution.py:108
Sparse Core Ops, SparseCore 0:
  110.7 37.5 reduce-scatter.1

commit v7 on v6

--- a/solution.py
+++ b/solution.py
@@ -14,10 +14,12 @@
 def shards(segment_ids, relayout, queries, keys, values, out_weight):
     rows = queries.shape[0]
     n_seq = lax.axis_size("y") * lax.axis_size("x")
-    n_z = lax.axis_size("z")
+    n_zh = lax.axis_size("zh")
+    n_zl = lax.axis_size("zl")
+    n_z = n_zh * n_zl
     n_core = lax.axis_size("core")
     s = lax.axis_index("y") * lax.axis_size("x") + lax.axis_index("x")
-    t = lax.axis_index("z") * n_core + lax.axis_index("core")
+    t = (lax.axis_index("zh") * n_zl + lax.axis_index("zl")) * n_core + lax.axis_index("core")
     heads_here = queries.shape[1] // HD
     group = QH // KVH
     kv_width = keys.shape[1]
@@ -32,7 +34,7 @@
     k_h = jnp.transpose(keys.reshape(keys.shape[0], kv_heads, HD), (1, 0, 2))
     v_h = jnp.transpose(values.reshape(values.shape[0], kv_heads, HD), (1, 0, 2))
     pieces = jnp.concatenate([k_h, v_h], axis=2)[heads_of]
-    row = lax.all_to_all(pieces, ("x", "z", "core"), split_axis=0, concat_axis=0, tiled=True)
+    row = lax.all_to_all(pieces, ("x", "zh", "zl", "core"), split_axis=0, concat_axis=0, tiled=True)
     row = row.reshape(n_x * rows, 2 * HD)
 
     n_y = lax.axis_size("y")
@@ -95,7 +97,7 @@
     nth = jnp.sum((before & (src[None, :] == src[:, None])).astype(jnp.int32), axis=1)
     slot = src * chunk + nth
     per_dev = rows // (n_z * n_core)
-    slot3 = slot.reshape(n_z, n_core, per_dev)
+    slot3 = jnp.transpose(slot.reshape(n_zh, n_zl, n_core, per_dev), (1, 0, 2, 3)).reshape(n_z, n_core, per_dev)
     cols = jnp.arange(rows, dtype=jnp.int32)[None, :]
 
     def project(which):
@@ -106,19 +108,22 @@
 
     part_other = project(n_core - 1 - c)
     got = lax.ppermute(part_other, "core", perm=[(0, 1), (1, 0)])
-    part_own = project(c)
+    part_own = lax.optimization_barrier(project(c))
     half = (part_own.astype(jnp.float32) + got.astype(jnp.float32)).astype(jnp.bfloat16)
-    return lax.psum_scatter(half, "z", scatter_dimension=0, tiled=True)
+    quarter = lax.psum_scatter(half, "zl", scatter_dimension=0, tiled=True)
+    return lax.psum_scatter(quarter, "zh", scatter_dimension=0, tiled=True)
 
 def solution(mesh):
     n_seq, n_tp = mesh.devices.shape
     n_x = 4
-    mesh4 = Mesh(mesh.devices.reshape(n_seq // n_x, n_x, n_tp // 2, 2), ("y", "x", "z", "core"))
+    n_zl = 4
+    shape = (n_seq // n_x, n_x, n_tp // (2 * n_zl), n_zl, 2)
+    mesh5 = Mesh(mesh.devices.reshape(shape), ("y", "x", "zh", "zl", "core"))
     seq = ("y", "x")
-    tp = ("z", "core")
+    tp = ("zh", "zl", "core")
     return jax.shard_map(
         shards,
-        mesh=mesh4,
+        mesh=mesh5,
         in_specs=(
             P(),
             P(),

time: 156 us -> 198 us (1.27)
  waiting for transfers between devices: 74 us -> 114 us
    reduce_scatter x1 -> x2, waiting for transfers between devices: 37.7 us -> 79 us  [the longest x1 44.1 us: shards(): quarter = lax.psum_scatter(half, 'zl', scatter_dimension=0, tiled=True)]
    convert_element_type x0 -> x1, other arithmetic: none -> 3.38 us  [shards(): (part_own.astype(jnp.float32) + got.astype(jnp.float32)).astype(jnp.bfloa...]
    ppermute x1, waiting for transfers between devices: 4.18 us -> 1.3 us  [shards(): got = lax.ppermute(part_other, 'core', perm=[(0, 1), (1, 0)])]
  transfers between devices with their start and end apart: 6 -> 7, of which waited for: 5 -> 6; matrix products, arithmetic and copies ran while one was open for 5% -> 5% of each run, Pallas kernels for 0% -> 0%
where the time goes in v7:
time: 198 us; the launch traced here: 196 us
  waiting for transfers between devices  114 us (58%)
  starting transfers between devices  39.6 us (20%)
  between operations  13.6 us (7%)
  other arithmetic  13.2 us (7%)
  matrix products  12.8 us (6%)
  local copies, waits for them, and re-layouts  3.15 us (2%)
    reduce_scatter x1, waiting for transfers between devices, shards(): quarter = lax.psum_scatter(half, 'zl', scatter_dimension=0, tiled=True)  44.1 us
    reduce_scatter x1, waiting for transfers between devices, shards(): return lax.psum_scatter(quarter, 'zh', scatter_dimension=0, tiled=True)  34.9 us
    all_to_all x1, starting transfers between devices, shards(): lax.all_to_all(to_send, ('y', 'x'), split_axis=0, concat_axis=0, tiled=True)  17.5 us
    all_to_all x1, waiting for transfers between devices, shards(): lax.all_to_all(pieces, ('x', 'zh', 'zl', 'core'), split_axis=0, concat_ax...  14.4 us
    all_to_all x1, starting transfers between devices, shards(): lax.all_to_all(pieces, ('x', 'zh', 'zl', 'core'), split_axis=0, concat_ax...  14 us
    ppermute x1, waiting for transfers between devices, shards(): fetched = lax.ppermute(row, ('y', 'core'), perm=perm)  10 us
    all_to_all x1, waiting for transfers between devices, shards(): lax.all_to_all(to_send, ('y', 'x'), split_axis=0, concat_axis=0, tiled=True)  9.12 us
    dot_general x2, matrix products, project(): jnp.dot(relaid, out_weight, preferred_element_type=jnp.float32)  7.45 us
  transfers between devices with their start and end apart: 7, of which 6 were waited for; matrix products, arithmetic and copies ran while one was open for 5% of the time, Pallas kernels for 0%

profile of v7, /device:TPU:6, one launch (start us, length us, event | category | flops | bytes accessed | tf_op | source)
XLA Modules:
  0.0 196.3 jit_solution(13217125964265655924)
XLA Ops:
  6.5 0.7 pad_clamp_fusion
  7.2 0.7 bitcast_bitcast_fusion
  8.0 1.4 gather_fusion
  9.4 14.0 %all-to-all-start = ((bf16[64,16,256]{2,1,0:T(8,128)(2,1)}), bf16[64,16,256]{2,1,0:T(8,128)(2,1)S(1)}, u32[]{:S(2)}, u32[]{:S(2)}) async-start(bf16[64,16,256]{2,1,0:T(8,128)(2,1)} %gather_fusion), calls=%async_computation | async-start | bytes 1048576 | tf_op jit(solution)/shard_map/all_to_all | solution.py:37
  23.4 0.8 dynamic_slice.14
  24.2 0.8 and_select_fusion
  25.0 0.8 pad_dynamic-slice_fusion.3
  25.7 14.4 %all-to-all-done = bf16[64,16,256]{2,1,0:T(8,128)(2,1)S(1)} async-done(((bf16[64,16,256]{2,1,0:T(8,128)(2,1)}), bf16[64,16,256]{2,1,0:T(8,128)(2,1)S(1)}, u32[]{:S(2)}, u32[]{:S(2)}) %all-to-all-start) | async-done | bytes 524320 | tf_op jit(solution)/shard_map/all_to_all | solution.py:37
  40.1 3.5 %collective-permute-start = (bf16[1024,256]{1,0:T(8,128)(2,1)S(1)}, bf16[1024,256]{1,0:T(8,128)(2,1)S(1)}, u32[]{:S(2)}, u32[]{:S(2)}) collective-permute-start(bf16[1024,256]{1,0:T(8,128)(2,1)S(1)} %bitcast.94), channel_id=1, source_target_pairs={{0,64},{64,128},{128,192},{192,256},{256,320},{320,384},{384,448},... | collective-permute-start | bytes 1572872 | tf_op jit(solution)/shard_map/ppermute | solution.py:50
  43.6 1.2 select_reduce_fusion
  44.9 0.2 convert_reduce_fusion
  45.1 0.2 convert_reduce_fusion.1
  45.2 10.0 %collective-permute-done = bf16[1024,256]{1,0:T(8,128)(2,1)S(1)} collective-permute-done((bf16[1024,256]{1,0:T(8,128)(2,1)S(1)}, bf16[1024,256]{1,0:T(8,128)(2,1)S(1)}, u32[]{:S(2)}, u32[]{:S(2)}) %collective-permute-start) | collective-permute-done | bytes 524320 | tf_op jit(solution)/shard_map/ppermute | solution.py:50
  55.3 2.6 %collective-permute-start.1 = (bf16[1024,256]{1,0:T(8,128)(2,1)S(1)}, bf16[1024,256]{1,0:T(8,128)(2,1)S(1)}, u32[]{:S(2)}, u32[]{:S(2)}) collective-permute-start(bf16[1024,256]{1,0:T(8,128)(2,1)S(1)} %collective-permute-done), channel_id=1, source_target_pairs={{0,1},{1,0},{2,3},{3,2},{4,5},{5,4},{6,7},{7,6},{8,9},{9,8},{10,11... | collective-permute-start | bytes 1572872 | tf_op jit(solution)/shard_map/ppermute | solution.py:51
  57.9 2.2 %and_and_fusion = pred[256,2304]{0,1:T(8,128)(4,1)S(1)} fusion(s32[256]{0:T(256)S(1)} %dynamic_slice.14, s32[256]{0:T(256)S(1)} %iota_add_fusion.1, s32[2304]{0:T(1024)S(1)} %get-tuple-element.23, s32[2304]{0:T(1024)S(1)} %get-tuple-element.24, pred[2304]{0:T(1024)(128)(4,1)S(1)} %broadcast_compare_fusion), kind=kLoop, calls=%fused_computation.14 | loop fusion | flops 2359296 | bytes 612608 | tf_op jit(solution)/shard_map/and | solution.py:66
  60.2 3.6 %fusion.9 = bf16[2304,256]{1,0:T(8,128)(2,1)S(1)} fusion(s32[]{:T(128)S(6)} %select_n.59, bf16[1024,256]{1,0:T(8,128)(2,1)S(1)} %get-tuple-element.18, bf16[1024,256]{1,0:T(8,128)(2,1)S(1)} %get-tuple-element.17, bf16[1024,256]{1,0:T(8,128)(2,1)S(1)} %bitcast.95), kind=kLoop, calls=%fused_computation.19 | loop fusion | flops 3538944 | bytes 2752516 | tf_op jit(solution)/shard_map/concatenate | solution.py:53
  63.8 2.2 %fusion.49 = f32[2,256]{1,0:T(2,128)S(1)} fusion(pred[256,2304]{0,1:T(8,128)(4,1)S(1)} %and_and_fusion, bf16[2304,256]{1,0:T(8,128)(2,1)S(1)} %fusion.9, bf16[256,256]{1,0:T(8,128)(2,1)S(1)} %copy-done), kind=kOutput, calls=%fused_computation.67 | convolution fusion | flops 307890432 | bytes 1902592 | tf_op jit(solution)/shard_map/sub | solution.py:75
  66.0 2.3 %fusion.16 = bf16[256,2,128]{0,2,1:T(8,128)(2,1)S(1)} fusion(bf16[2304,256]{1,0:T(8,128)(2,1)S(1)} %fusion.9, f32[256,2]{0,1:T(2,128)S(1)} %bitcast.99, pred[256,2304]{0,1:T(8,128)(4,1)S(1)} %and_and_fusion, bf16[256,256]{1,0:T(8,128)(2,1)S(1)} %copy-done), kind=kOutput, calls=%fused_computation.23 | convolution fusion | flops 610011904 | bytes 2623488 | tf_op jit(solution)/shard_map/hqk,kd->hqd/dot_general | solution.py:77
  68.3 0.9 fusion.19
  69.2 17.5 %all-to-all-start.1 = ((bf16[32,8,256]{2,1,0:T(8,128)(2,1)}), bf16[32,8,256]{2,1,0:T(8,128)(2,1)S(1)}, u32[]{:S(2)}, u32[]{:S(2)}) async-start(bf16[32,8,256]{2,1,0:T(8,128)(2,1)} %fusion.19), calls=%async_computation.1 | async-start | bytes 262144 | tf_op jit(solution)/shard_map/all_to_all | solution.py:93
  86.8 0.1 multiply_add_fusion
  86.9 0.1 reshape.115
  87.0 0.1 eq.107
  87.1 9.1 %all-to-all-done.1 = bf16[32,8,256]{2,1,0:T(8,128)(2,1)S(1)} async-done(((bf16[32,8,256]{2,1,0:T(8,128)(2,1)}), bf16[32,8,256]{2,1,0:T(8,128)(2,1)S(1)}, u32[]{:S(2)}, u32[]{:S(2)}) %all-to-all-start.1) | async-done | bytes 131104 | tf_op jit(solution)/shard_map/all_to_all | solution.py:93
  96.2 4.4 %convolution_convert_fusion = bf16[128,8192]{1,0:T(8,128)(2,1)} fusion(bf16[256,8192]{1,0:T(8,128)(2,1)} %param.15, bf16[32,8,256]{2,1,0:T(8,128)(2,1)S(1)} %all-to-all-done.1, s32[128]{0:T(128)S(1)} %eq.107), kind=kOutput, calls=%fused_computation.2 | convolution fusion | flops 554762240 | bytes 6423040 | tf_op jit(solution)/shard_map/dot_general | solution.py:107
  100.6 1.9 collective-permute-start.2
  102.5 0.1 eq.93
  102.6 3.1 %convolution_convert_fusion.1 = bf16[128,8192]{1,0:T(8,128)(2,1)S(1)} fusion(bf16[256,8192]{1,0:T(8,128)(2,1)} %param.15, bf16[32,8,256]{2,1,0:T(8,128)(2,1)S(1)} %all-to-all-done.1, s32[128]{0:T(128)S(1)} %eq.93), kind=kOutput, calls=%fused_computation.3 | convolution fusion | flops 554762240 | bytes 6423040 | tf_op jit(solution)/shard_map/dot_general | solution.py:107
  105.7 1.3 collective-permute-done.2
  107.0 3.4 %add_convert_fusion = bf16[128,8192]{1,0:T(8,128)(2,1)} fusion(bf16[128,8192]{1,0:T(8,128)(2,1)} %collective-permute-done.2, bf16[128,8192]{1,0:T(8,128)(2,1)S(1)} %convolution_convert_fusion.1), kind=kLoop, calls=%fused_computation.11 | loop fusion | flops 4194304 | bytes 6291456 | tf_op jit(solution)/shard_map/convert_element_type | solution.py:112
  110.4 44.1 %reduce-scatter.3.cloned.1.call-done = bf16[32,8192]{1,0:T(8,128)(2,1)} async-done(((bf16[128,8192]{1,0:T(8,128)(2,1)}), bf16[32,8192]{1,0:T(8,128)(2,1)}) %reduce-scatter.3.cloned.1.call-update) | async-done | bytes 524304 | tf_op jit(solution)/shard_map/reduce_scatter | solution.py:113
  154.5 34.9 %reduce-scatter.5.cloned.1.call-done = bf16[16,8192]{1,0:T(8,128)(2,1)} async-done(((bf16[32,8192]{1,0:T(8,128)(2,1)}), bf16[16,8192]{1,0:T(8,128)(2,1)}) %reduce-scatter.5.cloned.1.call-update) | async-done | bytes 262160 | tf_op jit(solution)/shard_map/reduce_scatter | solution.py:114
  (15 shorter events, 0.2 us)
Async XLA Ops:
  6.5 57.3 %copy-start = (bf16[256,256]{1,0:T(8,128)(2,1)S(1)}, bf16[256,256]{1,0:T(8,128)(2,1)}, u32[]{:S(2)}) copy-start(bf16[256,256]{1,0:T(8,128)(2,1)} %param.12) | copy-start | bytes 393220
  6.5 37.1 %copy-start.1 = (s32[8192]{0:T(1024)S(1)}, s32[8192]{0:T(1024)}, u32[]{:S(2)}) copy-start(s32[8192]{0:T(1024)} %param.11) | copy-start | bytes 98308
  9.4 30.7 %all-to-all-start = ((bf16[64,16,256]{2,1,0:T(8,128)(2,1)}), bf16[64,16,256]{2,1,0:T(8,128)(2,1)S(1)}, u32[]{:S(2)}, u32[]{:S(2)}) async-start(bf16[64,16,256]{2,1,0:T(8,128)(2,1)} %gather_fusion), calls=%async_computation | async-start | bytes 1048576 | tf_op jit(solution)/shard_map/all_to_all | solution.py:37
  40.1 15.2 %collective-permute-start = (bf16[1024,256]{1,0:T(8,128)(2,1)S(1)}, bf16[1024,256]{1,0:T(8,128)(2,1)S(1)}, u32[]{:S(2)}, u32[]{:S(2)}) collective-permute-start(bf16[1024,256]{1,0:T(8,128)(2,1)S(1)} %bitcast.94), channel_id=1, source_target_pairs={{0,64},{64,128},{128,192},{192,256},{256,320},{320,384},{384,448},... | collective-permute-start | bytes 1572872 | tf_op jit(solution)/shard_map/ppermute | solution.py:50
  55.3 4.8 %collective-permute-start.1 = (bf16[1024,256]{1,0:T(8,128)(2,1)S(1)}, bf16[1024,256]{1,0:T(8,128)(2,1)S(1)}, u32[]{:S(2)}, u32[]{:S(2)}) collective-permute-start(bf16[1024,256]{1,0:T(8,128)(2,1)S(1)} %collective-permute-done), channel_id=1, source_target_pairs={{0,1},{1,0},{2,3},{3,2},{4,5},{5,4},{6,7},{7,6},{8,9},{9,8},{10,11... | collective-permute-start | bytes 1572872 | tf_op jit(solution)/shard_map/ppermute | solution.py:51
  69.2 27.0 %all-to-all-start.1 = ((bf16[32,8,256]{2,1,0:T(8,128)(2,1)}), bf16[32,8,256]{2,1,0:T(8,128)(2,1)S(1)}, u32[]{:S(2)}, u32[]{:S(2)}) async-start(bf16[32,8,256]{2,1,0:T(8,128)(2,1)} %fusion.19), calls=%async_computation.1 | async-start | bytes 262144 | tf_op jit(solution)/shard_map/all_to_all | solution.py:93
  86.7 67.8 %reduce-scatter.3.cloned.1.call-start = ((), (), s32[]{:S(2)}) async-start(), calls=%async_computation.4 | async-start | bytes 2621440 | tf_op jit(solution)/shard_map/reduce_scatter | solution.py:113
  100.6 6.4 %collective-permute-start.2 = (bf16[128,8192]{1,0:T(8,128)(2,1)}, bf16[128,8192]{1,0:T(8,128)(2,1)}, u32[]{:S(2)}, u32[]{:S(2)}) collective-permute-start(bf16[128,8192]{1,0:T(8,128)(2,1)} %convolution_convert_fusion), channel_id=1, source_target_pairs={{0,1},{1,0},{2,3},{3,2},{4,5},{5,4},{6,7},{7,6},{8,9},{9,8},{10,11... | collective-permute-start | bytes 6291464 | tf_op jit(solution)/shard_map/ppermute | solution.py:110
  110.4 79.1 %reduce-scatter.5.cloned.1.call-start = ((), (), s32[]{:S(2)}) async-start(), calls=%async_computation.5 | async-start | bytes 786432 | tf_op jit(solution)/shard_map/reduce_scatter | solution.py:114
Sparse Core Ops, SparseCore 0:
  110.5 43.9 reduce-scatter.2
  157.5 31.8 reduce-scatter.4

commit v8 on v6

--- a/solution.py
+++ b/solution.py
@@ -106,7 +106,7 @@
 
     part_other = project(n_core - 1 - c)
     got = lax.ppermute(part_other, "core", perm=[(0, 1), (1, 0)])
-    part_own = project(c)
+    part_own = lax.optimization_barrier(project(c))
     half = (part_own.astype(jnp.float32) + got.astype(jnp.float32)).astype(jnp.bfloat16)
     return lax.psum_scatter(half, "z", scatter_dimension=0, tiled=True)
 

time: 156 us -> 156 us (level)
  other arithmetic: 11.3 us -> 13.2 us
    convert_element_type x0 -> x1, other arithmetic: none -> 3.38 us  [shards(): (part_own.astype(jnp.float32) + got.astype(jnp.float32)).astype(jnp.bfloa...]
    ppermute x1, waiting for transfers between devices: 4.18 us -> 1.3 us  [shards(): got = lax.ppermute(part_other, 'core', perm=[(0, 1), (1, 0)])]
  transfers between devices with their start and end apart: 6 -> 6, of which waited for: 5 -> 5; matrix products, arithmetic and copies ran while one was open for 5% -> 6% of each run, Pallas kernels for 0% -> 0%
where the time goes in v8:
time: 156 us; the launch traced here: 155 us
  waiting for transfers between devices  72.5 us (46%)
  starting transfers between devices  39.6 us (25%)
  between operations  13.6 us (9%)
  other arithmetic  13.2 us (8%)
  matrix products  12.8 us (8%)
  local copies, waits for them, and re-layouts  3.14 us (2%)
    reduce_scatter x1, waiting for transfers between devices, shards(): return lax.psum_scatter(half, 'z', scatter_dimension=0, tiled=True)  37.6 us
    all_to_all x1, starting transfers between devices, shards(): lax.all_to_all(to_send, ('y', 'x'), split_axis=0, concat_axis=0, tiled=True)  17.5 us
    all_to_all x1, waiting for transfers between devices, shards(): lax.all_to_all(pieces, ('x', 'z', 'core'), split_axis=0, concat_axis=0, t...  14.4 us
    all_to_all x1, starting transfers between devices, shards(): lax.all_to_all(pieces, ('x', 'z', 'core'), split_axis=0, concat_axis=0, t...  14 us
    ppermute x1, waiting for transfers between devices, shards(): fetched = lax.ppermute(row, ('y', 'core'), perm=perm)  10 us
    all_to_all x1, waiting for transfers between devices, shards(): lax.all_to_all(to_send, ('y', 'x'), split_axis=0, concat_axis=0, tiled=True)  9.13 us
    dot_general x2, matrix products, project(): jnp.dot(relaid, out_weight, preferred_element_type=jnp.float32)  7.45 us
    concatenate x1, other arithmetic, shards(): kv_all = jnp.concatenate(earlier + [row], axis=0)  3.63 us
  transfers between devices with their start and end apart: 6, of which 5 were waited for; matrix products, arithmetic and copies ran while one was open for 6% of the time, Pallas kernels for 0%

profile of v8, /device:TPU:6, one launch (start us, length us, event | category | flops | bytes accessed | tf_op | source)
XLA Modules:
  0.0 154.9 jit_solution(2459852856117311598)
XLA Ops:
  6.5 0.7 pad_clamp_fusion
  7.2 0.7 bitcast_bitcast_fusion
  8.0 1.4 gather_fusion
  9.4 14.0 %all-to-all-start = ((bf16[64,16,256]{2,1,0:T(8,128)(2,1)}), bf16[64,16,256]{2,1,0:T(8,128)(2,1)S(1)}, u32[]{:S(2)}, u32[]{:S(2)}) async-start(bf16[64,16,256]{2,1,0:T(8,128)(2,1)} %gather_fusion), calls=%async_computation | async-start | bytes 1048576 | tf_op jit(solution)/shard_map/all_to_all | solution.py:35
  23.4 0.8 dynamic_slice.14
  24.2 0.8 and_select_fusion
  25.0 0.8 pad_dynamic-slice_fusion.3
  25.7 14.4 %all-to-all-done = bf16[64,16,256]{2,1,0:T(8,128)(2,1)S(1)} async-done(((bf16[64,16,256]{2,1,0:T(8,128)(2,1)}), bf16[64,16,256]{2,1,0:T(8,128)(2,1)S(1)}, u32[]{:S(2)}, u32[]{:S(2)}) %all-to-all-start) | async-done | bytes 524320 | tf_op jit(solution)/shard_map/all_to_all | solution.py:35
  40.1 3.5 %collective-permute-start = (bf16[1024,256]{1,0:T(8,128)(2,1)S(1)}, bf16[1024,256]{1,0:T(8,128)(2,1)S(1)}, u32[]{:S(2)}, u32[]{:S(2)}) collective-permute-start(bf16[1024,256]{1,0:T(8,128)(2,1)S(1)} %bitcast.90), channel_id=1, source_target_pairs={{0,64},{64,128},{128,192},{192,256},{256,320},{320,384},{384,448},... | collective-permute-start | bytes 1572872 | tf_op jit(solution)/shard_map/ppermute | solution.py:48
  43.6 1.2 select_reduce_fusion
  44.9 0.2 convert_reduce_fusion
  45.1 0.2 convert_reduce_fusion.1
  45.2 10.0 %collective-permute-done = bf16[1024,256]{1,0:T(8,128)(2,1)S(1)} collective-permute-done((bf16[1024,256]{1,0:T(8,128)(2,1)S(1)}, bf16[1024,256]{1,0:T(8,128)(2,1)S(1)}, u32[]{:S(2)}, u32[]{:S(2)}) %collective-permute-start) | collective-permute-done | bytes 524320 | tf_op jit(solution)/shard_map/ppermute | solution.py:48
  55.3 2.6 %collective-permute-start.1 = (bf16[1024,256]{1,0:T(8,128)(2,1)S(1)}, bf16[1024,256]{1,0:T(8,128)(2,1)S(1)}, u32[]{:S(2)}, u32[]{:S(2)}) collective-permute-start(bf16[1024,256]{1,0:T(8,128)(2,1)S(1)} %collective-permute-done), channel_id=1, source_target_pairs={{0,1},{1,0},{2,3},{3,2},{4,5},{5,4},{6,7},{7,6},{8,9},{9,8},{10,11... | collective-permute-start | bytes 1572872 | tf_op jit(solution)/shard_map/ppermute | solution.py:49
  57.9 2.2 %and_and_fusion = pred[256,2304]{0,1:T(8,128)(4,1)S(1)} fusion(s32[256]{0:T(256)S(1)} %dynamic_slice.14, s32[256]{0:T(256)S(1)} %iota_add_fusion.1, s32[2304]{0:T(1024)S(1)} %get-tuple-element.23, s32[2304]{0:T(1024)S(1)} %get-tuple-element.24, pred[2304]{0:T(1024)(128)(4,1)S(1)} %broadcast_compare_fusion), kind=kLoop, calls=%fused_computation.14 | loop fusion | flops 2359296 | bytes 612608 | tf_op jit(solution)/shard_map/and | solution.py:64
  60.1 0.1 broadcast_select_fusion
  60.2 3.6 %fusion.9 = bf16[2304,256]{1,0:T(8,128)(2,1)S(1)} fusion(s32[]{:T(128)S(6)} %select_n.59, bf16[1024,256]{1,0:T(8,128)(2,1)S(1)} %get-tuple-element.18, bf16[1024,256]{1,0:T(8,128)(2,1)S(1)} %get-tuple-element.17, bf16[1024,256]{1,0:T(8,128)(2,1)S(1)} %bitcast.91), kind=kLoop, calls=%fused_computation.19 | loop fusion | flops 3538944 | bytes 2752516 | tf_op jit(solution)/shard_map/concatenate | solution.py:51
  63.8 2.2 %fusion.49 = f32[2,256]{1,0:T(2,128)S(1)} fusion(pred[256,2304]{0,1:T(8,128)(4,1)S(1)} %and_and_fusion, bf16[2304,256]{1,0:T(8,128)(2,1)S(1)} %fusion.9, bf16[256,256]{1,0:T(8,128)(2,1)S(1)} %copy-done), kind=kOutput, calls=%fused_computation.67 | convolution fusion | flops 307890432 | bytes 1902592 | tf_op jit(solution)/shard_map/sub | solution.py:73
  66.0 2.3 %fusion.16 = bf16[256,2,128]{0,2,1:T(8,128)(2,1)S(1)} fusion(bf16[2304,256]{1,0:T(8,128)(2,1)S(1)} %fusion.9, f32[256,2]{0,1:T(2,128)S(1)} %bitcast.95, pred[256,2304]{0,1:T(8,128)(4,1)S(1)} %and_and_fusion, bf16[256,256]{1,0:T(8,128)(2,1)S(1)} %copy-done), kind=kOutput, calls=%fused_computation.23 | convolution fusion | flops 610011904 | bytes 2623488 | tf_op jit(solution)/shard_map/hqk,kd->hqd/dot_general | solution.py:75
  68.3 0.9 fusion.19
  69.2 17.5 %all-to-all-start.1 = ((bf16[32,8,256]{2,1,0:T(8,128)(2,1)}), bf16[32,8,256]{2,1,0:T(8,128)(2,1)S(1)}, u32[]{:S(2)}, u32[]{:S(2)}) async-start(bf16[32,8,256]{2,1,0:T(8,128)(2,1)} %fusion.19), calls=%async_computation.1 | async-start | bytes 262144 | tf_op jit(solution)/shard_map/all_to_all | solution.py:91
  86.8 0.1 multiply_add_fusion
  86.9 0.1 reshape.112
  87.0 0.1 eq.107
  87.1 9.1 %all-to-all-done.1 = bf16[32,8,256]{2,1,0:T(8,128)(2,1)S(1)} async-done(((bf16[32,8,256]{2,1,0:T(8,128)(2,1)}), bf16[32,8,256]{2,1,0:T(8,128)(2,1)S(1)}, u32[]{:S(2)}, u32[]{:S(2)}) %all-to-all-start.1) | async-done | bytes 131104 | tf_op jit(solution)/shard_map/all_to_all | solution.py:91
  96.2 4.4 %convolution_convert_fusion = bf16[128,8192]{1,0:T(8,128)(2,1)} fusion(bf16[256,8192]{1,0:T(8,128)(2,1)} %param.15, bf16[32,8,256]{2,1,0:T(8,128)(2,1)S(1)} %all-to-all-done.1, s32[128]{0:T(128)S(1)} %eq.107), kind=kOutput, calls=%fused_computation.2 | convolution fusion | flops 554762240 | bytes 6423040 | tf_op jit(solution)/shard_map/dot_general | solution.py:105
  100.6 1.9 %collective-permute-start.2 = (bf16[128,8192]{1,0:T(8,128)(2,1)}, bf16[128,8192]{1,0:T(8,128)(2,1)}, u32[]{:S(2)}, u32[]{:S(2)}) collective-permute-start(bf16[128,8192]{1,0:T(8,128)(2,1)} %convolution_convert_fusion), channel_id=1, source_target_pairs={{0,1},{1,0},{2,3},{3,2},{4,5},{5,4},{6,7},{7,6},{8,9},{9,8},{10,11... | collective-permute-start | bytes 6291464 | tf_op jit(solution)/shard_map/ppermute | solution.py:108
  102.5 0.1 eq.93
  102.6 3.1 %convolution_convert_fusion.1 = bf16[128,8192]{1,0:T(8,128)(2,1)S(1)} fusion(bf16[256,8192]{1,0:T(8,128)(2,1)} %param.15, bf16[32,8,256]{2,1,0:T(8,128)(2,1)S(1)} %all-to-all-done.1, s32[128]{0:T(128)S(1)} %eq.93), kind=kOutput, calls=%fused_computation.3 | convolution fusion | flops 554762240 | bytes 6423040 | tf_op jit(solution)/shard_map/dot_general | solution.py:105
  105.7 1.3 collective-permute-done.2
  107.0 3.4 %add_convert_fusion = bf16[128,8192]{1,0:T(8,128)(2,1)} fusion(bf16[128,8192]{1,0:T(8,128)(2,1)} %collective-permute-done.2, bf16[128,8192]{1,0:T(8,128)(2,1)S(1)} %convolution_convert_fusion.1), kind=kLoop, calls=%fused_computation.11 | loop fusion | flops 4194304 | bytes 6291456 | tf_op jit(solution)/shard_map/convert_element_type | solution.py:110
  110.4 37.6 %reduce-scatter.2.cloned.1.call-done = bf16[16,8192]{1,0:T(8,128)(2,1)} async-done(((bf16[128,8192]{1,0:T(8,128)(2,1)}), bf16[16,8192]{1,0:T(8,128)(2,1)}) %reduce-scatter.2.cloned.1.call-update) | async-done | bytes 262160 | tf_op jit(solution)/shard_map/reduce_scatter | solution.py:111
  (11 shorter events, 0.1 us)
Async XLA Ops:
  6.5 57.3 %copy-start = (bf16[256,256]{1,0:T(8,128)(2,1)S(1)}, bf16[256,256]{1,0:T(8,128)(2,1)}, u32[]{:S(2)}) copy-start(bf16[256,256]{1,0:T(8,128)(2,1)} %param.12) | copy-start | bytes 393220
  6.5 37.1 %copy-start.1 = (s32[8192]{0:T(1024)S(1)}, s32[8192]{0:T(1024)}, u32[]{:S(2)}) copy-start(s32[8192]{0:T(1024)} %param.11) | copy-start | bytes 98308
  9.4 30.7 %all-to-all-start = ((bf16[64,16,256]{2,1,0:T(8,128)(2,1)}), bf16[64,16,256]{2,1,0:T(8,128)(2,1)S(1)}, u32[]{:S(2)}, u32[]{:S(2)}) async-start(bf16[64,16,256]{2,1,0:T(8,128)(2,1)} %gather_fusion), calls=%async_computation | async-start | bytes 1048576 | tf_op jit(solution)/shard_map/all_to_all | solution.py:35
  40.1 15.2 %collective-permute-start = (bf16[1024,256]{1,0:T(8,128)(2,1)S(1)}, bf16[1024,256]{1,0:T(8,128)(2,1)S(1)}, u32[]{:S(2)}, u32[]{:S(2)}) collective-permute-start(bf16[1024,256]{1,0:T(8,128)(2,1)S(1)} %bitcast.90), channel_id=1, source_target_pairs={{0,64},{64,128},{128,192},{192,256},{256,320},{320,384},{384,448},... | collective-permute-start | bytes 1572872 | tf_op jit(solution)/shard_map/ppermute | solution.py:48
  55.3 4.8 %collective-permute-start.1 = (bf16[1024,256]{1,0:T(8,128)(2,1)S(1)}, bf16[1024,256]{1,0:T(8,128)(2,1)S(1)}, u32[]{:S(2)}, u32[]{:S(2)}) collective-permute-start(bf16[1024,256]{1,0:T(8,128)(2,1)S(1)} %collective-permute-done), channel_id=1, source_target_pairs={{0,1},{1,0},{2,3},{3,2},{4,5},{5,4},{6,7},{7,6},{8,9},{9,8},{10,11... | collective-permute-start | bytes 1572872 | tf_op jit(solution)/shard_map/ppermute | solution.py:49
  69.2 27.0 %all-to-all-start.1 = ((bf16[32,8,256]{2,1,0:T(8,128)(2,1)}), bf16[32,8,256]{2,1,0:T(8,128)(2,1)S(1)}, u32[]{:S(2)}, u32[]{:S(2)}) async-start(bf16[32,8,256]{2,1,0:T(8,128)(2,1)} %fusion.19), calls=%async_computation.1 | async-start | bytes 262144 | tf_op jit(solution)/shard_map/all_to_all | solution.py:91
  86.7 61.3 %reduce-scatter.2.cloned.1.call-start = ((), (), s32[]{:S(2)}) async-start(), calls=%async_computation.3 | async-start | bytes 2359296 | tf_op jit(solution)/shard_map/reduce_scatter | solution.py:111
  100.6 6.4 %collective-permute-start.2 = (bf16[128,8192]{1,0:T(8,128)(2,1)}, bf16[128,8192]{1,0:T(8,128)(2,1)}, u32[]{:S(2)}, u32[]{:S(2)}) collective-permute-start(bf16[128,8192]{1,0:T(8,128)(2,1)} %convolution_convert_fusion), channel_id=1, source_target_pairs={{0,1},{1,0},{2,3},{3,2},{4,5},{5,4},{6,7},{7,6},{8,9},{9,8},{10,11... | collective-permute-start | bytes 6291464 | tf_op jit(solution)/shard_map/ppermute | solution.py:108
Sparse Core Ops, SparseCore 0:
  110.5 37.4 reduce-scatter.1

commit v9 on v8

--- a/solution.py
+++ b/solution.py
@@ -1,7 +1,10 @@
+import functools
+
 import jax
 import jax.numpy as jnp
 import numpy as np
 from jax import lax
+from jax.experimental import pallas as pl
 from jax.sharding import Mesh
 from jax.sharding import PartitionSpec as P
 
@@ -9,6 +12,53 @@
 KVH = 4
 HD = 128
 MOST_LEN = 2048
+
+
+def _attention_body(scale, q_ref, k_ref, v_ref, qp_ref, qs_ref, kp_ref, ks_ref, o_ref):
+    s = lax.dot_general(
+        q_ref[...], k_ref[...], (((1,), (1,)), ((), ())), preferred_element_type=jnp.float32
+    ) * scale
+    live = (kp_ref[...] <= qp_ref[...]) & (ks_ref[...] == qs_ref[...])
+    masked = jnp.where(live, s, jnp.float32(-1e30))
+    peak = jnp.max(masked, axis=1, keepdims=True)
+    expo = jnp.where(live, jnp.exp(masked - peak), jnp.float32(0.0))
+    denom = jnp.sum(expo, axis=1, keepdims=True)
+    summed = jnp.dot(expo.astype(jnp.bfloat16), v_ref[...], preferred_element_type=jnp.float32)
+    o_ref[...] = (summed / denom).astype(o_ref.dtype)
+
+
+def attention(q, kv, q_pos, q_seg, k_pos, k_seg, scale):
+    rows, width = q.shape
+    heads = width // HD
+    n_keys = kv.shape[0]
+    return pl.pallas_call(
+        functools.partial(_attention_body, scale),
+        grid=(heads,),
+        in_specs=[
+            pl.BlockSpec((rows, HD), lambda h: (0, h)),
+            pl.BlockSpec((n_keys, HD), lambda h: (0, 0)),
+            pl.BlockSpec((n_keys, HD), lambda h: (0, 1)),
+            pl.BlockSpec((rows, 1), lambda h: (0, 0)),
+            pl.BlockSpec((rows, 1), lambda h: (0, 0)),
+            pl.BlockSpec((1, n_keys), lambda h: (0, 0)),
+            pl.BlockSpec((1, n_keys), lambda h: (0, 0)),
+        ],
+        out_specs=pl.BlockSpec((rows, HD), lambda h: (0, h)),
+        out_shape=jax.ShapeDtypeStruct((rows, width), jnp.bfloat16),
+        cost_estimate=pl.CostEstimate(
+            flops=4 * rows * n_keys * HD * heads,
+            transcendentals=rows * n_keys * heads,
+            bytes_accessed=2 * (2 * rows * width + 2 * n_keys * HD),
+        ),
+    )(
+        q,
+        kv,
+        kv,
+        q_pos.reshape(rows, 1),
+        q_seg.reshape(rows, 1),
+        k_pos.reshape(1, n_keys),
+        k_seg.reshape(1, n_keys),
+    )
 
 
 def shards(segment_ids, relayout, queries, keys, values, out_weight):
@@ -52,31 +102,13 @@
     n_keys = (back + 1) * rows
     first = (rows_back * n_x - back + x) * rows
     kv_win = lax.dynamic_slice_in_dim(kv_all, first, n_keys, 0)
-    k_win = kv_win[:, :HD]
-    v_win = kv_win[:, HD:]
 
     q_pos = s * rows + jnp.arange(rows, dtype=jnp.int32)
     k_pos = (s - back) * rows + jnp.arange(n_keys, dtype=jnp.int32)
     q_seg = lax.dynamic_slice_in_dim(segment_ids, s * rows, rows, 0)
     seg_pad = jnp.concatenate([jnp.full((back * rows,), -1, jnp.int32), segment_ids])
     k_seg = lax.dynamic_slice_in_dim(seg_pad, s * rows, n_keys, 0)
-    live = (
-        (k_pos[None, :] <= q_pos[:, None])
-        & (k_seg[None, :] == q_seg[:, None])
-        & (k_pos[None, :] >= 0)
-    )
-
-    q = queries.reshape(rows, heads_here, HD)
-    scores = jnp.einsum("qhd,kd->hqk", q, k_win, preferred_element_type=jnp.float32) * scale
-    masked = jnp.where(live[None], scores, jnp.float32(-1e30))
-    peak = jnp.max(masked, axis=-1)
-    expo = jnp.where(live[None], jnp.exp(masked - peak[..., None]), jnp.float32(0.0))
-    denom = jnp.sum(expo, axis=-1)
-    summed = jnp.einsum(
-        "hqk,kd->hqd", expo.astype(jnp.bfloat16), v_win, preferred_element_type=jnp.float32
-    )
-    attn = summed / denom[..., None]
-    attn_rows = jnp.transpose(attn, (1, 0, 2)).reshape(rows, heads_here * HD).astype(jnp.bfloat16)
+    attn_rows = attention(queries, kv_win, q_pos, q_seg, k_pos, k_seg, scale)
 
     chunk = rows // n_seq
     total = relayout.shape[0]

time: 156 us -> 158 us (1.013)
  Pallas kernels: 0 us -> 5.47 us
  matrix products: 12.8 us -> 9.22 us
    pallas_call x0 -> x1, Pallas kernels: none -> 5.47 us  [attention(): pl.pallas_call(functools.partial(_attention_body, scale), grid=(heads,),...]
    dot_general x1 -> x0, matrix products: 2.29 us -> none  [shards(): jnp.einsum('hqk,kd->hqd', expo.astype(jnp.bfloat16), v_win, preferred_ele...]
    sub x1 -> x0, matrix products: 2.22 us -> none  [shards(): masked - peak[..., None]]
    and x1 -> x0, other arithmetic: 2.17 us -> none  [shards(): (k_pos[None, :] <= q_pos[:, None]) & (k_seg[None, :] == q_seg[:, None])]
  transfers between devices with their start and end apart: 6 -> 6, of which waited for: 5 -> 6; matrix products, arithmetic and copies ran while one was open for 6% -> 5% of each run, Pallas kernels for 0% -> 0%
where the time goes in v9:
time: 158 us; the launch traced here: 157 us
  waiting for transfers between devices  72.4 us (46%)
  starting transfers between devices  39.9 us (25%)
  between operations  13.5 us (9%)
  other arithmetic  11.9 us (8%)
  matrix products  9.22 us (6%)
  Pallas kernels  5.47 us (3%)
  local copies, waits for them, and re-layouts  4.64 us (3%)
    reduce_scatter x1, waiting for transfers between devices, shards(): return lax.psum_scatter(half, 'z', scatter_dimension=0, tiled=True)  37.7 us
    all_to_all x1, starting transfers between devices, shards(): lax.all_to_all(to_send, ('y', 'x'), split_axis=0, concat_axis=0, tiled=True)  17.8 us
    all_to_all x1, starting transfers between devices, shards(): lax.all_to_all(pieces, ('x', 'z', 'core'), split_axis=0, concat_axis=0, t...  14 us
    all_to_all x1, waiting for transfers between devices, shards(): lax.all_to_all(pieces, ('x', 'z', 'core'), split_axis=0, concat_axis=0, t...  13.8 us
    ppermute x1, waiting for transfers between devices, shards(): fetched = lax.ppermute(row, ('y', 'core'), perm=perm)  10.2 us
    all_to_all x1, waiting for transfers between devices, shards(): lax.all_to_all(to_send, ('y', 'x'), split_axis=0, concat_axis=0, tiled=True)  8.69 us
    dot_general x2, matrix products, project(): jnp.dot(relaid, out_weight, preferred_element_type=jnp.float32)  7.47 us
    pallas_call x1, Pallas kernels, attention(): pl.pallas_call(functools.partial(_attention_body, scale), grid=(heads,),...  5.47 us
  transfers between devices with their start and end apart: 6, of which 6 were waited for; matrix products, arithmetic and copies ran while one was open for 5% of the time, Pallas kernels for 0%

profile of v9, /device:TPU:6, one launch (start us, length us, event | category | flops | bytes accessed | tf_op | source)
XLA Modules:
  0.0 157.1 jit_solution(14350476890543888696)
XLA Ops:
  6.5 0.7 pad_clamp_fusion
  7.3 0.7 bitcast_bitcast_fusion
  8.0 1.4 gather_fusion
  9.4 14.0 %all-to-all-start = ((bf16[64,16,256]{2,1,0:T(8,128)(2,1)}), bf16[64,16,256]{2,1,0:T(8,128)(2,1)S(1)}, u32[]{:S(2)}, u32[]{:S(2)}) async-start(bf16[64,16,256]{2,1,0:T(8,128)(2,1)} %gather_fusion), calls=%async_computation | async-start | bytes 1048576 | tf_op jit(solution)/shard_map/all_to_all | solution.py:85
  23.4 0.8 dynamic_slice.14
  24.2 0.8 copy.15.qs_ref
  25.0 0.1 pad_dynamic-slice_fusion.3
  25.1 0.6 reshape.51.ks_ref
  25.7 0.7 iota_add_fusion.qp_ref
  26.3 13.8 %all-to-all-done = bf16[64,16,256]{2,1,0:T(8,128)(2,1)S(1)} async-done(((bf16[64,16,256]{2,1,0:T(8,128)(2,1)}), bf16[64,16,256]{2,1,0:T(8,128)(2,1)S(1)}, u32[]{:S(2)}, u32[]{:S(2)}) %all-to-all-start) | async-done | bytes 524320 | tf_op jit(solution)/shard_map/all_to_all | solution.py:85
  40.1 3.5 %collective-permute-start = (bf16[1024,256]{1,0:T(8,128)(2,1)S(1)}, bf16[1024,256]{1,0:T(8,128)(2,1)S(1)}, u32[]{:S(2)}, u32[]{:S(2)}) collective-permute-start(bf16[1024,256]{1,0:T(8,128)(2,1)S(1)} %bitcast.30), channel_id=1, source_target_pairs={{0,64},{64,128},{128,192},{192,256},{256,320},{320,384},{384,448},... | collective-permute-start | bytes 1572872 | tf_op jit(solution)/shard_map/ppermute | solution.py:98
  43.6 1.2 select_reduce_fusion
  44.9 0.2 convert_reduce_fusion
  45.1 10.2 %collective-permute-done = bf16[1024,256]{1,0:T(8,128)(2,1)S(1)} collective-permute-done((bf16[1024,256]{1,0:T(8,128)(2,1)S(1)}, bf16[1024,256]{1,0:T(8,128)(2,1)S(1)}, u32[]{:S(2)}, u32[]{:S(2)}) %collective-permute-start) | collective-permute-done | bytes 524320 | tf_op jit(solution)/shard_map/ppermute | solution.py:98
  55.3 2.6 %collective-permute-start.1 = (bf16[1024,256]{1,0:T(8,128)(2,1)S(1)}, bf16[1024,256]{1,0:T(8,128)(2,1)S(1)}, u32[]{:S(2)}, u32[]{:S(2)}) collective-permute-start(bf16[1024,256]{1,0:T(8,128)(2,1)S(1)} %collective-permute-done), channel_id=1, source_target_pairs={{0,1},{1,0},{2,3},{3,2},{4,5},{5,4},{6,7},{7,6},{8,9},{9,8},{10,11... | collective-permute-start | bytes 1572872 | tf_op jit(solution)/shard_map/ppermute | solution.py:99
  57.9 0.1 and_select_fusion
  58.0 0.2 convert_reduce_fusion.1
  58.2 0.6 iota_add_fusion.1.kp_ref
  58.8 0.6 collective-permute-done.1
  59.5 4.7 %fusion.1.k_ref.v_ref = bf16[2304,256]{1,0:T(8,128)(2,1)} fusion(s32[]{:T(128)S(6)} %select_n.51, bf16[1024,256]{1,0:T(8,128)(2,1)S(1)} %get-tuple-element.18, bf16[1024,256]{1,0:T(8,128)(2,1)S(1)} %get-tuple-element.17, bf16[1024,256]{1,0:T(8,128)(2,1)S(1)} %bitcast.31), kind=kLoop, calls=%fused_computation.9 | loop fusion | flops 3538944 | bytes 2752516 | tf_op jit(solution)/shard_map/concatenate | solution.py:101
  64.2 5.5 %shard_map.82 = bf16[256,256]{1,0:T(8,128)(2,1)} custom-call(bf16[256,256]{1,0:T(8,128)(2,1)} %q_ref.1, bf16[2304,256]{1,0:T(8,128)(2,1)} %fusion.1.k_ref.v_ref, bf16[2304,256]{1,0:T(8,128)(2,1)} %fusion.1.k_ref.v_ref, s32[256,1]{1,0:T(8,128)} %iota_add_fusion.qp_ref, s32[256,1]{1,0:T(8,128)} %copy.15.qs_ref, s32[1,2304]{1,0:T(1,128)} %iota_add_fusion.1.kp_ref, ...), custom_call_target="tpu_custom_call" | custom-call | flops 603979776 | bytes 1441792 | tf_op jit(solution)/shard_map/pallas_call | solution.py:34
  69.6 1.8 %fusion.2 = bf16[32,8,256]{2,1,0:T(8,128)(2,1)} fusion(bf16[256,256]{1,0:T(8,128)(2,1)} %shard_map.82, s32[256]{0:T(256)S(1)} %convert_reduce_fusion), kind=kOutput, calls=%fused_computation.11 | convolution fusion | flops 33685504 | bytes 263168 | tf_op jit(solution)/shard_map/dot_general | solution.py:122
  71.4 17.8 %all-to-all-start.1 = ((bf16[32,8,256]{2,1,0:T(8,128)(2,1)}), bf16[32,8,256]{2,1,0:T(8,128)(2,1)S(1)}, u32[]{:S(2)}, u32[]{:S(2)}) async-start(bf16[32,8,256]{2,1,0:T(8,128)(2,1)} %fusion.2), calls=%async_computation.1 | async-start | bytes 262144 | tf_op jit(solution)/shard_map/all_to_all | solution.py:123
  89.3 0.1 multiply_add_fusion
  89.4 0.1 reshape.46
  89.6 8.7 %all-to-all-done.1 = bf16[32,8,256]{2,1,0:T(8,128)(2,1)S(1)} async-done(((bf16[32,8,256]{2,1,0:T(8,128)(2,1)}), bf16[32,8,256]{2,1,0:T(8,128)(2,1)S(1)}, u32[]{:S(2)}, u32[]{:S(2)}) %all-to-all-start.1) | async-done | bytes 131104 | tf_op jit(solution)/shard_map/all_to_all | solution.py:123
  98.3 4.4 %convolution_convert_fusion = bf16[128,8192]{1,0:T(8,128)(2,1)} fusion(bf16[256,8192]{1,0:T(8,128)(2,1)} %param.15, bf16[32,8,256]{2,1,0:T(8,128)(2,1)S(1)} %all-to-all-done.1, s32[128]{0:T(128)S(1)} %eq.87), kind=kOutput, calls=%fused_computation.1 | convolution fusion | flops 554762240 | bytes 6423040 | tf_op jit(solution)/shard_map/dot_general | solution.py:137
  102.7 1.9 %collective-permute-start.2 = (bf16[128,8192]{1,0:T(8,128)(2,1)}, bf16[128,8192]{1,0:T(8,128)(2,1)}, u32[]{:S(2)}, u32[]{:S(2)}) collective-permute-start(bf16[128,8192]{1,0:T(8,128)(2,1)} %convolution_convert_fusion), channel_id=1, source_target_pairs={{0,1},{1,0},{2,3},{3,2},{4,5},{5,4},{6,7},{7,6},{8,9},{9,8},{10,11... | collective-permute-start | bytes 6291464 | tf_op jit(solution)/shard_map/ppermute | solution.py:140
  104.7 3.1 %convolution_convert_fusion.1 = bf16[128,8192]{1,0:T(8,128)(2,1)S(1)} fusion(bf16[256,8192]{1,0:T(8,128)(2,1)} %param.15, bf16[32,8,256]{2,1,0:T(8,128)(2,1)S(1)} %all-to-all-done.1, s32[128]{0:T(128)S(1)} %eq.76), kind=kOutput, calls=%fused_computation.2 | convolution fusion | flops 554762240 | bytes 6423040 | tf_op jit(solution)/shard_map/dot_general | solution.py:137
  107.7 1.3 collective-permute-done.2
  109.0 3.4 %add_convert_fusion = bf16[128,8192]{1,0:T(8,128)(2,1)} fusion(bf16[128,8192]{1,0:T(8,128)(2,1)} %collective-permute-done.2, bf16[128,8192]{1,0:T(8,128)(2,1)S(1)} %convolution_convert_fusion.1), kind=kLoop, calls=%fused_computation.4 | loop fusion | flops 4194304 | bytes 6291456 | tf_op jit(solution)/shard_map/convert_element_type | solution.py:142
  112.5 37.7 %reduce-scatter.2.cloned.1.call-done = bf16[16,8192]{1,0:T(8,128)(2,1)} async-done(((bf16[128,8192]{1,0:T(8,128)(2,1)}), bf16[16,8192]{1,0:T(8,128)(2,1)}) %reduce-scatter.2.cloned.1.call-update) | async-done | bytes 262160 | tf_op jit(solution)/shard_map/reduce_scatter | solution.py:143
  (14 shorter events, 0.4 us)
Async XLA Ops:
  6.5 0.7 copy-start
  6.5 18.4 %copy-start.2 = (s32[8192]{0:T(1024)S(1)}, s32[8192]{0:T(1024)}, u32[]{:S(2)}) copy-start(s32[8192]{0:T(1024)} %param.10) | copy-start | bytes 98308
  6.5 37.1 %copy-start.1 = (s32[8192]{0:T(1024)S(1)}, s32[8192]{0:T(1024)}, u32[]{:S(2)}) copy-start(s32[8192]{0:T(1024)} %param.11) | copy-start | bytes 98308
  9.4 30.7 %all-to-all-start = ((bf16[64,16,256]{2,1,0:T(8,128)(2,1)}), bf16[64,16,256]{2,1,0:T(8,128)(2,1)S(1)}, u32[]{:S(2)}, u32[]{:S(2)}) async-start(bf16[64,16,256]{2,1,0:T(8,128)(2,1)} %gather_fusion), calls=%async_computation | async-start | bytes 1048576 | tf_op jit(solution)/shard_map/all_to_all | solution.py:85
  40.1 15.2 %collective-permute-start = (bf16[1024,256]{1,0:T(8,128)(2,1)S(1)}, bf16[1024,256]{1,0:T(8,128)(2,1)S(1)}, u32[]{:S(2)}, u32[]{:S(2)}) collective-permute-start(bf16[1024,256]{1,0:T(8,128)(2,1)S(1)} %bitcast.30), channel_id=1, source_target_pairs={{0,64},{64,128},{128,192},{192,256},{256,320},{320,384},{384,448},... | collective-permute-start | bytes 1572872 | tf_op jit(solution)/shard_map/ppermute | solution.py:98
  55.3 4.1 %collective-permute-start.1 = (bf16[1024,256]{1,0:T(8,128)(2,1)S(1)}, bf16[1024,256]{1,0:T(8,128)(2,1)S(1)}, u32[]{:S(2)}, u32[]{:S(2)}) collective-permute-start(bf16[1024,256]{1,0:T(8,128)(2,1)S(1)} %collective-permute-done), channel_id=1, source_target_pairs={{0,1},{1,0},{2,3},{3,2},{4,5},{5,4},{6,7},{7,6},{8,9},{9,8},{10,11... | collective-permute-start | bytes 1572872 | tf_op jit(solution)/shard_map/ppermute | solution.py:99
  71.4 26.9 %all-to-all-start.1 = ((bf16[32,8,256]{2,1,0:T(8,128)(2,1)}), bf16[32,8,256]{2,1,0:T(8,128)(2,1)S(1)}, u32[]{:S(2)}, u32[]{:S(2)}) async-start(bf16[32,8,256]{2,1,0:T(8,128)(2,1)} %fusion.2), calls=%async_computation.1 | async-start | bytes 262144 | tf_op jit(solution)/shard_map/all_to_all | solution.py:123
  89.2 61.0 %reduce-scatter.2.cloned.1.call-start = ((), (), s32[]{:S(2)}) async-start(), calls=%async_computation.3 | async-start | bytes 2359296 | tf_op jit(solution)/shard_map/reduce_scatter | solution.py:143
  102.7 6.4 %collective-permute-start.2 = (bf16[128,8192]{1,0:T(8,128)(2,1)}, bf16[128,8192]{1,0:T(8,128)(2,1)}, u32[]{:S(2)}, u32[]{:S(2)}) collective-permute-start(bf16[128,8192]{1,0:T(8,128)(2,1)} %convolution_convert_fusion), channel_id=1, source_target_pairs={{0,1},{1,0},{2,3},{3,2},{4,5},{5,4},{6,7},{7,6},{8,9},{9,8},{10,11... | collective-permute-start | bytes 6291464 | tf_op jit(solution)/shard_map/ppermute | solution.py:140
Sparse Core Ops, SparseCore 0:
  112.6 37.5 reduce-scatter.1

commit v10 on v8

--- a/solution.py
+++ b/solution.py
@@ -1,7 +1,11 @@
+import functools
+
 import jax
 import jax.numpy as jnp
 import numpy as np
 from jax import lax
+from jax.experimental import pallas as pl
+from jax.experimental.pallas import tpu as pltpu
 from jax.sharding import Mesh
 from jax.sharding import PartitionSpec as P
 
@@ -9,6 +13,89 @@
 KVH = 4
 HD = 128
 MOST_LEN = 2048
+
+
+TILE = 256
+
+
+def _attention_body(scale, n_pieces, n_tiles, flags_ref, q_ref, *refs):
+    kv_refs = refs[:n_pieces]
+    qp_ref, qs_ref, kp_ref, ks_ref, o_ref, m_ref, l_ref, acc_ref = refs[n_pieces:]
+    q = q_ref[...]
+    qp = qp_ref[...]
+    qs = qs_ref[...]
+
+    def scores(p, j):
+        k = kv_refs[p][pl.ds(j * TILE, TILE), pl.ds(0, HD)]
+        s = lax.dot_general(q, k, (((1,), (1,)), ((), ())), preferred_element_type=jnp.float32) * scale
+        kp = kp_ref[pl.ds(p, 1), pl.ds(j * TILE, TILE)]
+        ks = ks_ref[pl.ds(p, 1), pl.ds(j * TILE, TILE)]
+        live = (kp <= qp) & (ks == qs)
+        return s, live
+
+    m_ref[...] = jnp.full(m_ref.shape, -1e30, jnp.float32)
+    l_ref[...] = jnp.zeros(l_ref.shape, jnp.float32)
+    acc_ref[...] = jnp.zeros(acc_ref.shape, jnp.float32)
+    for p in range(n_pieces):
+        for j in range(n_tiles):
+            @pl.when(flags_ref[p * n_tiles + j] > 0)
+            def _():
+                s, live = scores(p, j)
+                masked = jnp.where(live, s, jnp.float32(-1e30))
+                m_ref[...] = jnp.maximum(m_ref[...], jnp.max(masked, axis=1, keepdims=True))
+    for p in range(n_pieces):
+        for j in range(n_tiles):
+            @pl.when(flags_ref[p * n_tiles + j] > 0)
+            def _():
+                s, live = scores(p, j)
+                expo = jnp.where(live, jnp.exp(s - m_ref[...]), jnp.float32(0.0))
+                l_ref[...] += jnp.sum(expo, axis=1, keepdims=True)
+                v = kv_refs[p][pl.ds(j * TILE, TILE), pl.ds(HD, HD)]
+                acc_ref[...] += jnp.dot(expo.astype(jnp.bfloat16), v, preferred_element_type=jnp.float32)
+    o_ref[...] = (acc_ref[...] / l_ref[...]).astype(o_ref.dtype)
+
+
+def attention(q, pieces, q_pos, q_seg, k_pos, k_seg, scale):
+    rows, width = q.shape
+    heads = width // HD
+    n_pieces = len(pieces)
+    n = pieces[0].shape[0]
+    n_tiles = n // TILE
+    kp_t = k_pos.reshape(n_pieces, n_tiles, TILE)
+    ks_t = k_seg.reshape(n_pieces, n_tiles, TILE)
+    flags = (
+        (kp_t[:, :, 0] <= q_pos[-1])
+        & (ks_t[:, :, -1] >= q_seg[0])
+        & (ks_t[:, :, 0] <= q_seg[-1])
+    ).astype(jnp.int32).reshape(-1)
+    grid_spec = pltpu.PrefetchScalarGridSpec(
+        num_scalar_prefetch=1,
+        grid=(heads,),
+        in_specs=[pl.BlockSpec((rows, HD), lambda h, f: (0, h))]
+        + [pl.BlockSpec((n, 2 * HD), lambda h, f: (0, 0)) for _ in range(n_pieces)]
+        + [
+            pl.BlockSpec((rows, 1), lambda h, f: (0, 0)),
+            pl.BlockSpec((rows, 1), lambda h, f: (0, 0)),
+            pl.BlockSpec((n_pieces, n), lambda h, f: (0, 0)),
+            pl.BlockSpec((n_pieces, n), lambda h, f: (0, 0)),
+        ],
+        out_specs=pl.BlockSpec((rows, HD), lambda h, f: (0, h)),
+        scratch_shapes=[
+            pltpu.VMEM((rows, 1), jnp.float32),
+            pltpu.VMEM((rows, 1), jnp.float32),
+            pltpu.VMEM((rows, HD), jnp.float32),
+        ],
+    )
+    return pl.pallas_call(
+        functools.partial(_attention_body, scale, n_pieces, n_tiles),
+        grid_spec=grid_spec,
+        out_shape=jax.ShapeDtypeStruct((rows, width), jnp.bfloat16),
+        cost_estimate=pl.CostEstimate(
+            flops=6 * rows * n * n_pieces * HD * heads,
+            transcendentals=rows * n * n_pieces * heads,
+            bytes_accessed=2 * (2 * rows * width + 2 * n_pieces * n * HD),
+        ),
+    )(flags, q, *pieces, q_pos.reshape(rows, 1), q_seg.reshape(rows, 1), k_pos, k_seg)
 
 
 def shards(segment_ids, relayout, queries, keys, values, out_weight):
@@ -39,7 +126,7 @@
     x = lax.axis_index("x")
     c = lax.axis_index("core")
     rows_back = -(-back // n_x)
-    assert rows_back <= n_core
+    assert rows_back == n_core
     perm = []
     for cc in range(n_core):
         k = cc + 1
@@ -47,36 +134,16 @@
             perm += [(yy * n_core + cc, (yy + k) * n_core + cc) for yy in range(n_y - k)]
     fetched = lax.ppermute(row, ("y", "core"), perm=perm)
     swapped = lax.ppermute(fetched, "core", perm=[(i, (i + 1) % n_core) for i in range(n_core)])
-    earlier = [jnp.where(c == k - 1, fetched, swapped) for k in range(rows_back, 0, -1)]
-    kv_all = jnp.concatenate(earlier + [row], axis=0)
-    n_keys = (back + 1) * rows
-    first = (rows_back * n_x - back + x) * rows
-    kv_win = lax.dynamic_slice_in_dim(kv_all, first, n_keys, 0)
-    k_win = kv_win[:, :HD]
-    v_win = kv_win[:, HD:]
-
+    y = lax.axis_index("y")
+    span = n_x * rows
+    piece_rows = [y - 1 - c, y - n_core + c, y]
+    k_pos = jnp.stack([r * span + jnp.arange(span, dtype=jnp.int32) for r in piece_rows])
+    pad = rows_back * span
+    seg_pad = jnp.concatenate([jnp.full((pad,), -1, jnp.int32), segment_ids])
+    k_seg = jnp.stack([lax.dynamic_slice_in_dim(seg_pad, r * span + pad, span, 0) for r in piece_rows])
     q_pos = s * rows + jnp.arange(rows, dtype=jnp.int32)
-    k_pos = (s - back) * rows + jnp.arange(n_keys, dtype=jnp.int32)
     q_seg = lax.dynamic_slice_in_dim(segment_ids, s * rows, rows, 0)
-    seg_pad = jnp.concatenate([jnp.full((back * rows,), -1, jnp.int32), segment_ids])
-    k_seg = lax.dynamic_slice_in_dim(seg_pad, s * rows, n_keys, 0)
-    live = (
-        (k_pos[None, :] <= q_pos[:, None])
-        & (k_seg[None, :] == q_seg[:, None])
-        & (k_pos[None, :] >= 0)
-    )
-
-    q = queries.reshape(rows, heads_here, HD)
-    scores = jnp.einsum("qhd,kd->hqk", q, k_win, preferred_element_type=jnp.float32) * scale
-    masked = jnp.where(live[None], scores, jnp.float32(-1e30))
-    peak = jnp.max(masked, axis=-1)
-    expo = jnp.where(live[None], jnp.exp(masked - peak[..., None]), jnp.float32(0.0))
-    denom = jnp.sum(expo, axis=-1)
-    summed = jnp.einsum(
-        "hqk,kd->hqd", expo.astype(jnp.bfloat16), v_win, preferred_element_type=jnp.float32
-    )
-    attn = summed / denom[..., None]
-    attn_rows = jnp.transpose(attn, (1, 0, 2)).reshape(rows, heads_here * HD).astype(jnp.bfloat16)
+    attn_rows = attention(queries, [fetched, swapped, row], q_pos, q_seg, k_pos, k_seg, scale)
 
     chunk = rows // n_seq
     total = relayout.shape[0]

time: 156 us -> 160 us (1.026)
  Pallas kernels: 0 us -> 6 us
  local copies, waits for them, and re-layouts: 3.14 us -> 7.34 us
  waiting for transfers between devices: 72.5 us -> 68.5 us
  matrix products: 12.8 us -> 9.23 us
  starting transfers between devices: 39.6 us -> 42.7 us
    pallas_call x0 -> x1, Pallas kernels: none -> 6 us  [attention(): pl.pallas_call(functools.partial(_attention_body, scale, n_pieces, n_tile...]
    all_to_all x1, waiting for transfers between devices: 14.4 us -> 10.5 us  [shards(): lax.all_to_all(pieces, ('x', 'z', 'core'), split_axis=0, concat_axis=0, t...]
    concatenate x1 -> x0, other arithmetic: 3.63 us -> none  [shards(): kv_all = jnp.concatenate(earlier + [row], axis=0)]
    all_to_all x1, starting transfers between devices: 17.5 us -> 20.6 us  [shards(): lax.all_to_all(to_send, ('y', 'x'), split_axis=0, concat_axis=0, tiled=True)]
    dot_general x1 -> x0, matrix products: 2.29 us -> none  [shards(): jnp.einsum('hqk,kd->hqd', expo.astype(jnp.bfloat16), v_win, preferred_ele...]
    sub x1 -> x0, matrix products: 2.22 us -> none  [shards(): masked - peak[..., None]]
    and x1 -> x0, other arithmetic: 2.17 us -> none  [shards(): (k_pos[None, :] <= q_pos[:, None]) & (k_seg[None, :] == q_seg[:, None])]
    convert_element_type x0 -> x1, other arithmetic: none -> 2.05 us  [attention(): flags = ((kp_t[:, :, 0] <= q_pos[-1]) & (ks_t[:, :, -1] >= q_seg[0]) & (k...]
  transfers between devices with their start and end apart: 6 -> 6, of which waited for: 5 -> 5; matrix products, arithmetic and copies ran while one was open for 6% -> 10% of each run, Pallas kernels for 0% -> 0%
where the time goes in v10:
time: 160 us; the launch traced here: 159 us
  waiting for transfers between devices  68.5 us (43%)
  starting transfers between devices  42.7 us (27%)
  between operations  13.6 us (8%)
  other arithmetic  12 us (8%)
  matrix products  9.23 us (6%)
  local copies, waits for them, and re-layouts  7.34 us (5%)
  Pallas kernels  6 us (4%)
    reduce_scatter x1, waiting for transfers between devices, shards(): return lax.psum_scatter(half, 'z', scatter_dimension=0, tiled=True)  39.5 us
    all_to_all x1, starting transfers between devices, shards(): lax.all_to_all(to_send, ('y', 'x'), split_axis=0, concat_axis=0, tiled=True)  20.6 us
    all_to_all x1, starting transfers between devices, shards(): lax.all_to_all(pieces, ('x', 'z', 'core'), split_axis=0, concat_axis=0, t...  14 us
    all_to_all x1, waiting for transfers between devices, shards(): lax.all_to_all(pieces, ('x', 'z', 'core'), split_axis=0, concat_axis=0, t...  10.5 us
    ppermute x1, waiting for transfers between devices, shards(): fetched = lax.ppermute(row, ('y', 'core'), perm=perm)  8.97 us
    all_to_all x1, waiting for transfers between devices, shards(): lax.all_to_all(to_send, ('y', 'x'), split_axis=0, concat_axis=0, tiled=True)  8.31 us
    dot_general x2, matrix products, project(): jnp.dot(relaid, out_weight, preferred_element_type=jnp.float32)  7.48 us
    pallas_call x1, Pallas kernels, attention(): pl.pallas_call(functools.partial(_attention_body, scale, n_pieces, n_tile...  6 us
  transfers between devices with their start and end apart: 6, of which 5 were waited for; matrix products, arithmetic and copies ran while one was open for 10% of the time, Pallas kernels for 0%

profile of v10, /device:TPU:6, one launch (start us, length us, event | category | flops | bytes accessed | tf_op | source)
XLA Modules:
  0.0 159.4 jit_solution(5818573009792273849)
XLA Ops:
  6.5 0.7 pad_clamp_fusion
  7.3 0.7 bitcast_bitcast_fusion
  8.0 1.4 gather_fusion
  9.4 14.0 %all-to-all-start = ((bf16[64,16,256]{2,1,0:T(8,128)(2,1)}), bf16[64,16,256]{2,1,0:T(8,128)(2,1)S(1)}, u32[]{:S(2)}, u32[]{:S(2)}) async-start(bf16[64,16,256]{2,1,0:T(8,128)(2,1)} %gather_fusion), calls=%async_computation | async-start | bytes 1048576 | tf_op jit(solution)/shard_map/all_to_all | solution.py:122
  23.4 0.7 pad_dynamic-slice_fusion
  24.2 0.8 dynamic_slice.19
  24.9 0.6 slice.19
  25.5 0.6 fusion.17
  26.1 2.0 %convert_reduce_fusion.2 = s32[3,4]{1,0:T(4,128)S(1)} fusion(s32[3,4,256]{2,1,0:T(4,128)S(1)} %get-tuple-element.24, s32[1,4,256]{2,1,0:T(4,128)S(1)} %get-tuple-element.25, s32[1,4,256]{2,1,0:T(4,128)S(1)} %get-tuple-element.26, s32[1,4,256]{2,1,0:T(4,128)S(1)} %get-tuple-element.27, s32[]{:T(128)} %bitcast.3, s32[]{:T(128)} %bitcast.2, s32[]{:T(128)} %bitcast.1), kind=kLoop, calls=%fused_computation.40 | loop fusion | flops 96 | bytes 12444 | tf_op jit(solution)/shard_map/convert_element_type | solution.py:70
  28.2 0.7 reshape.151.flags_ref
  28.8 0.8 copy.15.refs_4_
  29.7 10.5 %all-to-all-done = bf16[64,16,256]{2,1,0:T(8,128)(2,1)S(1)} async-done(((bf16[64,16,256]{2,1,0:T(8,128)(2,1)}), bf16[64,16,256]{2,1,0:T(8,128)(2,1)S(1)}, u32[]{:S(2)}, u32[]{:S(2)}) %all-to-all-start) | async-done | bytes 524320 | tf_op jit(solution)/shard_map/all_to_all | solution.py:122
  40.1 3.5 %collective-permute-start = (bf16[1024,256]{1,0:T(8,128)(2,1)S(1)}, bf16[1024,256]{1,0:T(8,128)(2,1)S(1)}, u32[]{:S(2)}, u32[]{:S(2)}) collective-permute-start(bf16[1024,256]{1,0:T(8,128)(2,1)S(1)} %bitcast.36), channel_id=1, source_target_pairs={{0,64},{64,128},{128,192},{192,256},{256,320},{320,384},{384,448},... | collective-permute-start | bytes 1572872 | tf_op jit(solution)/shard_map/ppermute | solution.py:135
  43.6 0.8 and_select_fusion
  44.4 0.6 pad_add_fusion.1.refs_6_
  45.0 0.6 pad_add_fusion.refs_5_
  45.6 0.7 iota_add_fusion.refs_3_
  46.3 9.0 %collective-permute-done.refs_0_ = bf16[1024,256]{1,0:T(8,128)(2,1)S(1)} collective-permute-done((bf16[1024,256]{1,0:T(8,128)(2,1)S(1)}, bf16[1024,256]{1,0:T(8,128)(2,1)S(1)}, u32[]{:S(2)}, u32[]{:S(2)}) %collective-permute-start) | collective-permute-done | bytes 524320 | tf_op jit(solution)/shard_map/ppermute | solution.py:135
  55.3 2.6 %collective-permute-start.1 = (bf16[1024,256]{1,0:T(8,128)(2,1)S(1)}, bf16[1024,256]{1,0:T(8,128)(2,1)S(1)}, u32[]{:S(2)}, u32[]{:S(2)}) collective-permute-start(bf16[1024,256]{1,0:T(8,128)(2,1)S(1)} %collective-permute-done.refs_0_), channel_id=1, source_target_pairs={{0,1},{1,0},{2,3},{3,2},{4,5},{5,4},{6,7},{7,6},{8,9},{9,8},{10,11... | collective-permute-start | bytes 1572872 | tf_op jit(solution)/shard_map/ppermute | solution.py:136
  57.9 2.0 %select_reduce_fusion = s32[256]{0:T(256)S(1)} fusion(s32[8192]{0:T(1024)} %param.11, s32[256]{0:T(256)S(1)} %iota_add_fusion.4), kind=kLoop, calls=%fused_computation.3 | loop fusion | flops 6291200 | bytes 34816 | tf_op jit(solution)/shard_map/reduce_sum | solution.py:151
  60.3 0.8 copy-done.3
  61.1 6.0 %shard_map.82 = bf16[256,256]{1,0:T(8,128)(2,1)} custom-call(s32[12]{0:T(128)} %reshape.151.flags_ref, bf16[256,256]{1,0:T(8,128)(2,1)} %q_ref.1, bf16[1024,256]{1,0:T(8,128)(2,1)} %copy-done.2, bf16[1024,256]{1,0:T(8,128)(2,1)} %copy-done.3, bf16[1024,256]{1,0:T(8,128)(2,1)} %bitcast.37, s32[256,1]{1,0:T(8,128)} %iota_add_fusion.refs_3_, ...), custom_call_target="tpu_custom_call" | custom-call | flops 1207959552 | bytes 1835008 | tf_op jit(solution)/shard_map/pallas_call | solution.py:89
  67.1 1.8 %fusion = bf16[32,8,256]{2,1,0:T(8,128)(2,1)} fusion(bf16[256,256]{1,0:T(8,128)(2,1)} %shard_map.82, s32[256]{0:T(256)S(1)} %convert_reduce_fusion), kind=kOutput, calls=%fused_computation.6 | convolution fusion | flops 33685504 | bytes 263168 | tf_op jit(solution)/shard_map/dot_general | solution.py:157
  68.9 20.6 %all-to-all-start.1 = ((bf16[32,8,256]{2,1,0:T(8,128)(2,1)}), bf16[32,8,256]{2,1,0:T(8,128)(2,1)S(1)}, u32[]{:S(2)}, u32[]{:S(2)}) async-start(bf16[32,8,256]{2,1,0:T(8,128)(2,1)} %fusion), calls=%async_computation.1 | async-start | bytes 262144 | tf_op jit(solution)/shard_map/all_to_all | solution.py:158
  89.6 0.8 multiply_add_fusion.1
  90.5 8.3 %all-to-all-done.1 = bf16[32,8,256]{2,1,0:T(8,128)(2,1)S(1)} async-done(((bf16[32,8,256]{2,1,0:T(8,128)(2,1)}), bf16[32,8,256]{2,1,0:T(8,128)(2,1)S(1)}, u32[]{:S(2)}, u32[]{:S(2)}) %all-to-all-start.1) | async-done | bytes 131104 | tf_op jit(solution)/shard_map/all_to_all | solution.py:158
  98.9 4.4 %convolution_convert_fusion = bf16[128,8192]{1,0:T(8,128)(2,1)} fusion(bf16[256,8192]{1,0:T(8,128)(2,1)} %param.15, bf16[32,8,256]{2,1,0:T(8,128)(2,1)S(1)} %all-to-all-done.1, s32[128]{0:T(128)S(1)} %eq.79), kind=kOutput, calls=%fused_computation.1 | convolution fusion | flops 554762240 | bytes 6423040 | tf_op jit(solution)/shard_map/dot_general | solution.py:172
  103.3 1.9 %collective-permute-start.2 = (bf16[128,8192]{1,0:T(8,128)(2,1)}, bf16[128,8192]{1,0:T(8,128)(2,1)}, u32[]{:S(2)}, u32[]{:S(2)}) collective-permute-start(bf16[128,8192]{1,0:T(8,128)(2,1)} %convolution_convert_fusion), channel_id=1, source_target_pairs={{0,1},{1,0},{2,3},{3,2},{4,5},{5,4},{6,7},{7,6},{8,9},{9,8},{10,11... | collective-permute-start | bytes 6291464 | tf_op jit(solution)/shard_map/ppermute | solution.py:175
  105.3 3.1 %convolution_convert_fusion.1 = bf16[128,8192]{1,0:T(8,128)(2,1)S(1)} fusion(bf16[256,8192]{1,0:T(8,128)(2,1)} %param.15, bf16[32,8,256]{2,1,0:T(8,128)(2,1)S(1)} %all-to-all-done.1, s32[128]{0:T(128)S(1)} %eq.70), kind=kOutput, calls=%fused_computation.2 | convolution fusion | flops 554762240 | bytes 6423040 | tf_op jit(solution)/shard_map/dot_general | solution.py:172
  108.3 1.3 collective-permute-done.2
  109.6 3.4 %add_convert_fusion = bf16[128,8192]{1,0:T(8,128)(2,1)} fusion(bf16[128,8192]{1,0:T(8,128)(2,1)} %collective-permute-done.2, bf16[128,8192]{1,0:T(8,128)(2,1)S(1)} %convolution_convert_fusion.1), kind=kLoop, calls=%fused_computation.4 | loop fusion | flops 4194304 | bytes 6291456 | tf_op jit(solution)/shard_map/convert_element_type | solution.py:177
  113.1 39.5 %reduce-scatter.2.cloned.1.call-done = bf16[16,8192]{1,0:T(8,128)(2,1)} async-done(((bf16[128,8192]{1,0:T(8,128)(2,1)}), bf16[16,8192]{1,0:T(8,128)(2,1)}) %reduce-scatter.2.cloned.1.call-update) | async-done | bytes 262160 | tf_op jit(solution)/shard_map/reduce_scatter | solution.py:178
  (27 shorter events, 0.8 us)
Async XLA Ops:
  6.5 0.7 copy-start
  9.4 30.7 %all-to-all-start = ((bf16[64,16,256]{2,1,0:T(8,128)(2,1)}), bf16[64,16,256]{2,1,0:T(8,128)(2,1)S(1)}, u32[]{:S(2)}, u32[]{:S(2)}) async-start(bf16[64,16,256]{2,1,0:T(8,128)(2,1)} %gather_fusion), calls=%async_computation | async-start | bytes 1048576 | tf_op jit(solution)/shard_map/all_to_all | solution.py:122
  40.1 20.2 %copy-start.1 = (bf16[64,16,256]{2,1,0:T(8,128)(2,1)}, bf16[64,16,256]{2,1,0:T(8,128)(2,1)S(1)}, u32[]{:S(2)}) copy-start(bf16[64,16,256]{2,1,0:T(8,128)(2,1)S(1)} %all-to-all-done) | copy-start | bytes 1572868
  40.1 15.2 %collective-permute-start = (bf16[1024,256]{1,0:T(8,128)(2,1)S(1)}, bf16[1024,256]{1,0:T(8,128)(2,1)S(1)}, u32[]{:S(2)}, u32[]{:S(2)}) collective-permute-start(bf16[1024,256]{1,0:T(8,128)(2,1)S(1)} %bitcast.36), channel_id=1, source_target_pairs={{0,64},{64,128},{128,192},{192,256},{256,320},{320,384},{384,448},... | collective-permute-start | bytes 1572872 | tf_op jit(solution)/shard_map/ppermute | solution.py:135
  55.3 5.0 %copy-start.2 = (bf16[1024,256]{1,0:T(8,128)(2,1)}, bf16[1024,256]{1,0:T(8,128)(2,1)S(1)}, u32[]{:S(2)}) copy-start(bf16[1024,256]{1,0:T(8,128)(2,1)S(1)} %collective-permute-done.refs_0_) | copy-start | bytes 1572868
  55.3 5.0 %collective-permute-start.1 = (bf16[1024,256]{1,0:T(8,128)(2,1)S(1)}, bf16[1024,256]{1,0:T(8,128)(2,1)S(1)}, u32[]{:S(2)}, u32[]{:S(2)}) collective-permute-start(bf16[1024,256]{1,0:T(8,128)(2,1)S(1)} %collective-permute-done.refs_0_), channel_id=1, source_target_pairs={{0,1},{1,0},{2,3},{3,2},{4,5},{5,4},{6,7},{7,6},{8,9},{9,8},{10,11... | collective-permute-start | bytes 1572872 | tf_op jit(solution)/shard_map/ppermute | solution.py:136
  60.3 0.8 copy-start.3
  68.9 30.0 %all-to-all-start.1 = ((bf16[32,8,256]{2,1,0:T(8,128)(2,1)}), bf16[32,8,256]{2,1,0:T(8,128)(2,1)S(1)}, u32[]{:S(2)}, u32[]{:S(2)}) async-start(bf16[32,8,256]{2,1,0:T(8,128)(2,1)} %fusion), calls=%async_computation.1 | async-start | bytes 262144 | tf_op jit(solution)/shard_map/all_to_all | solution.py:158
  89.5 63.0 %reduce-scatter.2.cloned.1.call-start = ((), (), s32[]{:S(2)}) async-start(), calls=%async_computation.3 | async-start | bytes 2359296 | tf_op jit(solution)/shard_map/reduce_scatter | solution.py:178
  103.3 6.4 %collective-permute-start.2 = (bf16[128,8192]{1,0:T(8,128)(2,1)}, bf16[128,8192]{1,0:T(8,128)(2,1)}, u32[]{:S(2)}, u32[]{:S(2)}) collective-permute-start(bf16[128,8192]{1,0:T(8,128)(2,1)} %convolution_convert_fusion), channel_id=1, source_target_pairs={{0,1},{1,0},{2,3},{3,2},{4,5},{5,4},{6,7},{7,6},{8,9},{9,8},{10,11... | collective-permute-start | bytes 6291464 | tf_op jit(solution)/shard_map/ppermute | solution.py:175
Sparse Core Ops, SparseCore 0:
  113.2 39.2 reduce-scatter.1

commit v11 on v10

--- a/solution.py
+++ b/solution.py
@@ -18,44 +18,53 @@
 TILE = 256
 
 
-def _attention_body(scale, n_pieces, n_tiles, flags_ref, q_ref, *refs):
+def _attention_body(scale, n_pieces, n_tiles, carry_in, final, flags_ref, q_ref, *refs):
     kv_refs = refs[:n_pieces]
-    qp_ref, qs_ref, kp_ref, ks_ref, o_ref, m_ref, l_ref, acc_ref = refs[n_pieces:]
+    refs = refs[n_pieces:]
+    qp_ref, qs_ref, kp_ref, ks_ref = refs[:4]
+    refs = refs[4:]
+    if carry_in:
+        m_in, l_in, acc_in = refs[:3]
+        refs = refs[3:]
+    if final:
+        o_ref, m_ref, l_ref, acc_ref = refs
+    else:
+        m_ref, l_ref, acc_ref = refs
     q = q_ref[...]
     qp = qp_ref[...]
     qs = qs_ref[...]
-
-    def scores(p, j):
-        k = kv_refs[p][pl.ds(j * TILE, TILE), pl.ds(0, HD)]
-        s = lax.dot_general(q, k, (((1,), (1,)), ((), ())), preferred_element_type=jnp.float32) * scale
-        kp = kp_ref[pl.ds(p, 1), pl.ds(j * TILE, TILE)]
-        ks = ks_ref[pl.ds(p, 1), pl.ds(j * TILE, TILE)]
-        live = (kp <= qp) & (ks == qs)
-        return s, live
-
-    m_ref[...] = jnp.full(m_ref.shape, -1e30, jnp.float32)
-    l_ref[...] = jnp.zeros(l_ref.shape, jnp.float32)
-    acc_ref[...] = jnp.zeros(acc_ref.shape, jnp.float32)
+    if carry_in:
+        m_ref[0] = m_in[0]
+        l_ref[0] = l_in[0]
+        acc_ref[...] = acc_in[...]
+    else:
+        m_ref[...] = jnp.full(m_ref.shape, -1e30, jnp.float32)
+        l_ref[...] = jnp.zeros(l_ref.shape, jnp.float32)
+        acc_ref[...] = jnp.zeros(acc_ref.shape, jnp.float32)
     for p in range(n_pieces):
         for j in range(n_tiles):
             @pl.when(flags_ref[p * n_tiles + j] > 0)
             def _():
-                s, live = scores(p, j)
-                masked = jnp.where(live, s, jnp.float32(-1e30))
-                m_ref[...] = jnp.maximum(m_ref[...], jnp.max(masked, axis=1, keepdims=True))
-    for p in range(n_pieces):
-        for j in range(n_tiles):
-            @pl.when(flags_ref[p * n_tiles + j] > 0)
-            def _():
-                s, live = scores(p, j)
-                expo = jnp.where(live, jnp.exp(s - m_ref[...]), jnp.float32(0.0))
-                l_ref[...] += jnp.sum(expo, axis=1, keepdims=True)
+                k = kv_refs[p][pl.ds(j * TILE, TILE), pl.ds(0, HD)]
+                s = lax.dot_general(q, k, (((1,), (1,)), ((), ())), preferred_element_type=jnp.float32) * scale
+                kp = kp_ref[pl.ds(p, 1), pl.ds(j * TILE, TILE)]
+                ks = ks_ref[pl.ds(p, 1), pl.ds(j * TILE, TILE)]
+                live = (kp <= qp) & (ks == qs)
+                m_old = m_ref[0]
+                m_new = jnp.maximum(m_old, jnp.max(jnp.where(live, s, jnp.float32(-1e30)), axis=1, keepdims=True))
+                alpha = jnp.exp(m_old - m_new)
+                expo = jnp.where(live, jnp.exp(s - m_new), jnp.float32(0.0))
+                l_ref[0] = alpha * l_ref[0] + jnp.sum(expo, axis=1, keepdims=True)
                 v = kv_refs[p][pl.ds(j * TILE, TILE), pl.ds(HD, HD)]
-                acc_ref[...] += jnp.dot(expo.astype(jnp.bfloat16), v, preferred_element_type=jnp.float32)
-    o_ref[...] = (acc_ref[...] / l_ref[...]).astype(o_ref.dtype)
-
-
-def attention(q, pieces, q_pos, q_seg, k_pos, k_seg, scale):
+                acc_ref[...] = alpha * acc_ref[...] + jnp.dot(
+                    expo.astype(jnp.bfloat16), v, preferred_element_type=jnp.float32
+                )
+                m_ref[0] = m_new
+    if final:
+        o_ref[...] = (acc_ref[...] / l_ref[0]).astype(o_ref.dtype)
+
+
+def attention(q, pieces, q_pos, q_seg, k_pos, k_seg, scale, carry=None, final=True):
     rows, width = q.shape
     heads = width // HD
     n_pieces = len(pieces)
@@ -64,38 +73,55 @@
     kp_t = k_pos.reshape(n_pieces, n_tiles, TILE)
     ks_t = k_seg.reshape(n_pieces, n_tiles, TILE)
     flags = (
-        (kp_t[:, :, 0] <= q_pos[-1])
-        & (ks_t[:, :, -1] >= q_seg[0])
-        & (ks_t[:, :, 0] <= q_seg[-1])
+        (kp_t[:, :, 0] <= q_pos[-1]) & (ks_t[:, :, -1] >= q_seg[0]) & (ks_t[:, :, 0] <= q_seg[-1])
     ).astype(jnp.int32).reshape(-1)
-    grid_spec = pltpu.PrefetchScalarGridSpec(
-        num_scalar_prefetch=1,
-        grid=(heads,),
-        in_specs=[pl.BlockSpec((rows, HD), lambda h, f: (0, h))]
+    stat_spec = pl.BlockSpec((1, rows, 1), lambda h, f: (h, 0, 0))
+    acc_spec = pl.BlockSpec((rows, HD), lambda h, f: (0, h))
+    in_specs = (
+        [pl.BlockSpec((rows, HD), lambda h, f: (0, h))]
         + [pl.BlockSpec((n, 2 * HD), lambda h, f: (0, 0)) for _ in range(n_pieces)]
         + [
             pl.BlockSpec((rows, 1), lambda h, f: (0, 0)),
             pl.BlockSpec((rows, 1), lambda h, f: (0, 0)),
             pl.BlockSpec((n_pieces, n), lambda h, f: (0, 0)),
             pl.BlockSpec((n_pieces, n), lambda h, f: (0, 0)),
-        ],
-        out_specs=pl.BlockSpec((rows, HD), lambda h, f: (0, h)),
-        scratch_shapes=[
-            pltpu.VMEM((rows, 1), jnp.float32),
-            pltpu.VMEM((rows, 1), jnp.float32),
+        ]
+    )
+    args = [q, *pieces, q_pos.reshape(rows, 1), q_seg.reshape(rows, 1), k_pos, k_seg]
+    if carry is not None:
+        in_specs += [stat_spec, stat_spec, acc_spec]
+        args += list(carry)
+    stat_shape = jax.ShapeDtypeStruct((heads, rows, 1), jnp.float32)
+    acc_shape = jax.ShapeDtypeStruct((rows, width), jnp.float32)
+    if final:
+        out_specs = acc_spec
+        out_shape = jax.ShapeDtypeStruct((rows, width), jnp.bfloat16)
+        scratch = [
+            pltpu.VMEM((1, rows, 1), jnp.float32),
+            pltpu.VMEM((1, rows, 1), jnp.float32),
             pltpu.VMEM((rows, HD), jnp.float32),
-        ],
+        ]
+    else:
+        out_specs = [stat_spec, stat_spec, acc_spec]
+        out_shape = [stat_shape, stat_shape, acc_shape]
+        scratch = []
+    grid_spec = pltpu.PrefetchScalarGridSpec(
+        num_scalar_prefetch=1,
+        grid=(heads,),
+        in_specs=in_specs,
+        out_specs=out_specs,
+        scratch_shapes=scratch,
     )
     return pl.pallas_call(
-        functools.partial(_attention_body, scale, n_pieces, n_tiles),
+        functools.partial(_attention_body, scale, n_pieces, n_tiles, carry is not None, final),
         grid_spec=grid_spec,
-        out_shape=jax.ShapeDtypeStruct((rows, width), jnp.bfloat16),
+        out_shape=out_shape,
         cost_estimate=pl.CostEstimate(
-            flops=6 * rows * n * n_pieces * HD * heads,
+            flops=4 * rows * n * n_pieces * HD * heads,
             transcendentals=rows * n * n_pieces * heads,
             bytes_accessed=2 * (2 * rows * width + 2 * n_pieces * n * HD),
         ),
-    )(flags, q, *pieces, q_pos.reshape(rows, 1), q_seg.reshape(rows, 1), k_pos, k_seg)
+    )(flags, *args)
 
 
 def shards(segment_ids, relayout, queries, keys, values, out_weight):
@@ -133,7 +159,6 @@
         if k <= rows_back:
             perm += [(yy * n_core + cc, (yy + k) * n_core + cc) for yy in range(n_y - k)]
     fetched = lax.ppermute(row, ("y", "core"), perm=perm)
-    swapped = lax.ppermute(fetched, "core", perm=[(i, (i + 1) % n_core) for i in range(n_core)])
     y = lax.axis_index("y")
     span = n_x * rows
     piece_rows = [y - 1 - c, y - n_core + c, y]
@@ -143,7 +168,12 @@
     k_seg = jnp.stack([lax.dynamic_slice_in_dim(seg_pad, r * span + pad, span, 0) for r in piece_rows])
     q_pos = s * rows + jnp.arange(rows, dtype=jnp.int32)
     q_seg = lax.dynamic_slice_in_dim(segment_ids, s * rows, rows, 0)
-    attn_rows = attention(queries, [fetched, swapped, row], q_pos, q_seg, k_pos, k_seg, scale)
+    carry = attention(queries, [row], q_pos, q_seg, k_pos[2:], k_seg[2:], scale, final=False)
+    fetched, carry = lax.optimization_barrier((fetched, carry))
+    swapped = lax.ppermute(fetched, "core", perm=[(i, (i + 1) % n_core) for i in range(n_core)])
+    attn_rows = attention(
+        queries, [fetched, swapped], q_pos, q_seg, k_pos[:2], k_seg[:2], scale, carry=carry
+    )
 
     chunk = rows // n_seq
     total = relayout.shape[0]

time: 160 us -> 161 us (level)
  waiting for transfers between devices: 68.5 us -> 60.4 us
  Pallas kernels: 6 us -> 9.8 us
  other arithmetic: 12 us -> 15.3 us
    ppermute x1, waiting for transfers between devices: 8.97 us -> 0.01 us  [shards(): fetched = lax.ppermute(row, ('y', 'core'), perm=perm)]
    pallas_call x1 -> x2, Pallas kernels: 6 us -> 9.8 us  [attention(): pl.pallas_call(functools.partial(_attention_body, scale, n_pieces, n_tile...]
    convert_element_type x1 -> x2, other arithmetic: 2.05 us -> 4.8 us  [attention(): flags = ((kp_t[:, :, 0] <= q_pos[-1]) & (ks_t[:, :, -1] >= q_seg[0]) & (k...]
  transfers between devices with their start and end apart: 6 -> 6, of which waited for: 5 -> 4; matrix products, arithmetic and copies ran while one was open for 10% -> 12% of each run, Pallas kernels for 0% -> 4%
where the time goes in v11:
time: 161 us; the launch traced here: 160 us
  waiting for transfers between devices  60.4 us (38%)
  starting transfers between devices  44.1 us (27%)
  other arithmetic  15.3 us (10%)
  between operations  13.6 us (8%)
  Pallas kernels  9.8 us (6%)
  matrix products  9.22 us (6%)
  local copies, waits for them, and re-layouts  7.32 us (5%)
    reduce_scatter x1, waiting for transfers between devices, shards(): return lax.psum_scatter(half, 'z', scatter_dimension=0, tiled=True)  39.5 us
    all_to_all x1, starting transfers between devices, shards(): lax.all_to_all(to_send, ('y', 'x'), split_axis=0, concat_axis=0, tiled=True)  21.4 us
    all_to_all x1, starting transfers between devices, shards(): lax.all_to_all(pieces, ('x', 'z', 'core'), split_axis=0, concat_axis=0, t...  14 us
    all_to_all x1, waiting for transfers between devices, shards(): lax.all_to_all(pieces, ('x', 'z', 'core'), split_axis=0, concat_axis=0, t...  11.2 us
    pallas_call x2, Pallas kernels, attention(): pl.pallas_call(functools.partial(_attention_body, scale, n_pieces, n_tile...  9.8 us
    all_to_all x1, waiting for transfers between devices, shards(): lax.all_to_all(to_send, ('y', 'x'), split_axis=0, concat_axis=0, tiled=True)  8.45 us
    dot_general x2, matrix products, project(): jnp.dot(relaid, out_weight, preferred_element_type=jnp.float32)  7.47 us
    convert_element_type x2, other arithmetic, attention(): flags = ((kp_t[:, :, 0] <= q_pos[-1]) & (ks_t[:, :, -1] >= q_seg[0]) & (k...  4.8 us
  transfers between devices with their start and end apart: 6, of which 4 were waited for; matrix products, arithmetic and copies ran while one was open for 12% of the time, Pallas kernels for 4%

profile of v11, /device:TPU:6, one launch (start us, length us, event | category | flops | bytes accessed | tf_op | source)
XLA Modules:
  0.0 159.7 jit_solution(15776912140826726234)
XLA Ops:
  6.5 0.7 pad_clamp_fusion
  7.3 0.7 bitcast_bitcast_fusion
  8.0 1.4 gather_fusion
  9.4 14.0 %all-to-all-start = ((bf16[64,16,256]{2,1,0:T(8,128)(2,1)}), bf16[64,16,256]{2,1,0:T(8,128)(2,1)S(1)}, u32[]{:S(2)}, u32[]{:S(2)}) async-start(bf16[64,16,256]{2,1,0:T(8,128)(2,1)} %gather_fusion), calls=%async_computation | async-start | bytes 1048576 | tf_op jit(solution)/shard_map/all_to_all | solution.py:148
  23.4 0.7 slice.31
  24.1 0.8 dynamic_slice.18
  24.9 0.7 pad_dynamic-slice_fusion
  26.2 0.6 fusion.19
  26.8 2.1 %convert_reduce_fusion.2 = s32[2,4]{1,0:T(2,128)S(1)} fusion(s32[2,4,256]{2,1,0:T(4,128)S(1)} %get-tuple-element.38, s32[1,4,256]{2,1,0:T(4,128)S(1)} %get-tuple-element.39, s32[1,4,256]{2,1,0:T(4,128)S(1)} %fusion.15, s32[]{:T(128)} %bitcast.3, s32[]{:T(128)} %bitcast.2, s32[]{:T(128)} %bitcast.1), kind=kLoop, calls=%fused_computation.39 | loop fusion | flops 56 | bytes 8300 | tf_op jit(solution)/shard_map/convert_element_type | solution.py:77
  29.0 11.2 %all-to-all-done = bf16[64,16,256]{2,1,0:T(8,128)(2,1)S(1)} async-done(((bf16[64,16,256]{2,1,0:T(8,128)(2,1)}), bf16[64,16,256]{2,1,0:T(8,128)(2,1)S(1)}, u32[]{:S(2)}, u32[]{:S(2)}) %all-to-all-start) | async-done | bytes 524320 | tf_op jit(solution)/shard_map/all_to_all | solution.py:148
  40.1 3.5 %collective-permute-start = (bf16[1024,256]{1,0:T(8,128)(2,1)S(1)}, bf16[1024,256]{1,0:T(8,128)(2,1)S(1)}, u32[]{:S(2)}, u32[]{:S(2)}) collective-permute-start(bf16[1024,256]{1,0:T(8,128)(2,1)S(1)} %bitcast.36), channel_id=1, source_target_pairs={{0,64},{64,128},{128,192},{192,256},{256,320},{320,384},{384,448},... | collective-permute-start | bytes 1572872 | tf_op jit(solution)/shard_map/ppermute | solution.py:161
  43.6 0.8 and_select_fusion
  44.4 0.8 copy.17.refs_2_.refs_3_
  45.8 0.6 pad_add_fusion.1.refs_5_
  46.4 0.6 pad_add_fusion.refs_4_
  47.0 2.7 %convert_reduce_fusion.3.flags_ref = s32[4]{0:T(128)} fusion(s32[1,4,256]{2,1,0:T(4,128)S(1)} %reshape_stack.4, s32[1,4,256]{2,1,0:T(4,128)S(1)} %multiply_add_fusion, s32[]{:T(128)S(6)} %mul.30, s32[]{:T(128)} %bitcast.3, s32[]{:T(128)} %bitcast.2, s32[]{:T(128)} %bitcast.1), kind=kLoop, calls=%fused_computation.52 | loop fusion | flops 28 | bytes 80 | tf_op jit(solution)/shard_map/convert_element_type | solution.py:77
  49.7 0.7 iota_add_fusion.refs_1_.refs_2_
  50.3 6.5 %shard_map.82 = (f32[2,256,1]{2,1,0:T(8,128)}, f32[2,256,1]{2,1,0:T(8,128)}, f32[256,256]{1,0:T(8,128)}) custom-call(s32[4]{0:T(128)} %convert_reduce_fusion.3.flags_ref, bf16[256,256]{1,0:T(8,128)(2,1)} %q_ref.3, bf16[1024,256]{1,0:T(8,128)(2,1)} %bitcast.37, s32[256,1]{1,0:T(8,128)} %iota_add_fusion.refs_1_.refs_2_, s32[256,1]{1,0:T(8,128)} %copy.17.refs_2_.refs_3_, ...), custom_call_target="tpu_custom_call" | custom-call | flops 268435456 | bytes 786432 | tf_op jit(solution)/shard_map/pallas_call | solution.py:115
  56.8 3.3 %collective-permute-start.1 = (bf16[1024,256]{1,0:T(8,128)(2,1)S(1)}, bf16[1024,256]{1,0:T(8,128)(2,1)S(1)}, u32[]{:S(2)}, u32[]{:S(2)}) collective-permute-start(bf16[1024,256]{1,0:T(8,128)(2,1)S(1)} %collective-permute-done.refs_0_), channel_id=1, source_target_pairs={{0,1},{1,0},{2,3},{3,2},{4,5},{5,4},{6,7},{7,6},{8,9},{9,8},{10,11... | collective-permute-start | bytes 1572872 | tf_op jit(solution)/shard_map/ppermute | solution.py:173
  60.1 2.0 %select_reduce_fusion = s32[256]{0:T(256)S(1)} fusion(s32[8192]{0:T(1024)} %param.11, s32[256]{0:T(256)S(1)} %iota_add_fusion.4), kind=kLoop, calls=%fused_computation.3 | loop fusion | flops 6291200 | bytes 34816 | tf_op jit(solution)/shard_map/reduce_sum | solution.py:181
  62.5 0.8 copy-done.3
  63.3 3.3 %shard_map.83 = bf16[256,256]{1,0:T(8,128)(2,1)} custom-call(s32[8]{0:T(128)} %reshape.176.flags_ref, bf16[256,256]{1,0:T(8,128)(2,1)} %q_ref.3, bf16[1024,256]{1,0:T(8,128)(2,1)} %copy-done.2, bf16[1024,256]{1,0:T(8,128)(2,1)} %copy-done.3, s32[256,1]{1,0:T(8,128)} %iota_add_fusion.refs_1_.refs_2_, s32[256,1]{1,0:T(8,128)} %copy.17.refs_2_.refs_3_, ...), custom_call_target="tpu_custom_call" | custom-call | flops 536870912 | bytes 1310720 | tf_op jit(solution)/shard_map/pallas_call | solution.py:115
  66.6 1.8 %fusion = bf16[32,8,256]{2,1,0:T(8,128)(2,1)} fusion(bf16[256,256]{1,0:T(8,128)(2,1)} %shard_map.83, s32[256]{0:T(256)S(1)} %convert_reduce_fusion), kind=kOutput, calls=%fused_computation.6 | convolution fusion | flops 33685504 | bytes 263168 | tf_op jit(solution)/shard_map/dot_general | solution.py:187
  68.4 21.4 %all-to-all-start.1 = ((bf16[32,8,256]{2,1,0:T(8,128)(2,1)}), bf16[32,8,256]{2,1,0:T(8,128)(2,1)S(1)}, u32[]{:S(2)}, u32[]{:S(2)}) async-start(bf16[32,8,256]{2,1,0:T(8,128)(2,1)} %fusion), calls=%async_computation.1 | async-start | bytes 262144 | tf_op jit(solution)/shard_map/all_to_all | solution.py:188
  89.8 0.8 multiply_add_fusion.1
  90.8 8.4 %all-to-all-done.1 = bf16[32,8,256]{2,1,0:T(8,128)(2,1)S(1)} async-done(((bf16[32,8,256]{2,1,0:T(8,128)(2,1)}), bf16[32,8,256]{2,1,0:T(8,128)(2,1)S(1)}, u32[]{:S(2)}, u32[]{:S(2)}) %all-to-all-start.1) | async-done | bytes 131104 | tf_op jit(solution)/shard_map/all_to_all | solution.py:188
  99.2 4.4 %convolution_convert_fusion = bf16[128,8192]{1,0:T(8,128)(2,1)} fusion(bf16[256,8192]{1,0:T(8,128)(2,1)} %param.15, bf16[32,8,256]{2,1,0:T(8,128)(2,1)S(1)} %all-to-all-done.1, s32[128]{0:T(128)S(1)} %eq.79), kind=kOutput, calls=%fused_computation.1 | convolution fusion | flops 554762240 | bytes 6423040 | tf_op jit(solution)/shard_map/dot_general | solution.py:202
  103.6 1.9 %collective-permute-start.2 = (bf16[128,8192]{1,0:T(8,128)(2,1)}, bf16[128,8192]{1,0:T(8,128)(2,1)}, u32[]{:S(2)}, u32[]{:S(2)}) collective-permute-start(bf16[128,8192]{1,0:T(8,128)(2,1)} %convolution_convert_fusion), channel_id=1, source_target_pairs={{0,1},{1,0},{2,3},{3,2},{4,5},{5,4},{6,7},{7,6},{8,9},{9,8},{10,11... | collective-permute-start | bytes 6291464 | tf_op jit(solution)/shard_map/ppermute | solution.py:205
  105.6 3.1 %convolution_convert_fusion.1 = bf16[128,8192]{1,0:T(8,128)(2,1)S(1)} fusion(bf16[256,8192]{1,0:T(8,128)(2,1)} %param.15, bf16[32,8,256]{2,1,0:T(8,128)(2,1)S(1)} %all-to-all-done.1, s32[128]{0:T(128)S(1)} %eq.70), kind=kOutput, calls=%fused_computation.2 | convolution fusion | flops 554762240 | bytes 6423040 | tf_op jit(solution)/shard_map/dot_general | solution.py:202
  108.7 1.3 collective-permute-done.2
  110.0 3.4 %add_convert_fusion = bf16[128,8192]{1,0:T(8,128)(2,1)} fusion(bf16[128,8192]{1,0:T(8,128)(2,1)} %collective-permute-done.2, bf16[128,8192]{1,0:T(8,128)(2,1)S(1)} %convolution_convert_fusion.1), kind=kLoop, calls=%fused_computation.4 | loop fusion | flops 4194304 | bytes 6291456 | tf_op jit(solution)/shard_map/convert_element_type | solution.py:207
  113.4 39.5 %reduce-scatter.2.cloned.1.call-done = bf16[16,8192]{1,0:T(8,128)(2,1)} async-done(((bf16[128,8192]{1,0:T(8,128)(2,1)}), bf16[16,8192]{1,0:T(8,128)(2,1)}) %reduce-scatter.2.cloned.1.call-update) | async-done | bytes 262160 | tf_op jit(solution)/shard_map/reduce_scatter | solution.py:208
  (31 shorter events, 2.0 us)
Async XLA Ops:
  6.5 0.7 copy-start
  9.4 30.7 %all-to-all-start = ((bf16[64,16,256]{2,1,0:T(8,128)(2,1)}), bf16[64,16,256]{2,1,0:T(8,128)(2,1)S(1)}, u32[]{:S(2)}, u32[]{:S(2)}) async-start(bf16[64,16,256]{2,1,0:T(8,128)(2,1)} %gather_fusion), calls=%async_computation | async-start | bytes 1048576 | tf_op jit(solution)/shard_map/all_to_all | solution.py:148
  25.6 24.8 %copy-start.4 = (s32[1024]{0:T(1024)}, s32[1024]{0:T(1024)S(1)}, u32[]{:S(2)}) copy-start(s32[1024]{0:T(1024)S(1)} %get-tuple-element.31) | copy-start | bytes 12292
  40.1 10.2 %copy-start.1 = (bf16[64,16,256]{2,1,0:T(8,128)(2,1)}, bf16[64,16,256]{2,1,0:T(8,128)(2,1)S(1)}, u32[]{:S(2)}) copy-start(bf16[64,16,256]{2,1,0:T(8,128)(2,1)S(1)} %all-to-all-done) | copy-start | bytes 1572868
  40.1 16.7 %collective-permute-start = (bf16[1024,256]{1,0:T(8,128)(2,1)S(1)}, bf16[1024,256]{1,0:T(8,128)(2,1)S(1)}, u32[]{:S(2)}, u32[]{:S(2)}) collective-permute-start(bf16[1024,256]{1,0:T(8,128)(2,1)S(1)} %bitcast.36), channel_id=1, source_target_pairs={{0,64},{64,128},{128,192},{192,256},{256,320},{320,384},{384,448},... | collective-permute-start | bytes 1572872 | tf_op jit(solution)/shard_map/ppermute | solution.py:161
  56.8 5.7 %copy-start.2 = (bf16[1024,256]{1,0:T(8,128)(2,1)}, bf16[1024,256]{1,0:T(8,128)(2,1)S(1)}, u32[]{:S(2)}) copy-start(bf16[1024,256]{1,0:T(8,128)(2,1)S(1)} %collective-permute-done.refs_0_) | copy-start | bytes 1572868
  56.8 5.6 %collective-permute-start.1 = (bf16[1024,256]{1,0:T(8,128)(2,1)S(1)}, bf16[1024,256]{1,0:T(8,128)(2,1)S(1)}, u32[]{:S(2)}, u32[]{:S(2)}) collective-permute-start(bf16[1024,256]{1,0:T(8,128)(2,1)S(1)} %collective-permute-done.refs_0_), channel_id=1, source_target_pairs={{0,1},{1,0},{2,3},{3,2},{4,5},{5,4},{6,7},{7,6},{8,9},{9,8},{10,11... | collective-permute-start | bytes 1572872 | tf_op jit(solution)/shard_map/ppermute | solution.py:173
  62.5 0.8 copy-start.3
  68.4 30.9 %all-to-all-start.1 = ((bf16[32,8,256]{2,1,0:T(8,128)(2,1)}), bf16[32,8,256]{2,1,0:T(8,128)(2,1)S(1)}, u32[]{:S(2)}, u32[]{:S(2)}) async-start(bf16[32,8,256]{2,1,0:T(8,128)(2,1)} %fusion), calls=%async_computation.1 | async-start | bytes 262144 | tf_op jit(solution)/shard_map/all_to_all | solution.py:188
  89.7 63.1 %reduce-scatter.2.cloned.1.call-start = ((), (), s32[]{:S(2)}) async-start(), calls=%async_computation.3 | async-start | bytes 2359296 | tf_op jit(solution)/shard_map/reduce_scatter | solution.py:208
  103.6 6.4 %collective-permute-start.2 = (bf16[128,8192]{1,0:T(8,128)(2,1)}, bf16[128,8192]{1,0:T(8,128)(2,1)}, u32[]{:S(2)}, u32[]{:S(2)}) collective-permute-start(bf16[128,8192]{1,0:T(8,128)(2,1)} %convolution_convert_fusion), channel_id=1, source_target_pairs={{0,1},{1,0},{2,3},{3,2},{4,5},{5,4},{6,7},{7,6},{8,9},{9,8},{10,11... | collective-permute-start | bytes 6291464 | tf_op jit(solution)/shard_map/ppermute | solution.py:205
Sparse Core Ops, SparseCore 0:
  113.5 39.2 reduce-scatter.1

commit v12 on v8

--- a/solution.py
+++ b/solution.py
@@ -1,7 +1,10 @@
+import functools
+
 import jax
 import jax.numpy as jnp
 import numpy as np
 from jax import lax
+from jax.experimental import pallas as pl
 from jax.sharding import Mesh
 from jax.sharding import PartitionSpec as P
 
@@ -9,6 +12,81 @@
 KVH = 4
 HD = 128
 MOST_LEN = 2048
+
+
+def _attention_body(scale, n_pieces, heads, carry_in, final, q_ref, *refs):
+    kv_refs = refs[:n_pieces]
+    refs = refs[n_pieces:]
+    qp_ref, qs_ref, kp_ref, ks_ref = refs[:4]
+    refs = refs[4:]
+    if carry_in:
+        m_in, l_in, acc_in = refs[:3]
+        refs = refs[3:]
+    qp = qp_ref[...]
+    qs = qs_ref[...]
+    lives = [(kp_ref[pl.ds(p, 1), :] <= qp) & (ks_ref[pl.ds(p, 1), :] == qs) for p in range(n_pieces)]
+    for h in range(heads):
+        q = q_ref[:, pl.ds(h * HD, HD)]
+        scores = [
+            jnp.where(
+                lives[p],
+                lax.dot_general(
+                    q, kv_refs[p][:, pl.ds(0, HD)], (((1,), (1,)), ((), ())),
+                    preferred_element_type=jnp.float32,
+                ) * scale,
+                jnp.float32(-1e30),
+            )
+            for p in range(n_pieces)
+        ]
+        peak = functools.reduce(jnp.maximum, [jnp.max(s, axis=1, keepdims=True) for s in scores])
+        if carry_in:
+            peak = jnp.maximum(peak, m_in[h])
+        expos = [jnp.where(lives[p], jnp.exp(scores[p] - peak), jnp.float32(0.0)) for p in range(n_pieces)]
+        denom = functools.reduce(jnp.add, [jnp.sum(e, axis=1, keepdims=True) for e in expos])
+        summed = functools.reduce(
+            jnp.add,
+            [
+                jnp.dot(expos[p].astype(jnp.bfloat16), kv_refs[p][:, pl.ds(HD, HD)], preferred_element_type=jnp.float32)
+                for p in range(n_pieces)
+            ],
+        )
+        if carry_in:
+            alpha = jnp.exp(m_in[h] - peak)
+            denom = denom + alpha * l_in[h]
+            summed = summed + alpha * acc_in[:, pl.ds(h * HD, HD)]
+        if final:
+            refs[0][:, pl.ds(h * HD, HD)] = (summed / denom).astype(refs[0].dtype)
+        else:
+            refs[0][h] = peak
+            refs[1][h] = denom
+            refs[2][:, pl.ds(h * HD, HD)] = summed
+
+
+def attention(q, pieces, q_pos, q_seg, k_pos, k_seg, scale, carry=None, final=True):
+    rows, width = q.shape
+    heads = width // HD
+    n_pieces = len(pieces)
+    n = pieces[0].shape[0]
+    args = [q, *pieces, q_pos.reshape(rows, 1), q_seg.reshape(rows, 1), k_pos, k_seg]
+    if carry is not None:
+        args += list(carry)
+    if final:
+        out_shape = jax.ShapeDtypeStruct((rows, width), jnp.bfloat16)
+    else:
+        out_shape = [
+            jax.ShapeDtypeStruct((heads, rows, 1), jnp.float32),
+            jax.ShapeDtypeStruct((heads, rows, 1), jnp.float32),
+            jax.ShapeDtypeStruct((rows, width), jnp.float32),
+        ]
+    return pl.pallas_call(
+        functools.partial(_attention_body, scale, n_pieces, heads, carry is not None, final),
+        out_shape=out_shape,
+        cost_estimate=pl.CostEstimate(
+            flops=4 * rows * n * n_pieces * HD * heads,
+            transcendentals=rows * n * n_pieces * heads,
+            bytes_accessed=2 * (2 * rows * width + 2 * n_pieces * n * HD),
+        ),
+    )(*args)
 
 
 def shards(segment_ids, relayout, queries, keys, values, out_weight):
@@ -39,44 +117,28 @@
     x = lax.axis_index("x")
     c = lax.axis_index("core")
     rows_back = -(-back // n_x)
-    assert rows_back <= n_core
+    assert rows_back == n_core
     perm = []
     for cc in range(n_core):
         k = cc + 1
         if k <= rows_back:
             perm += [(yy * n_core + cc, (yy + k) * n_core + cc) for yy in range(n_y - k)]
     fetched = lax.ppermute(row, ("y", "core"), perm=perm)
+    y = lax.axis_index("y")
+    span = n_x * rows
+    piece_rows = [y - 1 - c, y - n_core + c, y]
+    k_pos = jnp.stack([r * span + jnp.arange(span, dtype=jnp.int32) for r in piece_rows])
+    pad = rows_back * span
+    seg_pad = jnp.concatenate([jnp.full((pad,), -1, jnp.int32), segment_ids])
+    k_seg = jnp.stack([lax.dynamic_slice_in_dim(seg_pad, r * span + pad, span, 0) for r in piece_rows])
+    q_pos = s * rows + jnp.arange(rows, dtype=jnp.int32)
+    q_seg = lax.dynamic_slice_in_dim(segment_ids, s * rows, rows, 0)
+    carry = attention(queries, [row], q_pos, q_seg, k_pos[2:], k_seg[2:], scale, final=False)
+    fetched, carry = lax.optimization_barrier((fetched, carry))
     swapped = lax.ppermute(fetched, "core", perm=[(i, (i + 1) % n_core) for i in range(n_core)])
-    earlier = [jnp.where(c == k - 1, fetched, swapped) for k in range(rows_back, 0, -1)]
-    kv_all = jnp.concatenate(earlier + [row], axis=0)
-    n_keys = (back + 1) * rows
-    first = (rows_back * n_x - back + x) * rows
-    kv_win = lax.dynamic_slice_in_dim(kv_all, first, n_keys, 0)
-    k_win = kv_win[:, :HD]
-    v_win = kv_win[:, HD:]
-
-    q_pos = s * rows + jnp.arange(rows, dtype=jnp.int32)
-    k_pos = (s - back) * rows + jnp.arange(n_keys, dtype=jnp.int32)
-    q_seg = lax.dynamic_slice_in_dim(segment_ids, s * rows, rows, 0)
-    seg_pad = jnp.concatenate([jnp.full((back * rows,), -1, jnp.int32), segment_ids])
-    k_seg = lax.dynamic_slice_in_dim(seg_pad, s * rows, n_keys, 0)
-    live = (
-        (k_pos[None, :] <= q_pos[:, None])
-        & (k_seg[None, :] == q_seg[:, None])
-        & (k_pos[None, :] >= 0)
+    attn_rows = attention(
+        queries, [fetched, swapped], q_pos, q_seg, k_pos[:2], k_seg[:2], scale, carry=carry
     )
-
-    q = queries.reshape(rows, heads_here, HD)
-    scores = jnp.einsum("qhd,kd->hqk", q, k_win, preferred_element_type=jnp.float32) * scale
-    masked = jnp.where(live[None], scores, jnp.float32(-1e30))
-    peak = jnp.max(masked, axis=-1)
-    expo = jnp.where(live[None], jnp.exp(masked - peak[..., None]), jnp.float32(0.0))
-    denom = jnp.sum(expo, axis=-1)
-    summed = jnp.einsum(
-        "hqk,kd->hqd", expo.astype(jnp.bfloat16), v_win, preferred_element_type=jnp.float32
-    )
-    attn = summed / denom[..., None]
-    attn_rows = jnp.transpose(attn, (1, 0, 2)).reshape(rows, heads_here * HD).astype(jnp.bfloat16)
 
     chunk = rows // n_seq
     total = relayout.shape[0]

time: 156 us -> 154 us (0.987)
  Pallas kernels: 0 us -> 8.22 us
  waiting for transfers between devices: 72.5 us -> 65.9 us
  matrix products: 12.8 us -> 9.22 us
  local copies, waits for them, and re-layouts: 3.14 us -> 6.02 us
  other arithmetic: 13.2 us -> 10.5 us
    pallas_call x0 -> x2, Pallas kernels: none -> 8.22 us  [attention(): pl.pallas_call(functools.partial(_attention_body, scale, n_pieces, heads,...]
    ppermute x1, waiting for transfers between devices: 10 us -> 2.89 us  [shards(): fetched = lax.ppermute(row, ('y', 'core'), perm=perm)]
    concatenate x1 -> x0, other arithmetic: 3.63 us -> none  [shards(): kv_all = jnp.concatenate(earlier + [row], axis=0)]
    dot_general x1 -> x0, matrix products: 2.29 us -> none  [shards(): jnp.einsum('hqk,kd->hqd', expo.astype(jnp.bfloat16), v_win, preferred_ele...]
    sub x1 -> x0, matrix products: 2.22 us -> none  [shards(): masked - peak[..., None]]
    and x1 -> x0, other arithmetic: 2.17 us -> none  [shards(): (k_pos[None, :] <= q_pos[:, None]) & (k_seg[None, :] == q_seg[:, None])]
    all_to_all x1, waiting for transfers between devices: 14.4 us -> 16.1 us  [shards(): lax.all_to_all(pieces, ('x', 'z', 'core'), split_axis=0, concat_axis=0, t...]
  transfers between devices with their start and end apart: 6 -> 6, of which waited for: 5 -> 5; matrix products, arithmetic and copies ran while one was open for 6% -> 8% of each run, Pallas kernels for 0% -> 2%
where the time goes in v12:
time: 154 us; the launch traced here: 153 us
  waiting for transfers between devices  65.9 us (43%)
  starting transfers between devices  39.6 us (26%)
  between operations  13.5 us (9%)
  other arithmetic  10.5 us (7%)
  matrix products  9.22 us (6%)
  Pallas kernels  8.22 us (5%)
  local copies, waits for them, and re-layouts  6.02 us (4%)
    reduce_scatter x1, waiting for transfers between devices, shards(): return lax.psum_scatter(half, 'z', scatter_dimension=0, tiled=True)  37.2 us
    all_to_all x1, starting transfers between devices, shards(): lax.all_to_all(to_send, ('y', 'x'), split_axis=0, concat_axis=0, tiled=True)  17.5 us
    all_to_all x1, waiting for transfers between devices, shards(): lax.all_to_all(pieces, ('x', 'z', 'core'), split_axis=0, concat_axis=0, t...  16.1 us
    all_to_all x1, starting transfers between devices, shards(): lax.all_to_all(pieces, ('x', 'z', 'core'), split_axis=0, concat_axis=0, t...  14 us
    all_to_all x1, waiting for transfers between devices, shards(): lax.all_to_all(to_send, ('y', 'x'), split_axis=0, concat_axis=0, tiled=True)  8.45 us
    pallas_call x2, Pallas kernels, attention(): pl.pallas_call(functools.partial(_attention_body, scale, n_pieces, heads,...  8.22 us
    dot_general x2, matrix products, project(): jnp.dot(relaid, out_weight, preferred_element_type=jnp.float32)  7.47 us
    ppermute x1, starting transfers between devices, shards(): fetched = lax.ppermute(row, ('y', 'core'), perm=perm)  3.5 us
  transfers between devices with their start and end apart: 6, of which 5 were waited for; matrix products, arithmetic and copies ran while one was open for 8% of the time, Pallas kernels for 2%

profile of v12, /device:TPU:6, one launch (start us, length us, event | category | flops | bytes accessed | tf_op | source)
XLA Modules:
  0.0 153.0 jit_solution(5046657710506829232)
XLA Ops:
  6.5 0.7 pad_clamp_fusion
  7.3 0.7 bitcast_bitcast_fusion
  8.0 1.4 gather_fusion
  9.4 14.0 %all-to-all-start = ((bf16[64,16,256]{2,1,0:T(8,128)(2,1)}), bf16[64,16,256]{2,1,0:T(8,128)(2,1)S(1)}, u32[]{:S(2)}, u32[]{:S(2)}) async-start(bf16[64,16,256]{2,1,0:T(8,128)(2,1)} %gather_fusion), calls=%async_computation | async-start | bytes 1048576 | tf_op jit(solution)/shard_map/all_to_all | solution.py:113
  23.4 0.6 iota_add_fusion.3.refs_3_
  24.0 16.1 %all-to-all-done = bf16[64,16,256]{2,1,0:T(8,128)(2,1)S(1)} async-done(((bf16[64,16,256]{2,1,0:T(8,128)(2,1)}), bf16[64,16,256]{2,1,0:T(8,128)(2,1)S(1)}, u32[]{:S(2)}, u32[]{:S(2)}) %all-to-all-start) | async-done | bytes 524320 | tf_op jit(solution)/shard_map/all_to_all | solution.py:113
  40.1 3.5 %collective-permute-start = (bf16[1024,256]{1,0:T(8,128)(2,1)S(1)}, bf16[1024,256]{1,0:T(8,128)(2,1)S(1)}, u32[]{:S(2)}, u32[]{:S(2)}) collective-permute-start(bf16[1024,256]{1,0:T(8,128)(2,1)S(1)} %bitcast.33), channel_id=1, source_target_pairs={{0,64},{64,128},{128,192},{192,256},{256,320},{320,384},{384,448},... | collective-permute-start | bytes 1572872 | tf_op jit(solution)/shard_map/ppermute | solution.py:126
  43.6 0.8 and_select_fusion
  44.4 0.8 dynamic_slice.16
  45.2 0.8 copy.17.refs_2_.refs_3_
  45.9 1.3 pad_dynamic-slice_fusion.1
  47.2 0.6 pad_add_fusion.1.refs_5_
  47.8 0.6 pad_add_fusion.refs_4_
  48.4 0.7 iota_add_fusion.refs_1_.refs_2_
  49.1 3.3 %shard_map.82 = (f32[2,256,1]{2,1,0:T(8,128)}, f32[2,256,1]{2,1,0:T(8,128)}, f32[256,256]{1,0:T(8,128)}) custom-call(bf16[256,256]{1,0:T(8,128)(2,1)} %q_ref.3, bf16[1024,256]{1,0:T(8,128)(2,1)} %bitcast.34, s32[256,1]{1,0:T(8,128)} %iota_add_fusion.refs_1_.refs_2_, s32[256,1]{1,0:T(8,128)} %copy.17.refs_2_.refs_3_, s32[1,1024]{1,0:T(1,128)} %iota_add_fusion.3.refs_3_, ...), custom_call_target="tpu_custom_call" | custom-call | flops 268435456 | bytes 786432 | tf_op jit(solution)/shard_map/pallas_call | solution.py:81
  52.4 2.9 %collective-permute-done.refs_0_ = bf16[1024,256]{1,0:T(8,128)(2,1)S(1)} collective-permute-done((bf16[1024,256]{1,0:T(8,128)(2,1)S(1)}, bf16[1024,256]{1,0:T(8,128)(2,1)S(1)}, u32[]{:S(2)}, u32[]{:S(2)}) %collective-permute-start) | collective-permute-done | bytes 524320 | tf_op jit(solution)/shard_map/ppermute | solution.py:126
  55.3 2.6 %collective-permute-start.1 = (bf16[1024,256]{1,0:T(8,128)(2,1)S(1)}, bf16[1024,256]{1,0:T(8,128)(2,1)S(1)}, u32[]{:S(2)}, u32[]{:S(2)}) collective-permute-start(bf16[1024,256]{1,0:T(8,128)(2,1)S(1)} %collective-permute-done.refs_0_), channel_id=1, source_target_pairs={{0,1},{1,0},{2,3},{3,2},{4,5},{5,4},{6,7},{7,6},{8,9},{9,8},{10,11... | collective-permute-start | bytes 1572872 | tf_op jit(solution)/shard_map/ppermute | solution.py:138
  57.9 2.0 %select_reduce_fusion = s32[256]{0:T(256)S(1)} fusion(s32[8192]{0:T(1024)} %param.11, s32[256]{0:T(256)S(1)} %iota_add_fusion.4), kind=kLoop, calls=%fused_computation.3 | loop fusion | flops 6291200 | bytes 34816 | tf_op jit(solution)/shard_map/reduce_sum | solution.py:146
  59.9 0.2 convert_reduce_fusion
  60.1 0.2 convert_reduce_fusion.1
  60.3 0.8 copy-done.3
  61.1 4.9 %shard_map.83 = bf16[256,256]{1,0:T(8,128)(2,1)} custom-call(bf16[256,256]{1,0:T(8,128)(2,1)} %q_ref.3, bf16[1024,256]{1,0:T(8,128)(2,1)} %copy-done.2, bf16[1024,256]{1,0:T(8,128)(2,1)} %copy-done.3, s32[256,1]{1,0:T(8,128)} %iota_add_fusion.refs_1_.refs_2_, s32[256,1]{1,0:T(8,128)} %copy.17.refs_2_.refs_3_, s32[2,1024]{1,0:T(2,128)} %pad_add_fusion.refs_4_, ...), custom_call_target="tpu_custom_call" | custom-call | flops 536870912 | bytes 1310720 | tf_op jit(solution)/shard_map/pallas_call | solution.py:81
  66.0 1.7 %fusion = bf16[32,8,256]{2,1,0:T(8,128)(2,1)} fusion(bf16[256,256]{1,0:T(8,128)(2,1)} %shard_map.83, s32[256]{0:T(256)S(1)} %convert_reduce_fusion), kind=kOutput, calls=%fused_computation.6 | convolution fusion | flops 33685504 | bytes 263168 | tf_op jit(solution)/shard_map/dot_general | solution.py:152
  67.8 17.5 %all-to-all-start.1 = ((bf16[32,8,256]{2,1,0:T(8,128)(2,1)}), bf16[32,8,256]{2,1,0:T(8,128)(2,1)S(1)}, u32[]{:S(2)}, u32[]{:S(2)}) async-start(bf16[32,8,256]{2,1,0:T(8,128)(2,1)} %fusion), calls=%async_computation.1 | async-start | bytes 262144 | tf_op jit(solution)/shard_map/all_to_all | solution.py:153
  85.3 0.8 multiply_add_fusion
  86.3 8.5 %all-to-all-done.1 = bf16[32,8,256]{2,1,0:T(8,128)(2,1)S(1)} async-done(((bf16[32,8,256]{2,1,0:T(8,128)(2,1)}), bf16[32,8,256]{2,1,0:T(8,128)(2,1)S(1)}, u32[]{:S(2)}, u32[]{:S(2)}) %all-to-all-start.1) | async-done | bytes 131104 | tf_op jit(solution)/shard_map/all_to_all | solution.py:153
  94.8 4.4 %convolution_convert_fusion = bf16[128,8192]{1,0:T(8,128)(2,1)} fusion(bf16[256,8192]{1,0:T(8,128)(2,1)} %param.15, bf16[32,8,256]{2,1,0:T(8,128)(2,1)S(1)} %all-to-all-done.1, s32[128]{0:T(128)S(1)} %eq.79), kind=kOutput, calls=%fused_computation.1 | convolution fusion | flops 554762240 | bytes 6423040 | tf_op jit(solution)/shard_map/dot_general | solution.py:167
  99.1 1.9 %collective-permute-start.2 = (bf16[128,8192]{1,0:T(8,128)(2,1)}, bf16[128,8192]{1,0:T(8,128)(2,1)}, u32[]{:S(2)}, u32[]{:S(2)}) collective-permute-start(bf16[128,8192]{1,0:T(8,128)(2,1)} %convolution_convert_fusion), channel_id=1, source_target_pairs={{0,1},{1,0},{2,3},{3,2},{4,5},{5,4},{6,7},{7,6},{8,9},{9,8},{10,11... | collective-permute-start | bytes 6291464 | tf_op jit(solution)/shard_map/ppermute | solution.py:170
  101.1 3.1 %convolution_convert_fusion.1 = bf16[128,8192]{1,0:T(8,128)(2,1)S(1)} fusion(bf16[256,8192]{1,0:T(8,128)(2,1)} %param.15, bf16[32,8,256]{2,1,0:T(8,128)(2,1)S(1)} %all-to-all-done.1, s32[128]{0:T(128)S(1)} %eq.70), kind=kOutput, calls=%fused_computation.2 | convolution fusion | flops 554762240 | bytes 6423040 | tf_op jit(solution)/shard_map/dot_general | solution.py:167
  104.2 1.3 collective-permute-done.2
  105.5 3.4 %add_convert_fusion = bf16[128,8192]{1,0:T(8,128)(2,1)} fusion(bf16[128,8192]{1,0:T(8,128)(2,1)} %collective-permute-done.2, bf16[128,8192]{1,0:T(8,128)(2,1)S(1)} %convolution_convert_fusion.1), kind=kLoop, calls=%fused_computation.4 | loop fusion | flops 4194304 | bytes 6291456 | tf_op jit(solution)/shard_map/convert_element_type | solution.py:172
  108.9 37.2 %reduce-scatter.2.cloned.1.call-done = bf16[16,8192]{1,0:T(8,128)(2,1)} async-done(((bf16[128,8192]{1,0:T(8,128)(2,1)}), bf16[16,8192]{1,0:T(8,128)(2,1)}) %reduce-scatter.2.cloned.1.call-update) | async-done | bytes 262160 | tf_op jit(solution)/shard_map/reduce_scatter | solution.py:173
  (17 shorter events, 0.4 us)
Async XLA Ops:
  6.5 0.7 copy-start
  9.4 30.7 %all-to-all-start = ((bf16[64,16,256]{2,1,0:T(8,128)(2,1)}), bf16[64,16,256]{2,1,0:T(8,128)(2,1)S(1)}, u32[]{:S(2)}, u32[]{:S(2)}) async-start(bf16[64,16,256]{2,1,0:T(8,128)(2,1)} %gather_fusion), calls=%async_computation | async-start | bytes 1048576 | tf_op jit(solution)/shard_map/all_to_all | solution.py:113
  40.1 9.0 %copy-start.1 = (bf16[64,16,256]{2,1,0:T(8,128)(2,1)}, bf16[64,16,256]{2,1,0:T(8,128)(2,1)S(1)}, u32[]{:S(2)}) copy-start(bf16[64,16,256]{2,1,0:T(8,128)(2,1)S(1)} %all-to-all-done) | copy-start | bytes 1572868
  40.1 15.2 %collective-permute-start = (bf16[1024,256]{1,0:T(8,128)(2,1)S(1)}, bf16[1024,256]{1,0:T(8,128)(2,1)S(1)}, u32[]{:S(2)}, u32[]{:S(2)}) collective-permute-start(bf16[1024,256]{1,0:T(8,128)(2,1)S(1)} %bitcast.33), channel_id=1, source_target_pairs={{0,64},{64,128},{128,192},{192,256},{256,320},{320,384},{384,448},... | collective-permute-start | bytes 1572872 | tf_op jit(solution)/shard_map/ppermute | solution.py:126
  55.3 5.0 %copy-start.2 = (bf16[1024,256]{1,0:T(8,128)(2,1)}, bf16[1024,256]{1,0:T(8,128)(2,1)S(1)}, u32[]{:S(2)}) copy-start(bf16[1024,256]{1,0:T(8,128)(2,1)S(1)} %collective-permute-done.refs_0_) | copy-start | bytes 1572868
  55.3 5.0 %collective-permute-start.1 = (bf16[1024,256]{1,0:T(8,128)(2,1)S(1)}, bf16[1024,256]{1,0:T(8,128)(2,1)S(1)}, u32[]{:S(2)}, u32[]{:S(2)}) collective-permute-start(bf16[1024,256]{1,0:T(8,128)(2,1)S(1)} %collective-permute-done.refs_0_), channel_id=1, source_target_pairs={{0,1},{1,0},{2,3},{3,2},{4,5},{5,4},{6,7},{7,6},{8,9},{9,8},{10,11... | collective-permute-start | bytes 1572872 | tf_op jit(solution)/shard_map/ppermute | solution.py:138
  60.3 0.8 copy-start.3
  67.8 27.0 %all-to-all-start.1 = ((bf16[32,8,256]{2,1,0:T(8,128)(2,1)}), bf16[32,8,256]{2,1,0:T(8,128)(2,1)S(1)}, u32[]{:S(2)}, u32[]{:S(2)}) async-start(bf16[32,8,256]{2,1,0:T(8,128)(2,1)} %fusion), calls=%async_computation.1 | async-start | bytes 262144 | tf_op jit(solution)/shard_map/all_to_all | solution.py:153
  85.3 60.9 %reduce-scatter.2.cloned.1.call-start = ((), (), s32[]{:S(2)}) async-start(), calls=%async_computation.3 | async-start | bytes 2359296 | tf_op jit(solution)/shard_map/reduce_scatter | solution.py:173
  99.1 6.4 %collective-permute-start.2 = (bf16[128,8192]{1,0:T(8,128)(2,1)}, bf16[128,8192]{1,0:T(8,128)(2,1)}, u32[]{:S(2)}, u32[]{:S(2)}) collective-permute-start(bf16[128,8192]{1,0:T(8,128)(2,1)} %convolution_convert_fusion), channel_id=1, source_target_pairs={{0,1},{1,0},{2,3},{3,2},{4,5},{5,4},{6,7},{7,6},{8,9},{9,8},{10,11... | collective-permute-start | bytes 6291464 | tf_op jit(solution)/shard_map/ppermute | solution.py:170
Sparse Core Ops, SparseCore 0:
  109.1 37.0 reduce-scatter.1

commit v13 on v12

--- a/solution.py
+++ b/solution.py
@@ -133,13 +133,6 @@
     k_seg = jnp.stack([lax.dynamic_slice_in_dim(seg_pad, r * span + pad, span, 0) for r in piece_rows])
     q_pos = s * rows + jnp.arange(rows, dtype=jnp.int32)
     q_seg = lax.dynamic_slice_in_dim(segment_ids, s * rows, rows, 0)
-    carry = attention(queries, [row], q_pos, q_seg, k_pos[2:], k_seg[2:], scale, final=False)
-    fetched, carry = lax.optimization_barrier((fetched, carry))
-    swapped = lax.ppermute(fetched, "core", perm=[(i, (i + 1) % n_core) for i in range(n_core)])
-    attn_rows = attention(
-        queries, [fetched, swapped], q_pos, q_seg, k_pos[:2], k_seg[:2], scale, carry=carry
-    )
-
     chunk = rows // n_seq
     total = relayout.shape[0]
     here = s * rows + jnp.arange(rows, dtype=jnp.int32)
@@ -148,8 +141,17 @@
         axis=1,
     )
     rank = jnp.sum((new_of[None, :] < new_of[:, None]).astype(jnp.int32), axis=1)
-    send_sel = (rank[None, :] == jnp.arange(rows, dtype=jnp.int32)[:, None]).astype(jnp.bfloat16)
-    to_send = jnp.dot(send_sel, attn_rows, preferred_element_type=jnp.float32).astype(jnp.bfloat16)
+    send_hit = rank[None, :] == jnp.arange(rows, dtype=jnp.int32)[:, None]
+    q_sent = jnp.dot(send_hit.astype(jnp.bfloat16), queries, preferred_element_type=jnp.float32).astype(jnp.bfloat16)
+    q_pos = jnp.sum(jnp.where(send_hit, here[None, :], 0), axis=1)
+    q_seg = jnp.sum(jnp.where(send_hit, q_seg[None, :], 0), axis=1)
+    carry = attention(q_sent, [row], q_pos, q_seg, k_pos[2:], k_seg[2:], scale, final=False)
+    fetched, carry = lax.optimization_barrier((fetched, carry))
+    swapped = lax.ppermute(fetched, "core", perm=[(i, (i + 1) % n_core) for i in range(n_core)])
+    to_send = attention(
+        q_sent, [fetched, swapped], q_pos, q_seg, k_pos[:2], k_seg[:2], scale, carry=carry
+    )
+
     arrived = lax.all_to_all(to_send, ("y", "x"), split_axis=0, concat_axis=0, tiled=True)
 
     src = lax.dynamic_slice_in_dim(relayout, s * rows, rows, 0) // rows

time: 154 us -> 152 us (0.987)
    all_to_all x1, waiting for transfers between devices: 16.1 us -> 13.8 us  [shards(): lax.all_to_all(pieces, ('x', 'z', 'core'), split_axis=0, concat_axis=0, t...]
  transfers between devices with their start and end apart: 6 -> 6, of which waited for: 5 -> 5; matrix products, arithmetic and copies ran while one was open for 8% -> 9% of each run, Pallas kernels for 2% -> 2%
where the time goes in v13:
time: 152 us; the launch traced here: 151 us
  waiting for transfers between devices  64.6 us (42%)
  starting transfers between devices  39.6 us (26%)
  between operations  13.6 us (9%)
  other arithmetic  9.99 us (7%)
  matrix products  8.31 us (5%)
  Pallas kernels  8.22 us (5%)
  local copies, waits for them, and re-layouts  6.81 us (4%)
    reduce_scatter x1, waiting for transfers between devices, shards(): return lax.psum_scatter(half, 'z', scatter_dimension=0, tiled=True)  37.2 us
    all_to_all x1, starting transfers between devices, shards(): lax.all_to_all(to_send, ('y', 'x'), split_axis=0, concat_axis=0, tiled=True)  17.5 us
    all_to_all x1, starting transfers between devices, shards(): lax.all_to_all(pieces, ('x', 'z', 'core'), split_axis=0, concat_axis=0, t...  14 us
    all_to_all x1, waiting for transfers between devices, shards(): lax.all_to_all(pieces, ('x', 'z', 'core'), split_axis=0, concat_axis=0, t...  13.8 us
    all_to_all x1, waiting for transfers between devices, shards(): lax.all_to_all(to_send, ('y', 'x'), split_axis=0, concat_axis=0, tiled=True)  8.45 us
    pallas_call x2, Pallas kernels, attention(): pl.pallas_call(functools.partial(_attention_body, scale, n_pieces, heads,...  8.22 us
    dot_general x2, matrix products, project(): jnp.dot(relaid, out_weight, preferred_element_type=jnp.float32)  7.47 us
    ppermute x1, waiting for transfers between devices, shards(): fetched = lax.ppermute(row, ('y', 'core'), perm=perm)  3.82 us
  transfers between devices with their start and end apart: 6, of which 5 were waited for; matrix products, arithmetic and copies ran while one was open for 9% of the time, Pallas kernels for 2%

profile of v13, /device:TPU:6, one launch (start us, length us, event | category | flops | bytes accessed | tf_op | source)
XLA Modules:
  0.0 151.1 jit_solution(12632863673535918462)
XLA Ops:
  6.5 0.7 pad_clamp_fusion
  7.2 0.7 bitcast_bitcast_fusion
  8.0 1.4 gather_fusion
  9.4 14.0 %all-to-all-start = ((bf16[64,16,256]{2,1,0:T(8,128)(2,1)}), bf16[64,16,256]{2,1,0:T(8,128)(2,1)S(1)}, u32[]{:S(2)}, u32[]{:S(2)}) async-start(bf16[64,16,256]{2,1,0:T(8,128)(2,1)} %gather_fusion), calls=%async_computation | async-start | bytes 1048576 | tf_op jit(solution)/shard_map/all_to_all | solution.py:113
  23.4 0.8 dynamic_slice.16
  24.2 2.0 %select_reduce_fusion = s32[256]{0:T(256)S(1)} fusion(s32[8192]{0:T(1024)} %param.11, s32[256]{0:T(256)S(1)} %iota_add_fusion.3), kind=kLoop, calls=%fused_computation.3 | loop fusion | flops 6291200 | bytes 34816 | tf_op jit(solution)/shard_map/reduce_sum | solution.py:139
  26.2 0.2 convert_reduce_fusion
  26.4 13.8 %all-to-all-done = bf16[64,16,256]{2,1,0:T(8,128)(2,1)S(1)} async-done(((bf16[64,16,256]{2,1,0:T(8,128)(2,1)}), bf16[64,16,256]{2,1,0:T(8,128)(2,1)S(1)}, u32[]{:S(2)}, u32[]{:S(2)}) %all-to-all-start) | async-done | bytes 524320 | tf_op jit(solution)/shard_map/all_to_all | solution.py:113
  40.1 3.5 %collective-permute-start = (bf16[1024,256]{1,0:T(8,128)(2,1)S(1)}, bf16[1024,256]{1,0:T(8,128)(2,1)S(1)}, u32[]{:S(2)}, u32[]{:S(2)}) collective-permute-start(bf16[1024,256]{1,0:T(8,128)(2,1)S(1)} %bitcast.34), channel_id=1, source_target_pairs={{0,64},{64,128},{128,192},{192,256},{256,320},{320,384},{384,448},... | collective-permute-start | bytes 1572872 | tf_op jit(solution)/shard_map/ppermute | solution.py:126
  43.8 0.8 copy.21.refs_1_.refs_2_
  44.6 0.8 copy.22.refs_2_.refs_3_
  45.4 0.6 iota_add_fusion.2.refs_3_
  46.0 1.3 pad_dynamic-slice_fusion.1
  47.3 0.8 convolution_convert_fusion.2.q_ref
  48.1 3.3 %shard_map.82 = (f32[2,256,1]{2,1,0:T(8,128)}, f32[2,256,1]{2,1,0:T(8,128)}, f32[256,256]{1,0:T(8,128)}) custom-call(bf16[256,256]{1,0:T(8,128)(2,1)} %convolution_convert_fusion.2.q_ref, bf16[1024,256]{1,0:T(8,128)(2,1)} %bitcast.35, s32[256,1]{1,0:T(8,128)} %copy.21.refs_1_.refs_2_, s32[256,1]{1,0:T(8,128)} %copy.22.refs_2_.refs_3_, ...), custom_call_target="tpu_custom_call" | custom-call | flops 268435456 | bytes 786432 | tf_op jit(solution)/shard_map/pallas_call | solution.py:81
  51.5 3.8 %collective-permute-done.refs_0_ = bf16[1024,256]{1,0:T(8,128)(2,1)S(1)} collective-permute-done((bf16[1024,256]{1,0:T(8,128)(2,1)S(1)}, bf16[1024,256]{1,0:T(8,128)(2,1)S(1)}, u32[]{:S(2)}, u32[]{:S(2)}) %collective-permute-start) | collective-permute-done | bytes 524320 | tf_op jit(solution)/shard_map/ppermute | solution.py:126
  55.3 2.6 %collective-permute-start.1 = (bf16[1024,256]{1,0:T(8,128)(2,1)S(1)}, bf16[1024,256]{1,0:T(8,128)(2,1)S(1)}, u32[]{:S(2)}, u32[]{:S(2)}) collective-permute-start(bf16[1024,256]{1,0:T(8,128)(2,1)S(1)} %collective-permute-done.refs_0_), channel_id=1, source_target_pairs={{0,1},{1,0},{2,3},{3,2},{4,5},{5,4},{6,7},{7,6},{8,9},{9,8},{10,11... | collective-permute-start | bytes 1572872 | tf_op jit(solution)/shard_map/ppermute | solution.py:150
  57.9 0.8 and_select_fusion
  58.7 0.6 pad_add_fusion.1.refs_5_
  59.3 0.6 pad_add_fusion.refs_4_
  59.9 0.2 convert_reduce_fusion.1
  60.1 0.8 copy-done.3
  60.9 4.9 %shard_map.83 = bf16[256,256]{1,0:T(8,128)(2,1)} custom-call(bf16[256,256]{1,0:T(8,128)(2,1)} %convolution_convert_fusion.2.q_ref, bf16[1024,256]{1,0:T(8,128)(2,1)} %copy-done.2, bf16[1024,256]{1,0:T(8,128)(2,1)} %copy-done.3, s32[256,1]{1,0:T(8,128)} %copy.21.refs_1_.refs_2_, s32[256,1]{1,0:T(8,128)} %copy.22.refs_2_.refs_3_, ...), custom_call_target="tpu_custom_call" | custom-call | flops 536870912 | bytes 1310720 | tf_op jit(solution)/shard_map/pallas_call | solution.py:81
  65.8 17.5 %all-to-all-start.1 = ((bf16[32,8,256]{2,1,0:T(8,128)(2,1)}), bf16[32,8,256]{2,1,0:T(8,128)(2,1)S(1)}, u32[]{:S(2)}, u32[]{:S(2)}) async-start(bf16[32,8,256]{2,1,0:T(8,128)(2,1)} %bitcast.33), calls=%async_computation.1 | async-start | bytes 262144 | tf_op jit(solution)/shard_map/all_to_all | solution.py:155
  83.4 0.8 multiply_add_fusion
  84.3 8.4 %all-to-all-done.1 = bf16[32,8,256]{2,1,0:T(8,128)(2,1)S(1)} async-done(((bf16[32,8,256]{2,1,0:T(8,128)(2,1)}), bf16[32,8,256]{2,1,0:T(8,128)(2,1)S(1)}, u32[]{:S(2)}, u32[]{:S(2)}) %all-to-all-start.1) | async-done | bytes 131104 | tf_op jit(solution)/shard_map/all_to_all | solution.py:155
  92.8 4.4 %convolution_convert_fusion = bf16[128,8192]{1,0:T(8,128)(2,1)} fusion(bf16[256,8192]{1,0:T(8,128)(2,1)} %param.15, bf16[32,8,256]{2,1,0:T(8,128)(2,1)S(1)} %all-to-all-done.1, s32[128]{0:T(128)S(1)} %eq.79), kind=kOutput, calls=%fused_computation.1 | convolution fusion | flops 554762240 | bytes 6423040 | tf_op jit(solution)/shard_map/dot_general | solution.py:169
  97.2 1.9 %collective-permute-start.2 = (bf16[128,8192]{1,0:T(8,128)(2,1)}, bf16[128,8192]{1,0:T(8,128)(2,1)}, u32[]{:S(2)}, u32[]{:S(2)}) collective-permute-start(bf16[128,8192]{1,0:T(8,128)(2,1)} %convolution_convert_fusion), channel_id=1, source_target_pairs={{0,1},{1,0},{2,3},{3,2},{4,5},{5,4},{6,7},{7,6},{8,9},{9,8},{10,11... | collective-permute-start | bytes 6291464 | tf_op jit(solution)/shard_map/ppermute | solution.py:172
  99.2 3.1 %convolution_convert_fusion.1 = bf16[128,8192]{1,0:T(8,128)(2,1)S(1)} fusion(bf16[256,8192]{1,0:T(8,128)(2,1)} %param.15, bf16[32,8,256]{2,1,0:T(8,128)(2,1)S(1)} %all-to-all-done.1, s32[128]{0:T(128)S(1)} %eq.70), kind=kOutput, calls=%fused_computation.2 | convolution fusion | flops 554762240 | bytes 6423040 | tf_op jit(solution)/shard_map/dot_general | solution.py:169
  102.3 1.3 collective-permute-done.2
  103.6 3.4 %add_convert_fusion = bf16[128,8192]{1,0:T(8,128)(2,1)} fusion(bf16[128,8192]{1,0:T(8,128)(2,1)} %collective-permute-done.2, bf16[128,8192]{1,0:T(8,128)(2,1)S(1)} %convolution_convert_fusion.1), kind=kLoop, calls=%fused_computation.4 | loop fusion | flops 4194304 | bytes 6291456 | tf_op jit(solution)/shard_map/convert_element_type | solution.py:174
  107.0 37.2 %reduce-scatter.2.cloned.1.call-done = bf16[16,8192]{1,0:T(8,128)(2,1)} async-done(((bf16[128,8192]{1,0:T(8,128)(2,1)}), bf16[16,8192]{1,0:T(8,128)(2,1)}) %reduce-scatter.2.cloned.1.call-update) | async-done | bytes 262160 | tf_op jit(solution)/shard_map/reduce_scatter | solution.py:175
  (18 shorter events, 0.5 us)
Async XLA Ops:
  6.5 40.8 %copy-start = (bf16[256,256]{1,0:T(8,128)(2,1)S(1)}, bf16[256,256]{1,0:T(8,128)(2,1)}, u32[]{:S(2)}) copy-start(bf16[256,256]{1,0:T(8,128)(2,1)} %param.12) | copy-start | bytes 393220
  9.4 30.7 %all-to-all-start = ((bf16[64,16,256]{2,1,0:T(8,128)(2,1)}), bf16[64,16,256]{2,1,0:T(8,128)(2,1)S(1)}, u32[]{:S(2)}, u32[]{:S(2)}) async-start(bf16[64,16,256]{2,1,0:T(8,128)(2,1)} %gather_fusion), calls=%async_computation | async-start | bytes 1048576 | tf_op jit(solution)/shard_map/all_to_all | solution.py:113
  40.1 8.0 %copy-start.1 = (bf16[64,16,256]{2,1,0:T(8,128)(2,1)}, bf16[64,16,256]{2,1,0:T(8,128)(2,1)S(1)}, u32[]{:S(2)}) copy-start(bf16[64,16,256]{2,1,0:T(8,128)(2,1)S(1)} %all-to-all-done) | copy-start | bytes 1572868
  40.1 15.2 %collective-permute-start = (bf16[1024,256]{1,0:T(8,128)(2,1)S(1)}, bf16[1024,256]{1,0:T(8,128)(2,1)S(1)}, u32[]{:S(2)}, u32[]{:S(2)}) collective-permute-start(bf16[1024,256]{1,0:T(8,128)(2,1)S(1)} %bitcast.34), channel_id=1, source_target_pairs={{0,64},{64,128},{128,192},{192,256},{256,320},{320,384},{384,448},... | collective-permute-start | bytes 1572872 | tf_op jit(solution)/shard_map/ppermute | solution.py:126
  55.3 4.8 %copy-start.2 = (bf16[1024,256]{1,0:T(8,128)(2,1)}, bf16[1024,256]{1,0:T(8,128)(2,1)S(1)}, u32[]{:S(2)}) copy-start(bf16[1024,256]{1,0:T(8,128)(2,1)S(1)} %collective-permute-done.refs_0_) | copy-start | bytes 1572868
  55.3 4.8 %collective-permute-start.1 = (bf16[1024,256]{1,0:T(8,128)(2,1)S(1)}, bf16[1024,256]{1,0:T(8,128)(2,1)S(1)}, u32[]{:S(2)}, u32[]{:S(2)}) collective-permute-start(bf16[1024,256]{1,0:T(8,128)(2,1)S(1)} %collective-permute-done.refs_0_), channel_id=1, source_target_pairs={{0,1},{1,0},{2,3},{3,2},{4,5},{5,4},{6,7},{7,6},{8,9},{9,8},{10,11... | collective-permute-start | bytes 1572872 | tf_op jit(solution)/shard_map/ppermute | solution.py:150
  60.1 0.8 copy-start.3
  65.8 27.0 %all-to-all-start.1 = ((bf16[32,8,256]{2,1,0:T(8,128)(2,1)}), bf16[32,8,256]{2,1,0:T(8,128)(2,1)S(1)}, u32[]{:S(2)}, u32[]{:S(2)}) async-start(bf16[32,8,256]{2,1,0:T(8,128)(2,1)} %bitcast.33), calls=%async_computation.1 | async-start | bytes 262144 | tf_op jit(solution)/shard_map/all_to_all | solution.py:155
  83.3 60.9 %reduce-scatter.2.cloned.1.call-start = ((), (), s32[]{:S(2)}) async-start(), calls=%async_computation.3 | async-start | bytes 2359296 | tf_op jit(solution)/shard_map/reduce_scatter | solution.py:175
  97.2 6.4 %collective-permute-start.2 = (bf16[128,8192]{1,0:T(8,128)(2,1)}, bf16[128,8192]{1,0:T(8,128)(2,1)}, u32[]{:S(2)}, u32[]{:S(2)}) collective-permute-start(bf16[128,8192]{1,0:T(8,128)(2,1)} %convolution_convert_fusion), channel_id=1, source_target_pairs={{0,1},{1,0},{2,3},{3,2},{4,5},{5,4},{6,7},{7,6},{8,9},{9,8},{10,11... | collective-permute-start | bytes 6291464 | tf_op jit(solution)/shard_map/ppermute | solution.py:172
Sparse Core Ops, SparseCore 0:
  107.1 37.0 reduce-scatter.1

commit v14 on v13

--- a/solution.py
+++ b/solution.py
@@ -152,7 +152,12 @@
         q_sent, [fetched, swapped], q_pos, q_seg, k_pos[:2], k_seg[:2], scale, carry=carry
     )
 
-    arrived = lax.all_to_all(to_send, ("y", "x"), split_axis=0, concat_axis=0, tiled=True)
+    width = to_send.shape[1]
+    by_dest = jnp.transpose(to_send.reshape(n_y, n_x, chunk, width), (1, 0, 2, 3))
+    over_x = lax.all_to_all(by_dest, "x", split_axis=0, concat_axis=0, tiled=True)
+    over_x = jnp.transpose(over_x, (1, 0, 2, 3))
+    arrived = lax.all_to_all(over_x, "y", split_axis=0, concat_axis=0, tiled=True)
+    arrived = arrived.reshape(rows, width)
 
     src = lax.dynamic_slice_in_dim(relayout, s * rows, rows, 0) // rows
     before = jnp.arange(rows)[None, :] < jnp.arange(rows)[:, None]

time: 152 us -> 160 us (1.053)
  waiting for transfers between devices: 64.6 us -> 68.8 us
  local copies, waits for them, and re-layouts: 6.81 us -> 9.05 us
  starting transfers between devices: 39.6 us -> 41.3 us
    all_to_all x1 -> x2, waiting for transfers between devices: 8.45 us -> 11.8 us  [the longest x1 8.05 us: shards(): lax.all_to_all(over_x, 'y', split_axis=0, concat_axis=0, tiled=True)]
    all_to_all x1 -> x2, starting transfers between devices: 17.5 us -> 19.2 us  [the longest x1 14.5 us: shards(): lax.all_to_all(over_x, 'y', split_axis=0, concat_axis=0, tiled=True)]
  transfers between devices with their start and end apart: 6 -> 7, of which waited for: 5 -> 6; matrix products, arithmetic and copies ran while one was open for 9% -> 9% of each run, Pallas kernels for 2% -> 2%
where the time goes in v14:
time: 160 us; the launch traced here: 159 us
  waiting for transfers between devices  68.8 us (43%)
  starting transfers between devices  41.3 us (26%)
  between operations  13.5 us (8%)
  other arithmetic  9.97 us (6%)
  local copies, waits for them, and re-layouts  9.05 us (6%)
  matrix products  8.32 us (5%)
  Pallas kernels  8.24 us (5%)
    reduce_scatter x1, waiting for transfers between devices, shards(): return lax.psum_scatter(half, 'z', scatter_dimension=0, tiled=True)  38.1 us
    all_to_all x1, starting transfers between devices, shards(): lax.all_to_all(over_x, 'y', split_axis=0, concat_axis=0, tiled=True)  14.5 us
    all_to_all x1, starting transfers between devices, shards(): lax.all_to_all(pieces, ('x', 'z', 'core'), split_axis=0, concat_axis=0, t...  14 us
    all_to_all x1, waiting for transfers between devices, shards(): lax.all_to_all(pieces, ('x', 'z', 'core'), split_axis=0, concat_axis=0, t...  13.8 us
    pallas_call x2, Pallas kernels, attention(): pl.pallas_call(functools.partial(_attention_body, scale, n_pieces, heads,...  8.24 us
    all_to_all x1, waiting for transfers between devices, shards(): lax.all_to_all(over_x, 'y', split_axis=0, concat_axis=0, tiled=True)  8.05 us
    dot_general x2, matrix products, project(): jnp.dot(relaid, out_weight, preferred_element_type=jnp.float32)  7.47 us
    all_to_all x1, starting transfers between devices, shards(): lax.all_to_all(by_dest, 'x', split_axis=0, concat_axis=0, tiled=True)  4.69 us
  transfers between devices with their start and end apart: 7, of which 6 were waited for; matrix products, arithmetic and copies ran while one was open for 9% of the time, Pallas kernels for 2%

profile of v14, /device:TPU:6, one launch (start us, length us, event | category | flops | bytes accessed | tf_op | source)
XLA Modules:
  0.0 159.2 jit_solution(780658604807277449)
XLA Ops:
  6.5 0.7 pad_clamp_fusion
  7.2 0.7 bitcast_bitcast_fusion
  8.0 1.4 gather_fusion
  9.4 14.0 %all-to-all-start = ((bf16[64,16,256]{2,1,0:T(8,128)(2,1)}), bf16[64,16,256]{2,1,0:T(8,128)(2,1)S(1)}, u32[]{:S(2)}, u32[]{:S(2)}) async-start(bf16[64,16,256]{2,1,0:T(8,128)(2,1)} %gather_fusion), calls=%async_computation | async-start | bytes 1048576 | tf_op jit(solution)/shard_map/all_to_all | solution.py:113
  23.4 0.8 dynamic_slice.16
  24.2 2.0 %select_reduce_fusion = s32[256]{0:T(256)S(1)} fusion(s32[8192]{0:T(1024)} %param.11, s32[256]{0:T(256)S(1)} %iota_add_fusion.3), kind=kLoop, calls=%fused_computation.3 | loop fusion | flops 6291200 | bytes 34816 | tf_op jit(solution)/shard_map/reduce_sum | solution.py:139
  26.4 13.8 %all-to-all-done = bf16[64,16,256]{2,1,0:T(8,128)(2,1)S(1)} async-done(((bf16[64,16,256]{2,1,0:T(8,128)(2,1)}), bf16[64,16,256]{2,1,0:T(8,128)(2,1)S(1)}, u32[]{:S(2)}, u32[]{:S(2)}) %all-to-all-start) | async-done | bytes 524320 | tf_op jit(solution)/shard_map/all_to_all | solution.py:113
  40.1 3.5 %collective-permute-start = (bf16[1024,256]{1,0:T(8,128)(2,1)S(1)}, bf16[1024,256]{1,0:T(8,128)(2,1)S(1)}, u32[]{:S(2)}, u32[]{:S(2)}) collective-permute-start(bf16[1024,256]{1,0:T(8,128)(2,1)S(1)} %bitcast.38), channel_id=1, source_target_pairs={{0,64},{64,128},{128,192},{192,256},{256,320},{320,384},{384,448},... | collective-permute-start | bytes 1572872 | tf_op jit(solution)/shard_map/ppermute | solution.py:126
  43.8 0.8 copy.36.refs_1_.refs_2_
  44.6 0.8 copy.37.refs_2_.refs_3_
  46.0 1.3 pad_dynamic-slice_fusion.1
  47.3 0.9 convolution_convert_fusion.2.q_ref
  48.1 3.3 %shard_map.82 = (f32[2,256,1]{2,1,0:T(8,128)}, f32[2,256,1]{2,1,0:T(8,128)}, f32[256,256]{1,0:T(8,128)}) custom-call(bf16[256,256]{1,0:T(8,128)(2,1)} %convolution_convert_fusion.2.q_ref, bf16[1024,256]{1,0:T(8,128)(2,1)} %bitcast.39, s32[256,1]{1,0:T(8,128)} %copy.36.refs_1_.refs_2_, s32[256,1]{1,0:T(8,128)} %copy.37.refs_2_.refs_3_, ...), custom_call_target="tpu_custom_call" | custom-call | flops 268435456 | bytes 786432 | tf_op jit(solution)/shard_map/pallas_call | solution.py:81
  51.5 3.8 %collective-permute-done.refs_0_ = bf16[1024,256]{1,0:T(8,128)(2,1)S(1)} collective-permute-done((bf16[1024,256]{1,0:T(8,128)(2,1)S(1)}, bf16[1024,256]{1,0:T(8,128)(2,1)S(1)}, u32[]{:S(2)}, u32[]{:S(2)}) %collective-permute-start) | collective-permute-done | bytes 524320 | tf_op jit(solution)/shard_map/ppermute | solution.py:126
  55.3 2.6 %collective-permute-start.1 = (bf16[1024,256]{1,0:T(8,128)(2,1)S(1)}, bf16[1024,256]{1,0:T(8,128)(2,1)S(1)}, u32[]{:S(2)}, u32[]{:S(2)}) collective-permute-start(bf16[1024,256]{1,0:T(8,128)(2,1)S(1)} %collective-permute-done.refs_0_), channel_id=1, source_target_pairs={{0,1},{1,0},{2,3},{3,2},{4,5},{5,4},{6,7},{7,6},{8,9},{9,8},{10,11... | collective-permute-start | bytes 1572872 | tf_op jit(solution)/shard_map/ppermute | solution.py:150
  57.9 0.8 and_select_fusion
  58.7 0.6 pad_add_fusion.1.refs_5_
  59.9 0.8 copy-done.3
  60.7 4.9 %shard_map.83 = bf16[256,256]{1,0:T(8,128)(2,1)} custom-call(bf16[256,256]{1,0:T(8,128)(2,1)} %convolution_convert_fusion.2.q_ref, bf16[1024,256]{1,0:T(8,128)(2,1)} %copy-done.2, bf16[1024,256]{1,0:T(8,128)(2,1)} %copy-done.3, s32[256,1]{1,0:T(8,128)} %copy.36.refs_1_.refs_2_, s32[256,1]{1,0:T(8,128)} %copy.37.refs_2_.refs_3_, ...), custom_call_target="tpu_custom_call" | custom-call | flops 536870912 | bytes 1310720 | tf_op jit(solution)/shard_map/pallas_call | solution.py:81
  65.6 1.6 copy.49
  67.2 4.7 %all-to-all-start.1 = ((bf16[4,8,8,256]{3,2,1,0:T(8,128)(2,1)}), bf16[4,8,8,256]{3,2,1,0:T(8,128)(2,1)S(1)}, u32[]{:S(2)}, u32[]{:S(2)}) async-start(bf16[4,8,8,256]{3,2,1,0:T(8,128)(2,1)} %bitcast.34), calls=%async_computation.1 | async-start | bytes 262144 | tf_op jit(solution)/shard_map/all_to_all | solution.py:157
  72.1 3.7 %all-to-all-done.1 = bf16[4,8,8,256]{3,2,1,0:T(8,128)(2,1)S(1)} async-done(((bf16[4,8,8,256]{3,2,1,0:T(8,128)(2,1)}), bf16[4,8,8,256]{3,2,1,0:T(8,128)(2,1)S(1)}, u32[]{:S(2)}, u32[]{:S(2)}) %all-to-all-start.1) | async-done | bytes 131104 | tf_op jit(solution)/shard_map/all_to_all | solution.py:157
  75.8 0.7 copy.48
  76.5 14.5 %all-to-all-start.2 = ((bf16[8,4,8,256]{3,2,1,0:T(8,128)(2,1)}), bf16[8,4,8,256]{3,2,1,0:T(8,128)(2,1)S(1)}, u32[]{:S(2)}, u32[]{:S(2)}) async-start(bf16[8,4,8,256]{3,2,1,0:T(8,128)(2,1)} %bitcast.33), calls=%async_computation.2 | async-start | bytes 262144 | tf_op jit(solution)/shard_map/all_to_all | solution.py:159
  91.0 0.8 multiply_add_fusion
  92.0 8.1 %all-to-all-done.2 = bf16[8,4,8,256]{3,2,1,0:T(8,128)(2,1)S(1)} async-done(((bf16[8,4,8,256]{3,2,1,0:T(8,128)(2,1)}), bf16[8,4,8,256]{3,2,1,0:T(8,128)(2,1)S(1)}, u32[]{:S(2)}, u32[]{:S(2)}) %all-to-all-start.2) | async-done | bytes 131104 | tf_op jit(solution)/shard_map/all_to_all | solution.py:159
  100.0 4.4 %convolution_convert_fusion = bf16[128,8192]{1,0:T(8,128)(2,1)} fusion(bf16[256,8192]{1,0:T(8,128)(2,1)} %param.15, bf16[256,256]{1,0:T(8,128)(2,1)S(1)} %bitcast.35, s32[128]{0:T(128)S(1)} %eq.79), kind=kOutput, calls=%fused_computation.1 | convolution fusion | flops 554762240 | bytes 6423040 | tf_op jit(solution)/shard_map/dot_general | solution.py:174
  104.4 1.9 %collective-permute-start.2 = (bf16[128,8192]{1,0:T(8,128)(2,1)}, bf16[128,8192]{1,0:T(8,128)(2,1)}, u32[]{:S(2)}, u32[]{:S(2)}) collective-permute-start(bf16[128,8192]{1,0:T(8,128)(2,1)} %convolution_convert_fusion), channel_id=1, source_target_pairs={{0,1},{1,0},{2,3},{3,2},{4,5},{5,4},{6,7},{7,6},{8,9},{9,8},{10,11... | collective-permute-start | bytes 6291464 | tf_op jit(solution)/shard_map/ppermute | solution.py:177
  106.4 3.1 %convolution_convert_fusion.1 = bf16[128,8192]{1,0:T(8,128)(2,1)S(1)} fusion(bf16[256,8192]{1,0:T(8,128)(2,1)} %param.15, bf16[256,256]{1,0:T(8,128)(2,1)S(1)} %bitcast.36, s32[128]{0:T(128)S(1)} %eq.70), kind=kOutput, calls=%fused_computation.2 | convolution fusion | flops 554762240 | bytes 6423040 | tf_op jit(solution)/shard_map/dot_general | solution.py:174
  109.5 1.3 collective-permute-done.2
  110.8 3.4 %add_convert_fusion = bf16[128,8192]{1,0:T(8,128)(2,1)} fusion(bf16[128,8192]{1,0:T(8,128)(2,1)} %collective-permute-done.2, bf16[128,8192]{1,0:T(8,128)(2,1)S(1)} %convolution_convert_fusion.1), kind=kLoop, calls=%fused_computation.4 | loop fusion | flops 4194304 | bytes 6291456 | tf_op jit(solution)/shard_map/convert_element_type | solution.py:179
  114.2 38.1 %reduce-scatter.2.cloned.1.call-done = bf16[16,8192]{1,0:T(8,128)(2,1)} async-done(((bf16[128,8192]{1,0:T(8,128)(2,1)}), bf16[16,8192]{1,0:T(8,128)(2,1)}) %reduce-scatter.2.cloned.1.call-update) | async-done | bytes 262160 | tf_op jit(solution)/shard_map/reduce_scatter | solution.py:180
  (22 shorter events, 2.1 us)
Async XLA Ops:
  6.5 40.7 %copy-start = (bf16[256,256]{1,0:T(8,128)(2,1)S(1)}, bf16[256,256]{1,0:T(8,128)(2,1)}, u32[]{:S(2)}) copy-start(bf16[256,256]{1,0:T(8,128)(2,1)} %param.12) | copy-start | bytes 393220
  9.4 30.7 %all-to-all-start = ((bf16[64,16,256]{2,1,0:T(8,128)(2,1)}), bf16[64,16,256]{2,1,0:T(8,128)(2,1)S(1)}, u32[]{:S(2)}, u32[]{:S(2)}) async-start(bf16[64,16,256]{2,1,0:T(8,128)(2,1)} %gather_fusion), calls=%async_computation | async-start | bytes 1048576 | tf_op jit(solution)/shard_map/all_to_all | solution.py:113
  40.1 8.0 %copy-start.1 = (bf16[64,16,256]{2,1,0:T(8,128)(2,1)}, bf16[64,16,256]{2,1,0:T(8,128)(2,1)S(1)}, u32[]{:S(2)}) copy-start(bf16[64,16,256]{2,1,0:T(8,128)(2,1)S(1)} %all-to-all-done) | copy-start | bytes 1572868
  40.1 15.2 %collective-permute-start = (bf16[1024,256]{1,0:T(8,128)(2,1)S(1)}, bf16[1024,256]{1,0:T(8,128)(2,1)S(1)}, u32[]{:S(2)}, u32[]{:S(2)}) collective-permute-start(bf16[1024,256]{1,0:T(8,128)(2,1)S(1)} %bitcast.38), channel_id=1, source_target_pairs={{0,64},{64,128},{128,192},{192,256},{256,320},{320,384},{384,448},... | collective-permute-start | bytes 1572872 | tf_op jit(solution)/shard_map/ppermute | solution.py:126
  55.3 4.6 %copy-start.2 = (bf16[1024,256]{1,0:T(8,128)(2,1)}, bf16[1024,256]{1,0:T(8,128)(2,1)S(1)}, u32[]{:S(2)}) copy-start(bf16[1024,256]{1,0:T(8,128)(2,1)S(1)} %collective-permute-done.refs_0_) | copy-start | bytes 1572868
  55.3 4.6 %collective-permute-start.1 = (bf16[1024,256]{1,0:T(8,128)(2,1)S(1)}, bf16[1024,256]{1,0:T(8,128)(2,1)S(1)}, u32[]{:S(2)}, u32[]{:S(2)}) collective-permute-start(bf16[1024,256]{1,0:T(8,128)(2,1)S(1)} %collective-permute-done.refs_0_), channel_id=1, source_target_pairs={{0,1},{1,0},{2,3},{3,2},{4,5},{5,4},{6,7},{7,6},{8,9},{9,8},{10,11... | collective-permute-start | bytes 1572872 | tf_op jit(solution)/shard_map/ppermute | solution.py:150
  59.9 0.8 copy-start.3
  67.2 8.6 %all-to-all-start.1 = ((bf16[4,8,8,256]{3,2,1,0:T(8,128)(2,1)}), bf16[4,8,8,256]{3,2,1,0:T(8,128)(2,1)S(1)}, u32[]{:S(2)}, u32[]{:S(2)}) async-start(bf16[4,8,8,256]{3,2,1,0:T(8,128)(2,1)} %bitcast.34), calls=%async_computation.1 | async-start | bytes 262144 | tf_op jit(solution)/shard_map/all_to_all | solution.py:157
  76.5 23.6 %all-to-all-start.2 = ((bf16[8,4,8,256]{3,2,1,0:T(8,128)(2,1)}), bf16[8,4,8,256]{3,2,1,0:T(8,128)(2,1)S(1)}, u32[]{:S(2)}, u32[]{:S(2)}) async-start(bf16[8,4,8,256]{3,2,1,0:T(8,128)(2,1)} %bitcast.33), calls=%async_computation.2 | async-start | bytes 262144 | tf_op jit(solution)/shard_map/all_to_all | solution.py:159
  91.0 61.4 %reduce-scatter.2.cloned.1.call-start = ((), (), s32[]{:S(2)}) async-start(), calls=%async_computation.4 | async-start | bytes 2359296 | tf_op jit(solution)/shard_map/reduce_scatter | solution.py:180
  104.4 6.4 %collective-permute-start.2 = (bf16[128,8192]{1,0:T(8,128)(2,1)}, bf16[128,8192]{1,0:T(8,128)(2,1)}, u32[]{:S(2)}, u32[]{:S(2)}) collective-permute-start(bf16[128,8192]{1,0:T(8,128)(2,1)} %convolution_convert_fusion), channel_id=1, source_target_pairs={{0,1},{1,0},{2,3},{3,2},{4,5},{5,4},{6,7},{7,6},{8,9},{9,8},{10,11... | collective-permute-start | bytes 6291464 | tf_op jit(solution)/shard_map/ppermute | solution.py:177
Sparse Core Ops, SparseCore 0:
  114.3 37.9 reduce-scatter.1

commit v15 on v13

--- a/solution.py
+++ b/solution.py
@@ -106,10 +106,14 @@
     n_tp = n_z * n_core
     kv_heads = kv_width // HD
     n_x = lax.axis_size("x")
-    heads_of = np.tile(np.arange(n_tp) * heads_here // group, n_x)
+    share = group // heads_here
+    assert n_tp == kv_heads * share
     k_h = jnp.transpose(keys.reshape(keys.shape[0], kv_heads, HD), (1, 0, 2))
     v_h = jnp.transpose(values.reshape(values.shape[0], kv_heads, HD), (1, 0, 2))
-    pieces = jnp.concatenate([k_h, v_h], axis=2)[heads_of]
+    kv_h = jnp.concatenate([k_h, v_h], axis=2)
+    pieces = jnp.broadcast_to(
+        kv_h[None, :, None], (n_x, kv_heads, share) + kv_h.shape[1:]
+    ).reshape((n_x * n_tp,) + kv_h.shape[1:])
     row = lax.all_to_all(pieces, ("x", "z", "core"), split_axis=0, concat_axis=0, tiled=True)
     row = row.reshape(n_x * rows, 2 * HD)
 

time: 152 us -> 152 us (level)
  no operation moved by 1% of the time
where the time goes in v15:
time: 152 us; the launch traced here: 151 us
  waiting for transfers between devices  64.7 us (43%)
  starting transfers between devices  39.6 us (26%)
  between operations  13.6 us (9%)
  other arithmetic  9.3 us (6%)
  matrix products  8.3 us (5%)
  Pallas kernels  8.23 us (5%)
  local copies, waits for them, and re-layouts  7 us (5%)
    reduce_scatter x1, waiting for transfers between devices, shards(): return lax.psum_scatter(half, 'z', scatter_dimension=0, tiled=True)  37.3 us
    all_to_all x1, starting transfers between devices, shards(): lax.all_to_all(to_send, ('y', 'x'), split_axis=0, concat_axis=0, tiled=True)  17.5 us
    all_to_all x1, starting transfers between devices, shards(): lax.all_to_all(pieces, ('x', 'z', 'core'), split_axis=0, concat_axis=0, t...  14 us
    all_to_all x1, waiting for transfers between devices, shards(): lax.all_to_all(pieces, ('x', 'z', 'core'), split_axis=0, concat_axis=0, t...  13.8 us
    all_to_all x1, waiting for transfers between devices, shards(): lax.all_to_all(to_send, ('y', 'x'), split_axis=0, concat_axis=0, tiled=True)  8.45 us
    pallas_call x2, Pallas kernels, attention(): pl.pallas_call(functools.partial(_attention_body, scale, n_pieces, heads,...  8.23 us
    dot_general x2, matrix products, project(): jnp.dot(relaid, out_weight, preferred_element_type=jnp.float32)  7.46 us
    ppermute x1, waiting for transfers between devices, shards(): fetched = lax.ppermute(row, ('y', 'core'), perm=perm)  3.81 us
  transfers between devices with their start and end apart: 6, of which 5 were waited for; matrix products, arithmetic and copies ran while one was open for 9% of the time, Pallas kernels for 2%

profile of v15, /device:TPU:6, one launch (start us, length us, event | category | flops | bytes accessed | tf_op | source)
XLA Modules:
  0.0 150.6 jit_solution(13436109679997810305)
XLA Ops:
  6.5 0.8 reshape.66
  7.3 0.7 reshape.67
  8.1 0.8 broadcast_in_dim.62
  8.9 14.0 %all-to-all-start = ((bf16[64,16,256]{2,1,0:T(8,128)(2,1)}), bf16[64,16,256]{2,1,0:T(8,128)(2,1)S(1)}, u32[]{:S(2)}, u32[]{:S(2)}) async-start(bf16[64,16,256]{2,1,0:T(8,128)(2,1)} %bitcast.3), calls=%async_computation | async-start | bytes 1048576 | tf_op jit(solution)/shard_map/all_to_all | solution.py:117
  22.9 0.8 dynamic_slice.16
  23.7 2.0 %select_reduce_fusion = s32[256]{0:T(256)S(1)} fusion(s32[8192]{0:T(1024)} %param.9, s32[256]{0:T(256)S(1)} %iota_add_fusion.3), kind=kLoop, calls=%fused_computation.2 | loop fusion | flops 6291200 | bytes 34816 | tf_op jit(solution)/shard_map/reduce_sum | solution.py:143
  25.7 0.2 convert_reduce_fusion
  25.9 13.8 %all-to-all-done = bf16[64,16,256]{2,1,0:T(8,128)(2,1)S(1)} async-done(((bf16[64,16,256]{2,1,0:T(8,128)(2,1)}), bf16[64,16,256]{2,1,0:T(8,128)(2,1)S(1)}, u32[]{:S(2)}, u32[]{:S(2)}) %all-to-all-start) | async-done | bytes 524320 | tf_op jit(solution)/shard_map/all_to_all | solution.py:117
  39.6 3.5 %collective-permute-start = (bf16[1024,256]{1,0:T(8,128)(2,1)S(1)}, bf16[1024,256]{1,0:T(8,128)(2,1)S(1)}, u32[]{:S(2)}, u32[]{:S(2)}) collective-permute-start(bf16[1024,256]{1,0:T(8,128)(2,1)S(1)} %bitcast.23), channel_id=1, source_target_pairs={{0,64},{64,128},{128,192},{192,256},{256,320},{320,384},{384,448},... | collective-permute-start | bytes 1572872 | tf_op jit(solution)/shard_map/ppermute | solution.py:130
  43.3 0.8 copy.14.refs_1_.refs_2_
  44.1 0.8 copy.15.refs_2_.refs_3_
  44.9 0.6 iota_add_fusion.2.refs_3_
  45.5 1.3 pad_dynamic-slice_fusion.1
  46.8 0.8 convolution_convert_fusion.2.q_ref
  47.6 3.3 %shard_map.64 = (f32[2,256,1]{2,1,0:T(8,128)}, f32[2,256,1]{2,1,0:T(8,128)}, f32[256,256]{1,0:T(8,128)}) custom-call(bf16[256,256]{1,0:T(8,128)(2,1)} %convolution_convert_fusion.2.q_ref, bf16[1024,256]{1,0:T(8,128)(2,1)} %bitcast.24, s32[256,1]{1,0:T(8,128)} %copy.14.refs_1_.refs_2_, s32[256,1]{1,0:T(8,128)} %copy.15.refs_2_.refs_3_, ...), custom_call_target="tpu_custom_call" | custom-call | flops 268435456 | bytes 786432 | tf_op jit(solution)/shard_map/pallas_call | solution.py:81
  51.0 3.8 %collective-permute-done.refs_0_ = bf16[1024,256]{1,0:T(8,128)(2,1)S(1)} collective-permute-done((bf16[1024,256]{1,0:T(8,128)(2,1)S(1)}, bf16[1024,256]{1,0:T(8,128)(2,1)S(1)}, u32[]{:S(2)}, u32[]{:S(2)}) %collective-permute-start) | collective-permute-done | bytes 524320 | tf_op jit(solution)/shard_map/ppermute | solution.py:130
  54.8 2.6 %collective-permute-start.1 = (bf16[1024,256]{1,0:T(8,128)(2,1)S(1)}, bf16[1024,256]{1,0:T(8,128)(2,1)S(1)}, u32[]{:S(2)}, u32[]{:S(2)}) collective-permute-start(bf16[1024,256]{1,0:T(8,128)(2,1)S(1)} %collective-permute-done.refs_0_), channel_id=1, source_target_pairs={{0,1},{1,0},{2,3},{3,2},{4,5},{5,4},{6,7},{7,6},{8,9},{9,8},{10,11... | collective-permute-start | bytes 1572872 | tf_op jit(solution)/shard_map/ppermute | solution.py:154
  57.4 0.8 and_select_fusion
  58.2 0.6 pad_add_fusion.1.refs_5_
  58.8 0.6 pad_add_fusion.refs_4_
  59.4 0.2 convert_reduce_fusion.1
  59.6 0.8 copy-done.3
  60.4 4.9 %shard_map.65 = bf16[256,256]{1,0:T(8,128)(2,1)} custom-call(bf16[256,256]{1,0:T(8,128)(2,1)} %convolution_convert_fusion.2.q_ref, bf16[1024,256]{1,0:T(8,128)(2,1)} %copy-done.2, bf16[1024,256]{1,0:T(8,128)(2,1)} %copy-done.3, s32[256,1]{1,0:T(8,128)} %copy.14.refs_1_.refs_2_, s32[256,1]{1,0:T(8,128)} %copy.15.refs_2_.refs_3_, ...), custom_call_target="tpu_custom_call" | custom-call | flops 536870912 | bytes 1310720 | tf_op jit(solution)/shard_map/pallas_call | solution.py:81
  65.3 17.5 %all-to-all-start.1 = ((bf16[32,8,256]{2,1,0:T(8,128)(2,1)}), bf16[32,8,256]{2,1,0:T(8,128)(2,1)S(1)}, u32[]{:S(2)}, u32[]{:S(2)}) async-start(bf16[32,8,256]{2,1,0:T(8,128)(2,1)} %bitcast.22), calls=%async_computation.1 | async-start | bytes 262144 | tf_op jit(solution)/shard_map/all_to_all | solution.py:159
  82.9 0.8 multiply_add_fusion
  83.8 8.4 %all-to-all-done.1 = bf16[32,8,256]{2,1,0:T(8,128)(2,1)S(1)} async-done(((bf16[32,8,256]{2,1,0:T(8,128)(2,1)}), bf16[32,8,256]{2,1,0:T(8,128)(2,1)S(1)}, u32[]{:S(2)}, u32[]{:S(2)}) %all-to-all-start.1) | async-done | bytes 131104 | tf_op jit(solution)/shard_map/all_to_all | solution.py:159
  92.3 4.4 %convolution_convert_fusion = bf16[128,8192]{1,0:T(8,128)(2,1)} fusion(bf16[256,8192]{1,0:T(8,128)(2,1)} %param.13, bf16[32,8,256]{2,1,0:T(8,128)(2,1)S(1)} %all-to-all-done.1, s32[128]{0:T(128)S(1)} %eq.79), kind=kOutput, calls=%fused_computation | convolution fusion | flops 554762240 | bytes 6423040 | tf_op jit(solution)/shard_map/dot_general | solution.py:173
  96.7 1.9 %collective-permute-start.2 = (bf16[128,8192]{1,0:T(8,128)(2,1)}, bf16[128,8192]{1,0:T(8,128)(2,1)}, u32[]{:S(2)}, u32[]{:S(2)}) collective-permute-start(bf16[128,8192]{1,0:T(8,128)(2,1)} %convolution_convert_fusion), channel_id=1, source_target_pairs={{0,1},{1,0},{2,3},{3,2},{4,5},{5,4},{6,7},{7,6},{8,9},{9,8},{10,11... | collective-permute-start | bytes 6291464 | tf_op jit(solution)/shard_map/ppermute | solution.py:176
  98.7 3.1 %convolution_convert_fusion.1 = bf16[128,8192]{1,0:T(8,128)(2,1)S(1)} fusion(bf16[256,8192]{1,0:T(8,128)(2,1)} %param.13, bf16[32,8,256]{2,1,0:T(8,128)(2,1)S(1)} %all-to-all-done.1, s32[128]{0:T(128)S(1)} %eq.70), kind=kOutput, calls=%fused_computation.1 | convolution fusion | flops 554762240 | bytes 6423040 | tf_op jit(solution)/shard_map/dot_general | solution.py:173
  101.8 1.3 collective-permute-done.2
  103.1 3.4 %add_convert_fusion = bf16[128,8192]{1,0:T(8,128)(2,1)} fusion(bf16[128,8192]{1,0:T(8,128)(2,1)} %collective-permute-done.2, bf16[128,8192]{1,0:T(8,128)(2,1)S(1)} %convolution_convert_fusion.1), kind=kLoop, calls=%fused_computation.3 | loop fusion | flops 4194304 | bytes 6291456 | tf_op jit(solution)/shard_map/convert_element_type | solution.py:178
  106.5 37.3 %reduce-scatter.2.cloned.1.call-done = bf16[16,8192]{1,0:T(8,128)(2,1)} async-done(((bf16[128,8192]{1,0:T(8,128)(2,1)}), bf16[16,8192]{1,0:T(8,128)(2,1)}) %reduce-scatter.2.cloned.1.call-update) | async-done | bytes 262160 | tf_op jit(solution)/shard_map/reduce_scatter | solution.py:179
  (19 shorter events, 0.5 us)
Async XLA Ops:
  6.5 40.3 %copy-start = (bf16[256,256]{1,0:T(8,128)(2,1)S(1)}, bf16[256,256]{1,0:T(8,128)(2,1)}, u32[]{:S(2)}) copy-start(bf16[256,256]{1,0:T(8,128)(2,1)} %param.10) | copy-start | bytes 393220
  8.9 30.7 %all-to-all-start = ((bf16[64,16,256]{2,1,0:T(8,128)(2,1)}), bf16[64,16,256]{2,1,0:T(8,128)(2,1)S(1)}, u32[]{:S(2)}, u32[]{:S(2)}) async-start(bf16[64,16,256]{2,1,0:T(8,128)(2,1)} %bitcast.3), calls=%async_computation | async-start | bytes 1048576 | tf_op jit(solution)/shard_map/all_to_all | solution.py:117
  39.6 8.0 %copy-start.1 = (bf16[64,16,256]{2,1,0:T(8,128)(2,1)}, bf16[64,16,256]{2,1,0:T(8,128)(2,1)S(1)}, u32[]{:S(2)}) copy-start(bf16[64,16,256]{2,1,0:T(8,128)(2,1)S(1)} %all-to-all-done) | copy-start | bytes 1572868
  39.6 15.2 %collective-permute-start = (bf16[1024,256]{1,0:T(8,128)(2,1)S(1)}, bf16[1024,256]{1,0:T(8,128)(2,1)S(1)}, u32[]{:S(2)}, u32[]{:S(2)}) collective-permute-start(bf16[1024,256]{1,0:T(8,128)(2,1)S(1)} %bitcast.23), channel_id=1, source_target_pairs={{0,64},{64,128},{128,192},{192,256},{256,320},{320,384},{384,448},... | collective-permute-start | bytes 1572872 | tf_op jit(solution)/shard_map/ppermute | solution.py:130
  54.8 4.8 %copy-start.2 = (bf16[1024,256]{1,0:T(8,128)(2,1)}, bf16[1024,256]{1,0:T(8,128)(2,1)S(1)}, u32[]{:S(2)}) copy-start(bf16[1024,256]{1,0:T(8,128)(2,1)S(1)} %collective-permute-done.refs_0_) | copy-start | bytes 1572868
  54.8 4.8 %collective-permute-start.1 = (bf16[1024,256]{1,0:T(8,128)(2,1)S(1)}, bf16[1024,256]{1,0:T(8,128)(2,1)S(1)}, u32[]{:S(2)}, u32[]{:S(2)}) collective-permute-start(bf16[1024,256]{1,0:T(8,128)(2,1)S(1)} %collective-permute-done.refs_0_), channel_id=1, source_target_pairs={{0,1},{1,0},{2,3},{3,2},{4,5},{5,4},{6,7},{7,6},{8,9},{9,8},{10,11... | collective-permute-start | bytes 1572872 | tf_op jit(solution)/shard_map/ppermute | solution.py:154
  59.6 0.8 copy-start.3
  65.3 27.0 %all-to-all-start.1 = ((bf16[32,8,256]{2,1,0:T(8,128)(2,1)}), bf16[32,8,256]{2,1,0:T(8,128)(2,1)S(1)}, u32[]{:S(2)}, u32[]{:S(2)}) async-start(bf16[32,8,256]{2,1,0:T(8,128)(2,1)} %bitcast.22), calls=%async_computation.1 | async-start | bytes 262144 | tf_op jit(solution)/shard_map/all_to_all | solution.py:159
  82.8 61.0 %reduce-scatter.2.cloned.1.call-start = ((), (), s32[]{:S(2)}) async-start(), calls=%async_computation.3 | async-start | bytes 2359296 | tf_op jit(solution)/shard_map/reduce_scatter | solution.py:179
  96.7 6.4 %collective-permute-start.2 = (bf16[128,8192]{1,0:T(8,128)(2,1)}, bf16[128,8192]{1,0:T(8,128)(2,1)}, u32[]{:S(2)}, u32[]{:S(2)}) collective-permute-start(bf16[128,8192]{1,0:T(8,128)(2,1)} %convolution_convert_fusion), channel_id=1, source_target_pairs={{0,1},{1,0},{2,3},{3,2},{4,5},{5,4},{6,7},{7,6},{8,9},{9,8},{10,11... | collective-permute-start | bytes 6291464 | tf_op jit(solution)/shard_map/ppermute | solution.py:176
Sparse Core Ops, SparseCore 0:
  106.6 37.1 reduce-scatter.1

commit v16 on v15

--- a/solution.py
+++ b/solution.py
@@ -150,18 +150,20 @@
     q_pos = jnp.sum(jnp.where(send_hit, here[None, :], 0), axis=1)
     q_seg = jnp.sum(jnp.where(send_hit, q_seg[None, :], 0), axis=1)
     carry = attention(q_sent, [row], q_pos, q_seg, k_pos[2:], k_seg[2:], scale, final=False)
-    fetched, carry = lax.optimization_barrier((fetched, carry))
-    swapped = lax.ppermute(fetched, "core", perm=[(i, (i + 1) % n_core) for i in range(n_core)])
-    to_send = attention(
-        q_sent, [fetched, swapped], q_pos, q_seg, k_pos[:2], k_seg[:2], scale, carry=carry
-    )
-
-    arrived = lax.all_to_all(to_send, ("y", "x"), split_axis=0, concat_axis=0, tiled=True)
-
     src = lax.dynamic_slice_in_dim(relayout, s * rows, rows, 0) // rows
     before = jnp.arange(rows)[None, :] < jnp.arange(rows)[:, None]
     nth = jnp.sum((before & (src[None, :] == src[:, None])).astype(jnp.int32), axis=1)
     slot = src * chunk + nth
+    fetched, carry, kp_early, ks_early, slot = lax.optimization_barrier(
+        (fetched, carry, k_pos[:2], k_seg[:2], slot)
+    )
+    swapped = lax.ppermute(fetched, "core", perm=[(i, (i + 1) % n_core) for i in range(n_core)])
+    to_send = attention(
+        q_sent, [fetched, swapped], q_pos, q_seg, kp_early, ks_early, scale, carry=carry
+    )
+
+    arrived = lax.all_to_all(to_send, ("y", "x"), split_axis=0, concat_axis=0, tiled=True)
+
     per_dev = rows // (n_z * n_core)
     slot3 = slot.reshape(n_z, n_core, per_dev)
     cols = jnp.arange(rows, dtype=jnp.int32)[None, :]

time: 152 us -> 151 us (level)
    all_to_all x1, waiting for transfers between devices: 13.8 us -> 10.1 us  [shards(): lax.all_to_all(pieces, ('x', 'z', 'core'), split_axis=0, concat_axis=0, t...]
  transfers between devices with their start and end apart: 6 -> 6, of which waited for: 5 -> 6; matrix products, arithmetic and copies ran while one was open for 9% -> 9% of each run, Pallas kernels for 2% -> 2%
where the time goes in v16:
time: 151 us; the launch traced here: 150 us
  waiting for transfers between devices  63.9 us (42%)
  starting transfers between devices  39.9 us (26%)
  between operations  13.5 us (9%)
  other arithmetic  9.3 us (6%)
  matrix products  8.31 us (6%)
  Pallas kernels  8.22 us (5%)
  local copies, waits for them, and re-layouts  6.99 us (5%)
    reduce_scatter x1, waiting for transfers between devices, shards(): return lax.psum_scatter(half, 'z', scatter_dimension=0, tiled=True)  37.6 us
    all_to_all x1, starting transfers between devices, shards(): lax.all_to_all(to_send, ('y', 'x'), split_axis=0, concat_axis=0, tiled=True)  17.9 us
    all_to_all x1, starting transfers between devices, shards(): lax.all_to_all(pieces, ('x', 'z', 'core'), split_axis=0, concat_axis=0, t...  14 us
    all_to_all x1, waiting for transfers between devices, shards(): lax.all_to_all(pieces, ('x', 'z', 'core'), split_axis=0, concat_axis=0, t...  10.1 us
    all_to_all x1, waiting for transfers between devices, shards(): lax.all_to_all(to_send, ('y', 'x'), split_axis=0, concat_axis=0, tiled=True)  8.79 us
    pallas_call x2, Pallas kernels, attention(): pl.pallas_call(functools.partial(_attention_body, scale, n_pieces, heads,...  8.22 us
    dot_general x2, matrix products, project(): jnp.dot(relaid, out_weight, preferred_element_type=jnp.float32)  7.46 us
    ppermute x1, waiting for transfers between devices, shards(): fetched = lax.ppermute(row, ('y', 'core'), perm=perm)  4.52 us
  transfers between devices with their start and end apart: 6, of which 6 were waited for; matrix products, arithmetic and copies ran while one was open for 9% of the time, Pallas kernels for 2%

profile of v16, /device:TPU:6, one launch (start us, length us, event | category | flops | bytes accessed | tf_op | source)
XLA Modules:
  0.0 150.2 jit_solution(5277609772272658034)
XLA Ops:
  6.5 0.8 reshape.66
  7.3 0.7 reshape.65
  8.1 0.8 broadcast_in_dim.60
  8.9 14.0 %all-to-all-start = ((bf16[64,16,256]{2,1,0:T(8,128)(2,1)}), bf16[64,16,256]{2,1,0:T(8,128)(2,1)S(1)}, u32[]{:S(2)}, u32[]{:S(2)}) async-start(bf16[64,16,256]{2,1,0:T(8,128)(2,1)} %bitcast.2), calls=%async_computation | async-start | bytes 1048576 | tf_op jit(solution)/shard_map/all_to_all | solution.py:117
  23.0 0.8 and_select_fusion
  23.7 0.8 dynamic_slice.15
  24.5 0.6 pad_add_fusion.refs_4_
  25.1 1.3 pad_dynamic-slice_fusion.1
  26.4 0.6 pad_add_fusion.1.refs_5_
  27.0 2.0 %select_reduce_fusion = s32[256]{0:T(256)S(1)} fusion(s32[8192]{0:T(1024)} %param.9, s32[256]{0:T(256)S(1)} %iota_add_fusion.3), kind=kLoop, calls=%fused_computation.2 | loop fusion | flops 6291200 | bytes 34816 | tf_op jit(solution)/shard_map/reduce_sum | solution.py:143
  29.2 0.2 convert_reduce_fusion
  29.5 10.1 %all-to-all-done = bf16[64,16,256]{2,1,0:T(8,128)(2,1)S(1)} async-done(((bf16[64,16,256]{2,1,0:T(8,128)(2,1)}), bf16[64,16,256]{2,1,0:T(8,128)(2,1)S(1)}, u32[]{:S(2)}, u32[]{:S(2)}) %all-to-all-start) | async-done | bytes 524320 | tf_op jit(solution)/shard_map/all_to_all | solution.py:117
  39.6 3.5 %collective-permute-start = (bf16[1024,256]{1,0:T(8,128)(2,1)S(1)}, bf16[1024,256]{1,0:T(8,128)(2,1)S(1)}, u32[]{:S(2)}, u32[]{:S(2)}) collective-permute-start(bf16[1024,256]{1,0:T(8,128)(2,1)S(1)} %bitcast.23), channel_id=1, source_target_pairs={{0,64},{64,128},{128,192},{192,256},{256,320},{320,384},{384,448},... | collective-permute-start | bytes 1572872 | tf_op jit(solution)/shard_map/ppermute | solution.py:130
  43.1 0.6 iota_add_fusion.2.refs_3_
  43.7 0.8 copy.14.refs_1_.refs_2_
  44.5 0.8 copy.15.refs_2_.refs_3_
  45.3 0.8 multiply_add_fusion
  46.1 0.8 convolution_convert_fusion.2.q_ref
  46.9 3.3 %shard_map.64 = (f32[2,256,1]{2,1,0:T(8,128)}, f32[2,256,1]{2,1,0:T(8,128)}, f32[256,256]{1,0:T(8,128)}) custom-call(bf16[256,256]{1,0:T(8,128)(2,1)} %convolution_convert_fusion.2.q_ref, bf16[1024,256]{1,0:T(8,128)(2,1)} %bitcast.24, s32[256,1]{1,0:T(8,128)} %copy.14.refs_1_.refs_2_, s32[256,1]{1,0:T(8,128)} %copy.15.refs_2_.refs_3_, ...), custom_call_target="tpu_custom_call" | custom-call | flops 268435456 | bytes 786432 | tf_op jit(solution)/shard_map/pallas_call | solution.py:81
  50.3 4.5 %collective-permute-done.refs_0_ = bf16[1024,256]{1,0:T(8,128)(2,1)S(1)} collective-permute-done((bf16[1024,256]{1,0:T(8,128)(2,1)S(1)}, bf16[1024,256]{1,0:T(8,128)(2,1)S(1)}, u32[]{:S(2)}, u32[]{:S(2)}) %collective-permute-start) | collective-permute-done | bytes 524320 | tf_op jit(solution)/shard_map/ppermute | solution.py:130
  54.8 2.6 %collective-permute-start.1 = (bf16[1024,256]{1,0:T(8,128)(2,1)S(1)}, bf16[1024,256]{1,0:T(8,128)(2,1)S(1)}, u32[]{:S(2)}, u32[]{:S(2)}) collective-permute-start(bf16[1024,256]{1,0:T(8,128)(2,1)S(1)} %collective-permute-done.refs_0_), channel_id=1, source_target_pairs={{0,1},{1,0},{2,3},{3,2},{4,5},{5,4},{6,7},{7,6},{8,9},{9,8},{10,11... | collective-permute-start | bytes 1572872 | tf_op jit(solution)/shard_map/ppermute | solution.py:160
  57.4 1.5 %collective-permute-done.1.refs_1_ = bf16[1024,256]{1,0:T(8,128)(2,1)S(1)} collective-permute-done((bf16[1024,256]{1,0:T(8,128)(2,1)S(1)}, bf16[1024,256]{1,0:T(8,128)(2,1)S(1)}, u32[]{:S(2)}, u32[]{:S(2)}) %collective-permute-start.1) | collective-permute-done | bytes 524320 | tf_op jit(solution)/shard_map/ppermute | solution.py:160
  58.9 0.8 copy-done.3
  59.7 4.9 %shard_map.65 = bf16[256,256]{1,0:T(8,128)(2,1)} custom-call(bf16[256,256]{1,0:T(8,128)(2,1)} %convolution_convert_fusion.2.q_ref, bf16[1024,256]{1,0:T(8,128)(2,1)} %copy-done.2, bf16[1024,256]{1,0:T(8,128)(2,1)} %copy-done.3, s32[256,1]{1,0:T(8,128)} %copy.14.refs_1_.refs_2_, s32[256,1]{1,0:T(8,128)} %copy.15.refs_2_.refs_3_, ...), custom_call_target="tpu_custom_call" | custom-call | flops 536870912 | bytes 1310720 | tf_op jit(solution)/shard_map/pallas_call | solution.py:81
  64.6 17.9 %all-to-all-start.1 = ((bf16[32,8,256]{2,1,0:T(8,128)(2,1)}), bf16[32,8,256]{2,1,0:T(8,128)(2,1)S(1)}, u32[]{:S(2)}, u32[]{:S(2)}) async-start(bf16[32,8,256]{2,1,0:T(8,128)(2,1)} %bitcast.22), calls=%async_computation.1 | async-start | bytes 262144 | tf_op jit(solution)/shard_map/all_to_all | solution.py:165
  82.8 8.8 %all-to-all-done.1 = bf16[32,8,256]{2,1,0:T(8,128)(2,1)S(1)} async-done(((bf16[32,8,256]{2,1,0:T(8,128)(2,1)}), bf16[32,8,256]{2,1,0:T(8,128)(2,1)S(1)}, u32[]{:S(2)}, u32[]{:S(2)}) %all-to-all-start.1) | async-done | bytes 131104 | tf_op jit(solution)/shard_map/all_to_all | solution.py:165
  91.5 4.4 %convolution_convert_fusion = bf16[128,8192]{1,0:T(8,128)(2,1)} fusion(bf16[256,8192]{1,0:T(8,128)(2,1)} %param.13, bf16[32,8,256]{2,1,0:T(8,128)(2,1)S(1)} %all-to-all-done.1, s32[128]{0:T(128)S(1)} %eq.85), kind=kOutput, calls=%fused_computation | convolution fusion | flops 554762240 | bytes 6423040 | tf_op jit(solution)/shard_map/dot_general | solution.py:175
  95.9 1.9 %collective-permute-start.2 = (bf16[128,8192]{1,0:T(8,128)(2,1)}, bf16[128,8192]{1,0:T(8,128)(2,1)}, u32[]{:S(2)}, u32[]{:S(2)}) collective-permute-start(bf16[128,8192]{1,0:T(8,128)(2,1)} %convolution_convert_fusion), channel_id=1, source_target_pairs={{0,1},{1,0},{2,3},{3,2},{4,5},{5,4},{6,7},{7,6},{8,9},{9,8},{10,11... | collective-permute-start | bytes 6291464 | tf_op jit(solution)/shard_map/ppermute | solution.py:178
  97.9 3.1 %convolution_convert_fusion.1 = bf16[128,8192]{1,0:T(8,128)(2,1)S(1)} fusion(bf16[256,8192]{1,0:T(8,128)(2,1)} %param.13, bf16[32,8,256]{2,1,0:T(8,128)(2,1)S(1)} %all-to-all-done.1, s32[128]{0:T(128)S(1)} %eq.81), kind=kOutput, calls=%fused_computation.1 | convolution fusion | flops 554762240 | bytes 6423040 | tf_op jit(solution)/shard_map/dot_general | solution.py:175
  101.0 1.3 collective-permute-done.2
  102.3 3.4 %add_convert_fusion = bf16[128,8192]{1,0:T(8,128)(2,1)} fusion(bf16[128,8192]{1,0:T(8,128)(2,1)} %collective-permute-done.2, bf16[128,8192]{1,0:T(8,128)(2,1)S(1)} %convolution_convert_fusion.1), kind=kLoop, calls=%fused_computation.3 | loop fusion | flops 4194304 | bytes 6291456 | tf_op jit(solution)/shard_map/convert_element_type | solution.py:180
  105.7 37.6 %reduce-scatter.2.cloned.1.call-done = bf16[16,8192]{1,0:T(8,128)(2,1)} async-done(((bf16[128,8192]{1,0:T(8,128)(2,1)}), bf16[16,8192]{1,0:T(8,128)(2,1)}) %reduce-scatter.2.cloned.1.call-update) | async-done | bytes 262160 | tf_op jit(solution)/shard_map/reduce_scatter | solution.py:181
  (19 shorter events, 0.7 us)
Async XLA Ops:
  6.5 39.6 %copy-start = (bf16[256,256]{1,0:T(8,128)(2,1)S(1)}, bf16[256,256]{1,0:T(8,128)(2,1)}, u32[]{:S(2)}) copy-start(bf16[256,256]{1,0:T(8,128)(2,1)} %param.10) | copy-start | bytes 393220
  8.9 30.7 %all-to-all-start = ((bf16[64,16,256]{2,1,0:T(8,128)(2,1)}), bf16[64,16,256]{2,1,0:T(8,128)(2,1)S(1)}, u32[]{:S(2)}, u32[]{:S(2)}) async-start(bf16[64,16,256]{2,1,0:T(8,128)(2,1)} %bitcast.2), calls=%async_computation | async-start | bytes 1048576 | tf_op jit(solution)/shard_map/all_to_all | solution.py:117
  39.6 7.3 %copy-start.1 = (bf16[64,16,256]{2,1,0:T(8,128)(2,1)}, bf16[64,16,256]{2,1,0:T(8,128)(2,1)S(1)}, u32[]{:S(2)}) copy-start(bf16[64,16,256]{2,1,0:T(8,128)(2,1)S(1)} %all-to-all-done) | copy-start | bytes 1572868
  39.6 15.2 %collective-permute-start = (bf16[1024,256]{1,0:T(8,128)(2,1)S(1)}, bf16[1024,256]{1,0:T(8,128)(2,1)S(1)}, u32[]{:S(2)}, u32[]{:S(2)}) collective-permute-start(bf16[1024,256]{1,0:T(8,128)(2,1)S(1)} %bitcast.23), channel_id=1, source_target_pairs={{0,64},{64,128},{128,192},{192,256},{256,320},{320,384},{384,448},... | collective-permute-start | bytes 1572872 | tf_op jit(solution)/shard_map/ppermute | solution.py:130
  54.8 4.1 %copy-start.2 = (bf16[1024,256]{1,0:T(8,128)(2,1)}, bf16[1024,256]{1,0:T(8,128)(2,1)S(1)}, u32[]{:S(2)}) copy-start(bf16[1024,256]{1,0:T(8,128)(2,1)S(1)} %collective-permute-done.refs_0_) | copy-start | bytes 1572868
  54.8 4.1 %collective-permute-start.1 = (bf16[1024,256]{1,0:T(8,128)(2,1)S(1)}, bf16[1024,256]{1,0:T(8,128)(2,1)S(1)}, u32[]{:S(2)}, u32[]{:S(2)}) collective-permute-start(bf16[1024,256]{1,0:T(8,128)(2,1)S(1)} %collective-permute-done.refs_0_), channel_id=1, source_target_pairs={{0,1},{1,0},{2,3},{3,2},{4,5},{5,4},{6,7},{7,6},{8,9},{9,8},{10,11... | collective-permute-start | bytes 1572872 | tf_op jit(solution)/shard_map/ppermute | solution.py:160
  58.9 0.8 copy-start.3
  64.6 26.9 %all-to-all-start.1 = ((bf16[32,8,256]{2,1,0:T(8,128)(2,1)}), bf16[32,8,256]{2,1,0:T(8,128)(2,1)S(1)}, u32[]{:S(2)}, u32[]{:S(2)}) async-start(bf16[32,8,256]{2,1,0:T(8,128)(2,1)} %bitcast.22), calls=%async_computation.1 | async-start | bytes 262144 | tf_op jit(solution)/shard_map/all_to_all | solution.py:165
  82.5 60.8 %reduce-scatter.2.cloned.1.call-start = ((), (), s32[]{:S(2)}) async-start(), calls=%async_computation.3 | async-start | bytes 2359296 | tf_op jit(solution)/shard_map/reduce_scatter | solution.py:181
  95.9 6.4 %collective-permute-start.2 = (bf16[128,8192]{1,0:T(8,128)(2,1)}, bf16[128,8192]{1,0:T(8,128)(2,1)}, u32[]{:S(2)}, u32[]{:S(2)}) collective-permute-start(bf16[128,8192]{1,0:T(8,128)(2,1)} %convolution_convert_fusion), channel_id=1, source_target_pairs={{0,1},{1,0},{2,3},{3,2},{4,5},{5,4},{6,7},{7,6},{8,9},{9,8},{10,11... | collective-permute-start | bytes 6291464 | tf_op jit(solution)/shard_map/ppermute | solution.py:178
Sparse Core Ops, SparseCore 0:
  105.8 37.4 reduce-scatter.1

commit v17 on v16

--- a/solution.py
+++ b/solution.py
@@ -158,8 +158,11 @@
         (fetched, carry, k_pos[:2], k_seg[:2], slot)
     )
     swapped = lax.ppermute(fetched, "core", perm=[(i, (i + 1) % n_core) for i in range(n_core)])
+    carry = attention(
+        q_sent, [fetched], q_pos, q_seg, kp_early[:1], ks_early[:1], scale, carry=carry, final=False
+    )
     to_send = attention(
-        q_sent, [fetched, swapped], q_pos, q_seg, kp_early, ks_early, scale, carry=carry
+        q_sent, [swapped], q_pos, q_seg, kp_early[1:], ks_early[1:], scale, carry=carry
     )
 
     arrived = lax.all_to_all(to_send, ("y", "x"), split_axis=0, concat_axis=0, tiled=True)

time: 151 us -> 154 us (1.020)
  Pallas kernels: 8.22 us -> 11 us
    pallas_call x2 -> x3, Pallas kernels: 8.22 us -> 11 us  [attention(): pl.pallas_call(functools.partial(_attention_body, scale, n_pieces, heads,...]
  transfers between devices with their start and end apart: 6 -> 6, of which waited for: 6 -> 5; matrix products, arithmetic and copies ran while one was open for 9% -> 9% of each run, Pallas kernels for 2% -> 5%
where the time goes in v17:
time: 154 us; the launch traced here: 153 us
  waiting for transfers between devices  64 us (42%)
  starting transfers between devices  39.6 us (26%)
  between operations  13.5 us (9%)
  Pallas kernels  11 us (7%)
  matrix products  8.32 us (5%)
  local copies, waits for them, and re-layouts  8.26 us (5%)
  other arithmetic  8.12 us (5%)
    reduce_scatter x1, waiting for transfers between devices, shards(): return lax.psum_scatter(half, 'z', scatter_dimension=0, tiled=True)  37.7 us
    all_to_all x1, starting transfers between devices, shards(): lax.all_to_all(to_send, ('y', 'x'), split_axis=0, concat_axis=0, tiled=True)  17.5 us
    all_to_all x1, starting transfers between devices, shards(): lax.all_to_all(pieces, ('x', 'z', 'core'), split_axis=0, concat_axis=0, t...  14 us
    all_to_all x1, waiting for transfers between devices, shards(): lax.all_to_all(pieces, ('x', 'z', 'core'), split_axis=0, concat_axis=0, t...  11.3 us
    pallas_call x3, Pallas kernels, attention(): pl.pallas_call(functools.partial(_attention_body, scale, n_pieces, heads,...  11 us
    all_to_all x1, waiting for transfers between devices, shards(): lax.all_to_all(to_send, ('y', 'x'), split_axis=0, concat_axis=0, tiled=True)  9.23 us
    dot_general x2, matrix products, project(): jnp.dot(relaid, out_weight, preferred_element_type=jnp.float32)  7.47 us
    ppermute x1, waiting for transfers between devices, shards(): fetched = lax.ppermute(row, ('y', 'core'), perm=perm)  4.52 us
  transfers between devices with their start and end apart: 6, of which 5 were waited for; matrix products, arithmetic and copies ran while one was open for 9% of the time, Pallas kernels for 5%

profile of v17, /device:TPU:6, one launch (start us, length us, event | category | flops | bytes accessed | tf_op | source)
XLA Modules:
  0.0 152.9 jit_solution(17860304236864254268)
XLA Ops:
  6.5 0.8 reshape.68
  7.3 0.7 reshape.67
  8.1 0.8 broadcast_in_dim.60
  8.9 14.0 %all-to-all-start = ((bf16[64,16,256]{2,1,0:T(8,128)(2,1)}), bf16[64,16,256]{2,1,0:T(8,128)(2,1)S(1)}, u32[]{:S(2)}, u32[]{:S(2)}) async-start(bf16[64,16,256]{2,1,0:T(8,128)(2,1)} %bitcast.2), calls=%async_computation | async-start | bytes 1048576 | tf_op jit(solution)/shard_map/all_to_all | solution.py:117
  23.0 0.8 and_select_fusion
  23.8 0.8 dynamic_slice.15
  24.5 1.3 pad_dynamic-slice_fusion.1
  25.9 2.0 %select_reduce_fusion = s32[256]{0:T(256)S(1)} fusion(s32[8192]{0:T(1024)} %param.9, s32[256]{0:T(256)S(1)} %iota_add_fusion.3), kind=kLoop, calls=%fused_computation.2 | loop fusion | flops 6291200 | bytes 34816 | tf_op jit(solution)/shard_map/reduce_sum | solution.py:143
  28.0 0.2 convert_reduce_fusion
  28.4 11.3 %all-to-all-done = bf16[64,16,256]{2,1,0:T(8,128)(2,1)S(1)} async-done(((bf16[64,16,256]{2,1,0:T(8,128)(2,1)}), bf16[64,16,256]{2,1,0:T(8,128)(2,1)S(1)}, u32[]{:S(2)}, u32[]{:S(2)}) %all-to-all-start) | async-done | bytes 524320 | tf_op jit(solution)/shard_map/all_to_all | solution.py:117
  39.6 3.5 %collective-permute-start = (bf16[1024,256]{1,0:T(8,128)(2,1)S(1)}, bf16[1024,256]{1,0:T(8,128)(2,1)S(1)}, u32[]{:S(2)}, u32[]{:S(2)}) collective-permute-start(bf16[1024,256]{1,0:T(8,128)(2,1)S(1)} %bitcast.23), channel_id=1, source_target_pairs={{0,64},{64,128},{128,192},{192,256},{256,320},{320,384},{384,448},... | collective-permute-start | bytes 1572872 | tf_op jit(solution)/shard_map/ppermute | solution.py:130
  43.2 0.6 iota_add_fusion.2.refs_3_
  43.7 0.8 copy.16.refs_1_
  44.6 0.8 copy.17.refs_2_
  45.4 0.8 multiply_add_fusion
  46.1 0.9 convolution_convert_fusion.2.q_ref
  47.0 3.3 %shard_map.64 = (f32[2,256,1]{2,1,0:T(8,128)}, f32[2,256,1]{2,1,0:T(8,128)}, f32[256,256]{1,0:T(8,128)}) custom-call(bf16[256,256]{1,0:T(8,128)(2,1)} %convolution_convert_fusion.2.q_ref, bf16[1024,256]{1,0:T(8,128)(2,1)} %bitcast.24, s32[256,1]{1,0:T(8,128)} %copy.16.refs_1_, s32[256,1]{1,0:T(8,128)} %copy.17.refs_2_, s32[1,1024]{1,0:T(1,128)} %iota_add_fusion.2.refs_3_, ...), custom_call_target="tpu_custom_call" | custom-call | flops 268435456 | bytes 786432 | tf_op jit(solution)/shard_map/pallas_call | solution.py:81
  50.3 4.5 %collective-permute-done.refs_0_ = bf16[1024,256]{1,0:T(8,128)(2,1)S(1)} collective-permute-done((bf16[1024,256]{1,0:T(8,128)(2,1)S(1)}, bf16[1024,256]{1,0:T(8,128)(2,1)S(1)}, u32[]{:S(2)}, u32[]{:S(2)}) %collective-permute-start) | collective-permute-done | bytes 524320 | tf_op jit(solution)/shard_map/ppermute | solution.py:130
  54.8 2.6 %collective-permute-start.1 = (bf16[1024,256]{1,0:T(8,128)(2,1)S(1)}, bf16[1024,256]{1,0:T(8,128)(2,1)S(1)}, u32[]{:S(2)}, u32[]{:S(2)}) collective-permute-start(bf16[1024,256]{1,0:T(8,128)(2,1)S(1)} %collective-permute-done.refs_0_), channel_id=1, source_target_pairs={{0,1},{1,0},{2,3},{3,2},{4,5},{5,4},{6,7},{7,6},{8,9},{9,8},{10,11... | collective-permute-start | bytes 1572872 | tf_op jit(solution)/shard_map/ppermute | solution.py:160
  57.4 0.6 fusion.11
  58.0 0.6 fusion.10
  58.6 3.9 %shard_map.65 = (f32[2,256,1]{2,1,0:T(8,128)}, f32[2,256,1]{2,1,0:T(8,128)}, f32[256,256]{1,0:T(8,128)}) custom-call(bf16[256,256]{1,0:T(8,128)(2,1)} %convolution_convert_fusion.2.q_ref, bf16[1024,256]{1,0:T(8,128)(2,1)} %copy-done.3, s32[256,1]{1,0:T(8,128)} %copy.16.refs_1_, s32[256,1]{1,0:T(8,128)} %copy.17.refs_2_, ...), custom_call_target="tpu_custom_call" | custom-call | flops 268435456 | bytes 786432 | tf_op jit(solution)/shard_map/pallas_call | solution.py:81
  62.5 0.8 copy-done.1
  63.3 3.8 %shard_map.66 = bf16[256,256]{1,0:T(8,128)(2,1)} custom-call(bf16[256,256]{1,0:T(8,128)(2,1)} %convolution_convert_fusion.2.q_ref, bf16[1024,256]{1,0:T(8,128)(2,1)} %copy-done.1, s32[256,1]{1,0:T(8,128)} %copy.16.refs_1_, s32[256,1]{1,0:T(8,128)} %copy.17.refs_2_, s32[1,1024]{1,0:T(1,128)} %get-tuple-element.53.refs_3_, ...), custom_call_target="tpu_custom_call" | custom-call | flops 268435456 | bytes 786432 | tf_op jit(solution)/shard_map/pallas_call | solution.py:81
  67.2 17.5 %all-to-all-start.1 = ((bf16[32,8,256]{2,1,0:T(8,128)(2,1)}), bf16[32,8,256]{2,1,0:T(8,128)(2,1)S(1)}, u32[]{:S(2)}, u32[]{:S(2)}) async-start(bf16[32,8,256]{2,1,0:T(8,128)(2,1)} %bitcast.22), calls=%async_computation.1 | async-start | bytes 262144 | tf_op jit(solution)/shard_map/all_to_all | solution.py:168
  84.9 9.2 %all-to-all-done.1 = bf16[32,8,256]{2,1,0:T(8,128)(2,1)S(1)} async-done(((bf16[32,8,256]{2,1,0:T(8,128)(2,1)}), bf16[32,8,256]{2,1,0:T(8,128)(2,1)S(1)}, u32[]{:S(2)}, u32[]{:S(2)}) %all-to-all-start.1) | async-done | bytes 131104 | tf_op jit(solution)/shard_map/all_to_all | solution.py:168
  94.1 4.4 %convolution_convert_fusion = bf16[128,8192]{1,0:T(8,128)(2,1)} fusion(bf16[256,8192]{1,0:T(8,128)(2,1)} %param.13, bf16[32,8,256]{2,1,0:T(8,128)(2,1)S(1)} %all-to-all-done.1, s32[128]{0:T(128)S(1)} %eq.85), kind=kOutput, calls=%fused_computation | convolution fusion | flops 554762240 | bytes 6423040 | tf_op jit(solution)/shard_map/dot_general | solution.py:178
  98.5 1.9 %collective-permute-start.2 = (bf16[128,8192]{1,0:T(8,128)(2,1)}, bf16[128,8192]{1,0:T(8,128)(2,1)}, u32[]{:S(2)}, u32[]{:S(2)}) collective-permute-start(bf16[128,8192]{1,0:T(8,128)(2,1)} %convolution_convert_fusion), channel_id=1, source_target_pairs={{0,1},{1,0},{2,3},{3,2},{4,5},{5,4},{6,7},{7,6},{8,9},{9,8},{10,11... | collective-permute-start | bytes 6291464 | tf_op jit(solution)/shard_map/ppermute | solution.py:181
  100.5 3.1 %convolution_convert_fusion.1 = bf16[128,8192]{1,0:T(8,128)(2,1)S(1)} fusion(bf16[256,8192]{1,0:T(8,128)(2,1)} %param.13, bf16[32,8,256]{2,1,0:T(8,128)(2,1)S(1)} %all-to-all-done.1, s32[128]{0:T(128)S(1)} %eq.81), kind=kOutput, calls=%fused_computation.1 | convolution fusion | flops 554762240 | bytes 6423040 | tf_op jit(solution)/shard_map/dot_general | solution.py:178
  103.6 1.3 collective-permute-done.2
  104.9 3.4 %add_convert_fusion = bf16[128,8192]{1,0:T(8,128)(2,1)} fusion(bf16[128,8192]{1,0:T(8,128)(2,1)} %collective-permute-done.2, bf16[128,8192]{1,0:T(8,128)(2,1)S(1)} %convolution_convert_fusion.1), kind=kLoop, calls=%fused_computation.3 | loop fusion | flops 4194304 | bytes 6291456 | tf_op jit(solution)/shard_map/convert_element_type | solution.py:183
  108.3 37.7 %reduce-scatter.2.cloned.1.call-done = bf16[16,8192]{1,0:T(8,128)(2,1)} async-done(((bf16[128,8192]{1,0:T(8,128)(2,1)}), bf16[16,8192]{1,0:T(8,128)(2,1)}) %reduce-scatter.2.cloned.1.call-update) | async-done | bytes 262160 | tf_op jit(solution)/shard_map/reduce_scatter | solution.py:184
  (22 shorter events, 0.7 us)
Async XLA Ops:
  6.5 39.6 %copy-start = (bf16[256,256]{1,0:T(8,128)(2,1)S(1)}, bf16[256,256]{1,0:T(8,128)(2,1)}, u32[]{:S(2)}) copy-start(bf16[256,256]{1,0:T(8,128)(2,1)} %param.10) | copy-start | bytes 393220
  8.9 30.7 %all-to-all-start = ((bf16[64,16,256]{2,1,0:T(8,128)(2,1)}), bf16[64,16,256]{2,1,0:T(8,128)(2,1)S(1)}, u32[]{:S(2)}, u32[]{:S(2)}) async-start(bf16[64,16,256]{2,1,0:T(8,128)(2,1)} %bitcast.2), calls=%async_computation | async-start | bytes 1048576 | tf_op jit(solution)/shard_map/all_to_all | solution.py:117
  39.6 7.3 %copy-start.2 = (bf16[64,16,256]{2,1,0:T(8,128)(2,1)}, bf16[64,16,256]{2,1,0:T(8,128)(2,1)S(1)}, u32[]{:S(2)}) copy-start(bf16[64,16,256]{2,1,0:T(8,128)(2,1)S(1)} %all-to-all-done) | copy-start | bytes 1572868
  39.6 15.2 %collective-permute-start = (bf16[1024,256]{1,0:T(8,128)(2,1)S(1)}, bf16[1024,256]{1,0:T(8,128)(2,1)S(1)}, u32[]{:S(2)}, u32[]{:S(2)}) collective-permute-start(bf16[1024,256]{1,0:T(8,128)(2,1)S(1)} %bitcast.23), channel_id=1, source_target_pairs={{0,64},{64,128},{128,192},{192,256},{256,320},{320,384},{384,448},... | collective-permute-start | bytes 1572872 | tf_op jit(solution)/shard_map/ppermute | solution.py:130
  54.8 3.8 %copy-start.3 = (bf16[1024,256]{1,0:T(8,128)(2,1)}, bf16[1024,256]{1,0:T(8,128)(2,1)S(1)}, u32[]{:S(2)}) copy-start(bf16[1024,256]{1,0:T(8,128)(2,1)S(1)} %collective-permute-done.refs_0_) | copy-start | bytes 1572868
  54.8 7.7 %collective-permute-start.1 = (bf16[1024,256]{1,0:T(8,128)(2,1)S(1)}, bf16[1024,256]{1,0:T(8,128)(2,1)S(1)}, u32[]{:S(2)}, u32[]{:S(2)}) collective-permute-start(bf16[1024,256]{1,0:T(8,128)(2,1)S(1)} %collective-permute-done.refs_0_), channel_id=1, source_target_pairs={{0,1},{1,0},{2,3},{3,2},{4,5},{5,4},{6,7},{7,6},{8,9},{9,8},{10,11... | collective-permute-start | bytes 1572872 | tf_op jit(solution)/shard_map/ppermute | solution.py:160
  62.5 0.8 copy-start.1
  67.2 27.0 %all-to-all-start.1 = ((bf16[32,8,256]{2,1,0:T(8,128)(2,1)}), bf16[32,8,256]{2,1,0:T(8,128)(2,1)S(1)}, u32[]{:S(2)}, u32[]{:S(2)}) async-start(bf16[32,8,256]{2,1,0:T(8,128)(2,1)} %bitcast.22), calls=%async_computation.1 | async-start | bytes 262144 | tf_op jit(solution)/shard_map/all_to_all | solution.py:168
  84.7 61.4 %reduce-scatter.2.cloned.1.call-start = ((), (), s32[]{:S(2)}) async-start(), calls=%async_computation.3 | async-start | bytes 2359296 | tf_op jit(solution)/shard_map/reduce_scatter | solution.py:184
  98.5 6.4 %collective-permute-start.2 = (bf16[128,8192]{1,0:T(8,128)(2,1)}, bf16[128,8192]{1,0:T(8,128)(2,1)}, u32[]{:S(2)}, u32[]{:S(2)}) collective-permute-start(bf16[128,8192]{1,0:T(8,128)(2,1)} %convolution_convert_fusion), channel_id=1, source_target_pairs={{0,1},{1,0},{2,3},{3,2},{4,5},{5,4},{6,7},{7,6},{8,9},{9,8},{10,11... | collective-permute-start | bytes 6291464 | tf_op jit(solution)/shard_map/ppermute | solution.py:181
Sparse Core Ops, SparseCore 0:
  108.4 37.5 reduce-scatter.1

commit v18 on v15

--- a/solution.py
+++ b/solution.py
@@ -166,15 +166,15 @@
     slot3 = slot.reshape(n_z, n_core, per_dev)
     cols = jnp.arange(rows, dtype=jnp.int32)[None, :]
 
-    def project(which):
-        chosen = jnp.take(slot3, which, axis=1).reshape(-1)
-        sel = (chosen[:, None] == cols).astype(jnp.bfloat16)
-        relaid = jnp.dot(sel, arrived, preferred_element_type=jnp.float32).astype(jnp.bfloat16)
-        return jnp.dot(relaid, out_weight, preferred_element_type=jnp.float32).astype(jnp.bfloat16)
-
-    part_other = project(n_core - 1 - c)
-    got = lax.ppermute(part_other, "core", perm=[(0, 1), (1, 0)])
-    part_own = lax.optimization_barrier(project(c))
+    order = jnp.concatenate(
+        [jnp.take(slot3, n_core - 1 - c, axis=1).reshape(-1), jnp.take(slot3, c, axis=1).reshape(-1)]
+    )
+    sel = (order[:, None] == cols).astype(jnp.bfloat16)
+    relaid = jnp.dot(sel, arrived, preferred_element_type=jnp.float32).astype(jnp.bfloat16)
+    part = jnp.dot(relaid, out_weight, preferred_element_type=jnp.float32).astype(jnp.bfloat16)
+    share_rows = rows // n_core
+    got = lax.ppermute(part[:share_rows], "core", perm=[(0, 1), (1, 0)])
+    part_own = part[share_rows:]
     half = (part_own.astype(jnp.float32) + got.astype(jnp.float32)).astype(jnp.bfloat16)
     return lax.psum_scatter(half, "z", scatter_dimension=0, tiled=True)
 

time: 152 us -> 153 us (level)
  waiting for transfers between devices: 64.7 us -> 67.5 us
  matrix products: 8.3 us -> 6.38 us
  local copies, waits for them, and re-layouts: 7 us -> 8.9 us
  other arithmetic: 9.3 us -> 7.76 us
    ppermute x1, waiting for transfers between devices: 1.3 us -> 4.13 us  [shards(): got = lax.ppermute(part[:share_rows], 'core', perm=[(0, 1), (1, 0)])]
    dot_general x2 -> x1, matrix products: 7.46 us -> 5.53 us  [shards(): jnp.dot(relaid, out_weight, preferred_element_type=jnp.float32)]
    slice x0 -> x1, local copies, waits for them, and re-layouts: none -> 1.88 us  [shards(): got = lax.ppermute(part[:share_rows], 'core', perm=[(0, 1), (1, 0)])]
    convert_element_type x1, other arithmetic: 3.39 us -> 1.83 us  [shards(): (part_own.astype(jnp.float32) + got.astype(jnp.float32)).astype(jnp.bfloa...]
  transfers between devices with their start and end apart: 6 -> 6, of which waited for: 5 -> 5; matrix products, arithmetic and copies ran while one was open for 9% -> 7% of each run, Pallas kernels for 2% -> 2%
where the time goes in v18:
time: 153 us; the launch traced here: 152 us
  waiting for transfers between devices  67.5 us (44%)
  starting transfers between devices  39.6 us (26%)
  between operations  13.6 us (9%)
  local copies, waits for them, and re-layouts  8.9 us (6%)
  Pallas kernels  8.22 us (5%)
  other arithmetic  7.76 us (5%)
  matrix products  6.38 us (4%)
    reduce_scatter x1, waiting for transfers between devices, shards(): return lax.psum_scatter(half, 'z', scatter_dimension=0, tiled=True)  37.4 us
    all_to_all x1, starting transfers between devices, shards(): lax.all_to_all(to_send, ('y', 'x'), split_axis=0, concat_axis=0, tiled=True)  17.5 us
    all_to_all x1, starting transfers between devices, shards(): lax.all_to_all(pieces, ('x', 'z', 'core'), split_axis=0, concat_axis=0, t...  14 us
    all_to_all x1, waiting for transfers between devices, shards(): lax.all_to_all(pieces, ('x', 'z', 'core'), split_axis=0, concat_axis=0, t...  13.8 us
    all_to_all x1, waiting for transfers between devices, shards(): lax.all_to_all(to_send, ('y', 'x'), split_axis=0, concat_axis=0, tiled=True)  8.36 us
    pallas_call x2, Pallas kernels, attention(): pl.pallas_call(functools.partial(_attention_body, scale, n_pieces, heads,...  8.22 us
    dot_general x1, matrix products, shards(): jnp.dot(relaid, out_weight, preferred_element_type=jnp.float32)  5.53 us
    ppermute x1, waiting for transfers between devices, shards(): got = lax.ppermute(part[:share_rows], 'core', perm=[(0, 1), (1, 0)])  4.13 us
  transfers between devices with their start and end apart: 6, of which 5 were waited for; matrix products, arithmetic and copies ran while one was open for 7% of the time, Pallas kernels for 2%

profile of v18, /device:TPU:6, one launch (start us, length us, event | category | flops | bytes accessed | tf_op | source)
XLA Modules:
  0.0 151.9 jit_solution(13425863239980705856)
XLA Ops:
  6.5 0.8 reshape.73
  7.3 0.7 reshape.74
  8.1 0.8 broadcast_in_dim.63
  8.9 14.0 %all-to-all-start = ((bf16[64,16,256]{2,1,0:T(8,128)(2,1)}), bf16[64,16,256]{2,1,0:T(8,128)(2,1)S(1)}, u32[]{:S(2)}, u32[]{:S(2)}) async-start(bf16[64,16,256]{2,1,0:T(8,128)(2,1)} %bitcast.4), calls=%async_computation | async-start | bytes 1048576 | tf_op jit(solution)/shard_map/all_to_all | solution.py:117
  22.9 0.8 dynamic_slice.16
  23.7 2.0 %select_reduce_fusion = s32[256]{0:T(256)S(1)} fusion(s32[8192]{0:T(1024)} %param.9, s32[256]{0:T(256)S(1)} %iota_add_fusion.3), kind=kLoop, calls=%fused_computation.1 | loop fusion | flops 6291200 | bytes 34816 | tf_op jit(solution)/shard_map/reduce_sum | solution.py:143
  25.7 0.2 convert_reduce_fusion
  25.9 13.8 %all-to-all-done = bf16[64,16,256]{2,1,0:T(8,128)(2,1)S(1)} async-done(((bf16[64,16,256]{2,1,0:T(8,128)(2,1)}), bf16[64,16,256]{2,1,0:T(8,128)(2,1)S(1)}, u32[]{:S(2)}, u32[]{:S(2)}) %all-to-all-start) | async-done | bytes 524320 | tf_op jit(solution)/shard_map/all_to_all | solution.py:117
  39.6 3.5 %collective-permute-start = (bf16[1024,256]{1,0:T(8,128)(2,1)S(1)}, bf16[1024,256]{1,0:T(8,128)(2,1)S(1)}, u32[]{:S(2)}, u32[]{:S(2)}) collective-permute-start(bf16[1024,256]{1,0:T(8,128)(2,1)S(1)} %bitcast.19), channel_id=1, source_target_pairs={{0,64},{64,128},{128,192},{192,256},{256,320},{320,384},{384,448},... | collective-permute-start | bytes 1572872 | tf_op jit(solution)/shard_map/ppermute | solution.py:130
  43.3 0.8 copy.14.refs_1_.refs_2_
  44.1 0.8 copy.15.refs_2_.refs_3_
  44.9 0.6 iota_add_fusion.2.refs_3_
  45.5 1.3 pad_dynamic-slice_fusion.1
  46.8 0.8 convolution_convert_fusion.2.q_ref
  47.7 3.3 %shard_map.64 = (f32[2,256,1]{2,1,0:T(8,128)}, f32[2,256,1]{2,1,0:T(8,128)}, f32[256,256]{1,0:T(8,128)}) custom-call(bf16[256,256]{1,0:T(8,128)(2,1)} %convolution_convert_fusion.2.q_ref, bf16[1024,256]{1,0:T(8,128)(2,1)} %bitcast.20, s32[256,1]{1,0:T(8,128)} %copy.14.refs_1_.refs_2_, s32[256,1]{1,0:T(8,128)} %copy.15.refs_2_.refs_3_, ...), custom_call_target="tpu_custom_call" | custom-call | flops 268435456 | bytes 786432 | tf_op jit(solution)/shard_map/pallas_call | solution.py:81
  51.0 3.8 %collective-permute-done.refs_0_ = bf16[1024,256]{1,0:T(8,128)(2,1)S(1)} collective-permute-done((bf16[1024,256]{1,0:T(8,128)(2,1)S(1)}, bf16[1024,256]{1,0:T(8,128)(2,1)S(1)}, u32[]{:S(2)}, u32[]{:S(2)}) %collective-permute-start) | collective-permute-done | bytes 524320 | tf_op jit(solution)/shard_map/ppermute | solution.py:130
  54.8 2.6 %collective-permute-start.1 = (bf16[1024,256]{1,0:T(8,128)(2,1)S(1)}, bf16[1024,256]{1,0:T(8,128)(2,1)S(1)}, u32[]{:S(2)}, u32[]{:S(2)}) collective-permute-start(bf16[1024,256]{1,0:T(8,128)(2,1)S(1)} %collective-permute-done.refs_0_), channel_id=1, source_target_pairs={{0,1},{1,0},{2,3},{3,2},{4,5},{5,4},{6,7},{7,6},{8,9},{9,8},{10,11... | collective-permute-start | bytes 1572872 | tf_op jit(solution)/shard_map/ppermute | solution.py:154
  57.4 0.8 and_select_fusion
  58.2 0.6 pad_add_fusion.refs_4_
  58.8 0.6 pad_add_fusion.1.refs_5_
  59.4 0.2 convert_reduce_fusion.1
  59.6 0.8 copy-done.4
  60.4 4.9 %shard_map.65 = bf16[256,256]{1,0:T(8,128)(2,1)} custom-call(bf16[256,256]{1,0:T(8,128)(2,1)} %convolution_convert_fusion.2.q_ref, bf16[1024,256]{1,0:T(8,128)(2,1)} %copy-done.3, bf16[1024,256]{1,0:T(8,128)(2,1)} %copy-done.4, s32[256,1]{1,0:T(8,128)} %copy.14.refs_1_.refs_2_, s32[256,1]{1,0:T(8,128)} %copy.15.refs_2_.refs_3_, ...), custom_call_target="tpu_custom_call" | custom-call | flops 536870912 | bytes 1310720 | tf_op jit(solution)/shard_map/pallas_call | solution.py:81
  65.3 17.5 %all-to-all-start.1 = ((bf16[32,8,256]{2,1,0:T(8,128)(2,1)}), bf16[32,8,256]{2,1,0:T(8,128)(2,1)S(1)}, u32[]{:S(2)}, u32[]{:S(2)}) async-start(bf16[32,8,256]{2,1,0:T(8,128)(2,1)} %bitcast.18), calls=%async_computation.1 | async-start | bytes 262144 | tf_op jit(solution)/shard_map/all_to_all | solution.py:159
  82.9 0.8 multiply_add_fusion
  84.0 8.4 %all-to-all-done.1 = bf16[32,8,256]{2,1,0:T(8,128)(2,1)S(1)} async-done(((bf16[32,8,256]{2,1,0:T(8,128)(2,1)}), bf16[32,8,256]{2,1,0:T(8,128)(2,1)S(1)}, u32[]{:S(2)}, u32[]{:S(2)}) %all-to-all-start.1) | async-done | bytes 131104 | tf_op jit(solution)/shard_map/all_to_all | solution.py:159
  92.3 5.5 %convolution_convert_fusion = bf16[256,8192]{1,0:T(8,128)(2,1)} fusion(bf16[256,8192]{1,0:T(8,128)(2,1)} %param.13, bf16[32,8,256]{2,1,0:T(8,128)(2,1)S(1)} %all-to-all-done.1, s32[256]{0:T(256)S(1)} %pad_add_fusion.2), kind=kOutput, calls=%fused_computation | convolution fusion | flops 1109524480 | bytes 8520704 | tf_op jit(solution)/shard_map/dot_general | solution.py:174
  97.9 1.9 %slice.18 = bf16[128,8192]{1,0:T(8,128)(2,1)S(1)} slice(bf16[256,8192]{1,0:T(8,128)(2,1)} %convolution_convert_fusion), slice={[0:128], [0:8192]} | slice | bytes 4194304 | tf_op jit(solution)/shard_map/slice | solution.py:176
  99.7 1.9 %collective-permute-start.2 = (bf16[128,8192]{1,0:T(8,128)(2,1)S(1)}, bf16[128,8192]{1,0:T(8,128)(2,1)S(1)}, u32[]{:S(2)}, u32[]{:S(2)}) collective-permute-start(bf16[128,8192]{1,0:T(8,128)(2,1)S(1)} %slice.18), channel_id=1, source_target_pairs={{0,1},{1,0},{2,3},{3,2},{4,5},{5,4},{6,7},{7,6},{8,9},{9,8},{10,11... | collective-permute-start | bytes 6291464 | tf_op jit(solution)/shard_map/ppermute | solution.py:176
  101.7 4.1 %collective-permute-done.2 = bf16[128,8192]{1,0:T(8,128)(2,1)S(1)} collective-permute-done((bf16[128,8192]{1,0:T(8,128)(2,1)S(1)}, bf16[128,8192]{1,0:T(8,128)(2,1)S(1)}, u32[]{:S(2)}, u32[]{:S(2)}) %collective-permute-start.2) | collective-permute-done | bytes 2097184 | tf_op jit(solution)/shard_map/ppermute | solution.py:176
  105.8 1.8 %add_convert_fusion = bf16[128,8192]{1,0:T(8,128)(2,1)} fusion(bf16[128,8192]{1,0:T(8,128)(2,1)S(1)} %collective-permute-done.2, bf16[256,8192]{1,0:T(8,128)(2,1)S(1)} %copy-done.1), kind=kLoop, calls=%fused_computation.2 | loop fusion | flops 4194304 | bytes 6291456 | tf_op jit(solution)/shard_map/convert_element_type | solution.py:178
  107.7 37.4 %reduce-scatter.2.cloned.1.call-done = bf16[16,8192]{1,0:T(8,128)(2,1)} async-done(((bf16[128,8192]{1,0:T(8,128)(2,1)}), bf16[16,8192]{1,0:T(8,128)(2,1)}) %reduce-scatter.2.cloned.1.call-update) | async-done | bytes 262160 | tf_op jit(solution)/shard_map/reduce_scatter | solution.py:179
  (22 shorter events, 0.5 us)
Async XLA Ops:
  6.5 40.3 %copy-start = (bf16[256,256]{1,0:T(8,128)(2,1)S(1)}, bf16[256,256]{1,0:T(8,128)(2,1)}, u32[]{:S(2)}) copy-start(bf16[256,256]{1,0:T(8,128)(2,1)} %param.10) | copy-start | bytes 393220
  8.9 30.7 %all-to-all-start = ((bf16[64,16,256]{2,1,0:T(8,128)(2,1)}), bf16[64,16,256]{2,1,0:T(8,128)(2,1)S(1)}, u32[]{:S(2)}, u32[]{:S(2)}) async-start(bf16[64,16,256]{2,1,0:T(8,128)(2,1)} %bitcast.4), calls=%async_computation | async-start | bytes 1048576 | tf_op jit(solution)/shard_map/all_to_all | solution.py:117
  39.6 8.0 %copy-start.2 = (bf16[64,16,256]{2,1,0:T(8,128)(2,1)}, bf16[64,16,256]{2,1,0:T(8,128)(2,1)S(1)}, u32[]{:S(2)}) copy-start(bf16[64,16,256]{2,1,0:T(8,128)(2,1)S(1)} %all-to-all-done) | copy-start | bytes 1572868
  39.6 15.2 %collective-permute-start = (bf16[1024,256]{1,0:T(8,128)(2,1)S(1)}, bf16[1024,256]{1,0:T(8,128)(2,1)S(1)}, u32[]{:S(2)}, u32[]{:S(2)}) collective-permute-start(bf16[1024,256]{1,0:T(8,128)(2,1)S(1)} %bitcast.19), channel_id=1, source_target_pairs={{0,64},{64,128},{128,192},{192,256},{256,320},{320,384},{384,448},... | collective-permute-start | bytes 1572872 | tf_op jit(solution)/shard_map/ppermute | solution.py:130
  54.8 4.8 %copy-start.3 = (bf16[1024,256]{1,0:T(8,128)(2,1)}, bf16[1024,256]{1,0:T(8,128)(2,1)S(1)}, u32[]{:S(2)}) copy-start(bf16[1024,256]{1,0:T(8,128)(2,1)S(1)} %collective-permute-done.refs_0_) | copy-start | bytes 1572868
  54.8 4.8 %collective-permute-start.1 = (bf16[1024,256]{1,0:T(8,128)(2,1)S(1)}, bf16[1024,256]{1,0:T(8,128)(2,1)S(1)}, u32[]{:S(2)}, u32[]{:S(2)}) collective-permute-start(bf16[1024,256]{1,0:T(8,128)(2,1)S(1)} %collective-permute-done.refs_0_), channel_id=1, source_target_pairs={{0,1},{1,0},{2,3},{3,2},{4,5},{5,4},{6,7},{7,6},{8,9},{9,8},{10,11... | collective-permute-start | bytes 1572872 | tf_op jit(solution)/shard_map/ppermute | solution.py:154
  59.6 0.8 copy-start.4
  65.3 27.0 %all-to-all-start.1 = ((bf16[32,8,256]{2,1,0:T(8,128)(2,1)}), bf16[32,8,256]{2,1,0:T(8,128)(2,1)S(1)}, u32[]{:S(2)}, u32[]{:S(2)}) async-start(bf16[32,8,256]{2,1,0:T(8,128)(2,1)} %bitcast.18), calls=%async_computation.1 | async-start | bytes 262144 | tf_op jit(solution)/shard_map/all_to_all | solution.py:159
  82.8 62.3 %reduce-scatter.2.cloned.1.call-start = ((), (), s32[]{:S(2)}) async-start(), calls=%async_computation.3 | async-start | bytes 2359296 | tf_op jit(solution)/shard_map/reduce_scatter | solution.py:179
  97.9 7.9 %copy-start.1 = (bf16[256,8192]{1,0:T(8,128)(2,1)S(1)}, bf16[256,8192]{1,0:T(8,128)(2,1)}, u32[]{:S(2)}) copy-start(bf16[256,8192]{1,0:T(8,128)(2,1)} %convolution_convert_fusion) | copy-start | bytes 12582916
  99.7 6.1 %collective-permute-start.2 = (bf16[128,8192]{1,0:T(8,128)(2,1)S(1)}, bf16[128,8192]{1,0:T(8,128)(2,1)S(1)}, u32[]{:S(2)}, u32[]{:S(2)}) collective-permute-start(bf16[128,8192]{1,0:T(8,128)(2,1)S(1)} %slice.18), channel_id=1, source_target_pairs={{0,1},{1,0},{2,3},{3,2},{4,5},{5,4},{6,7},{7,6},{8,9},{9,8},{10,11... | collective-permute-start | bytes 6291464 | tf_op jit(solution)/shard_map/ppermute | solution.py:176
Sparse Core Ops, SparseCore 0:
  107.8 37.2 reduce-scatter.1

commit v19 on v15

--- a/solution.py
+++ b/solution.py
@@ -165,17 +165,13 @@
     per_dev = rows // (n_z * n_core)
     slot3 = slot.reshape(n_z, n_core, per_dev)
     cols = jnp.arange(rows, dtype=jnp.int32)[None, :]
-
-    def project(which):
-        chosen = jnp.take(slot3, which, axis=1).reshape(-1)
-        sel = (chosen[:, None] == cols).astype(jnp.bfloat16)
-        relaid = jnp.dot(sel, arrived, preferred_element_type=jnp.float32).astype(jnp.bfloat16)
-        return jnp.dot(relaid, out_weight, preferred_element_type=jnp.float32).astype(jnp.bfloat16)
-
-    part_other = project(n_core - 1 - c)
-    got = lax.ppermute(part_other, "core", perm=[(0, 1), (1, 0)])
-    part_own = lax.optimization_barrier(project(c))
-    half = (part_own.astype(jnp.float32) + got.astype(jnp.float32)).astype(jnp.bfloat16)
+    swap_pairs = [(i, (i + 1) % n_core) for i in range(n_core)]
+    w_pair = jnp.concatenate([out_weight, lax.ppermute(out_weight, "core", perm=swap_pairs)], axis=0)
+    both = jnp.concatenate([arrived, lax.ppermute(arrived, "core", perm=swap_pairs)], axis=1)
+    mine = jnp.take(slot3, c, axis=1).reshape(-1)
+    sel = (mine[:, None] == cols).astype(jnp.bfloat16)
+    relaid = jnp.dot(sel, both, preferred_element_type=jnp.float32).astype(jnp.bfloat16)
+    half = jnp.dot(relaid, w_pair, preferred_element_type=jnp.float32).astype(jnp.bfloat16)
     return lax.psum_scatter(half, "z", scatter_dimension=0, tiled=True)
 
 def solution(mesh):

time: 152 us -> 148 us (0.974)
  other arithmetic: 9.3 us -> 5.92 us
  starting transfers between devices: 39.6 us -> 42.1 us
  matrix products: 8.3 us -> 6.2 us
    convert_element_type x1 -> x0, other arithmetic: 3.39 us -> none  [shards(): (part_own.astype(jnp.float32) + got.astype(jnp.float32)).astype(jnp.bfloa...]
    dot_general x2 -> x1, matrix products: 7.46 us -> 5.35 us  [shards(): jnp.dot(relaid, w_pair, preferred_element_type=jnp.float32)]
    ppermute x1 -> x2, starting transfers between devices: 1.91 us -> 3.95 us  [the longest x1 2.04 us: shards(): lax.ppermute(out_weight, 'core', perm=swap_pairs)]
  transfers between devices with their start and end apart: 6 -> 7, of which waited for: 5 -> 6; matrix products, arithmetic and copies ran while one was open for 9% -> 9% of each run, Pallas kernels for 2% -> 6%
where the time goes in v19:
time: 148 us; the launch traced here: 147 us
  waiting for transfers between devices  64 us (43%)
  starting transfers between devices  42.1 us (28%)
  between operations  13.5 us (9%)
  Pallas kernels  8.23 us (6%)
  local copies, waits for them, and re-layouts  6.93 us (5%)
  matrix products  6.2 us (4%)
  other arithmetic  5.92 us (4%)
    reduce_scatter x1, waiting for transfers between devices, shards(): return lax.psum_scatter(half, 'z', scatter_dimension=0, tiled=True)  37.8 us
    all_to_all x1, starting transfers between devices, shards(): lax.all_to_all(to_send, ('y', 'x'), split_axis=0, concat_axis=0, tiled=True)  17.9 us
    all_to_all x1, starting transfers between devices, shards(): lax.all_to_all(pieces, ('x', 'z', 'core'), split_axis=0, concat_axis=0, t...  14.1 us
    all_to_all x1, waiting for transfers between devices, shards(): lax.all_to_all(pieces, ('x', 'z', 'core'), split_axis=0, concat_axis=0, t...  13.8 us
    pallas_call x2, Pallas kernels, attention(): pl.pallas_call(functools.partial(_attention_body, scale, n_pieces, heads,...  8.23 us
    all_to_all x1, waiting for transfers between devices, shards(): lax.all_to_all(to_send, ('y', 'x'), split_axis=0, concat_axis=0, tiled=True)  8.02 us
    dot_general x1, matrix products, shards(): jnp.dot(relaid, w_pair, preferred_element_type=jnp.float32)  5.35 us
    ppermute x1, waiting for transfers between devices, shards(): fetched = lax.ppermute(row, ('y', 'core'), perm=perm)  3.83 us
  transfers between devices with their start and end apart: 7, of which 6 were waited for; matrix products, arithmetic and copies ran while one was open for 9% of the time, Pallas kernels for 6%

profile of v19, /device:TPU:6, one launch (start us, length us, event | category | flops | bytes accessed | tf_op | source)
XLA Modules:
  0.0 146.9 jit_solution(627412655395914171)
XLA Ops:
  6.5 2.0 %collective-permute-start.3 = (bf16[256,8192]{1,0:T(8,128)(2,1)}, bf16[256,8192]{1,0:T(8,128)(2,1)}, u32[]{:S(2)}, u32[]{:S(2)}) collective-permute-start(bf16[256,8192]{1,0:T(8,128)(2,1)} %param.11), channel_id=1, source_target_pairs={{0,1},{1,0},{2,3},{3,2},{4,5},{5,4},{6,7},{7,6},{8,9},{9,8},{10,11... | collective-permute-start | bytes 12582920 | tf_op jit(solution)/shard_map/ppermute | solution.py:169
  8.6 0.7 reshape.72
  9.3 0.7 reshape.73
  10.1 0.8 broadcast_in_dim.68
  10.9 14.1 %all-to-all-start = ((bf16[64,16,256]{2,1,0:T(8,128)(2,1)}), bf16[64,16,256]{2,1,0:T(8,128)(2,1)S(1)}, u32[]{:S(2)}, u32[]{:S(2)}) async-start(bf16[64,16,256]{2,1,0:T(8,128)(2,1)} %bitcast.2), calls=%async_computation | async-start | bytes 1048576 | tf_op jit(solution)/shard_map/all_to_all | solution.py:117
  25.1 0.8 dynamic_slice.16
  25.8 2.0 %select_reduce_fusion = s32[256]{0:T(256)S(1)} fusion(s32[8192]{0:T(1024)} %param.7, s32[256]{0:T(256)S(1)} %iota_add_fusion.3), kind=kLoop, calls=%fused_computation.4 | loop fusion | flops 6291200 | bytes 34816 | tf_op jit(solution)/shard_map/reduce_sum | solution.py:143
  27.8 0.2 convert_reduce_fusion
  28.0 13.8 %all-to-all-done = bf16[64,16,256]{2,1,0:T(8,128)(2,1)S(1)} async-done(((bf16[64,16,256]{2,1,0:T(8,128)(2,1)}), bf16[64,16,256]{2,1,0:T(8,128)(2,1)S(1)}, u32[]{:S(2)}, u32[]{:S(2)}) %all-to-all-start) | async-done | bytes 524320 | tf_op jit(solution)/shard_map/all_to_all | solution.py:117
  41.8 3.5 %collective-permute-start = (bf16[1024,256]{1,0:T(8,128)(2,1)S(1)}, bf16[1024,256]{1,0:T(8,128)(2,1)S(1)}, u32[]{:S(2)}, u32[]{:S(2)}) collective-permute-start(bf16[1024,256]{1,0:T(8,128)(2,1)S(1)} %bitcast.13), channel_id=1, source_target_pairs={{0,64},{64,128},{128,192},{192,256},{256,320},{320,384},{384,448},... | collective-permute-start | bytes 1572872 | tf_op jit(solution)/shard_map/ppermute | solution.py:130
  45.5 0.8 copy.14.refs_1_.refs_2_
  46.3 0.8 copy.15.refs_2_.refs_3_
  47.0 0.6 iota_add_fusion.2.refs_3_
  47.6 1.3 pad_dynamic-slice_fusion.1
  48.9 0.8 convolution_convert_fusion.2.q_ref
  49.8 3.3 %shard_map.64 = (f32[2,256,1]{2,1,0:T(8,128)}, f32[2,256,1]{2,1,0:T(8,128)}, f32[256,256]{1,0:T(8,128)}) custom-call(bf16[256,256]{1,0:T(8,128)(2,1)} %convolution_convert_fusion.2.q_ref, bf16[1024,256]{1,0:T(8,128)(2,1)} %bitcast.14, s32[256,1]{1,0:T(8,128)} %copy.14.refs_1_.refs_2_, s32[256,1]{1,0:T(8,128)} %copy.15.refs_2_.refs_3_, ...), custom_call_target="tpu_custom_call" | custom-call | flops 268435456 | bytes 786432 | tf_op jit(solution)/shard_map/pallas_call | solution.py:81
  53.1 3.8 %collective-permute-done.refs_0_ = bf16[1024,256]{1,0:T(8,128)(2,1)S(1)} collective-permute-done((bf16[1024,256]{1,0:T(8,128)(2,1)S(1)}, bf16[1024,256]{1,0:T(8,128)(2,1)S(1)}, u32[]{:S(2)}, u32[]{:S(2)}) %collective-permute-start) | collective-permute-done | bytes 524320 | tf_op jit(solution)/shard_map/ppermute | solution.py:130
  56.9 2.6 %collective-permute-start.1 = (bf16[1024,256]{1,0:T(8,128)(2,1)S(1)}, bf16[1024,256]{1,0:T(8,128)(2,1)S(1)}, u32[]{:S(2)}, u32[]{:S(2)}) collective-permute-start(bf16[1024,256]{1,0:T(8,128)(2,1)S(1)} %collective-permute-done.refs_0_), channel_id=1, source_target_pairs={{0,1},{1,0},{2,3},{3,2},{4,5},{5,4},{6,7},{7,6},{8,9},{9,8},{10,11... | collective-permute-start | bytes 1572872 | tf_op jit(solution)/shard_map/ppermute | solution.py:154
  59.6 0.6 pad_add_fusion.refs_4_
  60.2 0.6 pad_add_fusion.1.refs_5_
  60.8 0.3 collective-permute-done.1.refs_1_
  61.1 0.8 copy-done.3
  61.9 4.9 %shard_map.65 = bf16[256,256]{1,0:T(8,128)(2,1)} custom-call(bf16[256,256]{1,0:T(8,128)(2,1)} %convolution_convert_fusion.2.q_ref, bf16[1024,256]{1,0:T(8,128)(2,1)} %copy-done.2, bf16[1024,256]{1,0:T(8,128)(2,1)} %copy-done.3, s32[256,1]{1,0:T(8,128)} %copy.14.refs_1_.refs_2_, s32[256,1]{1,0:T(8,128)} %copy.15.refs_2_.refs_3_, ...), custom_call_target="tpu_custom_call" | custom-call | flops 536870912 | bytes 1310720 | tf_op jit(solution)/shard_map/pallas_call | solution.py:81
  66.8 17.9 %all-to-all-start.1 = ((bf16[32,8,256]{2,1,0:T(8,128)(2,1)}), bf16[32,8,256]{2,1,0:T(8,128)(2,1)S(1)}, u32[]{:S(2)}, u32[]{:S(2)}) async-start(bf16[32,8,256]{2,1,0:T(8,128)(2,1)} %bitcast.12), calls=%async_computation.1 | async-start | bytes 262144 | tf_op jit(solution)/shard_map/all_to_all | solution.py:159
  84.7 0.8 and_select_fusion
  85.5 0.2 convert_reduce_fusion.1
  85.7 8.0 %all-to-all-done.1 = bf16[32,8,256]{2,1,0:T(8,128)(2,1)S(1)} async-done(((bf16[32,8,256]{2,1,0:T(8,128)(2,1)}), bf16[32,8,256]{2,1,0:T(8,128)(2,1)S(1)}, u32[]{:S(2)}, u32[]{:S(2)}) %all-to-all-start.1) | async-done | bytes 131104 | tf_op jit(solution)/shard_map/all_to_all | solution.py:159
  93.7 1.9 %collective-permute-start.2 = (bf16[256,256]{1,0:T(8,128)(2,1)S(1)}, bf16[256,256]{1,0:T(8,128)(2,1)S(1)}, u32[]{:S(2)}, u32[]{:S(2)}) collective-permute-start(bf16[256,256]{1,0:T(8,128)(2,1)S(1)} %bitcast.15), channel_id=1, source_target_pairs={{0,1},{1,0},{2,3},{3,2},{4,5},{5,4},{6,7},{7,6},{8,9},{9,8},{10,11... | collective-permute-start | bytes 393224 | tf_op jit(solution)/shard_map/ppermute | solution.py:170
  95.6 0.8 multiply_add_fusion
  96.6 0.3 collective-permute-done.2
  96.9 5.4 %convolution_convert_fusion = bf16[128,8192]{1,0:T(8,128)(2,1)} fusion(bf16[256,8192]{1,0:T(8,128)(2,1)} %collective-permute-done.3, bf16[256,8192]{1,0:T(8,128)(2,1)} %param.11, bf16[256,256]{1,0:T(8,128)(2,1)S(1)} %collective-permute-done.2, bf16[256,256]{1,0:T(8,128)(2,1)S(1)} %bitcast.16, s32[128]{0:T(128)S(1)} %select_n.49), kind=kOutput, calls=%fused_computation | convolution fusion | flops 1125744640 | bytes 10748416 | tf_op jit(solution)/shard_map/dot_general | solution.py:174
  102.3 37.8 %reduce-scatter.2.cloned.1.call-done = bf16[16,8192]{1,0:T(8,128)(2,1)} async-done(((bf16[128,8192]{1,0:T(8,128)(2,1)}), bf16[16,8192]{1,0:T(8,128)(2,1)}) %reduce-scatter.2.cloned.1.call-update) | async-done | bytes 262160 | tf_op jit(solution)/shard_map/reduce_scatter | solution.py:175
  (18 shorter events, 0.5 us)
Async XLA Ops:
  6.5 42.4 %copy-start = (bf16[256,256]{1,0:T(8,128)(2,1)S(1)}, bf16[256,256]{1,0:T(8,128)(2,1)}, u32[]{:S(2)}) copy-start(bf16[256,256]{1,0:T(8,128)(2,1)} %param.8) | copy-start | bytes 393220
  6.5 90.4 %collective-permute-start.3 = (bf16[256,8192]{1,0:T(8,128)(2,1)}, bf16[256,8192]{1,0:T(8,128)(2,1)}, u32[]{:S(2)}, u32[]{:S(2)}) collective-permute-start(bf16[256,8192]{1,0:T(8,128)(2,1)} %param.11), channel_id=1, source_target_pairs={{0,1},{1,0},{2,3},{3,2},{4,5},{5,4},{6,7},{7,6},{8,9},{9,8},{10,11... | collective-permute-start | bytes 12582920 | tf_op jit(solution)/shard_map/ppermute | solution.py:169
  10.9 30.8 %all-to-all-start = ((bf16[64,16,256]{2,1,0:T(8,128)(2,1)}), bf16[64,16,256]{2,1,0:T(8,128)(2,1)S(1)}, u32[]{:S(2)}, u32[]{:S(2)}) async-start(bf16[64,16,256]{2,1,0:T(8,128)(2,1)} %bitcast.2), calls=%async_computation | async-start | bytes 1048576 | tf_op jit(solution)/shard_map/all_to_all | solution.py:117
  41.8 8.0 %copy-start.1 = (bf16[64,16,256]{2,1,0:T(8,128)(2,1)}, bf16[64,16,256]{2,1,0:T(8,128)(2,1)S(1)}, u32[]{:S(2)}) copy-start(bf16[64,16,256]{2,1,0:T(8,128)(2,1)S(1)} %all-to-all-done) | copy-start | bytes 1572868
  41.8 15.2 %collective-permute-start = (bf16[1024,256]{1,0:T(8,128)(2,1)S(1)}, bf16[1024,256]{1,0:T(8,128)(2,1)S(1)}, u32[]{:S(2)}, u32[]{:S(2)}) collective-permute-start(bf16[1024,256]{1,0:T(8,128)(2,1)S(1)} %bitcast.13), channel_id=1, source_target_pairs={{0,64},{64,128},{128,192},{192,256},{256,320},{320,384},{384,448},... | collective-permute-start | bytes 1572872 | tf_op jit(solution)/shard_map/ppermute | solution.py:130
  56.9 4.1 %copy-start.2 = (bf16[1024,256]{1,0:T(8,128)(2,1)}, bf16[1024,256]{1,0:T(8,128)(2,1)S(1)}, u32[]{:S(2)}) copy-start(bf16[1024,256]{1,0:T(8,128)(2,1)S(1)} %collective-permute-done.refs_0_) | copy-start | bytes 1572868
  56.9 4.1 %collective-permute-start.1 = (bf16[1024,256]{1,0:T(8,128)(2,1)S(1)}, bf16[1024,256]{1,0:T(8,128)(2,1)S(1)}, u32[]{:S(2)}, u32[]{:S(2)}) collective-permute-start(bf16[1024,256]{1,0:T(8,128)(2,1)S(1)} %collective-permute-done.refs_0_), channel_id=1, source_target_pairs={{0,1},{1,0},{2,3},{3,2},{4,5},{5,4},{6,7},{7,6},{8,9},{9,8},{10,11... | collective-permute-start | bytes 1572872 | tf_op jit(solution)/shard_map/ppermute | solution.py:154
  61.1 0.8 copy-start.3
  66.8 26.9 %all-to-all-start.1 = ((bf16[32,8,256]{2,1,0:T(8,128)(2,1)}), bf16[32,8,256]{2,1,0:T(8,128)(2,1)S(1)}, u32[]{:S(2)}, u32[]{:S(2)}) async-start(bf16[32,8,256]{2,1,0:T(8,128)(2,1)} %bitcast.12), calls=%async_computation.1 | async-start | bytes 262144 | tf_op jit(solution)/shard_map/all_to_all | solution.py:159
  84.7 55.4 %reduce-scatter.2.cloned.1.call-start = ((), (), s32[]{:S(2)}) async-start(), calls=%async_computation.3 | async-start | bytes 2359296 | tf_op jit(solution)/shard_map/reduce_scatter | solution.py:175
  93.7 3.2 %collective-permute-start.2 = (bf16[256,256]{1,0:T(8,128)(2,1)S(1)}, bf16[256,256]{1,0:T(8,128)(2,1)S(1)}, u32[]{:S(2)}, u32[]{:S(2)}) collective-permute-start(bf16[256,256]{1,0:T(8,128)(2,1)S(1)} %bitcast.15), channel_id=1, source_target_pairs={{0,1},{1,0},{2,3},{3,2},{4,5},{5,4},{6,7},{7,6},{8,9},{9,8},{10,11... | collective-permute-start | bytes 393224 | tf_op jit(solution)/shard_map/ppermute | solution.py:170
Sparse Core Ops, SparseCore 0:
  102.4 37.6 reduce-scatter.1

commit v20 on v19

--- a/solution.py
+++ b/solution.py
@@ -112,9 +112,11 @@
     v_h = jnp.transpose(values.reshape(values.shape[0], kv_heads, HD), (1, 0, 2))
     kv_h = jnp.concatenate([k_h, v_h], axis=2)
     pieces = jnp.broadcast_to(
-        kv_h[None, :, None], (n_x, kv_heads, share) + kv_h.shape[1:]
-    ).reshape((n_x * n_tp,) + kv_h.shape[1:])
-    row = lax.all_to_all(pieces, ("x", "z", "core"), split_axis=0, concat_axis=0, tiled=True)
+        kv_h[None, :, None], (n_x, kv_heads, n_z // kv_heads) + kv_h.shape[1:]
+    ).reshape((n_x * n_z,) + kv_h.shape[1:])
+    mine = lax.all_to_all(pieces, ("x", "z"), split_axis=0, concat_axis=0, tiled=True)
+    other = lax.ppermute(mine, "core", perm=[(i, (i + 1) % n_core) for i in range(n_core)])
+    row = jnp.stack([mine.reshape(n_x, n_z, -1, 2 * HD), other.reshape(n_x, n_z, -1, 2 * HD)], axis=2)
     row = row.reshape(n_x * rows, 2 * HD)
 
     n_y = lax.axis_size("y")
@@ -131,10 +133,20 @@
     y = lax.axis_index("y")
     span = n_x * rows
     piece_rows = [y - 1 - c, y - n_core + c, y]
-    k_pos = jnp.stack([r * span + jnp.arange(span, dtype=jnp.int32) for r in piece_rows])
+    makers = [c, n_core - 1 - c, c]
+
+    def in_order(vec, p):
+        v = vec.reshape(n_x, n_z, n_core, -1)
+        return jnp.where(p == 0, v, v[:, :, ::-1, :]).reshape(-1)
+
+    k_pos = jnp.stack(
+        [in_order(r * span + jnp.arange(span, dtype=jnp.int32), p) for r, p in zip(piece_rows, makers)]
+    )
     pad = rows_back * span
     seg_pad = jnp.concatenate([jnp.full((pad,), -1, jnp.int32), segment_ids])
-    k_seg = jnp.stack([lax.dynamic_slice_in_dim(seg_pad, r * span + pad, span, 0) for r in piece_rows])
+    k_seg = jnp.stack(
+        [in_order(lax.dynamic_slice_in_dim(seg_pad, r * span + pad, span, 0), p) for r, p in zip(piece_rows, makers)]
+    )
     q_pos = s * rows + jnp.arange(rows, dtype=jnp.int32)
     q_seg = lax.dynamic_slice_in_dim(segment_ids, s * rows, rows, 0)
     chunk = rows // n_seq

time: 148 us -> 146 us (0.986)
  waiting for transfers between devices: 64 us -> 60.1 us
  local copies, waits for them, and re-layouts: 6.93 us -> 8.71 us
    all_to_all x1, waiting for transfers between devices: 13.8 us -> 9.29 us  [shards(): lax.all_to_all(pieces, ('x', 'z'), split_axis=0, concat_axis=0, tiled=True)]
    another operation x0 -> x7, local copies, waits for them, and re-layouts: none -> 1.91 us  [the longest x3 0.92 us: shards(): jnp.stack([in_order(lax.dynamic_slice_in_dim(seg_pad, r * span + pad, spa...]
    ppermute x0 -> x1, starting transfers between devices: none -> 1.91 us  [shards(): lax.ppermute(mine, 'core', perm=[(i, (i + 1) % n_core) for i in range(n_c...]
  transfers between devices with their start and end apart: 7 -> 8, of which waited for: 6 -> 6; matrix products, arithmetic and copies ran while one was open for 9% -> 10% of each run, Pallas kernels for 6% -> 6%
where the time goes in v20:
time: 146 us; the launch traced here: 145 us
  waiting for transfers between devices  60.1 us (41%)
  starting transfers between devices  42.5 us (29%)
  between operations  13.6 us (9%)
  local copies, waits for them, and re-layouts  8.71 us (6%)
  Pallas kernels  8.24 us (6%)
  matrix products  6.2 us (4%)
  other arithmetic  5.48 us (4%)
    reduce_scatter x1, waiting for transfers between devices, shards(): return lax.psum_scatter(half, 'z', scatter_dimension=0, tiled=True)  38.1 us
    all_to_all x1, starting transfers between devices, shards(): lax.all_to_all(to_send, ('y', 'x'), split_axis=0, concat_axis=0, tiled=True)  17.3 us
    all_to_all x1, starting transfers between devices, shards(): lax.all_to_all(pieces, ('x', 'z'), split_axis=0, concat_axis=0, tiled=True)  13.5 us
    all_to_all x1, waiting for transfers between devices, shards(): lax.all_to_all(pieces, ('x', 'z'), split_axis=0, concat_axis=0, tiled=True)  9.29 us
    all_to_all x1, waiting for transfers between devices, shards(): lax.all_to_all(to_send, ('y', 'x'), split_axis=0, concat_axis=0, tiled=True)  8.45 us
    pallas_call x2, Pallas kernels, attention(): pl.pallas_call(functools.partial(_attention_body, scale, n_pieces, heads,...  8.24 us
    dot_general x1, matrix products, shards(): jnp.dot(relaid, w_pair, preferred_element_type=jnp.float32)  5.35 us
    ppermute x1, waiting for transfers between devices, shards(): fetched = lax.ppermute(row, ('y', 'core'), perm=perm)  3.65 us
  transfers between devices with their start and end apart: 8, of which 6 were waited for; matrix products, arithmetic and copies ran while one was open for 10% of the time, Pallas kernels for 6%

profile of v20, /device:TPU:6, one launch (start us, length us, event | category | flops | bytes accessed | tf_op | source)
XLA Modules:
  0.0 144.8 jit_solution(157174663378922744)
XLA Ops:
  6.5 2.0 %collective-permute-start.4 = (bf16[256,8192]{1,0:T(8,128)(2,1)}, bf16[256,8192]{1,0:T(8,128)(2,1)}, u32[]{:S(2)}, u32[]{:S(2)}) collective-permute-start(bf16[256,8192]{1,0:T(8,128)(2,1)} %param.11), channel_id=1, source_target_pairs={{0,1},{1,0},{2,3},{3,2},{4,5},{5,4},{6,7},{7,6},{8,9},{9,8},{10,11... | collective-permute-start | bytes 12582920 | tf_op jit(solution)/shard_map/ppermute | solution.py:181
  8.6 0.7 reshape.66
  9.3 0.7 reshape.67
  10.1 0.7 broadcast_in_dim.68
  10.8 13.5 %all-to-all-start = ((bf16[32,16,256]{2,1,0:T(8,128)(2,1)}), bf16[32,16,256]{2,1,0:T(8,128)(2,1)S(1)}, u32[]{:S(2)}, u32[]{:S(2)}) async-start(bf16[32,16,256]{2,1,0:T(8,128)(2,1)} %bitcast.2), calls=%async_computation | async-start | bytes 524288 | tf_op jit(solution)/shard_map/all_to_all | solution.py:117
  24.3 2.0 %select_reduce_fusion = s32[256]{0:T(256)S(1)} fusion(s32[8192]{0:T(1024)} %param.7, s32[256]{0:T(256)S(1)} %iota_add_fusion), kind=kLoop, calls=%fused_computation.4 | loop fusion | flops 6291200 | bytes 34816 | tf_op jit(solution)/shard_map/reduce_sum | solution.py:155
  26.3 9.3 %all-to-all-done = bf16[32,16,256]{2,1,0:T(8,128)(2,1)S(1)} async-done(((bf16[32,16,256]{2,1,0:T(8,128)(2,1)}), bf16[32,16,256]{2,1,0:T(8,128)(2,1)S(1)}, u32[]{:S(2)}, u32[]{:S(2)}) %all-to-all-start) | async-done | bytes 262176 | tf_op jit(solution)/shard_map/all_to_all | solution.py:117
  35.6 1.9 %collective-permute-start = (bf16[32,16,256]{2,1,0:T(8,128)(2,1)S(1)}, bf16[32,16,256]{2,1,0:T(8,128)(2,1)S(1)}, u32[]{:S(2)}, u32[]{:S(2)}) collective-permute-start(bf16[32,16,256]{2,1,0:T(8,128)(2,1)S(1)} %all-to-all-done), channel_id=1, source_target_pairs={{0,1},{1,0},{2,3},{3,2},{4,5},{5,4},{6,7},{7,6},{8,9},{9,8},{10,11... | collective-permute-start | bytes 786440 | tf_op jit(solution)/shard_map/ppermute | solution.py:118
  37.5 0.7 pad_dynamic-slice_fusion.1
  38.8 0.3 collective-permute-done
  39.1 3.5 %collective-permute-start.1 = (bf16[1024,256]{1,0:T(8,128)(2,1)S(1)}, bf16[1024,256]{1,0:T(8,128)(2,1)S(1)}, u32[]{:S(2)}, u32[]{:S(2)}) collective-permute-start(bf16[1024,256]{1,0:T(8,128)(2,1)S(1)} %bitcast.19), channel_id=1, source_target_pairs={{0,64},{64,128},{128,192},{192,256},{256,320},{320,384},{384,448},... | collective-permute-start | bytes 1572872 | tf_op jit(solution)/shard_map/ppermute | solution.py:132
  42.6 0.8 dynamic_slice.16
  43.4 0.7 stack_reshape.27.refs_4_
  44.1 0.7 stack_reshape.26.refs_3_
  45.2 0.8 copy.14.refs_1_.refs_2_
  46.0 0.8 copy.15.refs_2_.refs_3_
  46.8 0.8 convolution_convert_fusion.2.q_ref
  47.6 3.3 %shard_map.64 = (f32[2,256,1]{2,1,0:T(8,128)}, f32[2,256,1]{2,1,0:T(8,128)}, f32[256,256]{1,0:T(8,128)}) custom-call(bf16[256,256]{1,0:T(8,128)(2,1)} %convolution_convert_fusion.2.q_ref, bf16[1024,256]{1,0:T(8,128)(2,1)} %bitcast.20, s32[256,1]{1,0:T(8,128)} %copy.14.refs_1_.refs_2_, s32[256,1]{1,0:T(8,128)} %copy.15.refs_2_.refs_3_, ...), custom_call_target="tpu_custom_call" | custom-call | flops 268435456 | bytes 786432 | tf_op jit(solution)/shard_map/pallas_call | solution.py:81
  50.9 3.6 %collective-permute-done.1.refs_0_ = bf16[1024,256]{1,0:T(8,128)(2,1)S(1)} collective-permute-done((bf16[1024,256]{1,0:T(8,128)(2,1)S(1)}, bf16[1024,256]{1,0:T(8,128)(2,1)S(1)}, u32[]{:S(2)}, u32[]{:S(2)}) %collective-permute-start.1) | collective-permute-done | bytes 524320 | tf_op jit(solution)/shard_map/ppermute | solution.py:132
  54.6 2.3 %collective-permute-start.2 = (bf16[1024,256]{1,0:T(8,128)(2,1)S(1)}, bf16[1024,256]{1,0:T(8,128)(2,1)S(1)}, u32[]{:S(2)}, u32[]{:S(2)}) collective-permute-start(bf16[1024,256]{1,0:T(8,128)(2,1)S(1)} %collective-permute-done.1.refs_0_), channel_id=1, source_target_pairs={{0,1},{1,0},{2,3},{3,2},{4,5},{5,4},{6,7},{7,6},{8,9},{9,8},{10,11... | collective-permute-start | bytes 1572872 | tf_op jit(solution)/shard_map/ppermute | solution.py:166
  57.6 0.6 pad_add_fusion.refs_4_
  58.2 0.6 pad_add_fusion.1.refs_5_
  58.8 0.8 copy-done.3
  59.6 4.9 %shard_map.65 = bf16[256,256]{1,0:T(8,128)(2,1)} custom-call(bf16[256,256]{1,0:T(8,128)(2,1)} %convolution_convert_fusion.2.q_ref, bf16[1024,256]{1,0:T(8,128)(2,1)} %copy-done.2, bf16[1024,256]{1,0:T(8,128)(2,1)} %copy-done.3, s32[256,1]{1,0:T(8,128)} %copy.14.refs_1_.refs_2_, s32[256,1]{1,0:T(8,128)} %copy.15.refs_2_.refs_3_, ...), custom_call_target="tpu_custom_call" | custom-call | flops 536870912 | bytes 1310720 | tf_op jit(solution)/shard_map/pallas_call | solution.py:81
  64.5 17.3 %all-to-all-start.1 = ((bf16[32,8,256]{2,1,0:T(8,128)(2,1)}), bf16[32,8,256]{2,1,0:T(8,128)(2,1)S(1)}, u32[]{:S(2)}, u32[]{:S(2)}) async-start(bf16[32,8,256]{2,1,0:T(8,128)(2,1)} %bitcast.18), calls=%async_computation.1 | async-start | bytes 262144 | tf_op jit(solution)/shard_map/all_to_all | solution.py:171
  81.9 0.8 and_select_fusion
  82.8 8.4 %all-to-all-done.1 = bf16[32,8,256]{2,1,0:T(8,128)(2,1)S(1)} async-done(((bf16[32,8,256]{2,1,0:T(8,128)(2,1)}), bf16[32,8,256]{2,1,0:T(8,128)(2,1)S(1)}, u32[]{:S(2)}, u32[]{:S(2)}) %all-to-all-start.1) | async-done | bytes 131104 | tf_op jit(solution)/shard_map/all_to_all | solution.py:171
  91.3 1.9 %collective-permute-start.3 = (bf16[256,256]{1,0:T(8,128)(2,1)S(1)}, bf16[256,256]{1,0:T(8,128)(2,1)S(1)}, u32[]{:S(2)}, u32[]{:S(2)}) collective-permute-start(bf16[256,256]{1,0:T(8,128)(2,1)S(1)} %bitcast.28), channel_id=1, source_target_pairs={{0,1},{1,0},{2,3},{3,2},{4,5},{5,4},{6,7},{7,6},{8,9},{9,8},{10,11... | collective-permute-start | bytes 393224 | tf_op jit(solution)/shard_map/ppermute | solution.py:182
  93.2 0.8 multiply_add_fusion.1
  94.2 0.3 collective-permute-done.3
  94.5 5.4 %convolution_convert_fusion = bf16[128,8192]{1,0:T(8,128)(2,1)} fusion(bf16[256,8192]{1,0:T(8,128)(2,1)} %collective-permute-done.4, bf16[256,8192]{1,0:T(8,128)(2,1)} %param.11, bf16[256,256]{1,0:T(8,128)(2,1)S(1)} %collective-permute-done.3, bf16[256,256]{1,0:T(8,128)(2,1)S(1)} %bitcast.29, s32[128]{0:T(128)S(1)} %select_n.79), kind=kOutput, calls=%fused_computation | convolution fusion | flops 1125744640 | bytes 10748416 | tf_op jit(solution)/shard_map/dot_general | solution.py:186
  99.9 38.1 %reduce-scatter.2.cloned.1.call-done = bf16[16,8192]{1,0:T(8,128)(2,1)} async-done(((bf16[128,8192]{1,0:T(8,128)(2,1)}), bf16[16,8192]{1,0:T(8,128)(2,1)}) %reduce-scatter.2.cloned.1.call-update) | async-done | bytes 262160 | tf_op jit(solution)/shard_map/reduce_scatter | solution.py:187
  (36 shorter events, 2.0 us)
Async XLA Ops:
  6.5 40.2 %copy-start = (bf16[256,256]{1,0:T(8,128)(2,1)S(1)}, bf16[256,256]{1,0:T(8,128)(2,1)}, u32[]{:S(2)}) copy-start(bf16[256,256]{1,0:T(8,128)(2,1)} %param.8) | copy-start | bytes 393220
  6.5 88.0 %collective-permute-start.4 = (bf16[256,8192]{1,0:T(8,128)(2,1)}, bf16[256,8192]{1,0:T(8,128)(2,1)}, u32[]{:S(2)}, u32[]{:S(2)}) collective-permute-start(bf16[256,8192]{1,0:T(8,128)(2,1)} %param.11), channel_id=1, source_target_pairs={{0,1},{1,0},{2,3},{3,2},{4,5},{5,4},{6,7},{7,6},{8,9},{9,8},{10,11... | collective-permute-start | bytes 12582920 | tf_op jit(solution)/shard_map/ppermute | solution.py:181
  10.8 24.8 %all-to-all-start = ((bf16[32,16,256]{2,1,0:T(8,128)(2,1)}), bf16[32,16,256]{2,1,0:T(8,128)(2,1)S(1)}, u32[]{:S(2)}, u32[]{:S(2)}) async-start(bf16[32,16,256]{2,1,0:T(8,128)(2,1)} %bitcast.2), calls=%async_computation | async-start | bytes 524288 | tf_op jit(solution)/shard_map/all_to_all | solution.py:117
  35.6 3.4 %collective-permute-start = (bf16[32,16,256]{2,1,0:T(8,128)(2,1)S(1)}, bf16[32,16,256]{2,1,0:T(8,128)(2,1)S(1)}, u32[]{:S(2)}, u32[]{:S(2)}) collective-permute-start(bf16[32,16,256]{2,1,0:T(8,128)(2,1)S(1)} %all-to-all-done), channel_id=1, source_target_pairs={{0,1},{1,0},{2,3},{3,2},{4,5},{5,4},{6,7},{7,6},{8,9},{9,8},{10,11... | collective-permute-start | bytes 786440 | tf_op jit(solution)/shard_map/ppermute | solution.py:118
  39.1 8.5 %copy-start.1 = (bf16[4,8,2,16,256]{4,3,2,1,0:T(8,128)(2,1)}, bf16[4,8,2,16,256]{4,3,2,1,0:T(8,128)(2,1)S(1)}, u32[]{:S(2)}) copy-start(bf16[4,8,2,16,256]{4,3,2,1,0:T(8,128)(2,1)S(1)} %pad_maximum_fusion) | copy-start | bytes 1572868
  39.1 15.5 %collective-permute-start.1 = (bf16[1024,256]{1,0:T(8,128)(2,1)S(1)}, bf16[1024,256]{1,0:T(8,128)(2,1)S(1)}, u32[]{:S(2)}, u32[]{:S(2)}) collective-permute-start(bf16[1024,256]{1,0:T(8,128)(2,1)S(1)} %bitcast.19), channel_id=1, source_target_pairs={{0,64},{64,128},{128,192},{192,256},{256,320},{320,384},{384,448},... | collective-permute-start | bytes 1572872 | tf_op jit(solution)/shard_map/ppermute | solution.py:132
  54.6 4.2 %copy-start.2 = (bf16[1024,256]{1,0:T(8,128)(2,1)}, bf16[1024,256]{1,0:T(8,128)(2,1)S(1)}, u32[]{:S(2)}) copy-start(bf16[1024,256]{1,0:T(8,128)(2,1)S(1)} %collective-permute-done.1.refs_0_) | copy-start | bytes 1572868
  54.6 4.2 %collective-permute-start.2 = (bf16[1024,256]{1,0:T(8,128)(2,1)S(1)}, bf16[1024,256]{1,0:T(8,128)(2,1)S(1)}, u32[]{:S(2)}, u32[]{:S(2)}) collective-permute-start(bf16[1024,256]{1,0:T(8,128)(2,1)S(1)} %collective-permute-done.1.refs_0_), channel_id=1, source_target_pairs={{0,1},{1,0},{2,3},{3,2},{4,5},{5,4},{6,7},{7,6},{8,9},{9,8},{10,11... | collective-permute-start | bytes 1572872 | tf_op jit(solution)/shard_map/ppermute | solution.py:166
  58.8 0.8 copy-start.3
  64.5 26.8 %all-to-all-start.1 = ((bf16[32,8,256]{2,1,0:T(8,128)(2,1)}), bf16[32,8,256]{2,1,0:T(8,128)(2,1)S(1)}, u32[]{:S(2)}, u32[]{:S(2)}) async-start(bf16[32,8,256]{2,1,0:T(8,128)(2,1)} %bitcast.18), calls=%async_computation.1 | async-start | bytes 262144 | tf_op jit(solution)/shard_map/all_to_all | solution.py:171
  81.8 56.1 %reduce-scatter.2.cloned.1.call-start = ((), (), s32[]{:S(2)}) async-start(), calls=%async_computation.3 | async-start | bytes 2359296 | tf_op jit(solution)/shard_map/reduce_scatter | solution.py:187
  91.3 3.2 %collective-permute-start.3 = (bf16[256,256]{1,0:T(8,128)(2,1)S(1)}, bf16[256,256]{1,0:T(8,128)(2,1)S(1)}, u32[]{:S(2)}, u32[]{:S(2)}) collective-permute-start(bf16[256,256]{1,0:T(8,128)(2,1)S(1)} %bitcast.28), channel_id=1, source_target_pairs={{0,1},{1,0},{2,3},{3,2},{4,5},{5,4},{6,7},{7,6},{8,9},{9,8},{10,11... | collective-permute-start | bytes 393224 | tf_op jit(solution)/shard_map/ppermute | solution.py:182
Sparse Core Ops, SparseCore 0:
  100.0 37.8 reduce-scatter.1

commit v21 on v20

--- a/solution.py
+++ b/solution.py
@@ -115,6 +115,7 @@
         kv_h[None, :, None], (n_x, kv_heads, n_z // kv_heads) + kv_h.shape[1:]
     ).reshape((n_x * n_z,) + kv_h.shape[1:])
     mine = lax.all_to_all(pieces, ("x", "z"), split_axis=0, concat_axis=0, tiled=True)
+    mine, w_late = lax.optimization_barrier((mine, out_weight))
     other = lax.ppermute(mine, "core", perm=[(i, (i + 1) % n_core) for i in range(n_core)])
     row = jnp.stack([mine.reshape(n_x, n_z, -1, 2 * HD), other.reshape(n_x, n_z, -1, 2 * HD)], axis=2)
     row = row.reshape(n_x * rows, 2 * HD)
@@ -178,7 +179,7 @@
     slot3 = slot.reshape(n_z, n_core, per_dev)
     cols = jnp.arange(rows, dtype=jnp.int32)[None, :]
     swap_pairs = [(i, (i + 1) % n_core) for i in range(n_core)]
-    w_pair = jnp.concatenate([out_weight, lax.ppermute(out_weight, "core", perm=swap_pairs)], axis=0)
+    w_pair = jnp.concatenate([out_weight, lax.ppermute(w_late, "core", perm=swap_pairs)], axis=0)
     both = jnp.concatenate([arrived, lax.ppermute(arrived, "core", perm=swap_pairs)], axis=1)
     mine = jnp.take(slot3, c, axis=1).reshape(-1)
     sel = (mine[:, None] == cols).astype(jnp.bfloat16)

time: 146 us -> 148 us (1.014)
  blocking collectives: 0 us -> 23.8 us
  starting transfers between devices: 42.5 us -> 29.1 us
  waiting for transfers between devices: 60.1 us -> 52.5 us
    all_to_all x0 -> x1, blocking collectives: none -> 23.8 us  [shards(): lax.all_to_all(pieces, ('x', 'z'), split_axis=0, concat_axis=0, tiled=True)]
    all_to_all x1 -> x0, starting transfers between devices: 13.5 us -> none  [shards(): lax.all_to_all(pieces, ('x', 'z'), split_axis=0, concat_axis=0, tiled=True)]
    all_to_all x1 -> x0, waiting for transfers between devices: 9.29 us -> none  [shards(): lax.all_to_all(pieces, ('x', 'z'), split_axis=0, concat_axis=0, tiled=True)]
    ppermute x1, waiting for transfers between devices: 0.26 us -> 1.79 us  [shards(): lax.ppermute(mine, 'core', perm=[(i, (i + 1) % n_core) for i in range(n_c...]
  transfers between devices with their start and end apart: 8 -> 7, of which waited for: 6 -> 5; matrix products, arithmetic and copies ran while one was open for 10% -> 8% of each run, Pallas kernels for 6% -> 6%
where the time goes in v21:
time: 148 us; the launch traced here: 147 us
  waiting for transfers between devices  52.5 us (35%)
  starting transfers between devices  29.1 us (20%)
  blocking collectives  23.8 us (16%)
  between operations  13.6 us (9%)
  Pallas kernels  8.24 us (6%)
  local copies, waits for them, and re-layouts  8.04 us (5%)
  matrix products  6.2 us (4%)
  other arithmetic  5.48 us (4%)
    reduce_scatter x1, waiting for transfers between devices, shards(): return lax.psum_scatter(half, 'z', scatter_dimension=0, tiled=True)  38.1 us
    all_to_all x1, blocking collectives, shards(): lax.all_to_all(pieces, ('x', 'z'), split_axis=0, concat_axis=0, tiled=True)  23.8 us
    all_to_all x1, starting transfers between devices, shards(): lax.all_to_all(to_send, ('y', 'x'), split_axis=0, concat_axis=0, tiled=True)  17.2 us
    all_to_all x1, waiting for transfers between devices, shards(): lax.all_to_all(to_send, ('y', 'x'), split_axis=0, concat_axis=0, tiled=True)  8.45 us
    pallas_call x2, Pallas kernels, attention(): pl.pallas_call(functools.partial(_attention_body, scale, n_pieces, heads,...  8.24 us
    dot_general x1, matrix products, shards(): jnp.dot(relaid, w_pair, preferred_element_type=jnp.float32)  5.35 us
    ppermute x1, waiting for transfers between devices, shards(): fetched = lax.ppermute(row, ('y', 'core'), perm=perm)  3.78 us
    ppermute x1, starting transfers between devices, shards(): fetched = lax.ppermute(row, ('y', 'core'), perm=perm)  3.51 us
  transfers between devices with their start and end apart: 7, of which 5 were waited for; matrix products, arithmetic and copies ran while one was open for 8% of the time, Pallas kernels for 6%

profile of v21, /device:TPU:6, one launch (start us, length us, event | category | flops | bytes accessed | tf_op | source)
XLA Modules:
  0.0 147.0 jit_solution(14824326951699546666)
XLA Ops:
  6.5 0.8 reshape.66
  7.3 0.7 reshape.67
  8.1 23.8 %all_to_all.17 = bf16[32,16,256]{2,1,0:T(8,128)(2,1)S(1)} all-to-all(bf16[32,16,256]{2,1,0:T(8,128)(2,1)S(1)} %bitcast.17), channel_id=1, replica_groups=mesh['y'=8,'x'=4,'z'=8,'core'=2] {'x','z'}, dimensions={0} | all-to-all | bytes 524288 | tf_op jit(solution)/shard_map/all_to_all | solution.py:117
  31.9 1.9 %collective-permute-start.4 = (bf16[256,8192]{1,0:T(8,128)(2,1)}, bf16[256,8192]{1,0:T(8,128)(2,1)}, u32[]{:S(2)}, u32[]{:S(2)}) collective-permute-start(bf16[256,8192]{1,0:T(8,128)(2,1)} %param.11), channel_id=1, source_target_pairs={{0,1},{1,0},{2,3},{3,2},{4,5},{5,4},{6,7},{7,6},{8,9},{9,8},{10,11... | collective-permute-start | bytes 12582920 | tf_op jit(solution)/shard_map/ppermute | solution.py:182
  33.9 2.0 %select_reduce_fusion = s32[256]{0:T(256)S(1)} fusion(s32[8192]{0:T(1024)} %param.7, s32[256]{0:T(256)S(1)} %iota_add_fusion), kind=kLoop, calls=%fused_computation.4 | loop fusion | flops 6291200 | bytes 34816 | tf_op jit(solution)/shard_map/reduce_sum | solution.py:156
  35.9 2.4 %collective-permute-start = (bf16[32,16,256]{2,1,0:T(8,128)(2,1)S(1)}, bf16[32,16,256]{2,1,0:T(8,128)(2,1)S(1)}, u32[]{:S(2)}, u32[]{:S(2)}) collective-permute-start(bf16[32,16,256]{2,1,0:T(8,128)(2,1)S(1)} %all_to_all.17), channel_id=1, source_target_pairs={{0,1},{1,0},{2,3},{3,2},{4,5},{5,4},{6,7},{7,6},{8,9},{9,8},{10,11... | collective-permute-start | bytes 786440 | tf_op jit(solution)/shard_map/ppermute | solution.py:119
  38.3 0.7 pad_dynamic-slice_fusion.1
  39.5 1.8 %collective-permute-done = bf16[32,16,256]{2,1,0:T(8,128)(2,1)S(1)} collective-permute-done((bf16[32,16,256]{2,1,0:T(8,128)(2,1)S(1)}, bf16[32,16,256]{2,1,0:T(8,128)(2,1)S(1)}, u32[]{:S(2)}, u32[]{:S(2)}) %collective-permute-start) | collective-permute-done | bytes 262176 | tf_op jit(solution)/shard_map/ppermute | solution.py:119
  41.4 3.5 %collective-permute-start.1 = (bf16[1024,256]{1,0:T(8,128)(2,1)S(1)}, bf16[1024,256]{1,0:T(8,128)(2,1)S(1)}, u32[]{:S(2)}, u32[]{:S(2)}) collective-permute-start(bf16[1024,256]{1,0:T(8,128)(2,1)S(1)} %bitcast.20), channel_id=1, source_target_pairs={{0,64},{64,128},{128,192},{192,256},{256,320},{320,384},{384,448},... | collective-permute-start | bytes 1572872 | tf_op jit(solution)/shard_map/ppermute | solution.py:133
  45.0 0.8 dynamic_slice.16
  45.7 0.7 stack_reshape.27.refs_4_
  46.4 0.7 stack_reshape.26.refs_3_
  47.1 0.2 convert_reduce_fusion
  47.5 0.8 copy.14.refs_1_.refs_2_
  48.3 0.8 copy.15.refs_2_.refs_3_
  49.1 0.8 convolution_convert_fusion.2.q_ref
  49.9 3.3 %shard_map.64 = (f32[2,256,1]{2,1,0:T(8,128)}, f32[2,256,1]{2,1,0:T(8,128)}, f32[256,256]{1,0:T(8,128)}) custom-call(bf16[256,256]{1,0:T(8,128)(2,1)} %convolution_convert_fusion.2.q_ref, bf16[1024,256]{1,0:T(8,128)(2,1)} %bitcast.21, s32[256,1]{1,0:T(8,128)} %copy.14.refs_1_.refs_2_, s32[256,1]{1,0:T(8,128)} %copy.15.refs_2_.refs_3_, ...), custom_call_target="tpu_custom_call" | custom-call | flops 268435456 | bytes 786432 | tf_op jit(solution)/shard_map/pallas_call | solution.py:81
  53.2 3.8 %collective-permute-done.1.refs_0_ = bf16[1024,256]{1,0:T(8,128)(2,1)S(1)} collective-permute-done((bf16[1024,256]{1,0:T(8,128)(2,1)S(1)}, bf16[1024,256]{1,0:T(8,128)(2,1)S(1)}, u32[]{:S(2)}, u32[]{:S(2)}) %collective-permute-start.1) | collective-permute-done | bytes 524320 | tf_op jit(solution)/shard_map/ppermute | solution.py:133
  57.0 2.2 %collective-permute-start.2 = (bf16[1024,256]{1,0:T(8,128)(2,1)S(1)}, bf16[1024,256]{1,0:T(8,128)(2,1)S(1)}, u32[]{:S(2)}, u32[]{:S(2)}) collective-permute-start(bf16[1024,256]{1,0:T(8,128)(2,1)S(1)} %collective-permute-done.1.refs_0_), channel_id=1, source_target_pairs={{0,1},{1,0},{2,3},{3,2},{4,5},{5,4},{6,7},{7,6},{8,9},{9,8},{10,11... | collective-permute-start | bytes 1572872 | tf_op jit(solution)/shard_map/ppermute | solution.py:167
  59.9 0.6 pad_add_fusion.refs_4_
  60.5 0.6 pad_add_fusion.1.refs_5_
  61.1 0.8 copy-done.3
  61.9 4.9 %shard_map.65 = bf16[256,256]{1,0:T(8,128)(2,1)} custom-call(bf16[256,256]{1,0:T(8,128)(2,1)} %convolution_convert_fusion.2.q_ref, bf16[1024,256]{1,0:T(8,128)(2,1)} %copy-done.2, bf16[1024,256]{1,0:T(8,128)(2,1)} %copy-done.3, s32[256,1]{1,0:T(8,128)} %copy.14.refs_1_.refs_2_, s32[256,1]{1,0:T(8,128)} %copy.15.refs_2_.refs_3_, ...), custom_call_target="tpu_custom_call" | custom-call | flops 536870912 | bytes 1310720 | tf_op jit(solution)/shard_map/pallas_call | solution.py:81
  66.8 17.2 %all-to-all-start.1 = ((bf16[32,8,256]{2,1,0:T(8,128)(2,1)}), bf16[32,8,256]{2,1,0:T(8,128)(2,1)S(1)}, u32[]{:S(2)}, u32[]{:S(2)}) async-start(bf16[32,8,256]{2,1,0:T(8,128)(2,1)} %bitcast.19), calls=%async_computation.1 | async-start | bytes 262144 | tf_op jit(solution)/shard_map/all_to_all | solution.py:172
  84.0 0.8 and_select_fusion
  84.8 0.2 convert_reduce_fusion.1
  85.0 8.4 %all-to-all-done.1 = bf16[32,8,256]{2,1,0:T(8,128)(2,1)S(1)} async-done(((bf16[32,8,256]{2,1,0:T(8,128)(2,1)}), bf16[32,8,256]{2,1,0:T(8,128)(2,1)S(1)}, u32[]{:S(2)}, u32[]{:S(2)}) %all-to-all-start.1) | async-done | bytes 131104 | tf_op jit(solution)/shard_map/all_to_all | solution.py:172
  93.4 1.9 %collective-permute-start.3 = (bf16[256,256]{1,0:T(8,128)(2,1)S(1)}, bf16[256,256]{1,0:T(8,128)(2,1)S(1)}, u32[]{:S(2)}, u32[]{:S(2)}) collective-permute-start(bf16[256,256]{1,0:T(8,128)(2,1)S(1)} %bitcast.29), channel_id=1, source_target_pairs={{0,1},{1,0},{2,3},{3,2},{4,5},{5,4},{6,7},{7,6},{8,9},{9,8},{10,11... | collective-permute-start | bytes 393224 | tf_op jit(solution)/shard_map/ppermute | solution.py:183
  95.4 0.8 multiply_add_fusion.1
  96.3 0.3 collective-permute-done.3
  96.7 5.4 %convolution_convert_fusion = bf16[128,8192]{1,0:T(8,128)(2,1)} fusion(bf16[256,8192]{1,0:T(8,128)(2,1)} %collective-permute-done.4, bf16[256,8192]{1,0:T(8,128)(2,1)} %param.11, bf16[256,256]{1,0:T(8,128)(2,1)S(1)} %collective-permute-done.3, bf16[256,256]{1,0:T(8,128)(2,1)S(1)} %bitcast.30, s32[128]{0:T(128)S(1)} %select_n.79), kind=kOutput, calls=%fused_computation | convolution fusion | flops 1125744640 | bytes 10748416 | tf_op jit(solution)/shard_map/dot_general | solution.py:187
  102.0 38.1 %reduce-scatter.2.cloned.1.call-done = bf16[16,8192]{1,0:T(8,128)(2,1)} async-done(((bf16[128,8192]{1,0:T(8,128)(2,1)}), bf16[16,8192]{1,0:T(8,128)(2,1)}) %reduce-scatter.2.cloned.1.call-update) | async-done | bytes 262160 | tf_op jit(solution)/shard_map/reduce_scatter | solution.py:188
  (35 shorter events, 1.7 us)
Async XLA Ops:
  6.5 42.5 %copy-start = (bf16[256,256]{1,0:T(8,128)(2,1)S(1)}, bf16[256,256]{1,0:T(8,128)(2,1)}, u32[]{:S(2)}) copy-start(bf16[256,256]{1,0:T(8,128)(2,1)} %param.8) | copy-start | bytes 393220
  31.9 64.7 %collective-permute-start.4 = (bf16[256,8192]{1,0:T(8,128)(2,1)}, bf16[256,8192]{1,0:T(8,128)(2,1)}, u32[]{:S(2)}, u32[]{:S(2)}) collective-permute-start(bf16[256,8192]{1,0:T(8,128)(2,1)} %param.11), channel_id=1, source_target_pairs={{0,1},{1,0},{2,3},{3,2},{4,5},{5,4},{6,7},{7,6},{8,9},{9,8},{10,11... | collective-permute-start | bytes 12582920 | tf_op jit(solution)/shard_map/ppermute | solution.py:182
  35.9 5.4 %collective-permute-start = (bf16[32,16,256]{2,1,0:T(8,128)(2,1)S(1)}, bf16[32,16,256]{2,1,0:T(8,128)(2,1)S(1)}, u32[]{:S(2)}, u32[]{:S(2)}) collective-permute-start(bf16[32,16,256]{2,1,0:T(8,128)(2,1)S(1)} %all_to_all.17), channel_id=1, source_target_pairs={{0,1},{1,0},{2,3},{3,2},{4,5},{5,4},{6,7},{7,6},{8,9},{9,8},{10,11... | collective-permute-start | bytes 786440 | tf_op jit(solution)/shard_map/ppermute | solution.py:119
  41.4 8.5 %copy-start.1 = (bf16[4,8,2,16,256]{4,3,2,1,0:T(8,128)(2,1)}, bf16[4,8,2,16,256]{4,3,2,1,0:T(8,128)(2,1)S(1)}, u32[]{:S(2)}) copy-start(bf16[4,8,2,16,256]{4,3,2,1,0:T(8,128)(2,1)S(1)} %pad_maximum_fusion) | copy-start | bytes 1572868
  41.4 15.6 %collective-permute-start.1 = (bf16[1024,256]{1,0:T(8,128)(2,1)S(1)}, bf16[1024,256]{1,0:T(8,128)(2,1)S(1)}, u32[]{:S(2)}, u32[]{:S(2)}) collective-permute-start(bf16[1024,256]{1,0:T(8,128)(2,1)S(1)} %bitcast.20), channel_id=1, source_target_pairs={{0,64},{64,128},{128,192},{192,256},{256,320},{320,384},{384,448},... | collective-permute-start | bytes 1572872 | tf_op jit(solution)/shard_map/ppermute | solution.py:133
  57.0 4.1 %copy-start.2 = (bf16[1024,256]{1,0:T(8,128)(2,1)}, bf16[1024,256]{1,0:T(8,128)(2,1)S(1)}, u32[]{:S(2)}) copy-start(bf16[1024,256]{1,0:T(8,128)(2,1)S(1)} %collective-permute-done.1.refs_0_) | copy-start | bytes 1572868
  57.0 4.0 %collective-permute-start.2 = (bf16[1024,256]{1,0:T(8,128)(2,1)S(1)}, bf16[1024,256]{1,0:T(8,128)(2,1)S(1)}, u32[]{:S(2)}, u32[]{:S(2)}) collective-permute-start(bf16[1024,256]{1,0:T(8,128)(2,1)S(1)} %collective-permute-done.1.refs_0_), channel_id=1, source_target_pairs={{0,1},{1,0},{2,3},{3,2},{4,5},{5,4},{6,7},{7,6},{8,9},{9,8},{10,11... | collective-permute-start | bytes 1572872 | tf_op jit(solution)/shard_map/ppermute | solution.py:167
  61.1 0.8 copy-start.3
  66.8 26.6 %all-to-all-start.1 = ((bf16[32,8,256]{2,1,0:T(8,128)(2,1)}), bf16[32,8,256]{2,1,0:T(8,128)(2,1)S(1)}, u32[]{:S(2)}, u32[]{:S(2)}) async-start(bf16[32,8,256]{2,1,0:T(8,128)(2,1)} %bitcast.19), calls=%async_computation.1 | async-start | bytes 262144 | tf_op jit(solution)/shard_map/all_to_all | solution.py:172
  84.0 56.2 %reduce-scatter.2.cloned.1.call-start = ((), (), s32[]{:S(2)}) async-start(), calls=%async_computation.3 | async-start | bytes 2359296 | tf_op jit(solution)/shard_map/reduce_scatter | solution.py:188
  93.4 3.2 %collective-permute-start.3 = (bf16[256,256]{1,0:T(8,128)(2,1)S(1)}, bf16[256,256]{1,0:T(8,128)(2,1)S(1)}, u32[]{:S(2)}, u32[]{:S(2)}) collective-permute-start(bf16[256,256]{1,0:T(8,128)(2,1)S(1)} %bitcast.29), channel_id=1, source_target_pairs={{0,1},{1,0},{2,3},{3,2},{4,5},{5,4},{6,7},{7,6},{8,9},{9,8},{10,11... | collective-permute-start | bytes 393224 | tf_op jit(solution)/shard_map/ppermute | solution.py:183
Sparse Core Ops, SparseCore 0:
  102.2 37.9 reduce-scatter.1

commit v22 on v21

--- a/solution.py
+++ b/solution.py
@@ -115,7 +115,6 @@
         kv_h[None, :, None], (n_x, kv_heads, n_z // kv_heads) + kv_h.shape[1:]
     ).reshape((n_x * n_z,) + kv_h.shape[1:])
     mine = lax.all_to_all(pieces, ("x", "z"), split_axis=0, concat_axis=0, tiled=True)
-    mine, w_late = lax.optimization_barrier((mine, out_weight))
     other = lax.ppermute(mine, "core", perm=[(i, (i + 1) % n_core) for i in range(n_core)])
     row = jnp.stack([mine.reshape(n_x, n_z, -1, 2 * HD), other.reshape(n_x, n_z, -1, 2 * HD)], axis=2)
     row = row.reshape(n_x * rows, 2 * HD)
@@ -163,7 +162,7 @@
     q_pos = jnp.sum(jnp.where(send_hit, here[None, :], 0), axis=1)
     q_seg = jnp.sum(jnp.where(send_hit, q_seg[None, :], 0), axis=1)
     carry = attention(q_sent, [row], q_pos, q_seg, k_pos[2:], k_seg[2:], scale, final=False)
-    fetched, carry = lax.optimization_barrier((fetched, carry))
+    fetched, carry, w_late = lax.optimization_barrier((fetched, carry, out_weight))
     swapped = lax.ppermute(fetched, "core", perm=[(i, (i + 1) % n_core) for i in range(n_core)])
     to_send = attention(
         q_sent, [fetched, swapped], q_pos, q_seg, k_pos[:2], k_seg[:2], scale, carry=carry

time: 148 us -> 149 us (level)
  blocking collectives: 23.8 us -> 0 us
  starting transfers between devices: 29.1 us -> 42.8 us
  waiting for transfers between devices: 52.5 us -> 62.8 us
    all_to_all x1 -> x0, blocking collectives: 23.8 us -> none  [shards(): lax.all_to_all(pieces, ('x', 'z'), split_axis=0, concat_axis=0, tiled=True)]
    all_to_all x0 -> x1, starting transfers between devices: none -> 13.5 us  [shards(): lax.all_to_all(pieces, ('x', 'z'), split_axis=0, concat_axis=0, tiled=True)]
    all_to_all x0 -> x1, waiting for transfers between devices: none -> 8.52 us  [shards(): lax.all_to_all(pieces, ('x', 'z'), split_axis=0, concat_axis=0, tiled=True)]
    ppermute x1, waiting for transfers between devices: 0.01 us -> 3.67 us  [shards(): lax.ppermute(fetched, 'core', perm=[(i, (i + 1) % n_core) for i in range(...]
    ppermute x1, waiting for transfers between devices: 1.79 us -> 0.26 us  [shards(): lax.ppermute(mine, 'core', perm=[(i, (i + 1) % n_core) for i in range(n_c...]
  transfers between devices with their start and end apart: 7 -> 8, of which waited for: 5 -> 7; matrix products, arithmetic and copies ran while one was open for 8% -> 8% of each run, Pallas kernels for 6% -> 6%
where the time goes in v22:
time: 149 us; the launch traced here: 148 us
  waiting for transfers between devices  62.8 us (42%)
  starting transfers between devices  42.8 us (29%)
  between operations  13.6 us (9%)
  local copies, waits for them, and re-layouts  8.74 us (6%)
  Pallas kernels  8.24 us (6%)
  matrix products  6.2 us (4%)
  other arithmetic  5.48 us (4%)
    reduce_scatter x1, waiting for transfers between devices, shards(): return lax.psum_scatter(half, 'z', scatter_dimension=0, tiled=True)  38.3 us
    all_to_all x1, starting transfers between devices, shards(): lax.all_to_all(to_send, ('y', 'x'), split_axis=0, concat_axis=0, tiled=True)  17.6 us
    all_to_all x1, starting transfers between devices, shards(): lax.all_to_all(pieces, ('x', 'z'), split_axis=0, concat_axis=0, tiled=True)  13.5 us
    all_to_all x1, waiting for transfers between devices, shards(): lax.all_to_all(pieces, ('x', 'z'), split_axis=0, concat_axis=0, tiled=True)  8.52 us
    pallas_call x2, Pallas kernels, attention(): pl.pallas_call(functools.partial(_attention_body, scale, n_pieces, heads,...  8.24 us
    all_to_all x1, waiting for transfers between devices, shards(): lax.all_to_all(to_send, ('y', 'x'), split_axis=0, concat_axis=0, tiled=True)  8.02 us
    dot_general x1, matrix products, shards(): jnp.dot(relaid, w_pair, preferred_element_type=jnp.float32)  5.35 us
    ppermute x1, waiting for transfers between devices, shards(): lax.ppermute(fetched, 'core', perm=[(i, (i + 1) % n_core) for i in range(...  3.67 us
  transfers between devices with their start and end apart: 8, of which 7 were waited for; matrix products, arithmetic and copies ran while one was open for 8% of the time, Pallas kernels for 6%

profile of v22, /device:TPU:6, one launch (start us, length us, event | category | flops | bytes accessed | tf_op | source)
XLA Modules:
  0.0 147.8 jit_solution(5644390945786209959)
XLA Ops:
  6.5 0.8 reshape.66
  7.3 0.7 reshape.67
  8.1 0.7 broadcast_in_dim.68
  8.8 13.5 %all-to-all-start = ((bf16[32,16,256]{2,1,0:T(8,128)(2,1)}), bf16[32,16,256]{2,1,0:T(8,128)(2,1)S(1)}, u32[]{:S(2)}, u32[]{:S(2)}) async-start(bf16[32,16,256]{2,1,0:T(8,128)(2,1)} %bitcast.2), calls=%async_computation | async-start | bytes 524288 | tf_op jit(solution)/shard_map/all_to_all | solution.py:117
  22.3 2.0 %select_reduce_fusion = s32[256]{0:T(256)S(1)} fusion(s32[8192]{0:T(1024)} %param.7, s32[256]{0:T(256)S(1)} %iota_add_fusion), kind=kLoop, calls=%fused_computation.4 | loop fusion | flops 6291200 | bytes 34816 | tf_op jit(solution)/shard_map/reduce_sum | solution.py:155
  24.3 8.5 %all-to-all-done = bf16[32,16,256]{2,1,0:T(8,128)(2,1)S(1)} async-done(((bf16[32,16,256]{2,1,0:T(8,128)(2,1)}), bf16[32,16,256]{2,1,0:T(8,128)(2,1)S(1)}, u32[]{:S(2)}, u32[]{:S(2)}) %all-to-all-start) | async-done | bytes 262176 | tf_op jit(solution)/shard_map/all_to_all | solution.py:117
  32.8 1.9 %collective-permute-start = (bf16[32,16,256]{2,1,0:T(8,128)(2,1)S(1)}, bf16[32,16,256]{2,1,0:T(8,128)(2,1)S(1)}, u32[]{:S(2)}, u32[]{:S(2)}) collective-permute-start(bf16[32,16,256]{2,1,0:T(8,128)(2,1)S(1)} %all-to-all-done), channel_id=1, source_target_pairs={{0,1},{1,0},{2,3},{3,2},{4,5},{5,4},{6,7},{7,6},{8,9},{9,8},{10,11... | collective-permute-start | bytes 786440 | tf_op jit(solution)/shard_map/ppermute | solution.py:118
  34.7 0.7 pad_dynamic-slice_fusion.1
  36.3 3.5 %collective-permute-start.1 = (bf16[1024,256]{1,0:T(8,128)(2,1)S(1)}, bf16[1024,256]{1,0:T(8,128)(2,1)S(1)}, u32[]{:S(2)}, u32[]{:S(2)}) collective-permute-start(bf16[1024,256]{1,0:T(8,128)(2,1)S(1)} %bitcast.19), channel_id=1, source_target_pairs={{0,64},{64,128},{128,192},{192,256},{256,320},{320,384},{384,448},... | collective-permute-start | bytes 1572872 | tf_op jit(solution)/shard_map/ppermute | solution.py:132
  39.9 0.8 dynamic_slice.16
  40.6 0.7 stack_reshape.27.refs_4_
  41.3 0.7 stack_reshape.26.refs_3_
  42.4 0.8 copy.14.refs_1_.refs_2_
  43.2 0.8 copy.15.refs_2_.refs_3_
  44.0 0.8 convolution_convert_fusion.2.q_ref
  44.8 3.3 %shard_map.64 = (f32[2,256,1]{2,1,0:T(8,128)}, f32[2,256,1]{2,1,0:T(8,128)}, f32[256,256]{1,0:T(8,128)}) custom-call(bf16[256,256]{1,0:T(8,128)(2,1)} %convolution_convert_fusion.2.q_ref, bf16[1024,256]{1,0:T(8,128)(2,1)} %bitcast.20, s32[256,1]{1,0:T(8,128)} %copy.14.refs_1_.refs_2_, s32[256,1]{1,0:T(8,128)} %copy.15.refs_2_.refs_3_, ...), custom_call_target="tpu_custom_call" | custom-call | flops 268435456 | bytes 786432 | tf_op jit(solution)/shard_map/pallas_call | solution.py:81
  48.1 3.7 %collective-permute-done.1.refs_0_ = bf16[1024,256]{1,0:T(8,128)(2,1)S(1)} collective-permute-done((bf16[1024,256]{1,0:T(8,128)(2,1)S(1)}, bf16[1024,256]{1,0:T(8,128)(2,1)S(1)}, u32[]{:S(2)}, u32[]{:S(2)}) %collective-permute-start.1) | collective-permute-done | bytes 524320 | tf_op jit(solution)/shard_map/ppermute | solution.py:132
  51.8 2.3 %collective-permute-start.4 = (bf16[256,8192]{1,0:T(8,128)(2,1)}, bf16[256,8192]{1,0:T(8,128)(2,1)}, u32[]{:S(2)}, u32[]{:S(2)}) collective-permute-start(bf16[256,8192]{1,0:T(8,128)(2,1)} %param.11), channel_id=1, source_target_pairs={{0,1},{1,0},{2,3},{3,2},{4,5},{5,4},{6,7},{7,6},{8,9},{9,8},{10,11... | collective-permute-start | bytes 12582920 | tf_op jit(solution)/shard_map/ppermute | solution.py:181
  54.1 2.0 %collective-permute-start.2 = (bf16[1024,256]{1,0:T(8,128)(2,1)S(1)}, bf16[1024,256]{1,0:T(8,128)(2,1)S(1)}, u32[]{:S(2)}, u32[]{:S(2)}) collective-permute-start(bf16[1024,256]{1,0:T(8,128)(2,1)S(1)} %collective-permute-done.1.refs_0_), channel_id=1, source_target_pairs={{0,1},{1,0},{2,3},{3,2},{4,5},{5,4},{6,7},{7,6},{8,9},{9,8},{10,11... | collective-permute-start | bytes 1572872 | tf_op jit(solution)/shard_map/ppermute | solution.py:166
  56.8 0.6 pad_add_fusion.refs_4_
  57.4 0.6 pad_add_fusion.1.refs_5_
  58.0 3.7 %collective-permute-done.2.refs_1_ = bf16[1024,256]{1,0:T(8,128)(2,1)S(1)} collective-permute-done((bf16[1024,256]{1,0:T(8,128)(2,1)S(1)}, bf16[1024,256]{1,0:T(8,128)(2,1)S(1)}, u32[]{:S(2)}, u32[]{:S(2)}) %collective-permute-start.2) | collective-permute-done | bytes 524320 | tf_op jit(solution)/shard_map/ppermute | solution.py:166
  61.7 0.8 copy-done.3
  62.5 4.9 %shard_map.65 = bf16[256,256]{1,0:T(8,128)(2,1)} custom-call(bf16[256,256]{1,0:T(8,128)(2,1)} %convolution_convert_fusion.2.q_ref, bf16[1024,256]{1,0:T(8,128)(2,1)} %copy-done.2, bf16[1024,256]{1,0:T(8,128)(2,1)} %copy-done.3, s32[256,1]{1,0:T(8,128)} %copy.14.refs_1_.refs_2_, s32[256,1]{1,0:T(8,128)} %copy.15.refs_2_.refs_3_, ...), custom_call_target="tpu_custom_call" | custom-call | flops 536870912 | bytes 1310720 | tf_op jit(solution)/shard_map/pallas_call | solution.py:81
  67.4 17.6 %all-to-all-start.1 = ((bf16[32,8,256]{2,1,0:T(8,128)(2,1)}), bf16[32,8,256]{2,1,0:T(8,128)(2,1)S(1)}, u32[]{:S(2)}, u32[]{:S(2)}) async-start(bf16[32,8,256]{2,1,0:T(8,128)(2,1)} %bitcast.18), calls=%async_computation.1 | async-start | bytes 262144 | tf_op jit(solution)/shard_map/all_to_all | solution.py:171
  85.1 0.8 and_select_fusion
  86.0 8.0 %all-to-all-done.1 = bf16[32,8,256]{2,1,0:T(8,128)(2,1)S(1)} async-done(((bf16[32,8,256]{2,1,0:T(8,128)(2,1)}), bf16[32,8,256]{2,1,0:T(8,128)(2,1)S(1)}, u32[]{:S(2)}, u32[]{:S(2)}) %all-to-all-start.1) | async-done | bytes 131104 | tf_op jit(solution)/shard_map/all_to_all | solution.py:171
  94.0 1.9 %collective-permute-start.3 = (bf16[256,256]{1,0:T(8,128)(2,1)S(1)}, bf16[256,256]{1,0:T(8,128)(2,1)S(1)}, u32[]{:S(2)}, u32[]{:S(2)}) collective-permute-start(bf16[256,256]{1,0:T(8,128)(2,1)S(1)} %bitcast.28), channel_id=1, source_target_pairs={{0,1},{1,0},{2,3},{3,2},{4,5},{5,4},{6,7},{7,6},{8,9},{9,8},{10,11... | collective-permute-start | bytes 393224 | tf_op jit(solution)/shard_map/ppermute | solution.py:182
  96.0 0.8 multiply_add_fusion.1
  96.9 0.3 collective-permute-done.3
  97.3 5.4 %convolution_convert_fusion = bf16[128,8192]{1,0:T(8,128)(2,1)} fusion(bf16[256,8192]{1,0:T(8,128)(2,1)} %collective-permute-done.4, bf16[256,8192]{1,0:T(8,128)(2,1)} %param.11, bf16[256,256]{1,0:T(8,128)(2,1)S(1)} %collective-permute-done.3, bf16[256,256]{1,0:T(8,128)(2,1)S(1)} %bitcast.29, s32[128]{0:T(128)S(1)} %select_n.79), kind=kOutput, calls=%fused_computation | convolution fusion | flops 1125744640 | bytes 10748416 | tf_op jit(solution)/shard_map/dot_general | solution.py:186
  102.7 38.3 %reduce-scatter.2.cloned.1.call-done = bf16[16,8192]{1,0:T(8,128)(2,1)} async-done(((bf16[128,8192]{1,0:T(8,128)(2,1)}), bf16[16,8192]{1,0:T(8,128)(2,1)}) %reduce-scatter.2.cloned.1.call-update) | async-done | bytes 262160 | tf_op jit(solution)/shard_map/reduce_scatter | solution.py:187
  (36 shorter events, 2.3 us)
Async XLA Ops:
  6.5 37.4 %copy-start = (bf16[256,256]{1,0:T(8,128)(2,1)S(1)}, bf16[256,256]{1,0:T(8,128)(2,1)}, u32[]{:S(2)}) copy-start(bf16[256,256]{1,0:T(8,128)(2,1)} %param.8) | copy-start | bytes 393220
  8.8 24.0 %all-to-all-start = ((bf16[32,16,256]{2,1,0:T(8,128)(2,1)}), bf16[32,16,256]{2,1,0:T(8,128)(2,1)S(1)}, u32[]{:S(2)}, u32[]{:S(2)}) async-start(bf16[32,16,256]{2,1,0:T(8,128)(2,1)} %bitcast.2), calls=%async_computation | async-start | bytes 524288 | tf_op jit(solution)/shard_map/all_to_all | solution.py:117
  32.8 3.4 %collective-permute-start = (bf16[32,16,256]{2,1,0:T(8,128)(2,1)S(1)}, bf16[32,16,256]{2,1,0:T(8,128)(2,1)S(1)}, u32[]{:S(2)}, u32[]{:S(2)}) collective-permute-start(bf16[32,16,256]{2,1,0:T(8,128)(2,1)S(1)} %all-to-all-done), channel_id=1, source_target_pairs={{0,1},{1,0},{2,3},{3,2},{4,5},{5,4},{6,7},{7,6},{8,9},{9,8},{10,11... | collective-permute-start | bytes 786440 | tf_op jit(solution)/shard_map/ppermute | solution.py:118
  36.3 8.5 %copy-start.1 = (bf16[4,8,2,16,256]{4,3,2,1,0:T(8,128)(2,1)}, bf16[4,8,2,16,256]{4,3,2,1,0:T(8,128)(2,1)S(1)}, u32[]{:S(2)}) copy-start(bf16[4,8,2,16,256]{4,3,2,1,0:T(8,128)(2,1)S(1)} %pad_maximum_fusion) | copy-start | bytes 1572868
  36.3 15.5 %collective-permute-start.1 = (bf16[1024,256]{1,0:T(8,128)(2,1)S(1)}, bf16[1024,256]{1,0:T(8,128)(2,1)S(1)}, u32[]{:S(2)}, u32[]{:S(2)}) collective-permute-start(bf16[1024,256]{1,0:T(8,128)(2,1)S(1)} %bitcast.19), channel_id=1, source_target_pairs={{0,64},{64,128},{128,192},{192,256},{256,320},{320,384},{384,448},... | collective-permute-start | bytes 1572872 | tf_op jit(solution)/shard_map/ppermute | solution.py:132
  51.8 9.9 %copy-start.2 = (bf16[1024,256]{1,0:T(8,128)(2,1)}, bf16[1024,256]{1,0:T(8,128)(2,1)S(1)}, u32[]{:S(2)}) copy-start(bf16[1024,256]{1,0:T(8,128)(2,1)S(1)} %collective-permute-done.1.refs_0_) | copy-start | bytes 1572868
  51.8 45.5 %collective-permute-start.4 = (bf16[256,8192]{1,0:T(8,128)(2,1)}, bf16[256,8192]{1,0:T(8,128)(2,1)}, u32[]{:S(2)}, u32[]{:S(2)}) collective-permute-start(bf16[256,8192]{1,0:T(8,128)(2,1)} %param.11), channel_id=1, source_target_pairs={{0,1},{1,0},{2,3},{3,2},{4,5},{5,4},{6,7},{7,6},{8,9},{9,8},{10,11... | collective-permute-start | bytes 12582920 | tf_op jit(solution)/shard_map/ppermute | solution.py:181
  54.1 7.5 %collective-permute-start.2 = (bf16[1024,256]{1,0:T(8,128)(2,1)S(1)}, bf16[1024,256]{1,0:T(8,128)(2,1)S(1)}, u32[]{:S(2)}, u32[]{:S(2)}) collective-permute-start(bf16[1024,256]{1,0:T(8,128)(2,1)S(1)} %collective-permute-done.1.refs_0_), channel_id=1, source_target_pairs={{0,1},{1,0},{2,3},{3,2},{4,5},{5,4},{6,7},{7,6},{8,9},{9,8},{10,11... | collective-permute-start | bytes 1572872 | tf_op jit(solution)/shard_map/ppermute | solution.py:166
  61.7 0.8 copy-start.3
  67.4 26.7 %all-to-all-start.1 = ((bf16[32,8,256]{2,1,0:T(8,128)(2,1)}), bf16[32,8,256]{2,1,0:T(8,128)(2,1)S(1)}, u32[]{:S(2)}, u32[]{:S(2)}) async-start(bf16[32,8,256]{2,1,0:T(8,128)(2,1)} %bitcast.18), calls=%async_computation.1 | async-start | bytes 262144 | tf_op jit(solution)/shard_map/all_to_all | solution.py:171
  85.0 56.0 %reduce-scatter.2.cloned.1.call-start = ((), (), s32[]{:S(2)}) async-start(), calls=%async_computation.3 | async-start | bytes 2359296 | tf_op jit(solution)/shard_map/reduce_scatter | solution.py:187
  94.0 3.2 %collective-permute-start.3 = (bf16[256,256]{1,0:T(8,128)(2,1)S(1)}, bf16[256,256]{1,0:T(8,128)(2,1)S(1)}, u32[]{:S(2)}, u32[]{:S(2)}) collective-permute-start(bf16[256,256]{1,0:T(8,128)(2,1)S(1)} %bitcast.28), channel_id=1, source_target_pairs={{0,1},{1,0},{2,3},{3,2},{4,5},{5,4},{6,7},{7,6},{8,9},{9,8},{10,11... | collective-permute-start | bytes 393224 | tf_op jit(solution)/shard_map/ppermute | solution.py:182
Sparse Core Ops, SparseCore 0:
  102.8 38.1 reduce-scatter.1
